TPU v7x, 512 devices: a whole 4x4x16 slice. The times are simulated.
512 devices in a mesh: seq: 64 (over x, z), head: 8 (over y, core).
Axes of the slice: x: 4, y: 4, z: 16, core: 2. Of those that a mesh axis runs over, the one named last changes fastest.
Arguments:
- tokens: bfloat16 [16384, 4096], P('seq', 'head'), may hold values from -40 to 40
- queries: bfloat16 [16384, 4096], P('seq', 'head'), may hold values from -6 to 6
- key_rows: bfloat16 [16384, 4096], P('seq', 'head'), may hold values from -6 to 6
- values: bfloat16 [16384, 4096], P('seq', 'head'), may hold values from -6 to 6
- log_decay: float32 [32, 16384], P('head', 'seq'), may hold values from -1 to 0
- head_gain: float32 [4096], P('head'), may hold values from 0.5 to 1.5
- expert_gain: float32 [4096], P('head'), may hold values from 0.5 to 1.5
- route_ids: int32 [16384, 2], P('seq'), may hold values from 0 to 31, all different within a row; in each aligned block of 256 rows (0 to 255, 256 to 511, ...) at most 20 rows name the same one
- route_weight: float32 [16384, 2], P('seq'), may hold values from 0.2 to 1
- expert_in: bfloat16 [64, 4096, 1408], P('seq', 'head'), may hold values from -0.09375 to 0.09375
- expert_out: bfloat16 [64, 704, 4096], P('seq', None, 'head'), may hold values from -0.15625 to 0.15625
Outputs:
- mixed: bfloat16 [16384, 4096], P('seq', 'head')
Inputs may be any that keep to these rules, and one draw needn't show every extreme that they name: `route_ids`: within the rows of one device (aligned blocks of 256 tokens) no expert is named by more than 20 tokens, a bound that some block reaches; a token's two experts differ.
All inputs are finite; a program needn't handle non-finite values.
Results may differ from a plain program's by a relative error of at most 0.015.
Values may be sent and summed in bfloat16 or wider, within the bound.
No kernel may reach another device: no remote copies, remote signals or barrier semaphores. Data moves between devices by JAX's collectives and lax.ppermute only.
A program may use at most 64 MiB of HBM per device.

v0:
```python
import jax
import jax.numpy as jnp
from jax import lax
from jax.sharding import PartitionSpec as P

D = 4096
EXPERTS = 32
CAP = 20


EPSILON = 1e-06


def entering_2(array, axis, join, neutral):
    place = lax.axis_index(axis)
    gathered = jax.tree.map(
        lambda a, kind: lax.all_gather(a.astype(kind), axis), array, (jnp.bfloat16, jnp.bfloat16)
    )
    state = jax.tree.map(lambda a, e: jnp.zeros_like(a) + jnp.asarray(e, a.dtype), array, neutral)

    def one(lap, state):
        return join(
            state,
            jax.tree.map(
                lambda a, own: lax.dynamic_index_in_dim(a, lap, 0, False).astype(own.dtype),
                gathered,
                array,
            ),
        )

    return lax.fori_loop(0, place, one, state)


def combine_states(earlier, latter):
    return (earlier[0] * latter[0], latter[0][:, None, None] * earlier[1] + latter[1])


def per_device(
    tokens,
    queries,
    key_rows,
    values,
    log_decay,
    head_gain,
    expert_gain,
    route_ids,
    route_weight,
    expert_in,
    expert_out,
):
    length = tokens.shape[0]
    local_width = tokens.shape[1]
    heads_here = log_decay.shape[0]
    head_size = queries.shape[1] // heads_here
    score_scale = head_size ** (-0.5)
    query_heads = queries.reshape(length, heads_here, head_size)
    key_heads = key_rows.reshape(length, heads_here, head_size)
    value_heads = values.reshape(length, heads_here, head_size)
    cumulative = jnp.cumsum(log_decay, axis=1)
    causal = (jnp.arange(length)[:, None] >= jnp.arange(length)[None, :])[None]
    scores = (
        jnp.einsum("thd,shd->hts", query_heads, key_heads, preferred_element_type=jnp.float32)
        * score_scale
    )
    spread = cumulative[:, :, None] - cumulative[:, None, :]
    mixing = jnp.where(causal, scores * jnp.exp(jnp.where(causal, spread, 0.0)), 0.0).astype(
        jnp.bfloat16
    )
    inside = jnp.einsum("hts,shd->thd", mixing, value_heads, preferred_element_type=jnp.float32)
    to_end = jnp.exp(cumulative[:, -1:] - cumulative)
    carried_keys = (key_heads.astype(jnp.float32) * to_end.T[:, :, None]).astype(jnp.bfloat16)
    block_state = jnp.einsum(
        "shd,she->hde", carried_keys, value_heads, preferred_element_type=jnp.float32
    )
    block_decay = jnp.exp(cumulative[:, -1])
    identity = (jnp.ones_like(block_decay), jnp.zeros_like(block_state))
    prefix = entering_2((block_decay, block_state), "seq", combine_states, identity)
    entering = prefix[1]
    from_before = jnp.einsum(
        "thd,hde->the",
        query_heads.astype(jnp.float32),
        entering,
        precision=lax.Precision.HIGHEST,
        preferred_element_type=jnp.float32,
    )
    attended = inside + from_before * (jnp.exp(cumulative).T[:, :, None] * score_scale)
    head_rms = lax.rsqrt(jnp.mean(attended * attended, axis=2, keepdims=True) + EPSILON)
    normed_heads = (attended * head_rms).reshape(length, local_width)
    hidden_state = (tokens.astype(jnp.float32) + normed_heads * head_gain).astype(jnp.bfloat16)
    hidden_wide = hidden_state.astype(jnp.float32)
    local_squares = jnp.sum(hidden_wide * hidden_wide, axis=1)
    total_squares = lax.psum(local_squares, "head")
    inverse_rms = lax.rsqrt(total_squares / D + EPSILON)
    expert_input = (hidden_wide * inverse_rms[:, None] * expert_gain).astype(jnp.bfloat16)
    capacity = CAP
    expert_count = EXPERTS
    flat_ids = route_ids.reshape(-1)
    pair_count = flat_ids.shape[0]
    chosen = (flat_ids[:, None] == jnp.arange(expert_count)[None, :]).astype(jnp.float32)
    strictly_before = (jnp.arange(pair_count)[:, None] > jnp.arange(pair_count)[None, :]).astype(
        jnp.float32
    )
    earlier_counts = jnp.dot(
        strictly_before, chosen, precision=lax.Precision.HIGHEST, preferred_element_type=jnp.float32
    )
    slot_index = jnp.sum(earlier_counts * chosen, axis=1).astype(jnp.int32)
    position = (flat_ids * capacity + slot_index).reshape(length, route_ids.shape[1])
    slot_ids = jnp.arange(expert_count * capacity, dtype=jnp.int32)
    picks = position[None, :, :] == slot_ids[:, None, None]
    dispatch_matrix = jnp.any(picks, axis=2).astype(jnp.bfloat16)
    send_rows = jnp.dot(dispatch_matrix, expert_input, preferred_element_type=jnp.float32).astype(
        jnp.bfloat16
    )
    hidden_split = expert_in.shape[0] * lax.axis_size("seq") // expert_count
    send_buffer = jnp.repeat(
        send_rows.reshape(expert_count, 1, capacity, local_width), hidden_split, axis=0
    )
    block_units = expert_out.shape[1]
    arrived = lax.all_to_all(send_buffer, "seq", split_axis=0, concat_axis=1, tiled=True)
    blocks_here, sources, item_count, feature_count = arrived.shape
    flat_rows = arrived.reshape(blocks_here, sources * item_count, feature_count)
    partial_sums = jnp.einsum(
        "erd,edh->erh", flat_rows, expert_in, preferred_element_type=jnp.float32
    )
    partial_sums = partial_sums.reshape(blocks_here, sources, item_count, 2, block_units)
    gate_up = lax.psum(partial_sums.astype(jnp.bfloat16), "head").astype(jnp.float32)
    activated = (jax.nn.silu(gate_up[:, :, :, 0]) * gate_up[:, :, :, 1]).astype(jnp.bfloat16)
    activated = activated.reshape(blocks_here, sources * item_count, block_units)
    produced = jnp.einsum(
        "erh,ehd->erd", activated, expert_out, preferred_element_type=jnp.float32
    ).astype(jnp.bfloat16)
    computed = produced.reshape(blocks_here, sources, item_count, feature_count)
    returned = lax.all_to_all(computed, "seq", split_axis=1, concat_axis=0, tiled=True)
    merged = jnp.sum(
        returned.reshape(expert_count, hidden_split, capacity, local_width).astype(jnp.float32),
        axis=1,
    )
    merged = merged.reshape(expert_count * capacity, local_width)
    slot_rows = merged[position]
    expert_mix = jnp.sum(slot_rows * route_weight[:, :, None], axis=1)
    return (hidden_wide + expert_mix).astype(jnp.bfloat16)


def solution(mesh):
    return jax.shard_map(
        per_device,
        mesh=mesh,
        in_specs=(
            P("seq", "head"),
            P("seq", "head"),
            P("seq", "head"),
            P("seq", "head"),
            P("head", "seq"),
            P("head"),
            P("head"),
            P("seq", None),
            P("seq", None),
            P("seq", "head", None),
            P("seq", None, "head"),
        ),
        out_specs=P("seq", "head"),
        check_vma=False,
    )
```

profile of v0, /device:TPU:6, one launch (start us, length us, event | category | flops | bytes accessed | tf_op | source)
XLA Modules:
  0.0 537.3 jit_solution(9276026053909076159)
XLA Ops:
  7.4 1.2 reduce-window.6
  9.2 1.1 copy.102
  10.3 1.8 convolution_convert_fusion.2
  12.2 1.2 dynamic-slice
  14.3 129.3 %all-reduce = bf16[256]{0:T(256)(128)(2,1)S(1)} all-reduce(bf16[256]{0:T(256)(128)(2,1)S(1)} %dynamic-update-slice), channel_id=2, replica_groups=mesh['seq'=64,'head'=8] {'seq'}, use_global_device_ids=true, to_apply=%add | all-reduce | flops 256 | bytes 1024
  146.1 26.3 %all-gather.4.cloned.1.call-done = bf16[256,128,128]{2,1,0:T(8,128)(2,1)} async-done(((bf16[4,128,128]{2,1,0:T(8,128)(2,1)}), bf16[256,128,128]{2,1,0:T(8,128)(2,1)}) %all-gather.4.cloned.1.call-update) | async-done | bytes 8388624 | tf_op jit(solution)/shard_map/all_gather | solution.py:17
  172.4 51.1 %while.12 = (s32[]{:T(128)}, f32[4,128,128]{2,1,0:T(8,128)S(1)}, s32[]{:T(128)}, bf16[64,4]{1,0:T(8,128)(2,1)S(1)}, bf16[64,4,128,128]{3,2,1,0:T(8,128)(2,1)}, /*index=5*/s32[]{:T(128)}, s32[]{:T(128)}, s32[]{:T(128)}) while((s32[]{:T(128)}, f32[4,128,128]{2,1,0:T(8,128)S(1)}, s32[]{:T(128)}, bf16[64,4]{1,0:T(8,128)(2,1)S(1)}, ...), condition=%wide.region_3.4_spmd, body=%wide.region_2.3_spmd.sunk | while | flops 196617 | bytes 655527 | solution.py:31
  172.4 1.0 convert_add_fusion.3
  173.5 1.0 convert_add_fusion.3
  174.6 1.0 convert_add_fusion.3
  175.6 1.0 convert_add_fusion.3
  176.7 1.0 convert_add_fusion.3
  177.8 1.0 convert_add_fusion.3
  178.8 1.0 convert_add_fusion.3
  179.9 1.0 convert_add_fusion.3
  184.1 1.0 convert_add_fusion.3
  188.4 1.0 convert_add_fusion.3
  189.5 1.0 convert_add_fusion.3
  193.7 1.0 convert_add_fusion.3
  194.8 1.0 convert_add_fusion.3
  199.0 1.0 convert_add_fusion.3
  200.1 1.0 convert_add_fusion.3
  204.4 1.0 convert_add_fusion.3
  208.6 1.0 convert_add_fusion.3
  209.7 1.0 convert_add_fusion.3
  213.9 1.0 convert_add_fusion.3
  215.0 1.0 convert_add_fusion.3
  219.2 1.0 convert_add_fusion.3
  220.3 1.0 convert_add_fusion.3
  224.6 12.4 %psum.14 = f32[256]{0:T(256)S(1)} all-reduce(f32[256]{0:T(256)S(1)} %get-tuple-element.62), channel_id=1, replica_groups=mesh['seq'=64,'head'=8] {'head'}, use_global_device_ids=true, to_apply=%region_8.9 | all-reduce | flops 256 | bytes 2048 | tf_op jit(solution)/shard_map/psum | solution.py:92
  237.6 1.3 broadcast_in_dim.50
  238.9 23.3 %all-to-all-start = ((bf16[64,1,20,512]{3,2,1,0:T(8,128)(2,1)}), bf16[64,1,20,512]{3,2,1,0:T(8,128)(2,1)S(1)}, u32[]{:S(2)}, u32[]{:S(2)}) async-start(bf16[64,1,20,512]{3,2,1,0:T(8,128)(2,1)} %bitcast.12), calls=%async_computation | async-start | bytes 3145728 | tf_op jit(solution)/shard_map/all_to_all | solution.py:119
  262.3 2.5 copy.94
  264.8 73.6 %all-to-all-done = bf16[64,1,20,512]{3,2,1,0:T(8,128)(2,1)S(1)} async-done(((bf16[64,1,20,512]{3,2,1,0:T(8,128)(2,1)}), bf16[64,1,20,512]{3,2,1,0:T(8,128)(2,1)S(1)}, u32[]{:S(2)}, u32[]{:S(2)}) %all-to-all-start) | async-done | bytes 1310752 | tf_op jit(solution)/shard_map/all_to_all | solution.py:119
  338.4 5.5 %convert_bitcast_fusion = bf16[1,64,20,2,704]{4,1,3,2,0:T(8,128)(2,1)} fusion(bf16[2,704,512,1]{2,1,0,3:T(8,128)(2,1)} %bitcast.99, bf16[64,1,20,512]{3,2,1,0:T(8,128)(2,1)S(1)} %all-to-all-done), kind=kOutput, calls=%fused_computation.5 | convolution fusion | flops 1847296000 | bytes 6356992 | tf_op jit(solution)/shard_map/erd,edh->erh/dot_general | solution.py:122
  343.9 77.2 %all-reduce.3.cloned.1.call-done = bf16[1,64,20,2,704]{4,1,3,2,0:T(8,128)(2,1)} async-done(((bf16[1,64,20,2,704]{4,1,3,2,0:T(8,128)(2,1)}), bf16[1,64,20,2,704]{4,1,3,2,0:T(8,128)(2,1)}) %all-reduce.3.cloned.1.call-update) | async-done | bytes 3604496 | tf_op jit(solution)/shard_map/psum | solution.py:126
  421.1 3.1 convert_element_type.122
  424.2 1.3 fusion
  425.5 1.1 copy.95
  426.6 2.2 convert_element_type.124
  428.8 2.7 convolution_convert_fusion
  431.6 1.3 reshape.186
  432.9 16.0 %all-to-all-start.1 = ((bf16[1,64,20,512]{3,2,0,1:T(8,128)(2,1)}), bf16[1,64,20,512]{3,2,0,1:T(8,128)(2,1)S(1)}, u32[]{:S(2)}, u32[]{:S(2)}) async-start(bf16[1,64,20,512]{3,2,0,1:T(8,128)(2,1)} %bitcast.97), calls=%async_computation.1 | async-start | bytes 3145728 | tf_op jit(solution)/shard_map/all_to_all | solution.py:133
  449.4 73.8 %all-to-all-done.1 = bf16[1,64,20,512]{3,2,0,1:T(8,128)(2,1)S(1)} async-done(((bf16[1,64,20,512]{3,2,0,1:T(8,128)(2,1)}), bf16[1,64,20,512]{3,2,0,1:T(8,128)(2,1)S(1)}, u32[]{:S(2)}, u32[]{:S(2)}) %all-to-all-start.1) | async-done | bytes 1310752 | tf_op jit(solution)/shard_map/all_to_all | solution.py:133
  523.1 1.4 convert_reduce_fusion
  524.6 1.5 reshape.187
  526.1 1.6 gather_fusion
  528.3 1.3 multiply_reduce_fusion
  (138 shorter events, 34.7 us)
Async XLA Ops:
  6.5 422.3 %copy-start = (bf16[1,704,512]{2,1,0:T(8,128)(2,1)S(1)}, bf16[1,704,512]{2,1,0:T(8,128)(2,1)}, u32[]{:S(2)}) copy-start(bf16[1,704,512]{2,1,0:T(8,128)(2,1)} %param.23) | copy-start | bytes 2162692
  6.5 139.0 %copy-start.8 = (bf16[256,512]{1,0:T(8,128)(2,1)S(1)}, bf16[256,512]{1,0:T(8,128)(2,1)}, u32[]{:S(2)}) copy-start(bf16[256,512]{1,0:T(8,128)(2,1)} %param.16) | copy-start | bytes 786436
  6.5 138.7 %copy-start.5 = (s32[256,2]{0,1:T(2,128)S(1)}, s32[256,2]{0,1:T(2,128)}, u32[]{:S(2)}) copy-start(s32[256,2]{0,1:T(2,128)} %param.20) | copy-start | bytes 6148
  6.5 139.0 %copy-start.4 = (bf16[256,512]{1,0:T(8,128)(2,1)S(1)}, bf16[256,512]{1,0:T(8,128)(2,1)}, u32[]{:S(2)}) copy-start(bf16[256,512]{1,0:T(8,128)(2,1)} %param.14) | copy-start | bytes 786436
  6.5 165.8 %all-gather.4.cloned.1.call-start = ((), (), s32[]{:S(2)}) async-start(), calls=%async_computation.3 | async-start | bytes 8519680 | tf_op jit(solution)/shard_map/all_gather | solution.py:17
  223.5 1.0 copy-start.3
  223.5 0.9 copy-start.6
  224.0 13.1 %copy-start.9 = (f32[512]{0:T(512)S(1)}, f32[512]{0:T(512)}, u32[]{:S(2)}) copy-start(f32[512]{0:T(512)} %param.19) | copy-start | bytes 6148
  224.6 12.4 %copy-start.1 = (bf16[256,512]{1,0:T(8,128)(2,1)}, bf16[256,512]{1,0:T(8,128)(2,1)S(1)}, u32[]{:S(2)}) copy-start(bf16[256,512]{1,0:T(8,128)(2,1)S(1)} %get-tuple-element.63) | copy-start | bytes 786436
  238.9 99.5 %all-to-all-start = ((bf16[64,1,20,512]{3,2,1,0:T(8,128)(2,1)}), bf16[64,1,20,512]{3,2,1,0:T(8,128)(2,1)S(1)}, u32[]{:S(2)}, u32[]{:S(2)}) async-start(bf16[64,1,20,512]{3,2,1,0:T(8,128)(2,1)} %bitcast.12), calls=%async_computation | async-start | bytes 3145728 | tf_op jit(solution)/shard_map/all_to_all | solution.py:119
  262.2 158.9 %all-reduce.3.cloned.1.call-start = ((), (), s32[]{:S(2)}) async-start(), calls=%async_computation.2 | async-start | bytes 7864320 | tf_op jit(solution)/shard_map/psum | solution.py:126
  432.9 16.3 %copy-start.7 = (f32[256,2]{0,1:T(2,128)S(1)}, f32[256,2]{0,1:T(2,128)}, u32[]{:S(2)}) copy-start(f32[256,2]{0,1:T(2,128)} %param.21) | copy-start | bytes 6148
  432.9 90.3 %all-to-all-start.1 = ((bf16[1,64,20,512]{3,2,0,1:T(8,128)(2,1)}), bf16[1,64,20,512]{3,2,0,1:T(8,128)(2,1)S(1)}, u32[]{:S(2)}, u32[]{:S(2)}) async-start(bf16[1,64,20,512]{3,2,0,1:T(8,128)(2,1)} %bitcast.97), calls=%async_computation.1 | async-start | bytes 3145728 | tf_op jit(solution)/shard_map/all_to_all | solution.py:133
  527.7 2.0 copy-start.2
Sparse Core Ops, SparseCore 0:
  12.3 160.0 all-gather.3
  344.0 77.0 all-reduce.2
where the time goes:
time: 539 us; the launch traced here: 537 us
  waiting for transfers between devices  251 us (47%)
  blocking collectives  142 us (26%)
  other arithmetic  59.3 us (11%)
  starting transfers between devices  39.4 us (7%)
  local copies, waits for them, and re-layouts  18.2 us (3%)
  between operations  14.3 us (3%)
  matrix products  11.8 us (2%)
    unnamed x1, blocking collectives  129 us
    psum x1, waiting for transfers between devices, per_device(): lax.psum(partial_sums.astype(jnp.bfloat16), 'head').astype(jnp.float32)  77.2 us
    all_to_all x1, waiting for transfers between devices, per_device(): lax.all_to_all(computed, 'seq', split_axis=1, concat_axis=0, tiled=True)  73.8 us
    all_to_all x1, waiting for transfers between devices, per_device(): lax.all_to_all(send_buffer, 'seq', split_axis=0, concat_axis=1, tiled=True)  73.6 us
    add x48, other arithmetic, combine_states(): latter[0][:, None, None] * earlier[1] + latter[1]  48.9 us
    all_gather x1, waiting for transfers between devices, entering_2(): lax.all_gather(a.astype(kind), axis)  26.3 us
    all_to_all x1, starting transfers between devices, per_device(): lax.all_to_all(send_buffer, 'seq', split_axis=0, concat_axis=1, tiled=True)  23.3 us
    all_to_all x1, starting transfers between devices, per_device(): lax.all_to_all(computed, 'seq', split_axis=1, concat_axis=0, tiled=True)  16 us
  transfers between devices with their start and end apart: 4, of which 4 were waited for; matrix products, arithmetic and copies ran while one was open for 1% of the time, Pallas kernels for 0%

commit v1 on v0

--- a/solution.py
+++ b/solution.py
@@ -11,28 +11,34 @@
 EPSILON = 1e-06
 
 
-def entering_2(array, axis, join, neutral):
+def exclusive_scan(decay, state, axis):
     place = lax.axis_index(axis)
-    gathered = jax.tree.map(
-        lambda a, kind: lax.all_gather(a.astype(kind), axis), array, (jnp.bfloat16, jnp.bfloat16)
+    count = lax.axis_size(axis)
+    heads, rows, cols = state.shape
+    own = jnp.concatenate(
+        [state, jnp.broadcast_to(decay[:, None, None], (heads, 1, cols))], axis=1
     )
-    state = jax.tree.map(lambda a, e: jnp.zeros_like(a) + jnp.asarray(e, a.dtype), array, neutral)
-
-    def one(lap, state):
-        return join(
-            state,
-            jax.tree.map(
-                lambda a, own: lax.dynamic_index_in_dim(a, lap, 0, False).astype(own.dtype),
-                gathered,
-                array,
-            ),
+    window = own
+    before_decay = jnp.ones_like(decay)
+    before_state = jnp.zeros_like(state)
+    shift = 1
+    while shift < count:
+        pairs = [(j, j + shift) for j in range(count - shift)]
+        got = lax.ppermute(window, axis, pairs)
+        valid = place >= shift
+        got_state = got[:, :rows, :]
+        got_decay = jnp.where(valid, got[:, rows, 0], 1.0)
+        before_state = before_decay[:, None, None] * got_state + before_state
+        before_decay = before_decay * got_decay
+        window_decay = window[:, rows, 0]
+        window_state = window_decay[:, None, None] * got_state + window[:, :rows, :]
+        window_decay = window_decay * got_decay
+        window = jnp.concatenate(
+            [window_state, jnp.broadcast_to(window_decay[:, None, None], (heads, 1, cols))],
+            axis=1,
         )
-
-    return lax.fori_loop(0, place, one, state)
-
-
-def combine_states(earlier, latter):
-    return (earlier[0] * latter[0], latter[0][:, None, None] * earlier[1] + latter[1])
+        shift *= 2
+    return before_state
 
 
 def per_device(
@@ -73,9 +79,7 @@
         "shd,she->hde", carried_keys, value_heads, preferred_element_type=jnp.float32
     )
     block_decay = jnp.exp(cumulative[:, -1])
-    identity = (jnp.ones_like(block_decay), jnp.zeros_like(block_state))
-    prefix = entering_2((block_decay, block_state), "seq", combine_states, identity)
-    entering = prefix[1]
+    entering = exclusive_scan(block_decay, block_state, "seq")
     from_before = jnp.einsum(
         "thd,hde->the",
         query_heads.astype(jnp.float32),

time: 539 us -> 434 us (0.81)
  blocking collectives: 142 us -> 13.2 us
  waiting for transfers between devices: 251 us -> 323 us
  other arithmetic: 59.3 us -> 12.4 us
    unnamed x1 -> x0, blocking collectives: 129 us -> none
    ppermute x0 -> x6, waiting for transfers between devices: none -> 98.3 us  [exclusive_scan(): got = lax.ppermute(window, axis, pairs)]
    add x48 -> x5, other arithmetic: 48.9 us -> 0.47 us  [exclusive_scan(): window_state = window_decay[:, None, None] * got_state + window[:, :rows, :]]
    all_gather x1 -> x0, waiting for transfers between devices: 26.3 us -> none  [entering_2(): lax.all_gather(a.astype(kind), axis)]
    ppermute x0 -> x6, starting transfers between devices: none -> 12.2 us  [exclusive_scan(): got = lax.ppermute(window, axis, pairs)]
    all_to_all x1, starting transfers between devices: 23.3 us -> 12.6 us  [per_device(): lax.all_to_all(send_buffer, 'seq', split_axis=0, concat_axis=1, tiled=True)]
  transfers between devices with their start and end apart: 4 -> 9, of which waited for: 4 -> 9; matrix products, arithmetic and copies ran while one was open for 1% -> 1% of each run, Pallas kernels for 0% -> 0%
where the time goes in v1:
time: 434 us
  waiting for transfers between devices  323 us (74%)
  starting transfers between devices  41 us (9%)
  local copies, waits for them, and re-layouts  16.9 us (4%)
  between operations  13.9 us (3%)
  matrix products  13.3 us (3%)
  blocking collectives  13.2 us (3%)
  other arithmetic  12.4 us (3%)
    ppermute x6, waiting for transfers between devices, exclusive_scan(): got = lax.ppermute(window, axis, pairs)  98.3 us
    psum x1, waiting for transfers between devices, per_device(): lax.psum(partial_sums.astype(jnp.bfloat16), 'head').astype(jnp.float32)  77.2 us
    all_to_all x1, waiting for transfers between devices, per_device(): lax.all_to_all(computed, 'seq', split_axis=1, concat_axis=0, tiled=True)  73.8 us
    all_to_all x1, waiting for transfers between devices, per_device(): lax.all_to_all(send_buffer, 'seq', split_axis=0, concat_axis=1, tiled=True)  73.5 us
    all_to_all x1, starting transfers between devices, per_device(): lax.all_to_all(computed, 'seq', split_axis=1, concat_axis=0, tiled=True)  16 us
    psum x1, blocking collectives, per_device(): total_squares = lax.psum(local_squares, 'head')  13.2 us
    all_to_all x1, starting transfers between devices, per_device(): lax.all_to_all(send_buffer, 'seq', split_axis=0, concat_axis=1, tiled=True)  12.6 us
    ppermute x6, starting transfers between devices, exclusive_scan(): got = lax.ppermute(window, axis, pairs)  12.2 us
  transfers between devices with their start and end apart: 9, of which 9 were waited for; matrix products, arithmetic and copies ran while one was open for 1% of the time, Pallas kernels for 0%

profile of v1, /device:TPU:6, one launch (start us, length us, event | category | flops | bytes accessed | tf_op | source)
XLA Modules:
  0.0 433.5 jit_solution(4045963600680185097)
XLA Ops:
  6.5 0.8 reshape.241
  7.3 1.2 reduce-window.6
  9.2 1.1 copy.107
  10.3 1.2 fusion.25
  11.5 3.8 collective-permute-start
  15.4 14.5 %collective-permute-done = f32[4,129,128]{2,1,0:T(8,128)S(1)} collective-permute-done((f32[4,129,128]{2,1,0:T(8,128)S(1)}, f32[4,129,128]{2,1,0:T(8,128)S(1)}, u32[]{:S(2)}, u32[]{:S(2)}) %collective-permute-start) | collective-permute-done | bytes 264224 | tf_op jit(solution)/shard_map/ppermute | solution.py:27
  30.2 1.9 collective-permute-start.1
  32.2 16.2 %collective-permute-done.1 = f32[4,129,128]{2,1,0:T(8,128)S(1)} collective-permute-done((f32[4,129,128]{2,1,0:T(8,128)S(1)}, f32[4,129,128]{2,1,0:T(8,128)S(1)}, u32[]{:S(2)}, u32[]{:S(2)}) %collective-permute-start.1) | collective-permute-done | bytes 264224 | tf_op jit(solution)/shard_map/ppermute | solution.py:27
  48.7 1.9 collective-permute-start.2
  50.7 26.8 %collective-permute-done.2 = f32[4,129,128]{2,1,0:T(8,128)S(1)} collective-permute-done((f32[4,129,128]{2,1,0:T(8,128)S(1)}, f32[4,129,128]{2,1,0:T(8,128)S(1)}, u32[]{:S(2)}, u32[]{:S(2)}) %collective-permute-start.2) | collective-permute-done | bytes 264224 | tf_op jit(solution)/shard_map/ppermute | solution.py:27
  77.8 1.9 collective-permute-start.3
  79.9 0.1 eq.28
  80.0 0.3 fusion.11
  80.5 24.3 %collective-permute-done.3 = f32[4,129,128]{2,1,0:T(8,128)S(1)} collective-permute-done((f32[4,129,128]{2,1,0:T(8,128)S(1)}, f32[4,129,128]{2,1,0:T(8,128)S(1)}, u32[]{:S(2)}, u32[]{:S(2)}) %collective-permute-start.3) | collective-permute-done | bytes 264224 | tf_op jit(solution)/shard_map/ppermute | solution.py:27
  105.2 1.3 collective-permute-start.4
  106.5 0.9 fusion.5
  107.4 8.2 %collective-permute-done.4 = f32[4,129,128]{2,1,0:T(8,128)S(1)} collective-permute-done((f32[4,129,128]{2,1,0:T(8,128)S(1)}, f32[4,129,128]{2,1,0:T(8,128)S(1)}, u32[]{:S(2)}, u32[]{:S(2)}) %collective-permute-start.4) | collective-permute-done | bytes 264224 | tf_op jit(solution)/shard_map/ppermute | solution.py:27
  115.9 0.7 pad_maximum_fusion.5
  116.6 1.3 collective-permute-start.5
  117.9 1.6 fusion.8
  119.6 8.4 %collective-permute-done.5 = f32[4,129,128]{2,1,0:T(8,128)} collective-permute-done((f32[4,129,128]{2,1,0:T(8,128)}, f32[4,129,128]{2,1,0:T(8,128)}, u32[]{:S(2)}, u32[]{:S(2)}) %collective-permute-start.5) | collective-permute-done | bytes 264224 | tf_op jit(solution)/shard_map/ppermute | solution.py:27
  127.9 1.5 multiply_reduce_fusion.1
  129.6 0.2 copy.95
  129.8 0.6 copy-done.3
  130.4 0.2 fusion.16
  130.6 13.2 %psum.14 = f32[256]{0:T(256)S(1)} all-reduce(f32[256]{0:T(256)S(1)} %get-tuple-element.16), channel_id=1, replica_groups=mesh['seq'=64,'head'=8] {'head'}, use_global_device_ids=true, to_apply=%region_6.7 | all-reduce | flops 256 | bytes 2048 | tf_op jit(solution)/shard_map/psum | solution.py:96
  143.8 0.4 convolution_convert_fusion.1
  144.4 1.3 broadcast_in_dim.56
  145.7 12.6 %all-to-all-start = ((bf16[64,1,20,512]{3,2,1,0:T(8,128)(2,1)}), bf16[64,1,20,512]{3,2,1,0:T(8,128)(2,1)S(1)}, u32[]{:S(2)}, u32[]{:S(2)}) async-start(bf16[64,1,20,512]{3,2,1,0:T(8,128)(2,1)} %bitcast.8), calls=%async_computation | async-start | bytes 3145728 | tf_op jit(solution)/shard_map/all_to_all | solution.py:123
  158.3 0.2 all-reduce.2.cloned.1.call-start
  158.6 2.5 copy.99
  161.1 73.5 %all-to-all-done = bf16[64,1,20,512]{3,2,1,0:T(8,128)(2,1)S(1)} async-done(((bf16[64,1,20,512]{3,2,1,0:T(8,128)(2,1)}), bf16[64,1,20,512]{3,2,1,0:T(8,128)(2,1)S(1)}, u32[]{:S(2)}, u32[]{:S(2)}) %all-to-all-start) | async-done | bytes 1310752 | tf_op jit(solution)/shard_map/all_to_all | solution.py:123
  234.6 5.5 %convert_bitcast_fusion = bf16[1,64,20,2,704]{4,1,3,2,0:T(8,128)(2,1)} fusion(bf16[2,704,512,1]{2,1,0,3:T(8,128)(2,1)} %bitcast.89, bf16[64,1,20,512]{3,2,1,0:T(8,128)(2,1)S(1)} %all-to-all-done), kind=kOutput, calls=%fused_computation.3 | convolution fusion | flops 1847296000 | bytes 6356992 | tf_op jit(solution)/shard_map/erd,edh->erh/dot_general | solution.py:126
  240.1 77.2 %all-reduce.2.cloned.1.call-done = bf16[1,64,20,2,704]{4,1,3,2,0:T(8,128)(2,1)} async-done(((bf16[1,64,20,2,704]{4,1,3,2,0:T(8,128)(2,1)}), bf16[1,64,20,2,704]{4,1,3,2,0:T(8,128)(2,1)}) %all-reduce.2.cloned.1.call-update) | async-done | bytes 3604496 | tf_op jit(solution)/shard_map/psum | solution.py:130
  317.3 3.1 convert_element_type.85
  320.4 1.3 fusion
  321.7 1.1 copy.100
  322.8 2.2 convert_element_type.87
  325.0 2.7 convolution_convert_fusion
  327.8 1.3 reshape.248
  329.1 16.0 %all-to-all-start.1 = ((bf16[1,64,20,512]{3,2,0,1:T(8,128)(2,1)}), bf16[1,64,20,512]{3,2,0,1:T(8,128)(2,1)S(1)}, u32[]{:S(2)}, u32[]{:S(2)}) async-start(bf16[1,64,20,512]{3,2,0,1:T(8,128)(2,1)} %bitcast.87), calls=%async_computation.1 | async-start | bytes 3145728 | tf_op jit(solution)/shard_map/all_to_all | solution.py:137
  345.6 73.8 %all-to-all-done.1 = bf16[1,64,20,512]{3,2,0,1:T(8,128)(2,1)S(1)} async-done(((bf16[1,64,20,512]{3,2,0,1:T(8,128)(2,1)}), bf16[1,64,20,512]{3,2,0,1:T(8,128)(2,1)S(1)}, u32[]{:S(2)}, u32[]{:S(2)}) %all-to-all-start.1) | async-done | bytes 1310752 | tf_op jit(solution)/shard_map/all_to_all | solution.py:137
  419.4 1.4 convert_reduce_fusion
  420.8 1.5 reshape.249
  422.3 1.6 gather_fusion
  423.9 0.6 reshape.252
  424.5 1.3 multiply_reduce_fusion
  425.9 0.8 fusion.19
  (72 shorter events, 3.4 us)
Async XLA Ops:
  6.5 318.5 %copy-start = (bf16[1,704,512]{2,1,0:T(8,128)(2,1)S(1)}, bf16[1,704,512]{2,1,0:T(8,128)(2,1)}, u32[]{:S(2)}) copy-start(bf16[1,704,512]{2,1,0:T(8,128)(2,1)} %param.21) | copy-start | bytes 2162692
  11.5 18.3 %collective-permute-start = (f32[4,129,128]{2,1,0:T(8,128)S(1)}, f32[4,129,128]{2,1,0:T(8,128)S(1)}, u32[]{:S(2)}, u32[]{:S(2)}) collective-permute-start(f32[4,129,128]{2,1,0:T(8,128)S(1)} %pad_maximum_fusion), channel_id=1, source_target_pairs={{0,8},{8,16},{16,24},{24,32},{32,40},{40,48},{48,56},{56,64},{64,7... | collective-permute-start | bytes 792584 | tf_op jit(solution)/shard_map/ppermute | solution.py:27
  30.0 49.8 %copy-start.6 = (s32[256,2]{0,1:T(2,128)S(1)}, s32[256,2]{0,1:T(2,128)}, u32[]{:S(2)}) copy-start(s32[256,2]{0,1:T(2,128)} %param.18) | copy-start | bytes 6148
  30.2 18.2 %collective-permute-start.1 = (f32[4,129,128]{2,1,0:T(8,128)S(1)}, f32[4,129,128]{2,1,0:T(8,128)S(1)}, u32[]{:S(2)}, u32[]{:S(2)}) collective-permute-start(f32[4,129,128]{2,1,0:T(8,128)S(1)} %pad_maximum_fusion.1), channel_id=1, source_target_pairs={{0,16},{8,24},{16,32},{24,40},{32,48},{40,56},{48,64},{56,72},{64,... | collective-permute-start | bytes 792584 | tf_op jit(solution)/shard_map/ppermute | solution.py:27
  48.7 28.8 %collective-permute-start.2 = (f32[4,129,128]{2,1,0:T(8,128)S(1)}, f32[4,129,128]{2,1,0:T(8,128)S(1)}, u32[]{:S(2)}, u32[]{:S(2)}) collective-permute-start(f32[4,129,128]{2,1,0:T(8,128)S(1)} %pad_maximum_fusion.2), channel_id=1, source_target_pairs={{0,32},{8,40},{16,48},{24,56},{32,64},{40,72},{48,80},{56,88},{64,... | collective-permute-start | bytes 792584 | tf_op jit(solution)/shard_map/ppermute | solution.py:27
  77.8 27.1 %collective-permute-start.3 = (f32[4,129,128]{2,1,0:T(8,128)S(1)}, f32[4,129,128]{2,1,0:T(8,128)S(1)}, u32[]{:S(2)}, u32[]{:S(2)}) collective-permute-start(f32[4,129,128]{2,1,0:T(8,128)S(1)} %pad_maximum_fusion.3), channel_id=1, source_target_pairs={{0,64},{8,72},{16,80},{24,88},{32,96},{40,104},{48,112},{56,120},{... | collective-permute-start | bytes 792584 | tf_op jit(solution)/shard_map/ppermute | solution.py:27
  105.2 10.4 %collective-permute-start.4 = (f32[4,129,128]{2,1,0:T(8,128)S(1)}, f32[4,129,128]{2,1,0:T(8,128)S(1)}, u32[]{:S(2)}, u32[]{:S(2)}) collective-permute-start(f32[4,129,128]{2,1,0:T(8,128)S(1)} %pad_maximum_fusion.4), channel_id=1, source_target_pairs={{0,128},{8,136},{16,144},{24,152},{32,160},{40,168},{48,176},{56,1... | collective-permute-start | bytes 792584 | tf_op jit(solution)/shard_map/ppermute | solution.py:27
  115.8 12.1 %copy-start.4 = (bf16[256,512]{1,0:T(8,128)(2,1)S(1)}, bf16[256,512]{1,0:T(8,128)(2,1)}, u32[]{:S(2)}) copy-start(bf16[256,512]{1,0:T(8,128)(2,1)} %param.12) | copy-start | bytes 786436
  116.6 11.3 %collective-permute-start.5 = (f32[4,129,128]{2,1,0:T(8,128)}, f32[4,129,128]{2,1,0:T(8,128)}, u32[]{:S(2)}, u32[]{:S(2)}) collective-permute-start(f32[4,129,128]{2,1,0:T(8,128)} %pad_maximum_fusion.5), channel_id=1, source_target_pairs={{0,256},{8,264},{16,272},{24,280},{32,288},{40,296},{48,304},{56,3... | collective-permute-start | bytes 792584 | tf_op jit(solution)/shard_map/ppermute | solution.py:27
  127.9 1.8 copy-start.7
  129.5 1.0 copy-start.3
  129.5 14.3 %copy-start.5 = (pred[640,256]{1,0:T(8,128)(4,1)S(1)}, pred[640,256]{1,0:T(8,128)(4,1)}, u32[]{:S(2)}) copy-start(pred[640,256]{1,0:T(8,128)(4,1)} %fusion.5) | copy-start | bytes 491524
  129.5 14.3 %copy-start.9 = (f32[512]{0:T(512)S(1)}, f32[512]{0:T(512)}, u32[]{:S(2)}) copy-start(f32[512]{0:T(512)} %param.17) | copy-start | bytes 6148
  130.6 13.2 %copy-start.1 = (bf16[256,512]{1,0:T(8,128)(2,1)}, bf16[256,512]{1,0:T(8,128)(2,1)S(1)}, u32[]{:S(2)}) copy-start(bf16[256,512]{1,0:T(8,128)(2,1)S(1)} %get-tuple-element.17) | copy-start | bytes 786436
  145.7 88.9 %all-to-all-start = ((bf16[64,1,20,512]{3,2,1,0:T(8,128)(2,1)}), bf16[64,1,20,512]{3,2,1,0:T(8,128)(2,1)S(1)}, u32[]{:S(2)}, u32[]{:S(2)}) async-start(bf16[64,1,20,512]{3,2,1,0:T(8,128)(2,1)} %bitcast.8), calls=%async_computation | async-start | bytes 3145728 | tf_op jit(solution)/shard_map/all_to_all | solution.py:123
  158.3 159.0 %all-reduce.2.cloned.1.call-start = ((), (), s32[]{:S(2)}) async-start(), calls=%async_computation.2 | async-start | bytes 7864320 | tf_op jit(solution)/shard_map/psum | solution.py:130
  329.1 16.3 %copy-start.8 = (f32[256,2]{0,1:T(2,128)S(1)}, f32[256,2]{0,1:T(2,128)}, u32[]{:S(2)}) copy-start(f32[256,2]{0,1:T(2,128)} %param.19) | copy-start | bytes 6148
  329.1 90.3 %all-to-all-start.1 = ((bf16[1,64,20,512]{3,2,0,1:T(8,128)(2,1)}), bf16[1,64,20,512]{3,2,0,1:T(8,128)(2,1)S(1)}, u32[]{:S(2)}, u32[]{:S(2)}) async-start(bf16[1,64,20,512]{3,2,0,1:T(8,128)(2,1)} %bitcast.87), calls=%async_computation.1 | async-start | bytes 3145728 | tf_op jit(solution)/shard_map/all_to_all | solution.py:137
  423.9 2.0 copy-start.2
Sparse Core Ops, SparseCore 0:
  240.2 77.0 all-reduce.1

commit v2 on v1

--- a/solution.py
+++ b/solution.py
@@ -6,6 +6,7 @@
 D = 4096
 EXPERTS = 32
 CAP = 20
+CHUNKS = ((0, 10), (10, 20))
 
 
 EPSILON = 1e-06
@@ -120,25 +121,38 @@
         send_rows.reshape(expert_count, 1, capacity, local_width), hidden_split, axis=0
     )
     block_units = expert_out.shape[1]
-    arrived = lax.all_to_all(send_buffer, "seq", split_axis=0, concat_axis=1, tiled=True)
-    blocks_here, sources, item_count, feature_count = arrived.shape
-    flat_rows = arrived.reshape(blocks_here, sources * item_count, feature_count)
-    partial_sums = jnp.einsum(
-        "erd,edh->erh", flat_rows, expert_in, preferred_element_type=jnp.float32
-    )
-    partial_sums = partial_sums.reshape(blocks_here, sources, item_count, 2, block_units)
-    gate_up = lax.psum(partial_sums.astype(jnp.bfloat16), "head").astype(jnp.float32)
-    activated = (jax.nn.silu(gate_up[:, :, :, 0]) * gate_up[:, :, :, 1]).astype(jnp.bfloat16)
-    activated = activated.reshape(blocks_here, sources * item_count, block_units)
-    produced = jnp.einsum(
-        "erh,ehd->erd", activated, expert_out, preferred_element_type=jnp.float32
-    ).astype(jnp.bfloat16)
-    computed = produced.reshape(blocks_here, sources, item_count, feature_count)
-    returned = lax.all_to_all(computed, "seq", split_axis=1, concat_axis=0, tiled=True)
-    merged = jnp.sum(
-        returned.reshape(expert_count, hidden_split, capacity, local_width).astype(jnp.float32),
-        axis=1,
-    )
+    pieces = []
+    earlier = None
+    for lo, hi in CHUNKS:
+        arrived = lax.all_to_all(
+            send_buffer[:, :, lo:hi], "seq", split_axis=0, concat_axis=1, tiled=True
+        )
+        blocks_here, sources, item_count, feature_count = arrived.shape
+        flat_rows = arrived.reshape(blocks_here, sources * item_count, feature_count)
+        partial_sums = jnp.einsum(
+            "erd,edh->erh", flat_rows, expert_in, preferred_element_type=jnp.float32
+        )
+        partial_sums = partial_sums.reshape(blocks_here, sources, item_count, 2, block_units)
+        if earlier is not None:
+            partial_sums, earlier = lax.optimization_barrier((partial_sums, earlier))
+        gate_up = lax.psum(partial_sums.astype(jnp.bfloat16), "head").astype(jnp.float32)
+        earlier = gate_up
+        activated = (jax.nn.silu(gate_up[:, :, :, 0]) * gate_up[:, :, :, 1]).astype(jnp.bfloat16)
+        activated = activated.reshape(blocks_here, sources * item_count, block_units)
+        produced = jnp.einsum(
+            "erh,ehd->erd", activated, expert_out, preferred_element_type=jnp.float32
+        ).astype(jnp.bfloat16)
+        computed = produced.reshape(blocks_here, sources, item_count, feature_count)
+        returned = lax.all_to_all(computed, "seq", split_axis=1, concat_axis=0, tiled=True)
+        pieces.append(
+            jnp.sum(
+                returned.reshape(expert_count, hidden_split, item_count, local_width).astype(
+                    jnp.float32
+                ),
+                axis=1,
+            )
+        )
+    merged = jnp.concatenate(pieces, axis=1)
     merged = merged.reshape(expert_count * capacity, local_width)
     slot_rows = merged[position]
     expert_mix = jnp.sum(slot_rows * route_weight[:, :, None], axis=1)

time: 434 us -> 503 us (1.16)
  blocking collectives: 13.2 us -> 79.6 us
  waiting for transfers between devices: 323 us -> 308 us
  starting transfers between devices: 41 us -> 51.3 us
    psum x1 -> x2, waiting for transfers between devices: 77.2 us -> 160 us  [per_device(): lax.psum(partial_sums.astype(jnp.bfloat16), 'head').astype(jnp.float32)]
    all_to_all x1, waiting for transfers between devices: 73.5 us -> 0.01 us  [per_device(): lax.all_to_all(send_buffer[:, :, lo:hi], 'seq', split_axis=0, concat_axis...]
    all_to_all x0 -> x1, blocking collectives: none -> 66.4 us  [per_device(): lax.all_to_all(send_buffer[:, :, lo:hi], 'seq', split_axis=0, concat_axis...]
    all_to_all x1 -> x2, waiting for transfers between devices: 73.8 us -> 50.1 us  [per_device(): lax.all_to_all(computed, 'seq', split_axis=1, concat_axis=0, tiled=True)]
    all_to_all x1 -> x2, starting transfers between devices: 16 us -> 32 us  [per_device(): lax.all_to_all(computed, 'seq', split_axis=1, concat_axis=0, tiled=True)]
    all_to_all x1, starting transfers between devices: 12.6 us -> 7.02 us  [per_device(): lax.all_to_all(send_buffer[:, :, lo:hi], 'seq', split_axis=0, concat_axis...]
  transfers between devices with their start and end apart: 9 -> 11, of which waited for: 9 -> 9; matrix products, arithmetic and copies ran while one was open for 1% -> 5% of each run, Pallas kernels for 0% -> 0%
where the time goes in v2:
time: 503 us; the launch traced here: 501 us
  waiting for transfers between devices  308 us (61%)
  blocking collectives  79.6 us (16%)
  starting transfers between devices  51.3 us (10%)
  local copies, waits for them, and re-layouts  17.3 us (3%)
  matrix products  15.4 us (3%)
  other arithmetic  15 us (3%)
  between operations  14 us (3%)
    psum x2, waiting for transfers between devices, per_device(): lax.psum(partial_sums.astype(jnp.bfloat16), 'head').astype(jnp.float32)  160 us
    ppermute x6, waiting for transfers between devices, exclusive_scan(): got = lax.ppermute(window, axis, pairs)  98.3 us
    all_to_all x1, blocking collectives, per_device(): lax.all_to_all(send_buffer[:, :, lo:hi], 'seq', split_axis=0, concat_axis...  66.4 us
    all_to_all x2, waiting for transfers between devices, per_device(): lax.all_to_all(computed, 'seq', split_axis=1, concat_axis=0, tiled=True)  50.1 us
    all_to_all x2, starting transfers between devices, per_device(): lax.all_to_all(computed, 'seq', split_axis=1, concat_axis=0, tiled=True)  32 us
    psum x1, blocking collectives, per_device(): total_squares = lax.psum(local_squares, 'head')  13.2 us
    ppermute x6, starting transfers between devices, exclusive_scan(): got = lax.ppermute(window, axis, pairs)  12.2 us
  transfers between devices with their start and end apart: 11, of which 9 were waited for; matrix products, arithmetic and copies ran while one was open for 5% of the time, Pallas kernels for 0%

profile of v2, /device:TPU:6, one launch (start us, length us, event | category | flops | bytes accessed | tf_op | source)
XLA Modules:
  0.0 500.6 jit_solution(16637249077426523019)
XLA Ops:
  6.5 0.8 reshape.296
  7.3 1.2 reduce-window.6
  9.2 1.1 copy.119
  10.3 1.2 fusion.29
  11.5 3.8 collective-permute-start
  15.4 14.5 %collective-permute-done = f32[4,129,128]{2,1,0:T(8,128)S(1)} collective-permute-done((f32[4,129,128]{2,1,0:T(8,128)S(1)}, f32[4,129,128]{2,1,0:T(8,128)S(1)}, u32[]{:S(2)}, u32[]{:S(2)}) %collective-permute-start) | collective-permute-done | bytes 264224 | tf_op jit(solution)/shard_map/ppermute | solution.py:28
  30.2 1.9 collective-permute-start.1
  32.2 16.2 %collective-permute-done.1 = f32[4,129,128]{2,1,0:T(8,128)S(1)} collective-permute-done((f32[4,129,128]{2,1,0:T(8,128)S(1)}, f32[4,129,128]{2,1,0:T(8,128)S(1)}, u32[]{:S(2)}, u32[]{:S(2)}) %collective-permute-start.1) | collective-permute-done | bytes 264224 | tf_op jit(solution)/shard_map/ppermute | solution.py:28
  48.7 1.9 collective-permute-start.2
  50.7 26.8 %collective-permute-done.2 = f32[4,129,128]{2,1,0:T(8,128)S(1)} collective-permute-done((f32[4,129,128]{2,1,0:T(8,128)S(1)}, f32[4,129,128]{2,1,0:T(8,128)S(1)}, u32[]{:S(2)}, u32[]{:S(2)}) %collective-permute-start.2) | collective-permute-done | bytes 264224 | tf_op jit(solution)/shard_map/ppermute | solution.py:28
  77.8 1.9 collective-permute-start.3
  80.5 24.3 %collective-permute-done.3 = f32[4,129,128]{2,1,0:T(8,128)S(1)} collective-permute-done((f32[4,129,128]{2,1,0:T(8,128)S(1)}, f32[4,129,128]{2,1,0:T(8,128)S(1)}, u32[]{:S(2)}, u32[]{:S(2)}) %collective-permute-start.3) | collective-permute-done | bytes 264224 | tf_op jit(solution)/shard_map/ppermute | solution.py:28
  105.2 1.3 collective-permute-start.4
  106.5 0.9 fusion.4
  107.4 8.2 %collective-permute-done.4 = f32[4,129,128]{2,1,0:T(8,128)S(1)} collective-permute-done((f32[4,129,128]{2,1,0:T(8,128)S(1)}, f32[4,129,128]{2,1,0:T(8,128)S(1)}, u32[]{:S(2)}, u32[]{:S(2)}) %collective-permute-start.4) | collective-permute-done | bytes 264224 | tf_op jit(solution)/shard_map/ppermute | solution.py:28
  115.9 0.7 pad_maximum_fusion.6
  116.6 1.3 collective-permute-start.5
  117.9 1.6 fusion.7
  119.6 8.4 %collective-permute-done.5 = f32[4,129,128]{2,1,0:T(8,128)} collective-permute-done((f32[4,129,128]{2,1,0:T(8,128)}, f32[4,129,128]{2,1,0:T(8,128)}, u32[]{:S(2)}, u32[]{:S(2)}) %collective-permute-start.5) | collective-permute-done | bytes 264224 | tf_op jit(solution)/shard_map/ppermute | solution.py:28
  127.9 1.5 multiply_reduce_fusion.1
  129.8 0.6 copy-done.5
  130.6 13.2 %psum.21 = f32[256]{0:T(256)S(1)} all-reduce(f32[256]{0:T(256)S(1)} %get-tuple-element.18), channel_id=1, replica_groups=mesh['seq'=64,'head'=8] {'head'}, use_global_device_ids=true, to_apply=%region_6.7 | all-reduce | flops 256 | bytes 2048 | tf_op jit(solution)/shard_map/psum | solution.py:97
  144.6 1.5 fusion.73
  146.1 66.4 %all_to_all.16 = bf16[64,1,10,512]{3,2,1,0:T(8,128)(2,1)S(1)} all-to-all(bf16[64,1,10,512]{3,2,1,0:T(8,128)(2,1)S(1)} %get-tuple-element.22), channel_id=1, replica_groups=mesh['seq'=64,'head'=8] {'seq'}, dimensions={0} | all-to-all | bytes 1310720 | tf_op jit(solution)/shard_map/all_to_all | solution.py:127
  212.5 7.0 %all-to-all-start.2 = ((bf16[64,1,10,512]{3,2,1,0:T(8,128)(2,1)}), bf16[64,1,10,512]{3,2,1,0:T(8,128)(2,1)}, u32[]{:S(2)}, u32[]{:S(2)}) async-start(bf16[64,1,10,512]{3,2,1,0:T(8,128)(2,1)} %get-tuple-element.23), calls=%async_computation.2 | async-start | bytes 2097152 | tf_op jit(solution)/shard_map/all_to_all | solution.py:127
  219.6 1.6 copy.107
  221.1 4.0 convert_bitcast_fusion
  225.1 79.9 %all-reduce.3.cloned.1.call-done = bf16[1,64,10,2,704]{4,1,3,2,0:T(8,128)(2,1)} async-done(((bf16[1,64,10,2,704]{4,1,3,2,0:T(8,128)(2,1)}), bf16[1,64,10,2,704]{4,1,3,2,0:T(8,128)(2,1)}) %all-reduce.3.cloned.1.call-update) | async-done | bytes 1802256 | tf_op jit(solution)/shard_map/psum | solution.py:138
  305.0 2.0 convert_element_type.115
  308.2 0.6 convert_element_type.117
  308.8 0.7 convolution_convert_fusion.1
  309.5 1.2 reshape.303
  310.7 15.9 %all-to-all-start.1 = ((bf16[1,64,10,512]{3,2,0,1:T(8,128)(2,1)}), bf16[1,64,10,512]{3,2,0,1:T(8,128)(2,1)S(1)}, u32[]{:S(2)}, u32[]{:S(2)}) async-start(bf16[1,64,10,512]{3,2,0,1:T(8,128)(2,1)} %bitcast.18), calls=%async_computation.1 | async-start | bytes 2097152 | tf_op jit(solution)/shard_map/all_to_all | solution.py:146
  326.7 3.8 convolution_bitcast_fusion
  330.5 79.7 %all-reduce.5.cloned.1.call-done = bf16[1,64,10,2,704]{4,1,3,2,0:T(8,128)(2,1)} async-done(((bf16[1,64,10,2,704]{4,1,3,2,0:T(8,128)(2,1)}), bf16[1,64,10,2,704]{4,1,3,2,0:T(8,128)(2,1)}) %all-reduce.5.cloned.1.call-update) | async-done | bytes 1802256 | tf_op jit(solution)/shard_map/psum | solution.py:138
  410.3 2.0 convert_element_type.122
  413.4 1.4 convert_element_type.124
  414.8 1.9 convolution_convert_fusion
  416.7 1.2 reshape.305
  417.9 16.1 %all-to-all-start.3 = ((bf16[1,64,10,512]{3,2,0,1:T(8,128)(2,1)}), bf16[1,64,10,512]{3,2,0,1:T(8,128)(2,1)}, u32[]{:S(2)}, u32[]{:S(2)}) async-start(bf16[1,64,10,512]{3,2,0,1:T(8,128)(2,1)} %bitcast.27), calls=%async_computation.3 | async-start | bytes 2097152 | tf_op jit(solution)/shard_map/all_to_all | solution.py:146
  434.8 50.1 %all-to-all-done.3 = bf16[1,64,10,512]{3,2,0,1:T(8,128)(2,1)} async-done(((bf16[1,64,10,512]{3,2,0,1:T(8,128)(2,1)}), bf16[1,64,10,512]{3,2,0,1:T(8,128)(2,1)}, u32[]{:S(2)}, u32[]{:S(2)}) %all-to-all-start.3) | async-done | bytes 655392 | tf_op jit(solution)/shard_map/all_to_all | solution.py:146
  484.8 1.6 convert_reduce_fusion
  486.5 1.4 pad_maximum_fusion
  487.9 1.5 reshape.306
  489.3 1.6 gather_fusion
  491.0 0.6 reshape.310
  491.6 1.3 multiply_reduce_fusion
  492.9 0.8 fusion.23
  (92 shorter events, 7.5 us)
Async XLA Ops:
  6.5 302.3 %copy-start = (bf16[1,704,512]{2,1,0:T(8,128)(2,1)S(1)}, bf16[1,704,512]{2,1,0:T(8,128)(2,1)}, u32[]{:S(2)}) copy-start(bf16[1,704,512]{2,1,0:T(8,128)(2,1)} %param.21) | copy-start | bytes 2162692
  11.5 18.3 %collective-permute-start = (f32[4,129,128]{2,1,0:T(8,128)S(1)}, f32[4,129,128]{2,1,0:T(8,128)S(1)}, u32[]{:S(2)}, u32[]{:S(2)}) collective-permute-start(f32[4,129,128]{2,1,0:T(8,128)S(1)} %pad_maximum_fusion.1), channel_id=1, source_target_pairs={{0,8},{8,16},{16,24},{24,32},{32,40},{40,48},{48,56},{56,64},{64,7... | collective-permute-start | bytes 792584 | tf_op jit(solution)/shard_map/ppermute | solution.py:28
  30.0 49.8 %copy-start.8 = (s32[256,2]{0,1:T(2,128)S(1)}, s32[256,2]{0,1:T(2,128)}, u32[]{:S(2)}) copy-start(s32[256,2]{0,1:T(2,128)} %param.18) | copy-start | bytes 6148
  30.2 18.2 %collective-permute-start.1 = (f32[4,129,128]{2,1,0:T(8,128)S(1)}, f32[4,129,128]{2,1,0:T(8,128)S(1)}, u32[]{:S(2)}, u32[]{:S(2)}) collective-permute-start(f32[4,129,128]{2,1,0:T(8,128)S(1)} %pad_maximum_fusion.2), channel_id=1, source_target_pairs={{0,16},{8,24},{16,32},{24,40},{32,48},{40,56},{48,64},{56,72},{64,... | collective-permute-start | bytes 792584 | tf_op jit(solution)/shard_map/ppermute | solution.py:28
  48.7 28.8 %collective-permute-start.2 = (f32[4,129,128]{2,1,0:T(8,128)S(1)}, f32[4,129,128]{2,1,0:T(8,128)S(1)}, u32[]{:S(2)}, u32[]{:S(2)}) collective-permute-start(f32[4,129,128]{2,1,0:T(8,128)S(1)} %pad_maximum_fusion.3), channel_id=1, source_target_pairs={{0,32},{8,40},{16,48},{24,56},{32,64},{40,72},{48,80},{56,88},{64,... | collective-permute-start | bytes 792584 | tf_op jit(solution)/shard_map/ppermute | solution.py:28
  77.8 27.1 %collective-permute-start.3 = (f32[4,129,128]{2,1,0:T(8,128)S(1)}, f32[4,129,128]{2,1,0:T(8,128)S(1)}, u32[]{:S(2)}, u32[]{:S(2)}) collective-permute-start(f32[4,129,128]{2,1,0:T(8,128)S(1)} %pad_maximum_fusion.4), channel_id=1, source_target_pairs={{0,64},{8,72},{16,80},{24,88},{32,96},{40,104},{48,112},{56,120},{... | collective-permute-start | bytes 792584 | tf_op jit(solution)/shard_map/ppermute | solution.py:28
  105.2 10.4 %collective-permute-start.4 = (f32[4,129,128]{2,1,0:T(8,128)S(1)}, f32[4,129,128]{2,1,0:T(8,128)S(1)}, u32[]{:S(2)}, u32[]{:S(2)}) collective-permute-start(f32[4,129,128]{2,1,0:T(8,128)S(1)} %pad_maximum_fusion.5), channel_id=1, source_target_pairs={{0,128},{8,136},{16,144},{24,152},{32,160},{40,168},{48,176},{56,1... | collective-permute-start | bytes 792584 | tf_op jit(solution)/shard_map/ppermute | solution.py:28
  115.8 12.1 %copy-start.6 = (bf16[256,512]{1,0:T(8,128)(2,1)S(1)}, bf16[256,512]{1,0:T(8,128)(2,1)}, u32[]{:S(2)}) copy-start(bf16[256,512]{1,0:T(8,128)(2,1)} %param.12) | copy-start | bytes 786436
  116.6 11.3 %collective-permute-start.5 = (f32[4,129,128]{2,1,0:T(8,128)}, f32[4,129,128]{2,1,0:T(8,128)}, u32[]{:S(2)}, u32[]{:S(2)}) collective-permute-start(f32[4,129,128]{2,1,0:T(8,128)} %pad_maximum_fusion.6), channel_id=1, source_target_pairs={{0,256},{8,264},{16,272},{24,280},{32,288},{40,296},{48,304},{56,3... | collective-permute-start | bytes 792584 | tf_op jit(solution)/shard_map/ppermute | solution.py:28
  127.9 1.8 copy-start.9
  129.5 1.0 copy-start.5
  129.5 14.3 %copy-start.7 = (pred[640,256]{1,0:T(8,128)(4,1)S(1)}, pred[640,256]{1,0:T(8,128)(4,1)}, u32[]{:S(2)}) copy-start(pred[640,256]{1,0:T(8,128)(4,1)} %fusion.4) | copy-start | bytes 491524
  129.5 14.3 %copy-start.11 = (f32[512]{0:T(512)S(1)}, f32[512]{0:T(512)}, u32[]{:S(2)}) copy-start(f32[512]{0:T(512)} %param.17) | copy-start | bytes 6148
  130.6 13.2 %copy-start.3 = (bf16[256,512]{1,0:T(8,128)(2,1)}, bf16[256,512]{1,0:T(8,128)(2,1)S(1)}, u32[]{:S(2)}) copy-start(bf16[256,512]{1,0:T(8,128)(2,1)S(1)} %get-tuple-element.19) | copy-start | bytes 786436
  146.1 73.5 %copy-start.1 = (bf16[1,512,1408]{2,1,0:T(8,128)(2,1)S(1)}, bf16[1,512,1408]{2,1,0:T(8,128)(2,1)}, u32[]{:S(2)}) copy-start(bf16[1,512,1408]{2,1,0:T(8,128)(2,1)} %param.20) | copy-start | bytes 4325380
  212.5 98.2 %all-to-all-start.2 = ((bf16[64,1,10,512]{3,2,1,0:T(8,128)(2,1)}), bf16[64,1,10,512]{3,2,1,0:T(8,128)(2,1)}, u32[]{:S(2)}, u32[]{:S(2)}) async-start(bf16[64,1,10,512]{3,2,1,0:T(8,128)(2,1)} %get-tuple-element.23), calls=%async_computation.2 | async-start | bytes 2097152 | tf_op jit(solution)/shard_map/all_to_all | solution.py:127
  219.5 85.5 %all-reduce.3.cloned.1.call-start = ((), (), s32[]{:S(2)}) async-start(), calls=%async_computation.4 | async-start | bytes 3932160 | tf_op jit(solution)/shard_map/psum | solution.py:138
  309.5 17.2 %copy-start.2 = (bf16[1,512,1408]{1,2,0:T(8,128)(2,1)S(1)}, bf16[1,512,1408]{1,2,0:T(8,128)(2,1)}, u32[]{:S(2)}) copy-start(bf16[1,512,1408]{1,2,0:T(8,128)(2,1)} %copy.107) | copy-start | bytes 4325380
  310.7 107.2 %all-to-all-start.1 = ((bf16[1,64,10,512]{3,2,0,1:T(8,128)(2,1)}), bf16[1,64,10,512]{3,2,0,1:T(8,128)(2,1)S(1)}, u32[]{:S(2)}, u32[]{:S(2)}) async-start(bf16[1,64,10,512]{3,2,0,1:T(8,128)(2,1)} %bitcast.18), calls=%async_computation.1 | async-start | bytes 2097152 | tf_op jit(solution)/shard_map/all_to_all | solution.py:146
  326.6 83.6 %all-reduce.5.cloned.1.call-start = ((), (), s32[]{:S(2)}) async-start(), calls=%async_computation.5 | async-start | bytes 3932160 | tf_op jit(solution)/shard_map/psum | solution.py:138
  416.7 17.3 %copy-start.10 = (f32[256,2]{0,1:T(2,128)S(1)}, f32[256,2]{0,1:T(2,128)}, u32[]{:S(2)}) copy-start(f32[256,2]{0,1:T(2,128)} %param.19) | copy-start | bytes 6148
  417.9 66.9 %all-to-all-start.3 = ((bf16[1,64,10,512]{3,2,0,1:T(8,128)(2,1)}), bf16[1,64,10,512]{3,2,0,1:T(8,128)(2,1)}, u32[]{:S(2)}, u32[]{:S(2)}) async-start(bf16[1,64,10,512]{3,2,0,1:T(8,128)(2,1)} %bitcast.27), calls=%async_computation.3 | async-start | bytes 2097152 | tf_op jit(solution)/shard_map/all_to_all | solution.py:146
  491.0 2.0 copy-start.4
Sparse Core Ops, SparseCore 0:
  225.2 79.7 all-reduce.2
  330.7 79.5 all-reduce.4

commit v3 on v1

--- a/solution.py
+++ b/solution.py
@@ -39,6 +39,31 @@
         )
         shift *= 2
     return before_state
+
+
+def head_reduce_activate(partial, axis, block_units):
+    place = lax.axis_index(axis)
+    count = lax.axis_size(axis)
+    blocks_here, rows, width = partial.shape
+    share = rows // count
+    pieces = partial.reshape(blocks_here, count, share, width)
+    total = lax.dynamic_index_in_dim(pieces, place, 1, False).astype(jnp.float32)
+    for shift in range(1, count):
+        target = (place + shift) % count
+        outgoing = lax.dynamic_index_in_dim(pieces, target, 1, False)
+        pairs = [(j, (j + shift) % count) for j in range(count)]
+        total = total + lax.ppermute(outgoing, axis, pairs).astype(jnp.float32)
+    gate = total[:, :, :block_units]
+    up = total[:, :, block_units:]
+    mine = (jax.nn.silu(gate) * up).astype(jnp.bfloat16)
+    gathered = [mine]
+    for shift in range(1, count):
+        pairs = [(j, (j + shift) % count) for j in range(count)]
+        gathered.append(lax.ppermute(mine, axis, pairs))
+    stacked = jnp.stack(gathered, axis=1)
+    origin = (place - jnp.arange(count)) % count
+    ordered = jnp.take(stacked, origin, axis=1)
+    return ordered.reshape(blocks_here, rows, block_units)
 
 
 def per_device(
@@ -126,10 +151,7 @@
     partial_sums = jnp.einsum(
         "erd,edh->erh", flat_rows, expert_in, preferred_element_type=jnp.float32
     )
-    partial_sums = partial_sums.reshape(blocks_here, sources, item_count, 2, block_units)
-    gate_up = lax.psum(partial_sums.astype(jnp.bfloat16), "head").astype(jnp.float32)
-    activated = (jax.nn.silu(gate_up[:, :, :, 0]) * gate_up[:, :, :, 1]).astype(jnp.bfloat16)
-    activated = activated.reshape(blocks_here, sources * item_count, block_units)
+    activated = head_reduce_activate(partial_sums.astype(jnp.bfloat16), "head", block_units)
     produced = jnp.einsum(
         "erh,ehd->erd", activated, expert_out, preferred_element_type=jnp.float32
     ).astype(jnp.bfloat16)

time: 434 us -> 418 us (0.963)
  waiting for transfers between devices: 323 us -> 285 us
  starting transfers between devices: 41 us -> 73.5 us
  between operations: 13.9 us -> 0.71 us
  local copies, waits for them, and re-layouts: 16.9 us -> 21.5 us
    psum x1 -> x0, waiting for transfers between devices: 77.2 us -> none  [per_device(): lax.psum(partial_sums.astype(jnp.bfloat16), 'head').astype(jnp.float32)]
    ppermute x0 -> x14, starting transfers between devices: none -> 36.1 us  [the longest x7 18.7 us: head_reduce_activate(): gathered.append(lax.ppermute(mine, axis, pairs))]
    ppermute x0 -> x14, waiting for transfers between devices: none -> 36 us  [the longest x7 23.7 us: head_reduce_activate(): total = total + lax.ppermute(outgoing, axis, pairs).astype(jnp.float32)]
    all_to_all x1, starting transfers between devices: 16 us -> 7.67 us  [per_device(): lax.all_to_all(computed, 'seq', split_axis=1, concat_axis=0, tiled=True)]
    all_to_all x1, starting transfers between devices: 12.6 us -> 17.6 us  [per_device(): lax.all_to_all(send_buffer, 'seq', split_axis=0, concat_axis=1, tiled=True)]
    convert_element_type x2 -> x0, other arithmetic: 4.38 us -> none  [the longest x1 3.11 us: per_device(): lax.psum(partial_sums.astype(jnp.bfloat16), 'head').astype(jnp.float32)]
  transfers between devices with their start and end apart: 9 -> 22, of which waited for: 9 -> 17; matrix products, arithmetic and copies ran while one was open for 1% -> 1% of each run, Pallas kernels for 0% -> 0%
where the time goes in v3:
time: 418 us; the launch traced here: 416 us
  waiting for transfers between devices  285 us (68%)
  starting transfers between devices  73.5 us (18%)
  local copies, waits for them, and re-layouts  21.5 us (5%)
  blocking collectives  13.2 us (3%)
  other arithmetic  11.5 us (3%)
  matrix products  10.8 us (3%)
    ppermute x6, waiting for transfers between devices, exclusive_scan(): got = lax.ppermute(window, axis, pairs)  97.9 us
    all_to_all x1, waiting for transfers between devices, per_device(): lax.all_to_all(send_buffer, 'seq', split_axis=0, concat_axis=1, tiled=True)  75.7 us
    all_to_all x1, waiting for transfers between devices, per_device(): lax.all_to_all(computed, 'seq', split_axis=1, concat_axis=0, tiled=True)  75.4 us
    ppermute x7, waiting for transfers between devices, head_reduce_activate(): total = total + lax.ppermute(outgoing, axis, pairs).astype(jnp.float32)  23.7 us
    ppermute x7, starting transfers between devices, head_reduce_activate(): gathered.append(lax.ppermute(mine, axis, pairs))  18.7 us
    all_to_all x1, starting transfers between devices, per_device(): lax.all_to_all(send_buffer, 'seq', split_axis=0, concat_axis=1, tiled=True)  17.6 us
    ppermute x7, starting transfers between devices, head_reduce_activate(): total = total + lax.ppermute(outgoing, axis, pairs).astype(jnp.float32)  17.4 us
    psum x1, blocking collectives, per_device(): total_squares = lax.psum(local_squares, 'head')  13.2 us
  transfers between devices with their start and end apart: 22, of which 17 were waited for; matrix products, arithmetic and copies ran while one was open for 1% of the time, Pallas kernels for 0%

profile of v3, /device:TPU:6, one launch (start us, length us, event | category | flops | bytes accessed | tf_op | source)
XLA Modules:
  0.0 416.3 jit_solution(15637011065831389418)
XLA Ops:
  5.0 3.8 collective-permute-start
  8.9 14.5 %collective-permute-done = f32[4,129,128]{2,1,0:T(8,128)S(1)} collective-permute-done((f32[4,129,128]{2,1,0:T(8,128)S(1)}, f32[4,129,128]{2,1,0:T(8,128)S(1)}, u32[]{:S(2)}, u32[]{:S(2)}) %collective-permute-start) | collective-permute-done | bytes 264224 | tf_op jit(solution)/shard_map/ppermute | solution.py:27
  23.7 1.9 collective-permute-start.1
  25.7 16.2 %collective-permute-done.1 = f32[4,129,128]{2,1,0:T(8,128)S(1)} collective-permute-done((f32[4,129,128]{2,1,0:T(8,128)S(1)}, f32[4,129,128]{2,1,0:T(8,128)S(1)}, u32[]{:S(2)}, u32[]{:S(2)}) %collective-permute-start.1) | collective-permute-done | bytes 264224 | tf_op jit(solution)/shard_map/ppermute | solution.py:27
  42.9 1.9 collective-permute-start.2
  44.8 26.9 %collective-permute-done.2 = f32[4,129,128]{2,1,0:T(8,128)S(1)} collective-permute-done((f32[4,129,128]{2,1,0:T(8,128)}, f32[4,129,128]{2,1,0:T(8,128)S(1)}, u32[]{:S(2)}, u32[]{:S(2)}) %collective-permute-start.2) | collective-permute-done | bytes 264224 | tf_op jit(solution)/shard_map/ppermute | solution.py:27
  72.7 1.9 collective-permute-start.3
  75.5 23.8 %collective-permute-done.3 = f32[4,129,128]{2,1,0:T(8,128)S(1)} collective-permute-done((f32[4,129,128]{2,1,0:T(8,128)}, f32[4,129,128]{2,1,0:T(8,128)S(1)}, u32[]{:S(2)}, u32[]{:S(2)}) %collective-permute-start.3) | collective-permute-done | bytes 264224 | tf_op jit(solution)/shard_map/ppermute | solution.py:27
  99.6 1.3 collective-permute-start.4
  101.1 8.9 %collective-permute-done.4 = f32[4,129,128]{2,1,0:T(8,128)S(1)} collective-permute-done((f32[4,129,128]{2,1,0:T(8,128)S(1)}, f32[4,129,128]{2,1,0:T(8,128)S(1)}, u32[]{:S(2)}, u32[]{:S(2)}) %collective-permute-start.4) | collective-permute-done | bytes 264224 | tf_op jit(solution)/shard_map/ppermute | solution.py:27
  112.4 2.4 fusion.6
  114.8 7.6 %collective-permute-done.5 = f32[4,129,128]{2,1,0:T(8,128)} collective-permute-done((f32[4,129,128]{2,1,0:T(8,128)}, f32[4,129,128]{2,1,0:T(8,128)}, u32[]{:S(2)}, u32[]{:S(2)}) %collective-permute-start.5) | collective-permute-done | bytes 264224 | tf_op jit(solution)/shard_map/ppermute | solution.py:27
  122.5 1.8 multiply_reduce_fusion.1
  125.4 13.2 %psum.7 = f32[256]{0:T(256)S(1)} all-reduce(f32[256]{0:T(256)S(1)} %get-tuple-element.18), channel_id=1, replica_groups=mesh['seq'=64,'head'=8] {'head'}, use_global_device_ids=true, to_apply=%region_6.7 | all-reduce | flops 256 | bytes 2048 | tf_op jit(solution)/shard_map/psum | solution.py:121
  139.3 1.3 broadcast_in_dim.114
  140.5 17.6 %all-to-all-start = ((bf16[64,1,20,512]{3,2,1,0:T(8,128)(2,1)}), bf16[64,1,20,512]{3,2,1,0:T(8,128)(2,1)S(1)}, u32[]{:S(2)}, u32[]{:S(2)}) async-start(bf16[64,1,20,512]{3,2,1,0:T(8,128)(2,1)} %bitcast.8), calls=%async_computation | async-start | bytes 3145728 | tf_op jit(solution)/shard_map/all_to_all | solution.py:148
  158.2 75.7 %all-to-all-done = bf16[64,1,20,512]{3,2,1,0:T(8,128)(2,1)S(1)} async-done(((bf16[64,1,20,512]{3,2,1,0:T(8,128)(2,1)}), bf16[64,1,20,512]{3,2,1,0:T(8,128)(2,1)S(1)}, u32[]{:S(2)}, u32[]{:S(2)}) %all-to-all-start) | async-done | bytes 1310752 | tf_op jit(solution)/shard_map/all_to_all | solution.py:148
  235.1 3.5 convolution_convert_fusion
  238.7 1.6 dynamic-slice_bitcast_fusion.6
  240.7 1.9 collective-permute-start.10
  242.6 2.4 collective-permute-start.11
  245.6 3.4 collective-permute-start.7
  249.1 6.2 %collective-permute-done.10 = bf16[1,160,1408]{2,1,0:T(8,128)(2,1)S(1)} collective-permute-done((bf16[1,160,1408]{2,1,0:T(8,128)(2,1)S(1)}, bf16[1,160,1408]{2,1,0:T(8,128)(2,1)S(1)}, u32[]{:S(2)}, u32[]{:S(2)}) %collective-permute-start.10) | collective-permute-done | bytes 450592 | tf_op jit(solution)/shard_map/ppermute | solution.py:55
  255.3 1.9 collective-permute-start.8
  257.2 2.8 collective-permute-done.11
  260.7 7.1 %collective-permute-start.9 = (bf16[1,160,1408]{2,1,0:T(8,128)(2,1)S(1)}, bf16[1,160,1408]{2,1,0:T(8,128)(2,1)}, u32[]{:S(2)}, u32[]{:S(2)}) collective-permute-start(bf16[1,160,1408]{2,1,0:T(8,128)(2,1)S(1)} %get-tuple-element.26), channel_id=1, source_target_pairs={{0,4},{1,5},{2,6},{3,7},{4,0},{5,1},{6,2},{7,3},{8,12},{9,13},{10,... | collective-permute-start | bytes 1351688 | tf_op jit(solution)/shard_map/ppermute | solution.py:55
  268.6 9.4 %collective-permute-done.8 = bf16[1,160,1408]{2,1,0:T(8,128)(2,1)} collective-permute-done((bf16[1,160,1408]{2,1,0:T(8,128)(2,1)S(1)}, bf16[1,160,1408]{2,1,0:T(8,128)(2,1)}, u32[]{:S(2)}, u32[]{:S(2)}) %collective-permute-start.8) | collective-permute-done | bytes 450592 | tf_op jit(solution)/shard_map/ppermute | solution.py:55
  278.0 4.6 %collective-permute-done.9 = bf16[1,160,1408]{2,1,0:T(8,128)(2,1)} collective-permute-done((bf16[1,160,1408]{2,1,0:T(8,128)(2,1)S(1)}, bf16[1,160,1408]{2,1,0:T(8,128)(2,1)}, u32[]{:S(2)}, u32[]{:S(2)}) %collective-permute-start.9) | collective-permute-done | bytes 450592 | tf_op jit(solution)/shard_map/ppermute | solution.py:55
  282.6 2.3 fusion.18
  285.1 2.3 collective-permute-start.13
  287.5 1.9 collective-permute-start.14
  289.4 2.4 collective-permute-start.15
  291.9 5.4 %collective-permute-start.16 = (bf16[1,160,704]{2,1,0:T(8,128)(2,1)S(1)}, bf16[1,160,704]{2,1,0:T(8,128)(2,1)S(1)}, u32[]{:S(2)}, u32[]{:S(2)}) collective-permute-start(bf16[1,160,704]{2,1,0:T(8,128)(2,1)S(1)} %get-tuple-element.17), channel_id=1, source_target_pairs={{0,4},{1,5},{2,6},{3,7},{4,0},{5,1},{6,2},{7,3},{8,12},{9,13},{10,... | collective-permute-start | bytes 675848 | tf_op jit(solution)/shard_map/ppermute | solution.py:62
  297.3 2.1 collective-permute-start.17
  299.4 4.5 %collective-permute-start.18 = (bf16[1,160,704]{2,1,0:T(8,128)(2,1)S(1)}, bf16[1,160,704]{2,1,0:T(8,128)(2,1)S(1)}, u32[]{:S(2)}, u32[]{:S(2)}) collective-permute-start(bf16[1,160,704]{2,1,0:T(8,128)(2,1)S(1)} %get-tuple-element.17), channel_id=1, source_target_pairs={{0,6},{1,7},{2,0},{3,1},{4,2},{5,3},{6,4},{7,5},{8,14},{9,15},{10,... | collective-permute-start | bytes 675848 | tf_op jit(solution)/shard_map/ppermute | solution.py:62
  304.1 3.7 collective-permute-done.16
  307.8 1.8 collective-permute-done.17
  309.7 5.1 %collective-permute-done.18 = bf16[1,160,704]{2,1,0:T(8,128)(2,1)S(1)} collective-permute-done((bf16[1,160,704]{2,1,0:T(8,128)(2,1)S(1)}, bf16[1,160,704]{2,1,0:T(8,128)(2,1)S(1)}, u32[]{:S(2)}, u32[]{:S(2)}) %collective-permute-start.18) | collective-permute-done | bytes 225312 | tf_op jit(solution)/shard_map/ppermute | solution.py:62
  314.8 1.6 collective-permute-done.19
  317.7 2.2 gather_fusion
  322.3 1.3 reshape.339
  323.6 7.7 %all-to-all-start.1 = ((bf16[1,64,20,512]{3,2,0,1:T(8,128)(2,1)}), bf16[1,64,20,512]{3,2,0,1:T(8,128)(2,1)S(1)}, u32[]{:S(2)}, u32[]{:S(2)}) async-start(bf16[1,64,20,512]{3,2,0,1:T(8,128)(2,1)} %bitcast.113), calls=%async_computation.1 | async-start | bytes 3145728 | tf_op jit(solution)/shard_map/all_to_all | solution.py:159
  331.7 75.4 %all-to-all-done.1 = bf16[1,64,20,512]{3,2,0,1:T(8,128)(2,1)S(1)} async-done(((bf16[1,64,20,512]{3,2,0,1:T(8,128)(2,1)}), bf16[1,64,20,512]{3,2,0,1:T(8,128)(2,1)S(1)}, u32[]{:S(2)}, u32[]{:S(2)}) %all-to-all-start.1) | async-done | bytes 1310752 | tf_op jit(solution)/shard_map/all_to_all | solution.py:159
  407.1 1.4 convert_reduce_fusion
  408.5 1.5 reshape.340
  410.0 2.3 gather_fusion.1
  412.3 1.9 reshape.354
  414.2 1.3 multiply_reduce_fusion
  (116 shorter events, 21.7 us)
Async XLA Ops:
  0.0 235.1 %copy-start = (bf16[1,512,1408]{2,1,0:T(8,128)(2,1)S(1)}, bf16[1,512,1408]{2,1,0:T(8,128)(2,1)}, u32[]{:S(2)}) copy-start(bf16[1,512,1408]{2,1,0:T(8,128)(2,1)} %param.20) | copy-start | bytes 4325380
  5.0 18.3 %collective-permute-start = (f32[4,129,128]{2,1,0:T(8,128)S(1)}, f32[4,129,128]{2,1,0:T(8,128)S(1)}, u32[]{:S(2)}, u32[]{:S(2)}) collective-permute-start(f32[4,129,128]{2,1,0:T(8,128)S(1)} %pad_maximum_fusion), channel_id=1, source_target_pairs={{0,8},{8,16},{16,24},{24,32},{32,40},{40,48},{48,56},{56,64},{64,7... | collective-permute-start | bytes 792584 | tf_op jit(solution)/shard_map/ppermute | solution.py:27
  23.5 51.2 %copy-start.9 = (s32[256,2]{0,1:T(2,128)S(1)}, s32[256,2]{0,1:T(2,128)}, u32[]{:S(2)}) copy-start(s32[256,2]{0,1:T(2,128)} %param.18) | copy-start | bytes 6148
  23.7 18.2 %collective-permute-start.1 = (f32[4,129,128]{2,1,0:T(8,128)S(1)}, f32[4,129,128]{2,1,0:T(8,128)S(1)}, u32[]{:S(2)}, u32[]{:S(2)}) collective-permute-start(f32[4,129,128]{2,1,0:T(8,128)S(1)} %pad_maximum_fusion.1), channel_id=1, source_target_pairs={{0,16},{8,24},{16,32},{24,40},{32,48},{40,56},{48,64},{56,72},{64,... | collective-permute-start | bytes 792584 | tf_op jit(solution)/shard_map/ppermute | solution.py:27
  42.9 28.8 %collective-permute-start.2 = (f32[4,129,128]{2,1,0:T(8,128)}, f32[4,129,128]{2,1,0:T(8,128)S(1)}, u32[]{:S(2)}, u32[]{:S(2)}) collective-permute-start(f32[4,129,128]{2,1,0:T(8,128)} %pad_maximum_fusion.2), channel_id=1, source_target_pairs={{0,32},{8,40},{16,48},{24,56},{32,64},{40,72},{48,80},{56,88},{64,... | collective-permute-start | bytes 792584 | tf_op jit(solution)/shard_map/ppermute | solution.py:27
  72.7 26.6 %collective-permute-start.3 = (f32[4,129,128]{2,1,0:T(8,128)}, f32[4,129,128]{2,1,0:T(8,128)S(1)}, u32[]{:S(2)}, u32[]{:S(2)}) collective-permute-start(f32[4,129,128]{2,1,0:T(8,128)} %pad_maximum_fusion.3), channel_id=1, source_target_pairs={{0,64},{8,72},{16,80},{24,88},{32,96},{40,104},{48,112},{56,120},{... | collective-permute-start | bytes 792584 | tf_op jit(solution)/shard_map/ppermute | solution.py:27
  99.6 10.4 %collective-permute-start.4 = (f32[4,129,128]{2,1,0:T(8,128)S(1)}, f32[4,129,128]{2,1,0:T(8,128)S(1)}, u32[]{:S(2)}, u32[]{:S(2)}) collective-permute-start(f32[4,129,128]{2,1,0:T(8,128)S(1)} %pad_maximum_fusion.4), channel_id=1, source_target_pairs={{0,128},{8,136},{16,144},{24,152},{32,160},{40,168},{48,176},{56,1... | collective-permute-start | bytes 792584 | tf_op jit(solution)/shard_map/ppermute | solution.py:27
  110.0 1.1 copy-start.5
  110.3 12.2 %copy-start.8 = (bf16[256,512]{1,0:T(8,128)(2,1)S(1)}, bf16[256,512]{1,0:T(8,128)(2,1)}, u32[]{:S(2)}) copy-start(bf16[256,512]{1,0:T(8,128)(2,1)} %param.12) | copy-start | bytes 786436
  111.1 11.4 %collective-permute-start.5 = (f32[4,129,128]{2,1,0:T(8,128)}, f32[4,129,128]{2,1,0:T(8,128)}, u32[]{:S(2)}, u32[]{:S(2)}) collective-permute-start(f32[4,129,128]{2,1,0:T(8,128)} %pad_maximum_fusion.5), channel_id=1, source_target_pairs={{0,256},{8,264},{16,272},{24,280},{32,288},{40,296},{48,304},{56,3... | collective-permute-start | bytes 792584 | tf_op jit(solution)/shard_map/ppermute | solution.py:27
  122.5 2.1 copy-start.10
  124.3 1.0 copy-start.7
  124.3 14.4 %copy-start.13 = (f32[512]{0:T(512)S(1)}, f32[512]{0:T(512)}, u32[]{:S(2)}) copy-start(f32[512]{0:T(512)} %param.17) | copy-start | bytes 6148
  125.4 13.3 %copy-start.3 = (bf16[256,512]{1,0:T(8,128)(2,1)}, bf16[256,512]{1,0:T(8,128)(2,1)S(1)}, u32[]{:S(2)}) copy-start(bf16[256,512]{1,0:T(8,128)(2,1)S(1)} %get-tuple-element.19) | copy-start | bytes 786436
  140.5 93.4 %all-to-all-start = ((bf16[64,1,20,512]{3,2,1,0:T(8,128)(2,1)}), bf16[64,1,20,512]{3,2,1,0:T(8,128)(2,1)S(1)}, u32[]{:S(2)}, u32[]{:S(2)}) async-start(bf16[64,1,20,512]{3,2,1,0:T(8,128)(2,1)} %bitcast.8), calls=%async_computation | async-start | bytes 3145728 | tf_op jit(solution)/shard_map/all_to_all | solution.py:148
  238.7 2.0 copy-start.1
  240.7 14.6 %collective-permute-start.10 = (bf16[1,160,1408]{2,1,0:T(8,128)(2,1)S(1)}, bf16[1,160,1408]{2,1,0:T(8,128)(2,1)S(1)}, u32[]{:S(2)}, u32[]{:S(2)}) collective-permute-start(bf16[1,160,1408]{2,1,0:T(8,128)(2,1)S(1)} %get-tuple-element.25), channel_id=1, source_target_pairs={{0,5},{1,6},{2,7},{3,0},{4,1},{5,2},{6,3},{7,4},{8,13},{9,14},{10,... | collective-permute-start | bytes 1351688 | tf_op jit(solution)/shard_map/ppermute | solution.py:55
  242.6 17.4 %collective-permute-start.11 = (bf16[1,160,1408]{2,1,0:T(8,128)(2,1)S(1)}, bf16[1,160,1408]{2,1,0:T(8,128)(2,1)S(1)}, u32[]{:S(2)}, u32[]{:S(2)}) collective-permute-start(bf16[1,160,1408]{2,1,0:T(8,128)(2,1)S(1)} %get-tuple-element.24), channel_id=1, source_target_pairs={{0,6},{1,7},{2,0},{3,1},{4,2},{5,3},{6,4},{7,5},{8,14},{9,15},{10,... | collective-permute-start | bytes 1351688 | tf_op jit(solution)/shard_map/ppermute | solution.py:55
  245.0 23.6 %collective-permute-start.12 = (bf16[1,160,1408]{2,1,0:T(8,128)(2,1)}, bf16[1,160,1408]{2,1,0:T(8,128)(2,1)}, u32[]{:S(2)}, u32[]{:S(2)}) collective-permute-start(bf16[1,160,1408]{2,1,0:T(8,128)(2,1)} %get-tuple-element.23), channel_id=1, source_target_pairs={{0,7},{1,0},{2,1},{3,2},{4,3},{5,4},{6,5},{7,6},{8,15},{9,8},{10,9... | collective-permute-start | bytes 1351688 | tf_op jit(solution)/shard_map/ppermute | solution.py:55
  245.6 22.9 %collective-permute-start.6 = (bf16[1,160,1408]{2,1,0:T(8,128)(2,1)}, bf16[1,160,1408]{2,1,0:T(8,128)(2,1)}, u32[]{:S(2)}, u32[]{:S(2)}) collective-permute-start(bf16[1,160,1408]{2,1,0:T(8,128)(2,1)} %get-tuple-element.22), channel_id=1, source_target_pairs={{0,1},{1,2},{2,3},{3,4},{4,5},{5,6},{6,7},{7,0},{8,9},{9,10},{10,1... | collective-permute-start | bytes 1351688 | tf_op jit(solution)/shard_map/ppermute | solution.py:55
  245.6 22.9 %collective-permute-start.7 = (bf16[1,160,1408]{2,1,0:T(8,128)(2,1)S(1)}, bf16[1,160,1408]{2,1,0:T(8,128)(2,1)}, u32[]{:S(2)}, u32[]{:S(2)}) collective-permute-start(bf16[1,160,1408]{2,1,0:T(8,128)(2,1)S(1)} %get-tuple-element.28), channel_id=1, source_target_pairs={{0,2},{1,3},{2,4},{3,5},{4,6},{5,7},{6,0},{7,1},{8,10},{9,11},{10,... | collective-permute-start | bytes 1351688 | tf_op jit(solution)/shard_map/ppermute | solution.py:55
  255.3 22.7 %collective-permute-start.8 = (bf16[1,160,1408]{2,1,0:T(8,128)(2,1)S(1)}, bf16[1,160,1408]{2,1,0:T(8,128)(2,1)}, u32[]{:S(2)}, u32[]{:S(2)}) collective-permute-start(bf16[1,160,1408]{2,1,0:T(8,128)(2,1)S(1)} %get-tuple-element.27), channel_id=1, source_target_pairs={{0,3},{1,4},{2,5},{3,6},{4,7},{5,0},{6,1},{7,2},{8,11},{9,12},{10,... | collective-permute-start | bytes 1351688 | tf_op jit(solution)/shard_map/ppermute | solution.py:55
  259.9 0.8 copy-start.6
  260.7 21.9 %collective-permute-start.9 = (bf16[1,160,1408]{2,1,0:T(8,128)(2,1)S(1)}, bf16[1,160,1408]{2,1,0:T(8,128)(2,1)}, u32[]{:S(2)}, u32[]{:S(2)}) collective-permute-start(bf16[1,160,1408]{2,1,0:T(8,128)(2,1)S(1)} %get-tuple-element.26), channel_id=1, source_target_pairs={{0,4},{1,5},{2,6},{3,7},{4,0},{5,1},{6,2},{7,3},{8,12},{9,13},{10,... | collective-permute-start | bytes 1351688 | tf_op jit(solution)/shard_map/ppermute | solution.py:55
  285.1 14.3 %collective-permute-start.13 = (bf16[1,160,704]{2,1,0:T(8,128)(2,1)S(1)}, bf16[1,160,704]{2,1,0:T(8,128)(2,1)S(1)}, u32[]{:S(2)}, u32[]{:S(2)}) collective-permute-start(bf16[1,160,704]{2,1,0:T(8,128)(2,1)S(1)} %get-tuple-element.17), channel_id=1, source_target_pairs={{0,1},{1,2},{2,3},{3,4},{4,5},{5,6},{6,7},{7,0},{8,9},{9,10},{10,1... | collective-permute-start | bytes 675848 | tf_op jit(solution)/shard_map/ppermute | solution.py:62
  287.5 16.4 %collective-permute-start.14 = (bf16[1,160,704]{2,1,0:T(8,128)(2,1)S(1)}, bf16[1,160,704]{2,1,0:T(8,128)(2,1)S(1)}, u32[]{:S(2)}, u32[]{:S(2)}) collective-permute-start(bf16[1,160,704]{2,1,0:T(8,128)(2,1)S(1)} %get-tuple-element.17), channel_id=1, source_target_pairs={{0,2},{1,3},{2,4},{3,5},{4,6},{5,7},{6,0},{7,1},{8,10},{9,11},{10,... | collective-permute-start | bytes 675848 | tf_op jit(solution)/shard_map/ppermute | solution.py:62
  289.4 14.6 %collective-permute-start.15 = (bf16[1,160,704]{2,1,0:T(8,128)(2,1)S(1)}, bf16[1,160,704]{2,1,0:T(8,128)(2,1)S(1)}, u32[]{:S(2)}, u32[]{:S(2)}) collective-permute-start(bf16[1,160,704]{2,1,0:T(8,128)(2,1)S(1)} %get-tuple-element.17), channel_id=1, source_target_pairs={{0,3},{1,4},{2,5},{3,6},{4,7},{5,0},{6,1},{7,2},{8,11},{9,12},{10,... | collective-permute-start | bytes 675848 | tf_op jit(solution)/shard_map/ppermute | solution.py:62
  291.9 15.9 %collective-permute-start.16 = (bf16[1,160,704]{2,1,0:T(8,128)(2,1)S(1)}, bf16[1,160,704]{2,1,0:T(8,128)(2,1)S(1)}, u32[]{:S(2)}, u32[]{:S(2)}) collective-permute-start(bf16[1,160,704]{2,1,0:T(8,128)(2,1)S(1)} %get-tuple-element.17), channel_id=1, source_target_pairs={{0,4},{1,5},{2,6},{3,7},{4,0},{5,1},{6,2},{7,3},{8,12},{9,13},{10,... | collective-permute-start | bytes 675848 | tf_op jit(solution)/shard_map/ppermute | solution.py:62
  297.3 12.3 %collective-permute-start.17 = (bf16[1,160,704]{2,1,0:T(8,128)(2,1)S(1)}, bf16[1,160,704]{2,1,0:T(8,128)(2,1)S(1)}, u32[]{:S(2)}, u32[]{:S(2)}) collective-permute-start(bf16[1,160,704]{2,1,0:T(8,128)(2,1)S(1)} %get-tuple-element.17), channel_id=1, source_target_pairs={{0,5},{1,6},{2,7},{3,0},{4,1},{5,2},{6,3},{7,4},{8,13},{9,14},{10,... | collective-permute-start | bytes 675848 | tf_op jit(solution)/shard_map/ppermute | solution.py:62
  299.4 15.4 %collective-permute-start.18 = (bf16[1,160,704]{2,1,0:T(8,128)(2,1)S(1)}, bf16[1,160,704]{2,1,0:T(8,128)(2,1)S(1)}, u32[]{:S(2)}, u32[]{:S(2)}) collective-permute-start(bf16[1,160,704]{2,1,0:T(8,128)(2,1)S(1)} %get-tuple-element.17), channel_id=1, source_target_pairs={{0,6},{1,7},{2,0},{3,1},{4,2},{5,3},{6,4},{7,5},{8,14},{9,15},{10,... | collective-permute-start | bytes 675848 | tf_op jit(solution)/shard_map/ppermute | solution.py:62
  304.0 12.5 %collective-permute-start.19 = (bf16[1,160,704]{2,1,0:T(8,128)(2,1)S(1)}, bf16[1,160,704]{2,1,0:T(8,128)(2,1)S(1)}, u32[]{:S(2)}, u32[]{:S(2)}) collective-permute-start(bf16[1,160,704]{2,1,0:T(8,128)(2,1)S(1)} %get-tuple-element.17), channel_id=1, source_target_pairs={{0,7},{1,0},{2,1},{3,2},{4,3},{5,4},{6,5},{7,6},{8,15},{9,8},{10,9... | collective-permute-start | bytes 675848 | tf_op jit(solution)/shard_map/ppermute | solution.py:62
  316.4 1.3 copy-start.2
  319.9 1.1 copy-start.12
  323.6 8.0 %copy-start.11 = (f32[256,2]{0,1:T(2,128)S(1)}, f32[256,2]{0,1:T(2,128)}, u32[]{:S(2)}) copy-start(f32[256,2]{0,1:T(2,128)} %param.19) | copy-start | bytes 6148
  323.6 83.5 %all-to-all-start.1 = ((bf16[1,64,20,512]{3,2,0,1:T(8,128)(2,1)}), bf16[1,64,20,512]{3,2,0,1:T(8,128)(2,1)S(1)}, u32[]{:S(2)}, u32[]{:S(2)}) async-start(bf16[1,64,20,512]{3,2,0,1:T(8,128)(2,1)} %bitcast.113), calls=%async_computation.1 | async-start | bytes 3145728 | tf_op jit(solution)/shard_map/all_to_all | solution.py:159
  412.3 3.2 copy-start.4

commit v4 on v3

--- a/solution.py
+++ b/solution.py
@@ -11,32 +11,34 @@
 EPSILON = 1e-06
 
 
+def pack_window(decay, state):
+    heads, rows, cols = state.shape
+    high = decay.astype(jnp.bfloat16)
+    low = (decay - high.astype(jnp.float32)).astype(jnp.bfloat16)
+    tail = jnp.broadcast_to(jnp.stack([high, low], axis=1)[:, :, None], (heads, 2, cols))
+    return jnp.concatenate([state.astype(jnp.bfloat16), tail], axis=1)
+
+
 def exclusive_scan(decay, state, axis):
     place = lax.axis_index(axis)
     count = lax.axis_size(axis)
-    heads, rows, cols = state.shape
-    own = jnp.concatenate(
-        [state, jnp.broadcast_to(decay[:, None, None], (heads, 1, cols))], axis=1
-    )
-    window = own
+    rows = state.shape[1]
+    window_decay = decay
+    window_state = state
     before_decay = jnp.ones_like(decay)
     before_state = jnp.zeros_like(state)
     shift = 1
     while shift < count:
         pairs = [(j, j + shift) for j in range(count - shift)]
-        got = lax.ppermute(window, axis, pairs)
+        got = lax.ppermute(pack_window(window_decay, window_state), axis, pairs)
         valid = place >= shift
-        got_state = got[:, :rows, :]
-        got_decay = jnp.where(valid, got[:, rows, 0], 1.0)
+        got_state = got[:, :rows, :].astype(jnp.float32)
+        got_decay = got[:, rows, 0].astype(jnp.float32) + got[:, rows + 1, 0].astype(jnp.float32)
+        got_decay = jnp.where(valid, got_decay, 1.0)
         before_state = before_decay[:, None, None] * got_state + before_state
         before_decay = before_decay * got_decay
-        window_decay = window[:, rows, 0]
-        window_state = window_decay[:, None, None] * got_state + window[:, :rows, :]
+        window_state = window_decay[:, None, None] * got_state + window_state
         window_decay = window_decay * got_decay
-        window = jnp.concatenate(
-            [window_state, jnp.broadcast_to(window_decay[:, None, None], (heads, 1, cols))],
-            axis=1,
-        )
         shift *= 2
     return before_state
 

time: 418 us -> 375 us (0.90)
  waiting for transfers between devices: 285 us -> 251 us
  starting transfers between devices: 73.5 us -> 67 us
    ppermute x6, waiting for transfers between devices: 97.9 us -> 64.6 us  [exclusive_scan(): got = lax.ppermute(pack_window(window_decay, window_state), axis, pairs)]
    all_to_all x1, starting transfers between devices: 17.6 us -> 9.93 us  [per_device(): lax.all_to_all(send_buffer, 'seq', split_axis=0, concat_axis=1, tiled=True)]
  transfers between devices with their start and end apart: 22 -> 22, of which waited for: 17 -> 16; matrix products, arithmetic and copies ran while one was open for 1% -> 1% of each run, Pallas kernels for 0% -> 0%
where the time goes in v4:
time: 375 us; the launch traced here: 373 us
  waiting for transfers between devices  251 us (67%)
  starting transfers between devices  67 us (18%)
  local copies, waits for them, and re-layouts  21.5 us (6%)
  blocking collectives  13.1 us (3%)
  matrix products  10.7 us (3%)
  other arithmetic  9.79 us (3%)
    all_to_all x1, waiting for transfers between devices, per_device(): lax.all_to_all(send_buffer, 'seq', split_axis=0, concat_axis=1, tiled=True)  75.6 us
    all_to_all x1, waiting for transfers between devices, per_device(): lax.all_to_all(computed, 'seq', split_axis=1, concat_axis=0, tiled=True)  75.4 us
    ppermute x6, waiting for transfers between devices, exclusive_scan(): got = lax.ppermute(pack_window(window_decay, window_state), axis, pairs)  64.6 us
    ppermute x7, waiting for transfers between devices, head_reduce_activate(): total = total + lax.ppermute(outgoing, axis, pairs).astype(jnp.float32)  22.6 us
    ppermute x7, starting transfers between devices, head_reduce_activate(): gathered.append(lax.ppermute(mine, axis, pairs))  18.7 us
    ppermute x7, starting transfers between devices, head_reduce_activate(): total = total + lax.ppermute(outgoing, axis, pairs).astype(jnp.float32)  18.5 us
    psum x1, blocking collectives, per_device(): total_squares = lax.psum(local_squares, 'head')  13.1 us
    ppermute x7, waiting for transfers between devices, head_reduce_activate(): gathered.append(lax.ppermute(mine, axis, pairs))  12.3 us
  transfers between devices with their start and end apart: 22, of which 16 were waited for; matrix products, arithmetic and copies ran while one was open for 1% of the time, Pallas kernels for 0%

profile of v4, /device:TPU:6, one launch (start us, length us, event | category | flops | bytes accessed | tf_op | source)
XLA Modules:
  0.0 373.4 jit_solution(11863729706242459132)
XLA Ops:
  5.2 3.8 %collective-permute-start = (bf16[4,130,128]{2,1,0:T(8,128)(2,1)S(1)}, bf16[4,130,128]{2,1,0:T(8,128)(2,1)S(1)}, u32[]{:S(2)}, u32[]{:S(2)}) collective-permute-start(bf16[4,130,128]{2,1,0:T(8,128)(2,1)S(1)} %pad_maximum_fusion), channel_id=1, source_target_pairs={{0,8},{8,16},{16,24},{24,32},{32,40},{40,48},{48,56},{56,64},{64,7... | collective-permute-start | bytes 399368 | tf_op jit(solution)/shard_map/ppermute | solution.py:33
  9.0 11.5 %collective-permute-done = bf16[4,130,128]{2,1,0:T(8,128)(2,1)S(1)} collective-permute-done((bf16[4,130,128]{2,1,0:T(8,128)(2,1)S(1)}, bf16[4,130,128]{2,1,0:T(8,128)(2,1)S(1)}, u32[]{:S(2)}, u32[]{:S(2)}) %collective-permute-start) | collective-permute-done | bytes 133152 | tf_op jit(solution)/shard_map/ppermute | solution.py:33
  21.0 1.9 collective-permute-start.1
  23.0 10.1 %collective-permute-done.1 = bf16[4,130,128]{2,1,0:T(8,128)(2,1)S(1)} collective-permute-done((bf16[4,130,128]{2,1,0:T(8,128)(2,1)S(1)}, bf16[4,130,128]{2,1,0:T(8,128)(2,1)S(1)}, u32[]{:S(2)}, u32[]{:S(2)}) %collective-permute-start.1) | collective-permute-done | bytes 133152 | tf_op jit(solution)/shard_map/ppermute | solution.py:33
  33.8 1.9 collective-permute-start.2
  36.0 15.0 %collective-permute-done.2 = bf16[4,130,128]{2,1,0:T(8,128)(2,1)S(1)} collective-permute-done((bf16[4,130,128]{2,1,0:T(8,128)(2,1)S(1)}, bf16[4,130,128]{2,1,0:T(8,128)(2,1)S(1)}, u32[]{:S(2)}, u32[]{:S(2)}) %collective-permute-start.2) | collective-permute-done | bytes 133152 | tf_op jit(solution)/shard_map/ppermute | solution.py:33
  51.5 1.9 collective-permute-start.3
  54.0 17.2 %collective-permute-done.3 = bf16[4,130,128]{2,1,0:T(8,128)(2,1)S(1)} collective-permute-done((bf16[4,130,128]{2,1,0:T(8,128)(2,1)S(1)}, bf16[4,130,128]{2,1,0:T(8,128)(2,1)S(1)}, u32[]{:S(2)}, u32[]{:S(2)}) %collective-permute-start.3) | collective-permute-done | bytes 133152 | tf_op jit(solution)/shard_map/ppermute | solution.py:33
  71.6 1.3 collective-permute-start.4
  73.0 2.3 fusion.6
  75.3 3.8 %collective-permute-done.4 = bf16[4,130,128]{2,1,0:T(8,128)(2,1)S(1)} collective-permute-done((bf16[4,130,128]{2,1,0:T(8,128)(2,1)S(1)}, bf16[4,130,128]{2,1,0:T(8,128)(2,1)S(1)}, u32[]{:S(2)}, u32[]{:S(2)}) %collective-permute-start.4) | collective-permute-done | bytes 133152 | tf_op jit(solution)/shard_map/ppermute | solution.py:33
  79.6 1.3 collective-permute-start.5
  81.2 6.9 %collective-permute-done.5 = bf16[4,130,128]{2,1,0:T(8,128)(2,1)S(1)} collective-permute-done((bf16[4,130,128]{2,1,0:T(8,128)(2,1)S(1)}, bf16[4,130,128]{2,1,0:T(8,128)(2,1)S(1)}, u32[]{:S(2)}, u32[]{:S(2)}) %collective-permute-start.5) | collective-permute-done | bytes 133152 | tf_op jit(solution)/shard_map/ppermute | solution.py:33
  88.1 1.8 multiply_reduce_fusion.1
  90.4 13.1 %psum.7 = f32[256]{0:T(256)S(1)} all-reduce(f32[256]{0:T(256)S(1)} %get-tuple-element.19), channel_id=1, replica_groups=mesh['seq'=64,'head'=8] {'head'}, use_global_device_ids=true, to_apply=%region_6.7 | all-reduce | flops 256 | bytes 2048 | tf_op jit(solution)/shard_map/psum | solution.py:123
  105.3 9.9 %all-to-all-start = ((bf16[64,1,20,512]{3,2,1,0:T(8,128)(2,1)}), bf16[64,1,20,512]{3,2,1,0:T(8,128)(2,1)S(1)}, u32[]{:S(2)}, u32[]{:S(2)}) async-start(bf16[64,1,20,512]{3,2,1,0:T(8,128)(2,1)} %bitcast.8), calls=%async_computation | async-start | bytes 3145728 | tf_op jit(solution)/shard_map/all_to_all | solution.py:150
  115.3 75.6 %all-to-all-done = bf16[64,1,20,512]{3,2,1,0:T(8,128)(2,1)S(1)} async-done(((bf16[64,1,20,512]{3,2,1,0:T(8,128)(2,1)}), bf16[64,1,20,512]{3,2,1,0:T(8,128)(2,1)S(1)}, u32[]{:S(2)}, u32[]{:S(2)}) %all-to-all-start) | async-done | bytes 1310752 | tf_op jit(solution)/shard_map/all_to_all | solution.py:150
  192.2 3.5 convolution_convert_fusion
  195.7 1.6 dynamic-slice_bitcast_fusion.6
  197.7 1.9 collective-permute-start.10
  199.6 2.4 collective-permute-start.11
  202.6 3.5 collective-permute-start.7
  206.1 6.2 %collective-permute-done.10 = bf16[1,160,1408]{2,1,0:T(8,128)(2,1)S(1)} collective-permute-done((bf16[1,160,1408]{2,1,0:T(8,128)(2,1)S(1)}, bf16[1,160,1408]{2,1,0:T(8,128)(2,1)S(1)}, u32[]{:S(2)}, u32[]{:S(2)}) %collective-permute-start.10) | collective-permute-done | bytes 450592 | tf_op jit(solution)/shard_map/ppermute | solution.py:57
  212.3 1.9 collective-permute-start.8
  214.2 1.8 collective-permute-done.11
  216.8 8.2 %collective-permute-start.9 = (bf16[1,160,1408]{2,1,0:T(8,128)(2,1)S(1)}, bf16[1,160,1408]{2,1,0:T(8,128)(2,1)}, u32[]{:S(2)}, u32[]{:S(2)}) collective-permute-start(bf16[1,160,1408]{2,1,0:T(8,128)(2,1)S(1)} %get-tuple-element.41), channel_id=1, source_target_pairs={{0,4},{1,5},{2,6},{3,7},{4,0},{5,1},{6,2},{7,3},{8,12},{9,13},{10,... | collective-permute-start | bytes 1351688 | tf_op jit(solution)/shard_map/ppermute | solution.py:57
  225.1 10.0 %collective-permute-done.8 = bf16[1,160,1408]{2,1,0:T(8,128)(2,1)} collective-permute-done((bf16[1,160,1408]{2,1,0:T(8,128)(2,1)S(1)}, bf16[1,160,1408]{2,1,0:T(8,128)(2,1)}, u32[]{:S(2)}, u32[]{:S(2)}) %collective-permute-start.8) | collective-permute-done | bytes 450592 | tf_op jit(solution)/shard_map/ppermute | solution.py:57
  235.0 4.6 %collective-permute-done.9 = bf16[1,160,1408]{2,1,0:T(8,128)(2,1)} collective-permute-done((bf16[1,160,1408]{2,1,0:T(8,128)(2,1)S(1)}, bf16[1,160,1408]{2,1,0:T(8,128)(2,1)}, u32[]{:S(2)}, u32[]{:S(2)}) %collective-permute-start.9) | collective-permute-done | bytes 450592 | tf_op jit(solution)/shard_map/ppermute | solution.py:57
  239.7 2.3 fusion.18
  242.2 2.3 collective-permute-start.13
  244.5 1.9 collective-permute-start.14
  246.5 2.4 collective-permute-start.15
  248.9 5.4 %collective-permute-start.16 = (bf16[1,160,704]{2,1,0:T(8,128)(2,1)S(1)}, bf16[1,160,704]{2,1,0:T(8,128)(2,1)S(1)}, u32[]{:S(2)}, u32[]{:S(2)}) collective-permute-start(bf16[1,160,704]{2,1,0:T(8,128)(2,1)S(1)} %get-tuple-element.18), channel_id=1, source_target_pairs={{0,4},{1,5},{2,6},{3,7},{4,0},{5,1},{6,2},{7,3},{8,12},{9,13},{10,... | collective-permute-start | bytes 675848 | tf_op jit(solution)/shard_map/ppermute | solution.py:64
  254.3 2.1 collective-permute-start.17
  256.4 4.5 %collective-permute-start.18 = (bf16[1,160,704]{2,1,0:T(8,128)(2,1)S(1)}, bf16[1,160,704]{2,1,0:T(8,128)(2,1)S(1)}, u32[]{:S(2)}, u32[]{:S(2)}) collective-permute-start(bf16[1,160,704]{2,1,0:T(8,128)(2,1)S(1)} %get-tuple-element.18), channel_id=1, source_target_pairs={{0,6},{1,7},{2,0},{3,1},{4,2},{5,3},{6,4},{7,5},{8,14},{9,15},{10,... | collective-permute-start | bytes 675848 | tf_op jit(solution)/shard_map/ppermute | solution.py:64
  261.1 3.7 %collective-permute-done.16 = bf16[1,160,704]{2,1,0:T(8,128)(2,1)S(1)} collective-permute-done((bf16[1,160,704]{2,1,0:T(8,128)(2,1)S(1)}, bf16[1,160,704]{2,1,0:T(8,128)(2,1)S(1)}, u32[]{:S(2)}, u32[]{:S(2)}) %collective-permute-start.16) | collective-permute-done | bytes 225312 | tf_op jit(solution)/shard_map/ppermute | solution.py:64
  264.9 1.8 collective-permute-done.17
  266.7 5.1 %collective-permute-done.18 = bf16[1,160,704]{2,1,0:T(8,128)(2,1)S(1)} collective-permute-done((bf16[1,160,704]{2,1,0:T(8,128)(2,1)S(1)}, bf16[1,160,704]{2,1,0:T(8,128)(2,1)S(1)}, u32[]{:S(2)}, u32[]{:S(2)}) %collective-permute-start.18) | collective-permute-done | bytes 225312 | tf_op jit(solution)/shard_map/ppermute | solution.py:64
  271.8 1.6 collective-permute-done.19
  274.8 2.2 gather_fusion
  279.3 1.3 reshape.485
  280.6 7.7 %all-to-all-start.1 = ((bf16[1,64,20,512]{3,2,0,1:T(8,128)(2,1)}), bf16[1,64,20,512]{3,2,0,1:T(8,128)(2,1)S(1)}, u32[]{:S(2)}, u32[]{:S(2)}) async-start(bf16[1,64,20,512]{3,2,0,1:T(8,128)(2,1)} %bitcast.139), calls=%async_computation.1 | async-start | bytes 3145728 | tf_op jit(solution)/shard_map/all_to_all | solution.py:161
  288.7 75.4 %all-to-all-done.1 = bf16[1,64,20,512]{3,2,0,1:T(8,128)(2,1)S(1)} async-done(((bf16[1,64,20,512]{3,2,0,1:T(8,128)(2,1)}), bf16[1,64,20,512]{3,2,0,1:T(8,128)(2,1)S(1)}, u32[]{:S(2)}, u32[]{:S(2)}) %all-to-all-start.1) | async-done | bytes 1310752 | tf_op jit(solution)/shard_map/all_to_all | solution.py:161
  364.1 1.4 convert_reduce_fusion
  365.6 1.5 reshape.486
  367.1 2.3 gather_fusion.1
  369.4 1.9 reshape.500
  371.3 1.3 multiply_reduce_fusion
  (132 shorter events, 19.1 us)
Async XLA Ops:
  0.0 192.2 %copy-start = (bf16[1,512,1408]{2,1,0:T(8,128)(2,1)S(1)}, bf16[1,512,1408]{2,1,0:T(8,128)(2,1)}, u32[]{:S(2)}) copy-start(bf16[1,512,1408]{2,1,0:T(8,128)(2,1)} %param.20) | copy-start | bytes 4325380
  0.0 35.7 %copy-start.8 = (s32[256,2]{0,1:T(2,128)S(1)}, s32[256,2]{0,1:T(2,128)}, u32[]{:S(2)}) copy-start(s32[256,2]{0,1:T(2,128)} %param.18) | copy-start | bytes 6148
  5.2 15.3 %collective-permute-start = (bf16[4,130,128]{2,1,0:T(8,128)(2,1)S(1)}, bf16[4,130,128]{2,1,0:T(8,128)(2,1)S(1)}, u32[]{:S(2)}, u32[]{:S(2)}) collective-permute-start(bf16[4,130,128]{2,1,0:T(8,128)(2,1)S(1)} %pad_maximum_fusion), channel_id=1, source_target_pairs={{0,8},{8,16},{16,24},{24,32},{32,40},{40,48},{48,56},{56,64},{64,7... | collective-permute-start | bytes 399368 | tf_op jit(solution)/shard_map/ppermute | solution.py:33
  21.0 12.2 %collective-permute-start.1 = (bf16[4,130,128]{2,1,0:T(8,128)(2,1)S(1)}, bf16[4,130,128]{2,1,0:T(8,128)(2,1)S(1)}, u32[]{:S(2)}, u32[]{:S(2)}) collective-permute-start(bf16[4,130,128]{2,1,0:T(8,128)(2,1)S(1)} %pad_maximum_fusion.1), channel_id=1, source_target_pairs={{0,16},{8,24},{16,32},{24,40},{32,48},{40,56},{48,64},{56,72},{64,... | collective-permute-start | bytes 399368 | tf_op jit(solution)/shard_map/ppermute | solution.py:33
  33.5 39.4 %copy-start.6 = (bf16[256,512]{1,0:T(8,128)(2,1)S(1)}, bf16[256,512]{1,0:T(8,128)(2,1)}, u32[]{:S(2)}) copy-start(bf16[256,512]{1,0:T(8,128)(2,1)} %param.14) | copy-start | bytes 786436
  33.8 17.3 %collective-permute-start.2 = (bf16[4,130,128]{2,1,0:T(8,128)(2,1)S(1)}, bf16[4,130,128]{2,1,0:T(8,128)(2,1)S(1)}, u32[]{:S(2)}, u32[]{:S(2)}) collective-permute-start(bf16[4,130,128]{2,1,0:T(8,128)(2,1)S(1)} %pad_maximum_fusion.2), channel_id=1, source_target_pairs={{0,32},{8,40},{16,48},{24,56},{32,64},{40,72},{48,80},{56,88},{64,... | collective-permute-start | bytes 399368 | tf_op jit(solution)/shard_map/ppermute | solution.py:33
  51.5 19.6 %collective-permute-start.3 = (bf16[4,130,128]{2,1,0:T(8,128)(2,1)S(1)}, bf16[4,130,128]{2,1,0:T(8,128)(2,1)S(1)}, u32[]{:S(2)}, u32[]{:S(2)}) collective-permute-start(bf16[4,130,128]{2,1,0:T(8,128)(2,1)S(1)} %pad_maximum_fusion.3), channel_id=1, source_target_pairs={{0,64},{8,72},{16,80},{24,88},{32,96},{40,104},{48,112},{56,120},{... | collective-permute-start | bytes 399368 | tf_op jit(solution)/shard_map/ppermute | solution.py:33
  71.6 7.5 %collective-permute-start.4 = (bf16[4,130,128]{2,1,0:T(8,128)(2,1)S(1)}, bf16[4,130,128]{2,1,0:T(8,128)(2,1)S(1)}, u32[]{:S(2)}, u32[]{:S(2)}) collective-permute-start(bf16[4,130,128]{2,1,0:T(8,128)(2,1)S(1)} %pad_maximum_fusion.4), channel_id=1, source_target_pairs={{0,128},{8,136},{16,144},{24,152},{32,160},{40,168},{48,176},{56,1... | collective-permute-start | bytes 399368 | tf_op jit(solution)/shard_map/ppermute | solution.py:33
  79.6 8.5 %collective-permute-start.5 = (bf16[4,130,128]{2,1,0:T(8,128)(2,1)S(1)}, bf16[4,130,128]{2,1,0:T(8,128)(2,1)S(1)}, u32[]{:S(2)}, u32[]{:S(2)}) collective-permute-start(bf16[4,130,128]{2,1,0:T(8,128)(2,1)S(1)} %pad_maximum_fusion.5), channel_id=1, source_target_pairs={{0,256},{8,264},{16,272},{24,280},{32,288},{40,296},{48,304},{56,3... | collective-permute-start | bytes 399368 | tf_op jit(solution)/shard_map/ppermute | solution.py:33
  88.1 2.1 copy-start.7
  88.1 2.1 copy-start.9
  89.9 13.6 %copy-start.12 = (f32[512]{0:T(512)S(1)}, f32[512]{0:T(512)}, u32[]{:S(2)}) copy-start(f32[512]{0:T(512)} %param.17) | copy-start | bytes 6148
  90.3 13.1 %copy-start.3 = (bf16[256,512]{1,0:T(8,128)(2,1)}, bf16[256,512]{1,0:T(8,128)(2,1)S(1)}, u32[]{:S(2)}) copy-start(bf16[256,512]{1,0:T(8,128)(2,1)S(1)} %get-tuple-element.20) | copy-start | bytes 786436
  105.3 85.7 %all-to-all-start = ((bf16[64,1,20,512]{3,2,1,0:T(8,128)(2,1)}), bf16[64,1,20,512]{3,2,1,0:T(8,128)(2,1)S(1)}, u32[]{:S(2)}, u32[]{:S(2)}) async-start(bf16[64,1,20,512]{3,2,1,0:T(8,128)(2,1)} %bitcast.8), calls=%async_computation | async-start | bytes 3145728 | tf_op jit(solution)/shard_map/all_to_all | solution.py:150
  195.7 2.0 copy-start.1
  197.7 14.6 %collective-permute-start.10 = (bf16[1,160,1408]{2,1,0:T(8,128)(2,1)S(1)}, bf16[1,160,1408]{2,1,0:T(8,128)(2,1)S(1)}, u32[]{:S(2)}, u32[]{:S(2)}) collective-permute-start(bf16[1,160,1408]{2,1,0:T(8,128)(2,1)S(1)} %get-tuple-element.40), channel_id=1, source_target_pairs={{0,5},{1,6},{2,7},{3,0},{4,1},{5,2},{6,3},{7,4},{8,13},{9,14},{10,... | collective-permute-start | bytes 1351688 | tf_op jit(solution)/shard_map/ppermute | solution.py:57
  199.6 16.4 %collective-permute-start.11 = (bf16[1,160,1408]{2,1,0:T(8,128)(2,1)S(1)}, bf16[1,160,1408]{2,1,0:T(8,128)(2,1)S(1)}, u32[]{:S(2)}, u32[]{:S(2)}) collective-permute-start(bf16[1,160,1408]{2,1,0:T(8,128)(2,1)S(1)} %get-tuple-element.39), channel_id=1, source_target_pairs={{0,6},{1,7},{2,0},{3,1},{4,2},{5,3},{6,4},{7,5},{8,14},{9,15},{10,... | collective-permute-start | bytes 1351688 | tf_op jit(solution)/shard_map/ppermute | solution.py:57
  202.1 23.0 %collective-permute-start.12 = (bf16[1,160,1408]{2,1,0:T(8,128)(2,1)}, bf16[1,160,1408]{2,1,0:T(8,128)(2,1)}, u32[]{:S(2)}, u32[]{:S(2)}) collective-permute-start(bf16[1,160,1408]{2,1,0:T(8,128)(2,1)} %get-tuple-element.38), channel_id=1, source_target_pairs={{0,7},{1,0},{2,1},{3,2},{4,3},{5,4},{6,5},{7,6},{8,15},{9,8},{10,9... | collective-permute-start | bytes 1351688 | tf_op jit(solution)/shard_map/ppermute | solution.py:57
  202.4 22.6 %collective-permute-start.6 = (bf16[1,160,1408]{2,1,0:T(8,128)(2,1)}, bf16[1,160,1408]{2,1,0:T(8,128)(2,1)}, u32[]{:S(2)}, u32[]{:S(2)}) collective-permute-start(bf16[1,160,1408]{2,1,0:T(8,128)(2,1)} %get-tuple-element.37), channel_id=1, source_target_pairs={{0,1},{1,2},{2,3},{3,4},{4,5},{5,6},{6,7},{7,0},{8,9},{9,10},{10,1... | collective-permute-start | bytes 1351688 | tf_op jit(solution)/shard_map/ppermute | solution.py:57
  202.6 22.5 %collective-permute-start.7 = (bf16[1,160,1408]{2,1,0:T(8,128)(2,1)S(1)}, bf16[1,160,1408]{2,1,0:T(8,128)(2,1)}, u32[]{:S(2)}, u32[]{:S(2)}) collective-permute-start(bf16[1,160,1408]{2,1,0:T(8,128)(2,1)S(1)} %get-tuple-element.43), channel_id=1, source_target_pairs={{0,2},{1,3},{2,4},{3,5},{4,6},{5,7},{6,0},{7,1},{8,10},{9,11},{10,... | collective-permute-start | bytes 1351688 | tf_op jit(solution)/shard_map/ppermute | solution.py:57
  212.3 22.7 %collective-permute-start.8 = (bf16[1,160,1408]{2,1,0:T(8,128)(2,1)S(1)}, bf16[1,160,1408]{2,1,0:T(8,128)(2,1)}, u32[]{:S(2)}, u32[]{:S(2)}) collective-permute-start(bf16[1,160,1408]{2,1,0:T(8,128)(2,1)S(1)} %get-tuple-element.42), channel_id=1, source_target_pairs={{0,3},{1,4},{2,5},{3,6},{4,7},{5,0},{6,1},{7,2},{8,11},{9,12},{10,... | collective-permute-start | bytes 1351688 | tf_op jit(solution)/shard_map/ppermute | solution.py:57
  216.0 0.8 copy-start.5
  216.8 22.9 %collective-permute-start.9 = (bf16[1,160,1408]{2,1,0:T(8,128)(2,1)S(1)}, bf16[1,160,1408]{2,1,0:T(8,128)(2,1)}, u32[]{:S(2)}, u32[]{:S(2)}) collective-permute-start(bf16[1,160,1408]{2,1,0:T(8,128)(2,1)S(1)} %get-tuple-element.41), channel_id=1, source_target_pairs={{0,4},{1,5},{2,6},{3,7},{4,0},{5,1},{6,2},{7,3},{8,12},{9,13},{10,... | collective-permute-start | bytes 1351688 | tf_op jit(solution)/shard_map/ppermute | solution.py:57
  242.2 14.3 %collective-permute-start.13 = (bf16[1,160,704]{2,1,0:T(8,128)(2,1)S(1)}, bf16[1,160,704]{2,1,0:T(8,128)(2,1)S(1)}, u32[]{:S(2)}, u32[]{:S(2)}) collective-permute-start(bf16[1,160,704]{2,1,0:T(8,128)(2,1)S(1)} %get-tuple-element.18), channel_id=1, source_target_pairs={{0,1},{1,2},{2,3},{3,4},{4,5},{5,6},{6,7},{7,0},{8,9},{9,10},{10,1... | collective-permute-start | bytes 675848 | tf_op jit(solution)/shard_map/ppermute | solution.py:64
  244.5 16.4 %collective-permute-start.14 = (bf16[1,160,704]{2,1,0:T(8,128)(2,1)S(1)}, bf16[1,160,704]{2,1,0:T(8,128)(2,1)S(1)}, u32[]{:S(2)}, u32[]{:S(2)}) collective-permute-start(bf16[1,160,704]{2,1,0:T(8,128)(2,1)S(1)} %get-tuple-element.18), channel_id=1, source_target_pairs={{0,2},{1,3},{2,4},{3,5},{4,6},{5,7},{6,0},{7,1},{8,10},{9,11},{10,... | collective-permute-start | bytes 675848 | tf_op jit(solution)/shard_map/ppermute | solution.py:64
  246.5 14.6 %collective-permute-start.15 = (bf16[1,160,704]{2,1,0:T(8,128)(2,1)S(1)}, bf16[1,160,704]{2,1,0:T(8,128)(2,1)S(1)}, u32[]{:S(2)}, u32[]{:S(2)}) collective-permute-start(bf16[1,160,704]{2,1,0:T(8,128)(2,1)S(1)} %get-tuple-element.18), channel_id=1, source_target_pairs={{0,3},{1,4},{2,5},{3,6},{4,7},{5,0},{6,1},{7,2},{8,11},{9,12},{10,... | collective-permute-start | bytes 675848 | tf_op jit(solution)/shard_map/ppermute | solution.py:64
  248.9 15.9 %collective-permute-start.16 = (bf16[1,160,704]{2,1,0:T(8,128)(2,1)S(1)}, bf16[1,160,704]{2,1,0:T(8,128)(2,1)S(1)}, u32[]{:S(2)}, u32[]{:S(2)}) collective-permute-start(bf16[1,160,704]{2,1,0:T(8,128)(2,1)S(1)} %get-tuple-element.18), channel_id=1, source_target_pairs={{0,4},{1,5},{2,6},{3,7},{4,0},{5,1},{6,2},{7,3},{8,12},{9,13},{10,... | collective-permute-start | bytes 675848 | tf_op jit(solution)/shard_map/ppermute | solution.py:64
  254.3 12.3 %collective-permute-start.17 = (bf16[1,160,704]{2,1,0:T(8,128)(2,1)S(1)}, bf16[1,160,704]{2,1,0:T(8,128)(2,1)S(1)}, u32[]{:S(2)}, u32[]{:S(2)}) collective-permute-start(bf16[1,160,704]{2,1,0:T(8,128)(2,1)S(1)} %get-tuple-element.18), channel_id=1, source_target_pairs={{0,5},{1,6},{2,7},{3,0},{4,1},{5,2},{6,3},{7,4},{8,13},{9,14},{10,... | collective-permute-start | bytes 675848 | tf_op jit(solution)/shard_map/ppermute | solution.py:64
  256.4 15.4 %collective-permute-start.18 = (bf16[1,160,704]{2,1,0:T(8,128)(2,1)S(1)}, bf16[1,160,704]{2,1,0:T(8,128)(2,1)S(1)}, u32[]{:S(2)}, u32[]{:S(2)}) collective-permute-start(bf16[1,160,704]{2,1,0:T(8,128)(2,1)S(1)} %get-tuple-element.18), channel_id=1, source_target_pairs={{0,6},{1,7},{2,0},{3,1},{4,2},{5,3},{6,4},{7,5},{8,14},{9,15},{10,... | collective-permute-start | bytes 675848 | tf_op jit(solution)/shard_map/ppermute | solution.py:64
  261.0 12.5 %collective-permute-start.19 = (bf16[1,160,704]{2,1,0:T(8,128)(2,1)S(1)}, bf16[1,160,704]{2,1,0:T(8,128)(2,1)S(1)}, u32[]{:S(2)}, u32[]{:S(2)}) collective-permute-start(bf16[1,160,704]{2,1,0:T(8,128)(2,1)S(1)} %get-tuple-element.18), channel_id=1, source_target_pairs={{0,7},{1,0},{2,1},{3,2},{4,3},{5,4},{6,5},{7,6},{8,15},{9,8},{10,9... | collective-permute-start | bytes 675848 | tf_op jit(solution)/shard_map/ppermute | solution.py:64
  273.5 1.3 copy-start.2
  277.0 1.1 copy-start.11
  280.6 8.0 %copy-start.10 = (f32[256,2]{0,1:T(2,128)S(1)}, f32[256,2]{0,1:T(2,128)}, u32[]{:S(2)}) copy-start(f32[256,2]{0,1:T(2,128)} %param.19) | copy-start | bytes 6148
  280.6 83.5 %all-to-all-start.1 = ((bf16[1,64,20,512]{3,2,0,1:T(8,128)(2,1)}), bf16[1,64,20,512]{3,2,0,1:T(8,128)(2,1)S(1)}, u32[]{:S(2)}, u32[]{:S(2)}) async-start(bf16[1,64,20,512]{3,2,0,1:T(8,128)(2,1)} %bitcast.139), calls=%async_computation.1 | async-start | bytes 3145728 | tf_op jit(solution)/shard_map/all_to_all | solution.py:161
  369.4 3.2 copy-start.4

commit v5 on v4

--- a/solution.py
+++ b/solution.py
@@ -46,26 +46,35 @@
 def head_reduce_activate(partial, axis, block_units):
     place = lax.axis_index(axis)
     count = lax.axis_size(axis)
+    chips = count // 2
+    core = place % 2
+    chip = place // 2
     blocks_here, rows, width = partial.shape
     share = rows // count
-    pieces = partial.reshape(blocks_here, count, share, width)
-    total = lax.dynamic_index_in_dim(pieces, place, 1, False).astype(jnp.float32)
-    for shift in range(1, count):
-        target = (place + shift) % count
-        outgoing = lax.dynamic_index_in_dim(pieces, target, 1, False)
-        pairs = [(j, (j + shift) % count) for j in range(count)]
+    pieces = partial.reshape(blocks_here, chips, 2, share, width)
+    sibling = [(j, j ^ 1) for j in range(count)]
+    kept = lax.dynamic_index_in_dim(pieces, core, 2, False).astype(jnp.float32)
+    handed = lax.dynamic_index_in_dim(pieces, 1 - core, 2, False)
+    pair_sum = kept + lax.ppermute(handed, axis, sibling).astype(jnp.float32)
+    total = lax.dynamic_index_in_dim(pair_sum, chip, 1, False)
+    for step in range(1, chips):
+        target = (chip + step) % chips
+        outgoing = lax.dynamic_index_in_dim(pair_sum, target, 1, False).astype(jnp.bfloat16)
+        pairs = [(j, (j + 2 * step) % count) for j in range(count)]
         total = total + lax.ppermute(outgoing, axis, pairs).astype(jnp.float32)
     gate = total[:, :, :block_units]
     up = total[:, :, block_units:]
     mine = (jax.nn.silu(gate) * up).astype(jnp.bfloat16)
     gathered = [mine]
-    for shift in range(1, count):
-        pairs = [(j, (j + shift) % count) for j in range(count)]
+    for step in range(1, chips):
+        pairs = [(j, (j + 2 * step) % count) for j in range(count)]
         gathered.append(lax.ppermute(mine, axis, pairs))
     stacked = jnp.stack(gathered, axis=1)
-    origin = (place - jnp.arange(count)) % count
-    ordered = jnp.take(stacked, origin, axis=1)
-    return ordered.reshape(blocks_here, rows, block_units)
+    ordered = jnp.take(stacked, (chip - jnp.arange(chips)) % chips, axis=1)
+    other = lax.ppermute(ordered, axis, sibling)
+    both = jnp.stack([ordered, other], axis=2)
+    full = jnp.take(both, jnp.arange(2) ^ core, axis=2)
+    return full.reshape(blocks_here, rows, block_units)
 
 
 def per_device(

time: 375 us -> 363 us (0.968)
  starting transfers between devices: 67 us -> 52 us
    ppermute x7 -> x3, starting transfers between devices: 18.5 us -> 8.96 us  [head_reduce_activate(): total = total + lax.ppermute(outgoing, axis, pairs).astype(jnp.float32)]
    ppermute x7 -> x3, starting transfers between devices: 18.7 us -> 9.83 us  [head_reduce_activate(): gathered.append(lax.ppermute(mine, axis, pairs))]
    ppermute x0 -> x2, waiting for transfers between devices: none -> 5.98 us  [the longest x1 3.83 us: head_reduce_activate(): pair_sum = kept + lax.ppermute(handed, axis, sibling).astype(jnp.float32)]
    ppermute x0 -> x2, starting transfers between devices: none -> 4.01 us  [the longest x1 2.1 us: head_reduce_activate(): other = lax.ppermute(ordered, axis, sibling)]
    ppermute x7 -> x3, waiting for transfers between devices: 12.3 us -> 8.37 us  [head_reduce_activate(): gathered.append(lax.ppermute(mine, axis, pairs))]
    ppermute x7 -> x3, waiting for transfers between devices: 22.6 us -> 18.7 us  [head_reduce_activate(): total = total + lax.ppermute(outgoing, axis, pairs).astype(jnp.float32)]
  transfers between devices with their start and end apart: 22 -> 16, of which waited for: 16 -> 15; matrix products, arithmetic and copies ran while one was open for 1% -> 1% of each run, Pallas kernels for 0% -> 0%
where the time goes in v5:
time: 363 us; the launch traced here: 362 us
  waiting for transfers between devices  249 us (69%)
  starting transfers between devices  52 us (14%)
  local copies, waits for them, and re-layouts  23.7 us (7%)
  other arithmetic  13.3 us (4%)
  blocking collectives  13.1 us (4%)
  matrix products  10.7 us (3%)
    all_to_all x1, waiting for transfers between devices, per_device(): lax.all_to_all(send_buffer, 'seq', split_axis=0, concat_axis=1, tiled=True)  75.7 us
    all_to_all x1, waiting for transfers between devices, per_device(): lax.all_to_all(computed, 'seq', split_axis=1, concat_axis=0, tiled=True)  75.2 us
    ppermute x6, waiting for transfers between devices, exclusive_scan(): got = lax.ppermute(pack_window(window_decay, window_state), axis, pairs)  64.6 us
    ppermute x3, waiting for transfers between devices, head_reduce_activate(): total = total + lax.ppermute(outgoing, axis, pairs).astype(jnp.float32)  18.7 us
    psum x1, blocking collectives, per_device(): total_squares = lax.psum(local_squares, 'head')  13.1 us
    ppermute x6, starting transfers between devices, exclusive_scan(): got = lax.ppermute(pack_window(window_decay, window_state), axis, pairs)  12.2 us
    all_to_all x1, starting transfers between devices, per_device(): lax.all_to_all(send_buffer, 'seq', split_axis=0, concat_axis=1, tiled=True)  9.93 us
    ppermute x3, starting transfers between devices, head_reduce_activate(): gathered.append(lax.ppermute(mine, axis, pairs))  9.83 us
  transfers between devices with their start and end apart: 16, of which 15 were waited for; matrix products, arithmetic and copies ran while one was open for 1% of the time, Pallas kernels for 0%

profile of v5, /device:TPU:6, one launch (start us, length us, event | category | flops | bytes accessed | tf_op | source)
XLA Modules:
  0.0 362.1 jit_solution(13154086013206094944)
XLA Ops:
  5.2 3.8 %collective-permute-start = (bf16[4,130,128]{2,1,0:T(8,128)(2,1)S(1)}, bf16[4,130,128]{2,1,0:T(8,128)(2,1)S(1)}, u32[]{:S(2)}, u32[]{:S(2)}) collective-permute-start(bf16[4,130,128]{2,1,0:T(8,128)(2,1)S(1)} %pad_maximum_fusion), channel_id=1, source_target_pairs={{0,8},{8,16},{16,24},{24,32},{32,40},{40,48},{48,56},{56,64},{64,7... | collective-permute-start | bytes 399368 | tf_op jit(solution)/shard_map/ppermute | solution.py:33
  9.0 11.5 %collective-permute-done = bf16[4,130,128]{2,1,0:T(8,128)(2,1)S(1)} collective-permute-done((bf16[4,130,128]{2,1,0:T(8,128)(2,1)S(1)}, bf16[4,130,128]{2,1,0:T(8,128)(2,1)S(1)}, u32[]{:S(2)}, u32[]{:S(2)}) %collective-permute-start) | collective-permute-done | bytes 133152 | tf_op jit(solution)/shard_map/ppermute | solution.py:33
  21.0 1.9 collective-permute-start.1
  23.0 10.1 %collective-permute-done.1 = bf16[4,130,128]{2,1,0:T(8,128)(2,1)S(1)} collective-permute-done((bf16[4,130,128]{2,1,0:T(8,128)(2,1)S(1)}, bf16[4,130,128]{2,1,0:T(8,128)(2,1)S(1)}, u32[]{:S(2)}, u32[]{:S(2)}) %collective-permute-start.1) | collective-permute-done | bytes 133152 | tf_op jit(solution)/shard_map/ppermute | solution.py:33
  33.8 1.9 collective-permute-start.2
  36.0 15.0 %collective-permute-done.2 = bf16[4,130,128]{2,1,0:T(8,128)(2,1)S(1)} collective-permute-done((bf16[4,130,128]{2,1,0:T(8,128)(2,1)S(1)}, bf16[4,130,128]{2,1,0:T(8,128)(2,1)S(1)}, u32[]{:S(2)}, u32[]{:S(2)}) %collective-permute-start.2) | collective-permute-done | bytes 133152 | tf_op jit(solution)/shard_map/ppermute | solution.py:33
  51.5 1.9 collective-permute-start.3
  54.0 17.2 %collective-permute-done.3 = bf16[4,130,128]{2,1,0:T(8,128)(2,1)S(1)} collective-permute-done((bf16[4,130,128]{2,1,0:T(8,128)(2,1)S(1)}, bf16[4,130,128]{2,1,0:T(8,128)(2,1)S(1)}, u32[]{:S(2)}, u32[]{:S(2)}) %collective-permute-start.3) | collective-permute-done | bytes 133152 | tf_op jit(solution)/shard_map/ppermute | solution.py:33
  71.6 1.3 collective-permute-start.4
  73.0 2.3 fusion.6
  75.3 3.8 %collective-permute-done.4 = bf16[4,130,128]{2,1,0:T(8,128)(2,1)S(1)} collective-permute-done((bf16[4,130,128]{2,1,0:T(8,128)(2,1)S(1)}, bf16[4,130,128]{2,1,0:T(8,128)(2,1)S(1)}, u32[]{:S(2)}, u32[]{:S(2)}) %collective-permute-start.4) | collective-permute-done | bytes 133152 | tf_op jit(solution)/shard_map/ppermute | solution.py:33
  79.6 1.3 collective-permute-start.5
  81.2 6.9 %collective-permute-done.5 = bf16[4,130,128]{2,1,0:T(8,128)(2,1)S(1)} collective-permute-done((bf16[4,130,128]{2,1,0:T(8,128)(2,1)S(1)}, bf16[4,130,128]{2,1,0:T(8,128)(2,1)S(1)}, u32[]{:S(2)}, u32[]{:S(2)}) %collective-permute-start.5) | collective-permute-done | bytes 133152 | tf_op jit(solution)/shard_map/ppermute | solution.py:33
  88.1 1.8 multiply_reduce_fusion.1
  90.4 13.1 %psum.7 = f32[256]{0:T(256)S(1)} all-reduce(f32[256]{0:T(256)S(1)} %get-tuple-element.17), channel_id=1, replica_groups=mesh['seq'=64,'head'=8] {'head'}, use_global_device_ids=true, to_apply=%region_6.7 | all-reduce | flops 256 | bytes 2048 | tf_op jit(solution)/shard_map/psum | solution.py:132
  104.0 1.3 broadcast_in_dim.131
  105.3 9.9 %all-to-all-start = ((bf16[64,1,20,512]{3,2,1,0:T(8,128)(2,1)}), bf16[64,1,20,512]{3,2,1,0:T(8,128)(2,1)S(1)}, u32[]{:S(2)}, u32[]{:S(2)}) async-start(bf16[64,1,20,512]{3,2,1,0:T(8,128)(2,1)} %bitcast.8), calls=%async_computation | async-start | bytes 3145728 | tf_op jit(solution)/shard_map/all_to_all | solution.py:159
  115.3 75.7 %all-to-all-done = bf16[64,1,20,512]{3,2,1,0:T(8,128)(2,1)S(1)} async-done(((bf16[64,1,20,512]{3,2,1,0:T(8,128)(2,1)}), bf16[64,1,20,512]{3,2,1,0:T(8,128)(2,1)S(1)}, u32[]{:S(2)}, u32[]{:S(2)}) %all-to-all-start) | async-done | bytes 1310752 | tf_op jit(solution)/shard_map/all_to_all | solution.py:159
  192.2 3.5 convolution_convert_fusion
  195.7 1.8 copy-done.2
  197.5 1.4 dynamic-slice_bitcast_fusion
  198.8 1.9 collective-permute-start.6
  200.8 3.8 %collective-permute-done.6 = bf16[1,4,160,1408]{3,2,1,0:T(8,128)(2,1)S(1)} collective-permute-done((bf16[1,4,160,1408]{3,2,1,0:T(8,128)(2,1)}, bf16[1,4,160,1408]{3,2,1,0:T(8,128)(2,1)S(1)}, u32[]{:S(2)}, u32[]{:S(2)}) %collective-permute-start.6) | collective-permute-done | bytes 1802272 | tf_op jit(solution)/shard_map/ppermute | solution.py:58
  204.7 1.8 convert_add_fusion
  206.5 1.8 copy-done.1
  209.2 1.9 collective-permute-start.7
  211.1 3.9 %collective-permute-start.8 = (bf16[1,160,1408]{2,1,0:T(8,128)(2,1)S(1)}, bf16[1,160,1408]{2,1,0:T(8,128)(2,1)S(1)}, u32[]{:S(2)}, u32[]{:S(2)}) collective-permute-start(bf16[1,160,1408]{2,1,0:T(8,128)(2,1)S(1)} %get-tuple-element.37), channel_id=1, source_target_pairs={{0,4},{1,5},{2,6},{3,7},{4,0},{5,1},{6,2},{7,3},{8,12},{9,13},{10,... | collective-permute-start | bytes 1351688 | tf_op jit(solution)/shard_map/ppermute | solution.py:64
  215.0 3.2 collective-permute-start.9
  218.2 16.3 %collective-permute-done.7 = bf16[1,160,1408]{2,1,0:T(8,128)(2,1)S(1)} collective-permute-done((bf16[1,160,1408]{2,1,0:T(8,128)(2,1)}, bf16[1,160,1408]{2,1,0:T(8,128)(2,1)S(1)}, u32[]{:S(2)}, u32[]{:S(2)}) %collective-permute-start.7) | collective-permute-done | bytes 450592 | tf_op jit(solution)/shard_map/ppermute | solution.py:64
  234.5 2.4 collective-permute-done.9
  236.9 1.5 fusion.15
  238.7 2.2 collective-permute-start.10
  240.9 5.8 %collective-permute-start.11 = (bf16[1,160,704]{2,1,0:T(8,128)(2,1)S(1)}, bf16[1,160,704]{2,1,0:T(8,128)(2,1)S(1)}, u32[]{:S(2)}, u32[]{:S(2)}) collective-permute-start(bf16[1,160,704]{2,1,0:T(8,128)(2,1)S(1)} %fusion.26), channel_id=1, source_target_pairs={{0,4},{1,5},{2,6},{3,7},{4,0},{5,1},{6,2},{7,3},{8,12},{9,13},{10,... | collective-permute-start | bytes 675848 | tf_op jit(solution)/shard_map/ppermute | solution.py:71
  246.6 1.9 collective-permute-start.12
  249.4 6.4 %collective-permute-done.11 = bf16[1,160,704]{2,1,0:T(8,128)(2,1)S(1)} collective-permute-done((bf16[1,160,704]{2,1,0:T(8,128)(2,1)S(1)}, bf16[1,160,704]{2,1,0:T(8,128)(2,1)S(1)}, u32[]{:S(2)}, u32[]{:S(2)}) %collective-permute-start.11) | collective-permute-done | bytes 225312 | tf_op jit(solution)/shard_map/ppermute | solution.py:71
  255.8 1.3 collective-permute-done.12
  258.0 2.1 collective-permute-start.13
  260.4 2.1 collective-permute-done.13
  262.7 2.0 gather_fusion.1
  264.6 1.8 bitcast_select_fusion
  268.8 1.3 reshape.563
  270.1 7.1 %all-to-all-start.1 = ((bf16[1,64,20,512]{3,2,0,1:T(8,128)(2,1)}), bf16[1,64,20,512]{3,2,0,1:T(8,128)(2,1)S(1)}, u32[]{:S(2)}, u32[]{:S(2)}) async-start(bf16[1,64,20,512]{3,2,0,1:T(8,128)(2,1)} %bitcast.144), calls=%async_computation.1 | async-start | bytes 3145728 | tf_op jit(solution)/shard_map/all_to_all | solution.py:170
  277.6 75.2 %all-to-all-done.1 = bf16[1,64,20,512]{3,2,0,1:T(8,128)(2,1)S(1)} async-done(((bf16[1,64,20,512]{3,2,0,1:T(8,128)(2,1)}), bf16[1,64,20,512]{3,2,0,1:T(8,128)(2,1)S(1)}, u32[]{:S(2)}, u32[]{:S(2)}) %all-to-all-start.1) | async-done | bytes 1310752 | tf_op jit(solution)/shard_map/all_to_all | solution.py:170
  352.8 1.4 convert_reduce_fusion
  354.3 1.5 reshape.564
  355.8 2.3 gather_fusion.2
  358.1 1.9 reshape.588
  360.0 1.3 multiply_reduce_fusion
  (123 shorter events, 17.7 us)
Async XLA Ops:
  0.0 192.2 %copy-start = (bf16[1,512,1408]{2,1,0:T(8,128)(2,1)S(1)}, bf16[1,512,1408]{2,1,0:T(8,128)(2,1)}, u32[]{:S(2)}) copy-start(bf16[1,512,1408]{2,1,0:T(8,128)(2,1)} %param.20) | copy-start | bytes 4325380
  0.0 35.7 %copy-start.7 = (s32[256,2]{0,1:T(2,128)S(1)}, s32[256,2]{0,1:T(2,128)}, u32[]{:S(2)}) copy-start(s32[256,2]{0,1:T(2,128)} %param.18) | copy-start | bytes 6148
  5.2 15.3 %collective-permute-start = (bf16[4,130,128]{2,1,0:T(8,128)(2,1)S(1)}, bf16[4,130,128]{2,1,0:T(8,128)(2,1)S(1)}, u32[]{:S(2)}, u32[]{:S(2)}) collective-permute-start(bf16[4,130,128]{2,1,0:T(8,128)(2,1)S(1)} %pad_maximum_fusion), channel_id=1, source_target_pairs={{0,8},{8,16},{16,24},{24,32},{32,40},{40,48},{48,56},{56,64},{64,7... | collective-permute-start | bytes 399368 | tf_op jit(solution)/shard_map/ppermute | solution.py:33
  21.0 12.2 %collective-permute-start.1 = (bf16[4,130,128]{2,1,0:T(8,128)(2,1)S(1)}, bf16[4,130,128]{2,1,0:T(8,128)(2,1)S(1)}, u32[]{:S(2)}, u32[]{:S(2)}) collective-permute-start(bf16[4,130,128]{2,1,0:T(8,128)(2,1)S(1)} %pad_maximum_fusion.1), channel_id=1, source_target_pairs={{0,16},{8,24},{16,32},{24,40},{32,48},{40,56},{48,64},{56,72},{64,... | collective-permute-start | bytes 399368 | tf_op jit(solution)/shard_map/ppermute | solution.py:33
  33.5 39.4 %copy-start.5 = (bf16[256,512]{1,0:T(8,128)(2,1)S(1)}, bf16[256,512]{1,0:T(8,128)(2,1)}, u32[]{:S(2)}) copy-start(bf16[256,512]{1,0:T(8,128)(2,1)} %param.14) | copy-start | bytes 786436
  33.8 17.3 %collective-permute-start.2 = (bf16[4,130,128]{2,1,0:T(8,128)(2,1)S(1)}, bf16[4,130,128]{2,1,0:T(8,128)(2,1)S(1)}, u32[]{:S(2)}, u32[]{:S(2)}) collective-permute-start(bf16[4,130,128]{2,1,0:T(8,128)(2,1)S(1)} %pad_maximum_fusion.2), channel_id=1, source_target_pairs={{0,32},{8,40},{16,48},{24,56},{32,64},{40,72},{48,80},{56,88},{64,... | collective-permute-start | bytes 399368 | tf_op jit(solution)/shard_map/ppermute | solution.py:33
  51.5 19.6 %collective-permute-start.3 = (bf16[4,130,128]{2,1,0:T(8,128)(2,1)S(1)}, bf16[4,130,128]{2,1,0:T(8,128)(2,1)S(1)}, u32[]{:S(2)}, u32[]{:S(2)}) collective-permute-start(bf16[4,130,128]{2,1,0:T(8,128)(2,1)S(1)} %pad_maximum_fusion.3), channel_id=1, source_target_pairs={{0,64},{8,72},{16,80},{24,88},{32,96},{40,104},{48,112},{56,120},{... | collective-permute-start | bytes 399368 | tf_op jit(solution)/shard_map/ppermute | solution.py:33
  71.6 7.5 %collective-permute-start.4 = (bf16[4,130,128]{2,1,0:T(8,128)(2,1)S(1)}, bf16[4,130,128]{2,1,0:T(8,128)(2,1)S(1)}, u32[]{:S(2)}, u32[]{:S(2)}) collective-permute-start(bf16[4,130,128]{2,1,0:T(8,128)(2,1)S(1)} %pad_maximum_fusion.4), channel_id=1, source_target_pairs={{0,128},{8,136},{16,144},{24,152},{32,160},{40,168},{48,176},{56,1... | collective-permute-start | bytes 399368 | tf_op jit(solution)/shard_map/ppermute | solution.py:33
  79.6 8.5 %collective-permute-start.5 = (bf16[4,130,128]{2,1,0:T(8,128)(2,1)S(1)}, bf16[4,130,128]{2,1,0:T(8,128)(2,1)S(1)}, u32[]{:S(2)}, u32[]{:S(2)}) collective-permute-start(bf16[4,130,128]{2,1,0:T(8,128)(2,1)S(1)} %pad_maximum_fusion.5), channel_id=1, source_target_pairs={{0,256},{8,264},{16,272},{24,280},{32,288},{40,296},{48,304},{56,3... | collective-permute-start | bytes 399368 | tf_op jit(solution)/shard_map/ppermute | solution.py:33
  88.1 2.1 copy-start.6
  88.1 2.1 copy-start.8
  89.9 13.6 %copy-start.11 = (f32[512]{0:T(512)S(1)}, f32[512]{0:T(512)}, u32[]{:S(2)}) copy-start(f32[512]{0:T(512)} %param.17) | copy-start | bytes 6148
  90.3 13.1 %copy-start.3 = (bf16[256,512]{1,0:T(8,128)(2,1)}, bf16[256,512]{1,0:T(8,128)(2,1)S(1)}, u32[]{:S(2)}) copy-start(bf16[256,512]{1,0:T(8,128)(2,1)S(1)} %get-tuple-element.18) | copy-start | bytes 786436
  105.3 85.7 %all-to-all-start = ((bf16[64,1,20,512]{3,2,1,0:T(8,128)(2,1)}), bf16[64,1,20,512]{3,2,1,0:T(8,128)(2,1)S(1)}, u32[]{:S(2)}, u32[]{:S(2)}) async-start(bf16[64,1,20,512]{3,2,1,0:T(8,128)(2,1)} %bitcast.8), calls=%async_computation | async-start | bytes 3145728 | tf_op jit(solution)/shard_map/all_to_all | solution.py:159
  195.7 1.8 copy-start.2
  198.8 5.8 %collective-permute-start.6 = (bf16[1,4,160,1408]{3,2,1,0:T(8,128)(2,1)}, bf16[1,4,160,1408]{3,2,1,0:T(8,128)(2,1)S(1)}, u32[]{:S(2)}, u32[]{:S(2)}) collective-permute-start(bf16[1,4,160,1408]{3,2,1,0:T(8,128)(2,1)} %dynamic-slice_bitcast_fusion), channel_id=1, source_target_pairs={{0,1},{1,0},{2,3},{3,2},{4,5},{5,4},{6,7},{7,6},{8,9},{9,8},{10,11... | collective-permute-start | bytes 5406728 | tf_op jit(solution)/shard_map/ppermute | solution.py:58
  206.5 1.8 copy-start.1
  209.2 25.3 %collective-permute-start.7 = (bf16[1,160,1408]{2,1,0:T(8,128)(2,1)}, bf16[1,160,1408]{2,1,0:T(8,128)(2,1)S(1)}, u32[]{:S(2)}, u32[]{:S(2)}) collective-permute-start(bf16[1,160,1408]{2,1,0:T(8,128)(2,1)} %get-tuple-element.35), channel_id=1, source_target_pairs={{0,2},{1,3},{2,4},{3,5},{4,6},{5,7},{6,0},{7,1},{8,10},{9,11},{10,... | collective-permute-start | bytes 1351688 | tf_op jit(solution)/shard_map/ppermute | solution.py:64
  211.1 23.4 %collective-permute-start.8 = (bf16[1,160,1408]{2,1,0:T(8,128)(2,1)S(1)}, bf16[1,160,1408]{2,1,0:T(8,128)(2,1)S(1)}, u32[]{:S(2)}, u32[]{:S(2)}) collective-permute-start(bf16[1,160,1408]{2,1,0:T(8,128)(2,1)S(1)} %get-tuple-element.37), channel_id=1, source_target_pairs={{0,4},{1,5},{2,6},{3,7},{4,0},{5,1},{6,2},{7,3},{8,12},{9,13},{10,... | collective-permute-start | bytes 1351688 | tf_op jit(solution)/shard_map/ppermute | solution.py:64
  215.0 22.0 %collective-permute-start.9 = (bf16[1,160,1408]{2,1,0:T(8,128)(2,1)S(1)}, bf16[1,160,1408]{2,1,0:T(8,128)(2,1)}, u32[]{:S(2)}, u32[]{:S(2)}) collective-permute-start(bf16[1,160,1408]{2,1,0:T(8,128)(2,1)S(1)} %get-tuple-element.36), channel_id=1, source_target_pairs={{0,6},{1,7},{2,0},{3,1},{4,2},{5,3},{6,4},{7,5},{8,14},{9,15},{10,... | collective-permute-start | bytes 1351688 | tf_op jit(solution)/shard_map/ppermute | solution.py:64
  238.7 10.7 %collective-permute-start.10 = (bf16[1,160,704]{2,1,0:T(8,128)(2,1)S(1)}, bf16[1,160,704]{2,1,0:T(8,128)(2,1)S(1)}, u32[]{:S(2)}, u32[]{:S(2)}) collective-permute-start(bf16[1,160,704]{2,1,0:T(8,128)(2,1)S(1)} %fusion.26), channel_id=1, source_target_pairs={{0,2},{1,3},{2,4},{3,5},{4,6},{5,7},{6,0},{7,1},{8,10},{9,11},{10,... | collective-permute-start | bytes 675848 | tf_op jit(solution)/shard_map/ppermute | solution.py:71
  240.9 14.9 %collective-permute-start.11 = (bf16[1,160,704]{2,1,0:T(8,128)(2,1)S(1)}, bf16[1,160,704]{2,1,0:T(8,128)(2,1)S(1)}, u32[]{:S(2)}, u32[]{:S(2)}) collective-permute-start(bf16[1,160,704]{2,1,0:T(8,128)(2,1)S(1)} %fusion.26), channel_id=1, source_target_pairs={{0,4},{1,5},{2,6},{3,7},{4,0},{5,1},{6,2},{7,3},{8,12},{9,13},{10,... | collective-permute-start | bytes 675848 | tf_op jit(solution)/shard_map/ppermute | solution.py:71
  246.6 10.5 %collective-permute-start.12 = (bf16[1,160,704]{2,1,0:T(8,128)(2,1)S(1)}, bf16[1,160,704]{2,1,0:T(8,128)(2,1)S(1)}, u32[]{:S(2)}, u32[]{:S(2)}) collective-permute-start(bf16[1,160,704]{2,1,0:T(8,128)(2,1)S(1)} %fusion.26), channel_id=1, source_target_pairs={{0,6},{1,7},{2,0},{3,1},{4,2},{5,3},{6,4},{7,5},{8,14},{9,15},{10,... | collective-permute-start | bytes 675848 | tf_op jit(solution)/shard_map/ppermute | solution.py:71
  258.0 4.5 %collective-permute-start.13 = (bf16[1,4,160,704]{3,2,1,0:T(8,128)(2,1)S(1)}, bf16[1,4,160,704]{3,2,1,0:T(8,128)(2,1)S(1)}, u32[]{:S(2)}, u32[]{:S(2)}) collective-permute-start(bf16[1,4,160,704]{3,2,1,0:T(8,128)(2,1)S(1)} %bitcast_select_fusion.1), channel_id=1, source_target_pairs={{0,1},{1,0},{2,3},{3,2},{4,5},{5,4},{6,7},{7,6},{8,9},{9,8},{10,11... | collective-permute-start | bytes 2703368 | tf_op jit(solution)/shard_map/ppermute | solution.py:74
  266.4 1.1 copy-start.10
  270.1 7.4 %copy-start.9 = (f32[256,2]{0,1:T(2,128)S(1)}, f32[256,2]{0,1:T(2,128)}, u32[]{:S(2)}) copy-start(f32[256,2]{0,1:T(2,128)} %param.19) | copy-start | bytes 6148
  270.1 82.8 %all-to-all-start.1 = ((bf16[1,64,20,512]{3,2,0,1:T(8,128)(2,1)}), bf16[1,64,20,512]{3,2,0,1:T(8,128)(2,1)S(1)}, u32[]{:S(2)}, u32[]{:S(2)}) async-start(bf16[1,64,20,512]{3,2,0,1:T(8,128)(2,1)} %bitcast.144), calls=%async_computation.1 | async-start | bytes 3145728 | tf_op jit(solution)/shard_map/all_to_all | solution.py:170
  358.1 3.2 copy-start.4

commit v6 on v5

--- a/solution.py
+++ b/solution.py
@@ -151,14 +151,18 @@
     send_rows = jnp.dot(dispatch_matrix, expert_input, preferred_element_type=jnp.float32).astype(
         jnp.bfloat16
     )
-    hidden_split = expert_in.shape[0] * lax.axis_size("seq") // expert_count
-    send_buffer = jnp.repeat(
-        send_rows.reshape(expert_count, 1, capacity, local_width), hidden_split, axis=0
-    )
+    half = capacity // 2
+    parity = lax.axis_index("seq") % 2
+    partner = [(j, j ^ 1) for j in range(lax.axis_size("seq"))]
+    send_buffer = send_rows.reshape(expert_count * 2, 1, half, local_width)
     block_units = expert_out.shape[1]
     arrived = lax.all_to_all(send_buffer, "seq", split_axis=0, concat_axis=1, tiled=True)
-    blocks_here, sources, item_count, feature_count = arrived.shape
-    flat_rows = arrived.reshape(blocks_here, sources * item_count, feature_count)
+    swapped = lax.ppermute(arrived, "seq", partner)
+    both = jnp.stack([arrived, swapped], axis=2)
+    arrived = jnp.take(both, jnp.arange(2) ^ parity, axis=2)
+    blocks_here, sources = arrived.shape[0], arrived.shape[1]
+    feature_count = arrived.shape[-1]
+    flat_rows = arrived.reshape(blocks_here, sources * capacity, feature_count)
     partial_sums = jnp.einsum(
         "erd,edh->erh", flat_rows, expert_in, preferred_element_type=jnp.float32
     )
@@ -166,12 +170,12 @@
     produced = jnp.einsum(
         "erh,ehd->erd", activated, expert_out, preferred_element_type=jnp.float32
     ).astype(jnp.bfloat16)
-    computed = produced.reshape(blocks_here, sources, item_count, feature_count)
-    returned = lax.all_to_all(computed, "seq", split_axis=1, concat_axis=0, tiled=True)
-    merged = jnp.sum(
-        returned.reshape(expert_count, hidden_split, capacity, local_width).astype(jnp.float32),
-        axis=1,
-    )
+    computed = produced.reshape(blocks_here, sources, 2, half, feature_count)
+    kept = lax.dynamic_index_in_dim(computed, parity, 2, False).astype(jnp.float32)
+    given = lax.dynamic_index_in_dim(computed, 1 - parity, 2, False)
+    summed = (kept + lax.ppermute(given, "seq", partner).astype(jnp.float32)).astype(jnp.bfloat16)
+    returned = lax.all_to_all(summed, "seq", split_axis=1, concat_axis=0, tiled=True)
+    merged = returned.reshape(expert_count, capacity, local_width).astype(jnp.float32)
     merged = merged.reshape(expert_count * capacity, local_width)
     slot_rows = merged[position]
     expert_mix = jnp.sum(slot_rows * route_weight[:, :, None], axis=1)

time: 363 us -> 365 us (level)
  waiting for transfers between devices: 249 us -> 177 us
  blocking collectives: 13.1 us -> 76 us
  local copies, waits for them, and re-layouts: 23.7 us -> 31 us
    all_to_all x2 -> x1, waiting for transfers between devices: 151 us -> 52.5 us  [per_device(): lax.all_to_all(summed, 'seq', split_axis=1, concat_axis=0, tiled=True)]
    all_to_all x0 -> x1, blocking collectives: none -> 63 us  [per_device(): lax.all_to_all(send_buffer, 'seq', split_axis=0, concat_axis=1, tiled=True)]
    ppermute x0 -> x2, waiting for transfers between devices: none -> 28.4 us  [the longest x1 15 us: per_device(): lax.ppermute(given, 'seq', partner).astype(jnp.float32)]
    all_to_all x2 -> x1, starting transfers between devices: 17 us -> 9.87 us  [per_device(): lax.all_to_all(summed, 'seq', split_axis=1, concat_axis=0, tiled=True)]
    ppermute x0 -> x2, starting transfers between devices: none -> 6.78 us  [the longest x1 3.64 us: per_device(): lax.ppermute(given, 'seq', partner).astype(jnp.float32)]
  transfers between devices with their start and end apart: 16 -> 17, of which waited for: 15 -> 15; matrix products, arithmetic and copies ran while one was open for 1% -> 1% of each run, Pallas kernels for 0% -> 0%
where the time goes in v6:
time: 365 us; the launch traced here: 364 us
  waiting for transfers between devices  177 us (48%)
  blocking collectives  76 us (21%)
  starting transfers between devices  51.4 us (14%)
  local copies, waits for them, and re-layouts  31 us (8%)
  other arithmetic  15.2 us (4%)
  matrix products  12.6 us (3%)
    ppermute x6, waiting for transfers between devices, exclusive_scan(): got = lax.ppermute(pack_window(window_decay, window_state), axis, pairs)  64.6 us
    all_to_all x1, blocking collectives, per_device(): lax.all_to_all(send_buffer, 'seq', split_axis=0, concat_axis=1, tiled=True)  63 us
    all_to_all x1, waiting for transfers between devices, per_device(): lax.all_to_all(summed, 'seq', split_axis=1, concat_axis=0, tiled=True)  52.5 us
    ppermute x3, waiting for transfers between devices, head_reduce_activate(): total = total + lax.ppermute(outgoing, axis, pairs).astype(jnp.float32)  18.9 us
    ppermute x1, waiting for transfers between devices, per_device(): lax.ppermute(given, 'seq', partner).astype(jnp.float32)  15 us
    ppermute x1, waiting for transfers between devices, per_device(): swapped = lax.ppermute(arrived, 'seq', partner)  13.3 us
    psum x1, blocking collectives, per_device(): total_squares = lax.psum(local_squares, 'head')  13.1 us
    ppermute x6, starting transfers between devices, exclusive_scan(): got = lax.ppermute(pack_window(window_decay, window_state), axis, pairs)  12.2 us
  transfers between devices with their start and end apart: 17, of which 15 were waited for; matrix products, arithmetic and copies ran while one was open for 1% of the time, Pallas kernels for 0%

profile of v6, /device:TPU:6, one launch (start us, length us, event | category | flops | bytes accessed | tf_op | source)
XLA Modules:
  0.0 363.9 jit_solution(6634485356096367606)
XLA Ops:
  5.2 3.8 %collective-permute-start = (bf16[4,130,128]{2,1,0:T(8,128)(2,1)S(1)}, bf16[4,130,128]{2,1,0:T(8,128)(2,1)S(1)}, u32[]{:S(2)}, u32[]{:S(2)}) collective-permute-start(bf16[4,130,128]{2,1,0:T(8,128)(2,1)S(1)} %pad_maximum_fusion), channel_id=1, source_target_pairs={{0,8},{8,16},{16,24},{24,32},{32,40},{40,48},{48,56},{56,64},{64,7... | collective-permute-start | bytes 399368 | tf_op jit(solution)/shard_map/ppermute | solution.py:33
  9.0 11.5 %collective-permute-done = bf16[4,130,128]{2,1,0:T(8,128)(2,1)S(1)} collective-permute-done((bf16[4,130,128]{2,1,0:T(8,128)(2,1)S(1)}, bf16[4,130,128]{2,1,0:T(8,128)(2,1)S(1)}, u32[]{:S(2)}, u32[]{:S(2)}) %collective-permute-start) | collective-permute-done | bytes 133152 | tf_op jit(solution)/shard_map/ppermute | solution.py:33
  21.0 1.9 collective-permute-start.1
  23.0 10.1 %collective-permute-done.1 = bf16[4,130,128]{2,1,0:T(8,128)(2,1)S(1)} collective-permute-done((bf16[4,130,128]{2,1,0:T(8,128)(2,1)S(1)}, bf16[4,130,128]{2,1,0:T(8,128)(2,1)S(1)}, u32[]{:S(2)}, u32[]{:S(2)}) %collective-permute-start.1) | collective-permute-done | bytes 133152 | tf_op jit(solution)/shard_map/ppermute | solution.py:33
  33.8 1.9 collective-permute-start.2
  36.0 15.0 %collective-permute-done.2 = bf16[4,130,128]{2,1,0:T(8,128)(2,1)S(1)} collective-permute-done((bf16[4,130,128]{2,1,0:T(8,128)(2,1)S(1)}, bf16[4,130,128]{2,1,0:T(8,128)(2,1)S(1)}, u32[]{:S(2)}, u32[]{:S(2)}) %collective-permute-start.2) | collective-permute-done | bytes 133152 | tf_op jit(solution)/shard_map/ppermute | solution.py:33
  51.5 1.9 collective-permute-start.3
  54.0 17.2 %collective-permute-done.3 = bf16[4,130,128]{2,1,0:T(8,128)(2,1)S(1)} collective-permute-done((bf16[4,130,128]{2,1,0:T(8,128)(2,1)S(1)}, bf16[4,130,128]{2,1,0:T(8,128)(2,1)S(1)}, u32[]{:S(2)}, u32[]{:S(2)}) %collective-permute-start.3) | collective-permute-done | bytes 133152 | tf_op jit(solution)/shard_map/ppermute | solution.py:33
  73.0 2.3 fusion.7
  75.3 3.8 %collective-permute-done.4 = bf16[4,130,128]{2,1,0:T(8,128)(2,1)S(1)} collective-permute-done((bf16[4,130,128]{2,1,0:T(8,128)(2,1)S(1)}, bf16[4,130,128]{2,1,0:T(8,128)(2,1)S(1)}, u32[]{:S(2)}, u32[]{:S(2)}) %collective-permute-start.4) | collective-permute-done | bytes 133152 | tf_op jit(solution)/shard_map/ppermute | solution.py:33
  81.2 6.9 %collective-permute-done.5 = bf16[4,130,128]{2,1,0:T(8,128)(2,1)S(1)} collective-permute-done((bf16[4,130,128]{2,1,0:T(8,128)(2,1)S(1)}, bf16[4,130,128]{2,1,0:T(8,128)(2,1)S(1)}, u32[]{:S(2)}, u32[]{:S(2)}) %collective-permute-start.5) | collective-permute-done | bytes 133152 | tf_op jit(solution)/shard_map/ppermute | solution.py:33
  88.1 1.8 multiply_reduce_fusion.1
  90.4 13.1 %psum.7 = f32[256]{0:T(256)S(1)} all-reduce(f32[256]{0:T(256)S(1)} %get-tuple-element.17), channel_id=1, replica_groups=mesh['seq'=64,'head'=8] {'head'}, use_global_device_ids=true, to_apply=%region_6.7 | all-reduce | flops 256 | bytes 2048 | tf_op jit(solution)/shard_map/psum | solution.py:132
  106.0 63.0 %all_to_all.21 = bf16[64,1,10,512]{3,2,1,0:T(8,128)(2,1)S(1)} all-to-all(bf16[64,1,10,512]{3,2,1,0:T(8,128)(2,1)S(1)} %bitcast.165), channel_id=1, replica_groups=mesh['seq'=64,'head'=8] {'seq'}, dimensions={0} | all-to-all | bytes 1310720 | tf_op jit(solution)/shard_map/all_to_all | solution.py:159
  170.2 3.1 collective-permute-start.6
  173.4 13.3 %collective-permute-done.6 = bf16[1,64,10,512]{3,1,2,0:T(8,128)(2,1)S(1)} collective-permute-done((bf16[1,64,10,512]{3,1,2,0:T(8,128)(2,1)}, bf16[1,64,10,512]{3,1,2,0:T(8,128)(2,1)S(1)}, u32[]{:S(2)}, u32[]{:S(2)}) %collective-permute-start.6) | collective-permute-done | bytes 655392 | tf_op jit(solution)/shard_map/ppermute | solution.py:160
  187.1 1.6 maximum_bitcast_fusion
  188.8 2.3 gather_fusion
  192.9 3.5 convolution_convert_fusion
  196.4 1.8 copy-done.2
  199.5 1.9 collective-permute-start.7
  201.5 3.8 %collective-permute-done.7 = bf16[1,4,160,1408]{3,2,1,0:T(8,128)(2,1)S(1)} collective-permute-done((bf16[1,4,160,1408]{3,2,1,0:T(8,128)(2,1)}, bf16[1,4,160,1408]{3,2,1,0:T(8,128)(2,1)S(1)}, u32[]{:S(2)}, u32[]{:S(2)}) %collective-permute-start.7) | collective-permute-done | bytes 1802272 | tf_op jit(solution)/shard_map/ppermute | solution.py:58
  205.3 1.8 convert_add_fusion
  207.2 1.8 copy-done.1
  209.9 2.5 collective-permute-start.10
  212.4 3.3 collective-permute-start.8
  215.7 2.5 collective-permute-start.9
  218.3 6.8 %collective-permute-done.10 = bf16[1,160,1408]{2,1,0:T(8,128)(2,1)S(1)} collective-permute-done((bf16[1,160,1408]{2,1,0:T(8,128)(2,1)}, bf16[1,160,1408]{2,1,0:T(8,128)(2,1)S(1)}, u32[]{:S(2)}, u32[]{:S(2)}) %collective-permute-start.10) | collective-permute-done | bytes 450592 | tf_op jit(solution)/shard_map/ppermute | solution.py:64
  225.1 12.1 %collective-permute-done.8 = bf16[1,160,1408]{2,1,0:T(8,128)(2,1)S(1)} collective-permute-done((bf16[1,160,1408]{2,1,0:T(8,128)(2,1)S(1)}, bf16[1,160,1408]{2,1,0:T(8,128)(2,1)S(1)}, u32[]{:S(2)}, u32[]{:S(2)}) %collective-permute-start.8) | collective-permute-done | bytes 450592 | tf_op jit(solution)/shard_map/ppermute | solution.py:64
  237.3 1.5 fusion.16
  239.0 1.9 collective-permute-start.11
  240.9 3.7 %collective-permute-start.12 = (bf16[1,160,704]{2,1,0:T(8,128)(2,1)S(1)}, bf16[1,160,704]{2,1,0:T(8,128)(2,1)S(1)}, u32[]{:S(2)}, u32[]{:S(2)}) collective-permute-start(bf16[1,160,704]{2,1,0:T(8,128)(2,1)S(1)} %fusion.27), channel_id=1, source_target_pairs={{0,4},{1,5},{2,6},{3,7},{4,0},{5,1},{6,2},{7,3},{8,12},{9,13},{10,... | collective-permute-start | bytes 675848 | tf_op jit(solution)/shard_map/ppermute | solution.py:71
  244.6 4.7 %collective-permute-start.13 = (bf16[1,160,704]{2,1,0:T(8,128)(2,1)S(1)}, bf16[1,160,704]{2,1,0:T(8,128)(2,1)S(1)}, u32[]{:S(2)}, u32[]{:S(2)}) collective-permute-start(bf16[1,160,704]{2,1,0:T(8,128)(2,1)S(1)} %fusion.27), channel_id=1, source_target_pairs={{0,6},{1,7},{2,0},{3,1},{4,2},{5,3},{6,4},{7,5},{8,14},{9,15},{10,... | collective-permute-start | bytes 675848 | tf_op jit(solution)/shard_map/ppermute | solution.py:71
  249.6 4.0 %collective-permute-done.11 = bf16[1,160,704]{2,1,0:T(8,128)(2,1)S(1)} collective-permute-done((bf16[1,160,704]{2,1,0:T(8,128)(2,1)S(1)}, bf16[1,160,704]{2,1,0:T(8,128)(2,1)S(1)}, u32[]{:S(2)}, u32[]{:S(2)}) %collective-permute-start.11) | collective-permute-done | bytes 225312 | tf_op jit(solution)/shard_map/ppermute | solution.py:71
  253.6 2.2 collective-permute-done.13
  256.7 1.9 collective-permute-start.14
  258.8 2.5 collective-permute-done.14
  261.3 2.7 maximum_bitcast_fusion.1
  263.9 2.2 gather_fusion.2
  267.5 2.3 convolution_convert_fusion.1
  269.8 2.4 reshape.629
  272.7 3.6 collective-permute-start.15
  276.4 15.0 %collective-permute-done.15 = bf16[1,64,10,512]{3,1,2,0:T(8,128)(2,1)S(1)} collective-permute-done((bf16[1,64,10,512]{3,1,2,0:T(8,128)(2,1)S(1)}, bf16[1,64,10,512]{3,1,2,0:T(8,128)(2,1)S(1)}, u32[]{:S(2)}, u32[]{:S(2)}) %collective-permute-start.15) | collective-permute-done | bytes 655392 | tf_op jit(solution)/shard_map/ppermute | solution.py:176
  291.9 1.4 copy.197
  293.3 9.9 %all-to-all-start.1 = ((bf16[1,64,10,512]{3,2,0,1:T(8,128)(2,1)}), bf16[1,64,10,512]{3,2,0,1:T(8,128)(2,1)}, u32[]{:S(2)}, u32[]{:S(2)}) async-start(bf16[1,64,10,512]{3,2,0,1:T(8,128)(2,1)} %copy.197), calls=%async_computation.1 | async-start | bytes 2097152 | tf_op jit(solution)/shard_map/all_to_all | solution.py:177
  303.7 52.5 %all-to-all-done.1 = bf16[1,64,10,512]{3,2,0,1:T(8,128)(2,1)} async-done(((bf16[1,64,10,512]{3,2,0,1:T(8,128)(2,1)}), bf16[1,64,10,512]{3,2,0,1:T(8,128)(2,1)}, u32[]{:S(2)}, u32[]{:S(2)}) %all-to-all-start.1) | async-done | bytes 655392 | tf_op jit(solution)/shard_map/all_to_all | solution.py:177
  357.5 2.3 gather_fusion.3
  359.8 1.9 reshape.664
  (136 shorter events, 27.7 us)
Async XLA Ops:
  0.0 192.9 %copy-start = (bf16[1,512,1408]{2,1,0:T(8,128)(2,1)S(1)}, bf16[1,512,1408]{2,1,0:T(8,128)(2,1)}, u32[]{:S(2)}) copy-start(bf16[1,512,1408]{2,1,0:T(8,128)(2,1)} %param.20) | copy-start | bytes 4325380
  0.0 35.7 %copy-start.7 = (s32[256,2]{0,1:T(2,128)S(1)}, s32[256,2]{0,1:T(2,128)}, u32[]{:S(2)}) copy-start(s32[256,2]{0,1:T(2,128)} %param.18) | copy-start | bytes 6148
  5.2 15.3 %collective-permute-start = (bf16[4,130,128]{2,1,0:T(8,128)(2,1)S(1)}, bf16[4,130,128]{2,1,0:T(8,128)(2,1)S(1)}, u32[]{:S(2)}, u32[]{:S(2)}) collective-permute-start(bf16[4,130,128]{2,1,0:T(8,128)(2,1)S(1)} %pad_maximum_fusion), channel_id=1, source_target_pairs={{0,8},{8,16},{16,24},{24,32},{32,40},{40,48},{48,56},{56,64},{64,7... | collective-permute-start | bytes 399368 | tf_op jit(solution)/shard_map/ppermute | solution.py:33
  21.0 12.2 %collective-permute-start.1 = (bf16[4,130,128]{2,1,0:T(8,128)(2,1)S(1)}, bf16[4,130,128]{2,1,0:T(8,128)(2,1)S(1)}, u32[]{:S(2)}, u32[]{:S(2)}) collective-permute-start(bf16[4,130,128]{2,1,0:T(8,128)(2,1)S(1)} %pad_maximum_fusion.1), channel_id=1, source_target_pairs={{0,16},{8,24},{16,32},{24,40},{32,48},{40,56},{48,64},{56,72},{64,... | collective-permute-start | bytes 399368 | tf_op jit(solution)/shard_map/ppermute | solution.py:33
  33.5 39.4 %copy-start.5 = (bf16[256,512]{1,0:T(8,128)(2,1)S(1)}, bf16[256,512]{1,0:T(8,128)(2,1)}, u32[]{:S(2)}) copy-start(bf16[256,512]{1,0:T(8,128)(2,1)} %param.14) | copy-start | bytes 786436
  33.8 17.3 %collective-permute-start.2 = (bf16[4,130,128]{2,1,0:T(8,128)(2,1)S(1)}, bf16[4,130,128]{2,1,0:T(8,128)(2,1)S(1)}, u32[]{:S(2)}, u32[]{:S(2)}) collective-permute-start(bf16[4,130,128]{2,1,0:T(8,128)(2,1)S(1)} %pad_maximum_fusion.2), channel_id=1, source_target_pairs={{0,32},{8,40},{16,48},{24,56},{32,64},{40,72},{48,80},{56,88},{64,... | collective-permute-start | bytes 399368 | tf_op jit(solution)/shard_map/ppermute | solution.py:33
  51.5 19.6 %collective-permute-start.3 = (bf16[4,130,128]{2,1,0:T(8,128)(2,1)S(1)}, bf16[4,130,128]{2,1,0:T(8,128)(2,1)S(1)}, u32[]{:S(2)}, u32[]{:S(2)}) collective-permute-start(bf16[4,130,128]{2,1,0:T(8,128)(2,1)S(1)} %pad_maximum_fusion.3), channel_id=1, source_target_pairs={{0,64},{8,72},{16,80},{24,88},{32,96},{40,104},{48,112},{56,120},{... | collective-permute-start | bytes 399368 | tf_op jit(solution)/shard_map/ppermute | solution.py:33
  71.6 7.5 %collective-permute-start.4 = (bf16[4,130,128]{2,1,0:T(8,128)(2,1)S(1)}, bf16[4,130,128]{2,1,0:T(8,128)(2,1)S(1)}, u32[]{:S(2)}, u32[]{:S(2)}) collective-permute-start(bf16[4,130,128]{2,1,0:T(8,128)(2,1)S(1)} %pad_maximum_fusion.4), channel_id=1, source_target_pairs={{0,128},{8,136},{16,144},{24,152},{32,160},{40,168},{48,176},{56,1... | collective-permute-start | bytes 399368 | tf_op jit(solution)/shard_map/ppermute | solution.py:33
  79.6 8.5 %collective-permute-start.5 = (bf16[4,130,128]{2,1,0:T(8,128)(2,1)S(1)}, bf16[4,130,128]{2,1,0:T(8,128)(2,1)S(1)}, u32[]{:S(2)}, u32[]{:S(2)}) collective-permute-start(bf16[4,130,128]{2,1,0:T(8,128)(2,1)S(1)} %pad_maximum_fusion.5), channel_id=1, source_target_pairs={{0,256},{8,264},{16,272},{24,280},{32,288},{40,296},{48,304},{56,3... | collective-permute-start | bytes 399368 | tf_op jit(solution)/shard_map/ppermute | solution.py:33
  88.1 2.1 copy-start.6
  88.1 2.1 copy-start.8
  89.9 13.6 %copy-start.11 = (f32[512]{0:T(512)S(1)}, f32[512]{0:T(512)}, u32[]{:S(2)}) copy-start(f32[512]{0:T(512)} %param.17) | copy-start | bytes 6148
  90.3 15.6 %copy-start.3 = (bf16[256,512]{1,0:T(8,128)(2,1)}, bf16[256,512]{1,0:T(8,128)(2,1)S(1)}, u32[]{:S(2)}) copy-start(bf16[256,512]{1,0:T(8,128)(2,1)S(1)} %get-tuple-element.18) | copy-start | bytes 786436
  170.2 16.6 %collective-permute-start.6 = (bf16[1,64,10,512]{3,1,2,0:T(8,128)(2,1)}, bf16[1,64,10,512]{3,1,2,0:T(8,128)(2,1)S(1)}, u32[]{:S(2)}, u32[]{:S(2)}) collective-permute-start(bf16[1,64,10,512]{3,1,2,0:T(8,128)(2,1)} %copy.190), channel_id=1, source_target_pairs={{0,8},{8,0},{16,24},{24,16},{32,40},{40,32},{48,56},{56,48},{64,72... | collective-permute-start | bytes 1966088 | tf_op jit(solution)/shard_map/ppermute | solution.py:160
  196.4 1.8 copy-start.2
  199.5 5.8 %collective-permute-start.7 = (bf16[1,4,160,1408]{3,2,1,0:T(8,128)(2,1)}, bf16[1,4,160,1408]{3,2,1,0:T(8,128)(2,1)S(1)}, u32[]{:S(2)}, u32[]{:S(2)}) collective-permute-start(bf16[1,4,160,1408]{3,2,1,0:T(8,128)(2,1)} %dynamic-slice_bitcast_fusion), channel_id=1, source_target_pairs={{0,1},{1,0},{2,3},{3,2},{4,5},{5,4},{6,7},{7,6},{8,9},{9,8},{10,11... | collective-permute-start | bytes 5406728 | tf_op jit(solution)/shard_map/ppermute | solution.py:58
  207.2 1.8 copy-start.1
  209.9 15.3 %collective-permute-start.10 = (bf16[1,160,1408]{2,1,0:T(8,128)(2,1)}, bf16[1,160,1408]{2,1,0:T(8,128)(2,1)S(1)}, u32[]{:S(2)}, u32[]{:S(2)}) collective-permute-start(bf16[1,160,1408]{2,1,0:T(8,128)(2,1)} %get-tuple-element.36), channel_id=1, source_target_pairs={{0,6},{1,7},{2,0},{3,1},{4,2},{5,3},{6,4},{7,5},{8,14},{9,15},{10,... | collective-permute-start | bytes 1351688 | tf_op jit(solution)/shard_map/ppermute | solution.py:64
  212.4 24.9 %collective-permute-start.8 = (bf16[1,160,1408]{2,1,0:T(8,128)(2,1)S(1)}, bf16[1,160,1408]{2,1,0:T(8,128)(2,1)S(1)}, u32[]{:S(2)}, u32[]{:S(2)}) collective-permute-start(bf16[1,160,1408]{2,1,0:T(8,128)(2,1)S(1)} %get-tuple-element.35), channel_id=1, source_target_pairs={{0,2},{1,3},{2,4},{3,5},{4,6},{5,7},{6,0},{7,1},{8,10},{9,11},{10,... | collective-permute-start | bytes 1351688 | tf_op jit(solution)/shard_map/ppermute | solution.py:64
  215.7 21.5 %collective-permute-start.9 = (bf16[1,160,1408]{2,1,0:T(8,128)(2,1)S(1)}, bf16[1,160,1408]{2,1,0:T(8,128)(2,1)}, u32[]{:S(2)}, u32[]{:S(2)}) collective-permute-start(bf16[1,160,1408]{2,1,0:T(8,128)(2,1)S(1)} %get-tuple-element.37), channel_id=1, source_target_pairs={{0,4},{1,5},{2,6},{3,7},{4,0},{5,1},{6,2},{7,3},{8,12},{9,13},{10,... | collective-permute-start | bytes 1351688 | tf_op jit(solution)/shard_map/ppermute | solution.py:64
  239.0 14.6 %collective-permute-start.11 = (bf16[1,160,704]{2,1,0:T(8,128)(2,1)S(1)}, bf16[1,160,704]{2,1,0:T(8,128)(2,1)S(1)}, u32[]{:S(2)}, u32[]{:S(2)}) collective-permute-start(bf16[1,160,704]{2,1,0:T(8,128)(2,1)S(1)} %fusion.27), channel_id=1, source_target_pairs={{0,2},{1,3},{2,4},{3,5},{4,6},{5,7},{6,0},{7,1},{8,10},{9,11},{10,... | collective-permute-start | bytes 675848 | tf_op jit(solution)/shard_map/ppermute | solution.py:71
  240.9 12.6 %collective-permute-start.12 = (bf16[1,160,704]{2,1,0:T(8,128)(2,1)S(1)}, bf16[1,160,704]{2,1,0:T(8,128)(2,1)S(1)}, u32[]{:S(2)}, u32[]{:S(2)}) collective-permute-start(bf16[1,160,704]{2,1,0:T(8,128)(2,1)S(1)} %fusion.27), channel_id=1, source_target_pairs={{0,4},{1,5},{2,6},{3,7},{4,0},{5,1},{6,2},{7,3},{8,12},{9,13},{10,... | collective-permute-start | bytes 675848 | tf_op jit(solution)/shard_map/ppermute | solution.py:71
  244.6 11.1 %collective-permute-start.13 = (bf16[1,160,704]{2,1,0:T(8,128)(2,1)S(1)}, bf16[1,160,704]{2,1,0:T(8,128)(2,1)S(1)}, u32[]{:S(2)}, u32[]{:S(2)}) collective-permute-start(bf16[1,160,704]{2,1,0:T(8,128)(2,1)S(1)} %fusion.27), channel_id=1, source_target_pairs={{0,6},{1,7},{2,0},{3,1},{4,2},{5,3},{6,4},{7,5},{8,14},{9,15},{10,... | collective-permute-start | bytes 675848 | tf_op jit(solution)/shard_map/ppermute | solution.py:71
  256.7 4.6 %collective-permute-start.14 = (bf16[1,4,160,704]{3,2,1,0:T(8,128)(2,1)S(1)}, bf16[1,4,160,704]{3,2,1,0:T(8,128)(2,1)}, u32[]{:S(2)}, u32[]{:S(2)}) collective-permute-start(bf16[1,4,160,704]{3,2,1,0:T(8,128)(2,1)S(1)} %bitcast_select_fusion.2), channel_id=1, source_target_pairs={{0,1},{1,0},{2,3},{3,2},{4,5},{5,4},{6,7},{7,6},{8,9},{9,8},{10,11... | collective-permute-start | bytes 2703368 | tf_op jit(solution)/shard_map/ppermute | solution.py:74
  266.4 1.1 copy-start.10
  272.7 18.7 %collective-permute-start.15 = (bf16[1,64,10,512]{3,1,2,0:T(8,128)(2,1)S(1)}, bf16[1,64,10,512]{3,1,2,0:T(8,128)(2,1)S(1)}, u32[]{:S(2)}, u32[]{:S(2)}) collective-permute-start(bf16[1,64,10,512]{3,1,2,0:T(8,128)(2,1)S(1)} %bitcast.173), channel_id=1, source_target_pairs={{0,8},{8,0},{16,24},{24,16},{32,40},{40,32},{48,56},{56,48},{64,72... | collective-permute-start | bytes 1966088 | tf_op jit(solution)/shard_map/ppermute | solution.py:176
  291.9 11.6 %copy-start.9 = (f32[256,2]{0,1:T(2,128)S(1)}, f32[256,2]{0,1:T(2,128)}, u32[]{:S(2)}) copy-start(f32[256,2]{0,1:T(2,128)} %param.19) | copy-start | bytes 6148
  293.3 62.8 %all-to-all-start.1 = ((bf16[1,64,10,512]{3,2,0,1:T(8,128)(2,1)}), bf16[1,64,10,512]{3,2,0,1:T(8,128)(2,1)}, u32[]{:S(2)}, u32[]{:S(2)}) async-start(bf16[1,64,10,512]{3,2,0,1:T(8,128)(2,1)} %copy.197), calls=%async_computation.1 | async-start | bytes 2097152 | tf_op jit(solution)/shard_map/all_to_all | solution.py:177
  359.8 3.2 copy-start.4

commit v7 on v5

--- a/solution.py
+++ b/solution.py
@@ -6,6 +6,8 @@
 D = 4096
 EXPERTS = 32
 CAP = 20
+SEQ = ("sx", "sz")
+Z_CHIPS = 16
 
 
 EPSILON = 1e-06
@@ -115,7 +117,7 @@
         "shd,she->hde", carried_keys, value_heads, preferred_element_type=jnp.float32
     )
     block_decay = jnp.exp(cumulative[:, -1])
-    entering = exclusive_scan(block_decay, block_state, "seq")
+    entering = exclusive_scan(block_decay, block_state, SEQ)
     from_before = jnp.einsum(
         "thd,hde->the",
         query_heads.astype(jnp.float32),
@@ -151,12 +153,17 @@
     send_rows = jnp.dot(dispatch_matrix, expert_input, preferred_element_type=jnp.float32).astype(
         jnp.bfloat16
     )
-    hidden_split = expert_in.shape[0] * lax.axis_size("seq") // expert_count
+    hidden_split = expert_in.shape[0] * lax.axis_size(SEQ) // expert_count
     send_buffer = jnp.repeat(
         send_rows.reshape(expert_count, 1, capacity, local_width), hidden_split, axis=0
     )
     block_units = expert_out.shape[1]
-    arrived = lax.all_to_all(send_buffer, "seq", split_axis=0, concat_axis=1, tiled=True)
+    rows_x = lax.axis_size("sx")
+    rows_z = lax.axis_size("sz")
+    staged = send_buffer.reshape(rows_x, rows_z, capacity, local_width)
+    staged = lax.all_to_all(staged, "sz", split_axis=1, concat_axis=1, tiled=True)
+    staged = lax.all_to_all(staged, "sx", split_axis=0, concat_axis=0, tiled=True)
+    arrived = staged.reshape(1, rows_x * rows_z, capacity, local_width)
     blocks_here, sources, item_count, feature_count = arrived.shape
     flat_rows = arrived.reshape(blocks_here, sources * item_count, feature_count)
     partial_sums = jnp.einsum(
@@ -167,7 +174,10 @@
         "erh,ehd->erd", activated, expert_out, preferred_element_type=jnp.float32
     ).astype(jnp.bfloat16)
     computed = produced.reshape(blocks_here, sources, item_count, feature_count)
-    returned = lax.all_to_all(computed, "seq", split_axis=1, concat_axis=0, tiled=True)
+    staged = computed.reshape(rows_x, rows_z, capacity, local_width)
+    staged = lax.all_to_all(staged, "sx", split_axis=0, concat_axis=0, tiled=True)
+    staged = lax.all_to_all(staged, "sz", split_axis=1, concat_axis=1, tiled=True)
+    returned = staged.reshape(rows_x * rows_z, 1, capacity, local_width)
     merged = jnp.sum(
         returned.reshape(expert_count, hidden_split, capacity, local_width).astype(jnp.float32),
         axis=1,
@@ -179,22 +189,25 @@
 
 
 def solution(mesh):
+    seq_count = mesh.shape["seq"]
+    split = mesh.devices.reshape(seq_count // Z_CHIPS, Z_CHIPS, mesh.shape["head"])
+    mesh = jax.sharding.Mesh(split, ("sx", "sz", "head"))
     return jax.shard_map(
         per_device,
         mesh=mesh,
         in_specs=(
-            P("seq", "head"),
-            P("seq", "head"),
-            P("seq", "head"),
-            P("seq", "head"),
-            P("head", "seq"),
+            P(SEQ, "head"),
+            P(SEQ, "head"),
+            P(SEQ, "head"),
+            P(SEQ, "head"),
+            P("head", SEQ),
             P("head"),
             P("head"),
-            P("seq", None),
-            P("seq", None),
-            P("seq", "head", None),
-            P("seq", None, "head"),
+            P(SEQ, None),
+            P(SEQ, None),
+            P(SEQ, "head", None),
+            P(SEQ, None, "head"),
         ),
-        out_specs=P("seq", "head"),
+        out_specs=P(SEQ, "head"),
         check_vma=False,
     )

time: 363 us -> 392 us (1.080)
  blocking collectives: 13.1 us -> 102 us
  waiting for transfers between devices: 249 us -> 169 us
  local copies, waits for them, and re-layouts: 23.7 us -> 35.6 us
  other arithmetic: 13.3 us -> 19.7 us
    all_to_all x0 -> x2, blocking collectives: none -> 89.3 us  [the longest x1 68.4 us: per_device(): lax.all_to_all(staged, 'sz', split_axis=1, concat_axis=1, tiled=True)]
    all_to_all x2, waiting for transfers between devices: 151 us -> 71.7 us  [the longest x1 61.4 us: per_device(): lax.all_to_all(staged, 'sz', split_axis=1, concat_axis=1, tiled=True)]
    all_to_all x0 -> x3, local copies, waits for them, and re-layouts: none -> 5.93 us  [the longest x2 4.13 us: per_device(): lax.all_to_all(staged, 'sx', split_axis=0, concat_axis=0, tiled=True)]
    convert_element_type x0 -> x2, local copies, waits for them, and re-layouts: none -> 4.99 us  [per_device(): returned.reshape(expert_count, hidden_split, capacity, local_width)]
where the time goes in v7:
time: 392 us; the launch traced here: 390 us
  waiting for transfers between devices  169 us (43%)
  blocking collectives  102 us (26%)
  starting transfers between devices  51.5 us (13%)
  local copies, waits for them, and re-layouts  35.6 us (9%)
  other arithmetic  19.7 us (5%)
  matrix products  10.7 us (3%)
    all_to_all x1, blocking collectives, per_device(): lax.all_to_all(staged, 'sz', split_axis=1, concat_axis=1, tiled=True)  68.4 us
    ppermute x6, waiting for transfers between devices, exclusive_scan(): got = lax.ppermute(pack_window(window_decay, window_state), axis, pairs)  64.5 us
    all_to_all x1, waiting for transfers between devices, per_device(): lax.all_to_all(staged, 'sz', split_axis=1, concat_axis=1, tiled=True)  61.4 us
    all_to_all x1, blocking collectives, per_device(): lax.all_to_all(staged, 'sx', split_axis=0, concat_axis=0, tiled=True)  20.9 us
    ppermute x3, waiting for transfers between devices, head_reduce_activate(): total = total + lax.ppermute(outgoing, axis, pairs).astype(jnp.float32)  18.4 us
    psum x1, blocking collectives, per_device(): total_squares = lax.psum(local_squares, 'head')  13.1 us
    ppermute x6, starting transfers between devices, exclusive_scan(): got = lax.ppermute(pack_window(window_decay, window_state), axis, pairs)  12.2 us
    all_to_all x1, starting transfers between devices, per_device(): lax.all_to_all(staged, 'sz', split_axis=1, concat_axis=1, tiled=True)  10.8 us
  transfers between devices with their start and end apart: 16, of which 15 were waited for; matrix products, arithmetic and copies ran while one was open for 1% of the time, Pallas kernels for 0%

profile of v7, /device:TPU:6, one launch (start us, length us, event | category | flops | bytes accessed | tf_op | source)
XLA Modules:
  0.0 390.0 jit_solution(285639701463688666)
XLA Ops:
  5.2 3.8 collective-permute-start
  9.0 11.5 %collective-permute-done = bf16[4,130,128]{2,1,0:T(8,128)(2,1)S(1)} collective-permute-done((bf16[4,130,128]{2,1,0:T(8,128)(2,1)S(1)}, bf16[4,130,128]{2,1,0:T(8,128)(2,1)S(1)}, u32[]{:S(2)}, u32[]{:S(2)}) %collective-permute-start) | collective-permute-done | bytes 133152 | tf_op jit(solution)/shard_map/ppermute | solution.py:35
  21.0 1.9 collective-permute-start.1
  23.0 10.1 %collective-permute-done.1 = bf16[4,130,128]{2,1,0:T(8,128)(2,1)S(1)} collective-permute-done((bf16[4,130,128]{2,1,0:T(8,128)(2,1)S(1)}, bf16[4,130,128]{2,1,0:T(8,128)(2,1)S(1)}, u32[]{:S(2)}, u32[]{:S(2)}) %collective-permute-start.1) | collective-permute-done | bytes 133152 | tf_op jit(solution)/shard_map/ppermute | solution.py:35
  33.7 1.9 collective-permute-start.2
  36.0 15.0 %collective-permute-done.2 = bf16[4,130,128]{2,1,0:T(8,128)(2,1)S(1)} collective-permute-done((bf16[4,130,128]{2,1,0:T(8,128)(2,1)S(1)}, bf16[4,130,128]{2,1,0:T(8,128)(2,1)S(1)}, u32[]{:S(2)}, u32[]{:S(2)}) %collective-permute-start.2) | collective-permute-done | bytes 133152 | tf_op jit(solution)/shard_map/ppermute | solution.py:35
  51.5 1.9 collective-permute-start.3
  54.0 17.1 %collective-permute-done.3 = bf16[4,130,128]{2,1,0:T(8,128)(2,1)S(1)} collective-permute-done((bf16[4,130,128]{2,1,0:T(8,128)(2,1)S(1)}, bf16[4,130,128]{2,1,0:T(8,128)(2,1)S(1)}, u32[]{:S(2)}, u32[]{:S(2)}) %collective-permute-start.3) | collective-permute-done | bytes 133152 | tf_op jit(solution)/shard_map/ppermute | solution.py:35
  72.9 2.4 fusion.6
  75.3 3.8 collective-permute-done.4
  81.1 6.9 %collective-permute-done.5 = bf16[4,130,128]{2,1,0:T(8,128)(2,1)S(1)} collective-permute-done((bf16[4,130,128]{2,1,0:T(8,128)(2,1)S(1)}, bf16[4,130,128]{2,1,0:T(8,128)(2,1)S(1)}, u32[]{:S(2)}, u32[]{:S(2)}) %collective-permute-start.5) | collective-permute-done | bytes 133152 | tf_op jit(solution)/shard_map/ppermute | solution.py:35
  88.1 1.8 multiply_reduce_fusion.1
  90.3 13.1 %psum.7 = f32[256]{0:T(256)S(1)} all-reduce(f32[256]{0:T(256)S(1)} %get-tuple-element.17), channel_id=1, replica_groups=mesh['sx'=4,'sz'=16,'head'=8] {'head'}, use_global_device_ids=true, to_apply=%region_6.7 | all-reduce | flops 256 | bytes 2048 | tf_op jit(solution)/shard_map/psum | solution.py:134
  106.6 2.3 copy.219
  109.0 68.4 %all_to_all.20 = bf16[4,16,20,512]{3,0,2,1:T(4,128)(2,1)S(1)} all-to-all(bf16[4,16,20,512]{3,0,2,1:T(4,128)(2,1)S(1)} %copy.219), channel_id=1, replica_groups=mesh['sx'=4,'sz'=16,'head'=8] {'sz'}, dimensions={1} | all-to-all | bytes 2621440 | tf_op jit(solution)/shard_map/all_to_all | solution.py:164
  177.4 1.8 copy.220
  179.2 5.8 %all-to-all-start.1 = ((bf16[4,16,20,512]{3,1,2,0:T(8,128)(2,1)}), bf16[4,16,20,512]{3,1,2,0:T(8,128)(2,1)}, u32[]{:S(2)}, u32[]{:S(2)}) async-start(bf16[4,16,20,512]{3,1,2,0:T(8,128)(2,1)} %copy.220), calls=%async_computation.1 | async-start | bytes 2621440 | tf_op jit(solution)/shard_map/all_to_all | solution.py:165
  184.9 10.3 %all-to-all-done.1 = bf16[4,16,20,512]{3,1,2,0:T(8,128)(2,1)} async-done(((bf16[4,16,20,512]{3,1,2,0:T(8,128)(2,1)}), bf16[4,16,20,512]{3,1,2,0:T(8,128)(2,1)}, u32[]{:S(2)}, u32[]{:S(2)}) %all-to-all-start.1) | async-done | bytes 1310752 | tf_op jit(solution)/shard_map/all_to_all | solution.py:165
  195.3 2.1 copy.221
  198.6 3.5 convolution_convert_fusion
  202.1 1.5 dynamic-slice_bitcast_fusion
  204.4 1.9 collective-permute-start.6
  206.4 3.8 collective-permute-done.6
  210.2 3.7 convert_add_fusion
  213.9 1.9 fusion.27
  215.8 1.9 collective-permute-start.7
  217.7 3.8 collective-permute-start.8
  221.5 3.4 collective-permute-start.9
  225.0 15.9 %collective-permute-done.7 = bf16[1,160,1408]{2,1,0:T(8,128)(2,1)S(1)} collective-permute-done((bf16[1,160,1408]{2,1,0:T(8,128)(2,1)S(1)}, bf16[1,160,1408]{2,1,0:T(8,128)(2,1)S(1)}, u32[]{:S(2)}, u32[]{:S(2)}) %collective-permute-start.7) | collective-permute-done | bytes 450592 | tf_op jit(solution)/shard_map/ppermute | solution.py:66
  240.9 2.5 collective-permute-done.9
  245.0 2.3 collective-permute-start.10
  247.4 5.6 %collective-permute-start.11 = (bf16[1,160,704]{2,1,0:T(8,128)(2,1)S(1)}, bf16[1,160,704]{2,1,0:T(8,128)(2,1)S(1)}, u32[]{:S(2)}, u32[]{:S(2)}) collective-permute-start(bf16[1,160,704]{2,1,0:T(8,128)(2,1)S(1)} %fusion.26), channel_id=1, source_target_pairs={{0,4},{1,5},{2,6},{3,7},{4,0},{5,1},{6,2},{7,3},{8,12},{9,13},{10,... | collective-permute-start | bytes 675848 | tf_op jit(solution)/shard_map/ppermute | solution.py:73
  253.0 1.9 collective-permute-start.12
  255.7 6.4 %collective-permute-done.11 = bf16[1,160,704]{2,1,0:T(8,128)(2,1)S(1)} collective-permute-done((bf16[1,160,704]{2,1,0:T(8,128)(2,1)S(1)}, bf16[1,160,704]{2,1,0:T(8,128)(2,1)S(1)}, u32[]{:S(2)}, u32[]{:S(2)}) %collective-permute-start.11) | collective-permute-done | bytes 225312 | tf_op jit(solution)/shard_map/ppermute | solution.py:73
  264.4 1.9 collective-permute-start.13
  266.5 2.3 collective-permute-done.13
  269.0 2.0 gather_fusion.1
  271.0 1.8 bitcast_select_fusion
  275.8 20.9 %all_to_all.21 = bf16[4,16,20,512]{3,1,2,0:T(8,128)(2,1)S(1)} all-to-all(bf16[4,16,20,512]{3,1,2,0:T(8,128)(2,1)S(1)} %copy.224), channel_id=1, replica_groups=mesh['sx'=4,'sz'=16,'head'=8] {'sx'}, dimensions={0} | all-to-all | bytes 2621440 | tf_op jit(solution)/shard_map/all_to_all | solution.py:178
  296.8 2.1 copy.225
  298.8 10.8 %all-to-all-start.3 = ((bf16[4,16,20,512]{3,0,2,1:T(4,128)(2,1)}), bf16[4,16,20,512]{3,0,2,1:T(4,128)(2,1)S(1)}, u32[]{:S(2)}, u32[]{:S(2)}) async-start(bf16[4,16,20,512]{3,0,2,1:T(4,128)(2,1)} %copy.225), calls=%async_computation.3 | async-start | bytes 2621440 | tf_op jit(solution)/shard_map/all_to_all | solution.py:179
  310.7 61.4 %all-to-all-done.3 = bf16[4,16,20,512]{3,0,2,1:T(4,128)(2,1)S(1)} async-done(((bf16[4,16,20,512]{3,0,2,1:T(4,128)(2,1)}), bf16[4,16,20,512]{3,0,2,1:T(4,128)(2,1)S(1)}, u32[]{:S(2)}, u32[]{:S(2)}) %all-to-all-start.3) | async-done | bytes 1310752 | tf_op jit(solution)/shard_map/all_to_all | solution.py:179
  372.9 1.7 copy.227
  374.6 3.2 reshape.549
  377.9 4.5 %reduce_sum.48 = f32[32,20,512]{2,0,1:T(8,128)} reduce(f32[32,2,20,512]{3,1,0,2:T(2,128)S(1)} %reshape.549, f32[]{:T(128)} %constant.122.clone.1), dimensions={1}, to_apply=%region_7.8 | reduce | flops 327680 | bytes 3932164 | tf_op jit(solution)/shard_map/reduce_sum | solution.py:181
  382.4 2.1 copy.228
  384.6 1.6 gather_fusion.2
  386.9 2.3 multiply_reduce_fusion
  (136 shorter events, 28.4 us)
Async XLA Ops:
  0.0 198.6 %copy-start = (bf16[1,512,1408]{2,1,0:T(8,128)(2,1)S(1)}, bf16[1,512,1408]{2,1,0:T(8,128)(2,1)}, u32[]{:S(2)}) copy-start(bf16[1,512,1408]{2,1,0:T(8,128)(2,1)} %param.20) | copy-start | bytes 4325380
  2.2 33.4 %copy-start.7 = (s32[256,2]{0,1:T(2,128)S(1)}, s32[256,2]{0,1:T(2,128)}, u32[]{:S(2)}) copy-start(s32[256,2]{0,1:T(2,128)} %param.18) | copy-start | bytes 6148
  5.2 15.3 %collective-permute-start = (bf16[4,130,128]{2,1,0:T(8,128)(2,1)S(1)}, bf16[4,130,128]{2,1,0:T(8,128)(2,1)S(1)}, u32[]{:S(2)}, u32[]{:S(2)}) collective-permute-start(bf16[4,130,128]{2,1,0:T(8,128)(2,1)S(1)} %pad_maximum_fusion), channel_id=1, source_target_pairs={{0,8},{8,16},{16,24},{24,32},{32,40},{40,48},{48,56},{56,64},{64,7... | collective-permute-start | bytes 399368 | tf_op jit(solution)/shard_map/ppermute | solution.py:35
  21.0 12.2 %collective-permute-start.1 = (bf16[4,130,128]{2,1,0:T(8,128)(2,1)S(1)}, bf16[4,130,128]{2,1,0:T(8,128)(2,1)S(1)}, u32[]{:S(2)}, u32[]{:S(2)}) collective-permute-start(bf16[4,130,128]{2,1,0:T(8,128)(2,1)S(1)} %pad_maximum_fusion.1), channel_id=1, source_target_pairs={{0,16},{8,24},{16,32},{24,40},{32,48},{40,56},{48,64},{56,72},{64,... | collective-permute-start | bytes 399368 | tf_op jit(solution)/shard_map/ppermute | solution.py:35
  33.6 39.3 %copy-start.5 = (bf16[256,512]{1,0:T(8,128)(2,1)S(1)}, bf16[256,512]{1,0:T(8,128)(2,1)}, u32[]{:S(2)}) copy-start(bf16[256,512]{1,0:T(8,128)(2,1)} %param.14) | copy-start | bytes 786436
  33.7 17.3 %collective-permute-start.2 = (bf16[4,130,128]{2,1,0:T(8,128)(2,1)S(1)}, bf16[4,130,128]{2,1,0:T(8,128)(2,1)S(1)}, u32[]{:S(2)}, u32[]{:S(2)}) collective-permute-start(bf16[4,130,128]{2,1,0:T(8,128)(2,1)S(1)} %pad_maximum_fusion.2), channel_id=1, source_target_pairs={{0,32},{8,40},{16,48},{24,56},{32,64},{40,72},{48,80},{56,88},{64,... | collective-permute-start | bytes 399368 | tf_op jit(solution)/shard_map/ppermute | solution.py:35
  51.5 19.6 %collective-permute-start.3 = (bf16[4,130,128]{2,1,0:T(8,128)(2,1)S(1)}, bf16[4,130,128]{2,1,0:T(8,128)(2,1)S(1)}, u32[]{:S(2)}, u32[]{:S(2)}) collective-permute-start(bf16[4,130,128]{2,1,0:T(8,128)(2,1)S(1)} %pad_maximum_fusion.3), channel_id=1, source_target_pairs={{0,64},{8,72},{16,80},{24,88},{32,96},{40,104},{48,112},{56,120},{... | collective-permute-start | bytes 399368 | tf_op jit(solution)/shard_map/ppermute | solution.py:35
  71.6 7.5 %collective-permute-start.4 = (bf16[4,130,128]{2,1,0:T(8,128)(2,1)S(1)}, bf16[4,130,128]{2,1,0:T(8,128)(2,1)S(1)}, u32[]{:S(2)}, u32[]{:S(2)}) collective-permute-start(bf16[4,130,128]{2,1,0:T(8,128)(2,1)S(1)} %pad_maximum_fusion.4), channel_id=1, source_target_pairs={{0,128},{8,136},{16,144},{24,152},{32,160},{40,168},{48,176},{56,1... | collective-permute-start | bytes 399368 | tf_op jit(solution)/shard_map/ppermute | solution.py:35
  79.6 8.5 %collective-permute-start.5 = (bf16[4,130,128]{2,1,0:T(8,128)(2,1)S(1)}, bf16[4,130,128]{2,1,0:T(8,128)(2,1)S(1)}, u32[]{:S(2)}, u32[]{:S(2)}) collective-permute-start(bf16[4,130,128]{2,1,0:T(8,128)(2,1)S(1)} %pad_maximum_fusion.5), channel_id=1, source_target_pairs={{0,256},{8,264},{16,272},{24,280},{32,288},{40,296},{48,304},{56,3... | collective-permute-start | bytes 399368 | tf_op jit(solution)/shard_map/ppermute | solution.py:35
  88.1 2.1 copy-start.6
  88.1 2.1 copy-start.8
  89.8 13.6 %copy-start.11 = (f32[512]{0:T(512)S(1)}, f32[512]{0:T(512)}, u32[]{:S(2)}) copy-start(f32[512]{0:T(512)} %param.17) | copy-start | bytes 6148
  90.3 13.1 %copy-start.3 = (bf16[256,512]{1,0:T(8,128)(2,1)}, bf16[256,512]{1,0:T(8,128)(2,1)S(1)}, u32[]{:S(2)}) copy-start(bf16[256,512]{1,0:T(8,128)(2,1)S(1)} %get-tuple-element.18) | copy-start | bytes 786436
  179.2 16.1 %all-to-all-start.1 = ((bf16[4,16,20,512]{3,1,2,0:T(8,128)(2,1)}), bf16[4,16,20,512]{3,1,2,0:T(8,128)(2,1)}, u32[]{:S(2)}, u32[]{:S(2)}) async-start(bf16[4,16,20,512]{3,1,2,0:T(8,128)(2,1)} %copy.220), calls=%async_computation.1 | async-start | bytes 2621440 | tf_op jit(solution)/shard_map/all_to_all | solution.py:165
  202.1 2.3 copy-start.2
  204.4 5.8 %collective-permute-start.6 = (bf16[1,4,160,1408]{3,2,1,0:T(8,128)(2,1)}, bf16[1,4,160,1408]{3,2,1,0:T(8,128)(2,1)S(1)}, u32[]{:S(2)}, u32[]{:S(2)}) collective-permute-start(bf16[1,4,160,1408]{3,2,1,0:T(8,128)(2,1)} %dynamic-slice_bitcast_fusion), channel_id=1, source_target_pairs={{0,1},{1,0},{2,3},{3,2},{4,5},{5,4},{6,7},{7,6},{8,9},{9,8},{10,11... | collective-permute-start | bytes 5406728 | tf_op jit(solution)/shard_map/ppermute | solution.py:60
  215.8 25.1 %collective-permute-start.7 = (bf16[1,160,1408]{2,1,0:T(8,128)(2,1)S(1)}, bf16[1,160,1408]{2,1,0:T(8,128)(2,1)S(1)}, u32[]{:S(2)}, u32[]{:S(2)}) collective-permute-start(bf16[1,160,1408]{2,1,0:T(8,128)(2,1)S(1)} %get-tuple-element.35), channel_id=1, source_target_pairs={{0,2},{1,3},{2,4},{3,5},{4,6},{5,7},{6,0},{7,1},{8,10},{9,11},{10,... | collective-permute-start | bytes 1351688 | tf_op jit(solution)/shard_map/ppermute | solution.py:66
  217.7 23.2 %collective-permute-start.8 = (bf16[1,160,1408]{2,1,0:T(8,128)(2,1)S(1)}, bf16[1,160,1408]{2,1,0:T(8,128)(2,1)S(1)}, u32[]{:S(2)}, u32[]{:S(2)}) collective-permute-start(bf16[1,160,1408]{2,1,0:T(8,128)(2,1)S(1)} %get-tuple-element.37), channel_id=1, source_target_pairs={{0,4},{1,5},{2,6},{3,7},{4,0},{5,1},{6,2},{7,3},{8,12},{9,13},{10,... | collective-permute-start | bytes 1351688 | tf_op jit(solution)/shard_map/ppermute | solution.py:66
  221.5 21.9 %collective-permute-start.9 = (bf16[1,160,1408]{2,1,0:T(8,128)(2,1)S(1)}, bf16[1,160,1408]{2,1,0:T(8,128)(2,1)S(1)}, u32[]{:S(2)}, u32[]{:S(2)}) collective-permute-start(bf16[1,160,1408]{2,1,0:T(8,128)(2,1)S(1)} %get-tuple-element.36), channel_id=1, source_target_pairs={{0,6},{1,7},{2,0},{3,1},{4,2},{5,3},{6,4},{7,5},{8,14},{9,15},{10,... | collective-permute-start | bytes 1351688 | tf_op jit(solution)/shard_map/ppermute | solution.py:66
  245.0 10.7 %collective-permute-start.10 = (bf16[1,160,704]{2,1,0:T(8,128)(2,1)S(1)}, bf16[1,160,704]{2,1,0:T(8,128)(2,1)S(1)}, u32[]{:S(2)}, u32[]{:S(2)}) collective-permute-start(bf16[1,160,704]{2,1,0:T(8,128)(2,1)S(1)} %fusion.26), channel_id=1, source_target_pairs={{0,2},{1,3},{2,4},{3,5},{4,6},{5,7},{6,0},{7,1},{8,10},{9,11},{10,... | collective-permute-start | bytes 675848 | tf_op jit(solution)/shard_map/ppermute | solution.py:73
  247.4 14.8 %collective-permute-start.11 = (bf16[1,160,704]{2,1,0:T(8,128)(2,1)S(1)}, bf16[1,160,704]{2,1,0:T(8,128)(2,1)S(1)}, u32[]{:S(2)}, u32[]{:S(2)}) collective-permute-start(bf16[1,160,704]{2,1,0:T(8,128)(2,1)S(1)} %fusion.26), channel_id=1, source_target_pairs={{0,4},{1,5},{2,6},{3,7},{4,0},{5,1},{6,2},{7,3},{8,12},{9,13},{10,... | collective-permute-start | bytes 675848 | tf_op jit(solution)/shard_map/ppermute | solution.py:73
  253.0 10.5 %collective-permute-start.12 = (bf16[1,160,704]{2,1,0:T(8,128)(2,1)S(1)}, bf16[1,160,704]{2,1,0:T(8,128)(2,1)S(1)}, u32[]{:S(2)}, u32[]{:S(2)}) collective-permute-start(bf16[1,160,704]{2,1,0:T(8,128)(2,1)S(1)} %fusion.26), channel_id=1, source_target_pairs={{0,6},{1,7},{2,0},{3,1},{4,2},{5,3},{6,4},{7,5},{8,14},{9,15},{10,... | collective-permute-start | bytes 675848 | tf_op jit(solution)/shard_map/ppermute | solution.py:73
  264.4 4.5 %collective-permute-start.13 = (bf16[1,4,160,704]{3,2,1,0:T(8,128)(2,1)S(1)}, bf16[1,4,160,704]{3,2,1,0:T(8,128)(2,1)S(1)}, u32[]{:S(2)}, u32[]{:S(2)}) collective-permute-start(bf16[1,4,160,704]{3,2,1,0:T(8,128)(2,1)S(1)} %bitcast_select_fusion.1), channel_id=1, source_target_pairs={{0,1},{1,0},{2,3},{3,2},{4,5},{5,4},{6,7},{7,6},{8,9},{9,8},{10,11... | collective-permute-start | bytes 2703368 | tf_op jit(solution)/shard_map/ppermute | solution.py:76
  272.8 1.1 copy-start.10
  298.8 11.1 %copy-start.9 = (f32[256,2]{0,1:T(2,128)S(1)}, f32[256,2]{0,1:T(2,128)}, u32[]{:S(2)}) copy-start(f32[256,2]{0,1:T(2,128)} %param.19) | copy-start | bytes 6148
  298.8 73.3 %all-to-all-start.3 = ((bf16[4,16,20,512]{3,0,2,1:T(4,128)(2,1)}), bf16[4,16,20,512]{3,0,2,1:T(4,128)(2,1)S(1)}, u32[]{:S(2)}, u32[]{:S(2)}) async-start(bf16[4,16,20,512]{3,0,2,1:T(4,128)(2,1)} %copy.225), calls=%async_computation.3 | async-start | bytes 2621440 | tf_op jit(solution)/shard_map/all_to_all | solution.py:179
  386.3 3.7 copy-start.1
  386.9 2.3 copy-start.4

commit v8 on v5

--- a/solution.py
+++ b/solution.py
@@ -19,28 +19,48 @@
     return jnp.concatenate([state.astype(jnp.bfloat16), tail], axis=1)
 
 
+def unpack_window(got, rows):
+    got_state = got[:, :rows, :].astype(jnp.float32)
+    got_decay = got[:, rows, 0].astype(jnp.float32) + got[:, rows + 1, 0].astype(jnp.float32)
+    return got_decay, got_state
+
+
 def exclusive_scan(decay, state, axis):
     place = lax.axis_index(axis)
     count = lax.axis_size(axis)
     rows = state.shape[1]
-    window_decay = decay
-    window_state = state
-    before_decay = jnp.ones_like(decay)
-    before_state = jnp.zeros_like(state)
-    shift = 1
-    while shift < count:
-        pairs = [(j, j + shift) for j in range(count - shift)]
-        got = lax.ppermute(pack_window(window_decay, window_state), axis, pairs)
-        valid = place >= shift
-        got_state = got[:, :rows, :].astype(jnp.float32)
-        got_decay = got[:, rows, 0].astype(jnp.float32) + got[:, rows + 1, 0].astype(jnp.float32)
-        got_decay = jnp.where(valid, got_decay, 1.0)
-        before_state = before_decay[:, None, None] * got_state + before_state
-        before_decay = before_decay * got_decay
-        window_state = window_decay[:, None, None] * got_state + window_state
-        window_decay = window_decay * got_decay
-        shift *= 2
-    return before_state
+    cur_decay = decay
+    cur_state = state
+    span = 1
+    while span < count:
+        ends = [i for i in range(count) if (i + 1) % (2 * span) == 0]
+        got = lax.ppermute(
+            pack_window(cur_decay, cur_state), axis, [(i - span, i) for i in ends]
+        )
+        got_decay, got_state = unpack_window(got, rows)
+        take = (place + 1) % (2 * span) == 0
+        cur_state = jnp.where(take, cur_decay[:, None, None] * got_state + cur_state, cur_state)
+        cur_decay = jnp.where(take, cur_decay * got_decay, cur_decay)
+        span *= 2
+    last = place == count - 1
+    cur_state = jnp.where(last, 0.0, cur_state)
+    cur_decay = jnp.where(last, 1.0, cur_decay)
+    span = count // 2
+    while span >= 1:
+        ends = [i for i in range(count) if (i + 1) % (2 * span) == 0]
+        packed = pack_window(cur_decay, cur_state)
+        leftward = lax.ppermute(packed, axis, [(i, i - span) for i in ends])
+        rightward = lax.ppermute(packed, axis, [(i - span, i) for i in ends])
+        prefix_decay, prefix_state = unpack_window(leftward, rows)
+        total_decay, total_state = unpack_window(rightward, rows)
+        is_right = (place + 1) % (2 * span) == 0
+        is_left = (place + 1) % (2 * span) == span
+        right_state = total_decay[:, None, None] * cur_state + total_state
+        right_decay = cur_decay * total_decay
+        cur_state = jnp.where(is_right, right_state, jnp.where(is_left, prefix_state, cur_state))
+        cur_decay = jnp.where(is_right, right_decay, jnp.where(is_left, prefix_decay, cur_decay))
+        span //= 2
+    return cur_state
 
 
 def head_reduce_activate(partial, axis, block_units):

time: 363 us -> 435 us (1.20)
  starting transfers between devices: 52 us -> 177 us
  waiting for transfers between devices: 249 us -> 191 us
  other arithmetic: 13.3 us -> 17.7 us
    ppermute x6 -> x18, starting transfers between devices: 12.2 us -> 135 us  [the longest x6 123 us: exclusive_scan(): rightward = lax.ppermute(packed, axis, [(i - span, i) for i in ends])]
    ppermute x6 -> x18, waiting for transfers between devices: 64.6 us -> 8.32 us  [the longest x6 4.39 us: exclusive_scan(): leftward = lax.ppermute(packed, axis, [(i, i - span) for i in ends])]
  transfers between devices with their start and end apart: 16 -> 28, of which waited for: 15 -> 12; matrix products, arithmetic and copies ran while one was open for 1% -> 1% of each run, Pallas kernels for 0% -> 0%
where the time goes in v8:
time: 435 us; the launch traced here: 434 us
  waiting for transfers between devices  191 us (44%)
  starting transfers between devices  177 us (41%)
  local copies, waits for them, and re-layouts  25.8 us (6%)
  other arithmetic  17.7 us (4%)
  blocking collectives  12.4 us (3%)
  matrix products  8.76 us (2%)
    ppermute x6, starting transfers between devices, exclusive_scan(): rightward = lax.ppermute(packed, axis, [(i - span, i) for i in ends])  123 us
    all_to_all x1, waiting for transfers between devices, per_device(): lax.all_to_all(send_buffer, 'seq', split_axis=0, concat_axis=1, tiled=True)  75.3 us
    all_to_all x1, waiting for transfers between devices, per_device(): lax.all_to_all(computed, 'seq', split_axis=1, concat_axis=0, tiled=True)  75.3 us
    ppermute x3, waiting for transfers between devices, head_reduce_activate(): total = total + lax.ppermute(outgoing, axis, pairs).astype(jnp.float32)  17.7 us
    psum x1, blocking collectives, per_device(): total_squares = lax.psum(local_squares, 'head')  12.4 us
    ppermute x3, starting transfers between devices, head_reduce_activate(): gathered.append(lax.ppermute(mine, axis, pairs))  10.2 us
    ppermute x3, starting transfers between devices, head_reduce_activate(): total = total + lax.ppermute(outgoing, axis, pairs).astype(jnp.float32)  10 us
    all_to_all x1, starting transfers between devices, per_device(): lax.all_to_all(send_buffer, 'seq', split_axis=0, concat_axis=1, tiled=True)  9.8 us
  transfers between devices with their start and end apart: 28, of which 12 were waited for; matrix products, arithmetic and copies ran while one was open for 1% of the time, Pallas kernels for 0%

profile of v8, /device:TPU:6, one launch (start us, length us, event | category | flops | bytes accessed | tf_op | source)
XLA Modules:
  0.0 433.8 jit_solution(12987149711935468175)
XLA Ops:
  0.8 1.2 reduce-window.6
  2.8 1.1 copy.194
  3.9 1.2 fusion.126
  5.2 3.8 collective-permute-start
  9.0 2.9 collective-permute-done
  22.8 1.1 fusion.106
  28.3 1.1 fusion.103
  32.9 119.7 %collective-permute-start.16 = (bf16[4,130,128]{2,1,0:T(8,128)(2,1)S(1)}, bf16[4,130,128]{2,1,0:T(8,128)(2,1)S(1)}, u32[]{:S(2)}, u32[]{:S(2)}) collective-permute-start(bf16[4,130,128]{2,1,0:T(8,128)(2,1)S(1)} %pad_maximum_fusion.11), channel_id=1, source_target_pairs={{0,8},{16,24},{32,40},{48,56},{64,72},{80,88},{96,104},{112,120},{... | collective-permute-start | bytes 399368 | tf_op jit(solution)/shard_map/ppermute | solution.py:53
  152.6 1.3 collective-permute-start.17
  154.1 1.0 collective-permute-done.16
  155.3 4.4 %collective-permute-done.17 = bf16[4,130,128]{2,1,0:T(8,128)(2,1)} collective-permute-done((bf16[4,130,128]{2,1,0:T(8,128)(2,1)S(1)}, bf16[4,130,128]{2,1,0:T(8,128)(2,1)}, u32[]{:S(2)}, u32[]{:S(2)}) %collective-permute-start.17) | collective-permute-done | bytes 133152 | tf_op jit(solution)/shard_map/ppermute | solution.py:52
  159.6 1.6 multiply_reduce_fusion.1
  161.7 12.4 %psum.7 = f32[256]{0:T(256)S(1)} all-reduce(f32[256]{0:T(256)S(1)} %get-tuple-element.13), channel_id=1, replica_groups=mesh['seq'=64,'head'=8] {'head'}, use_global_device_ids=true, to_apply=%region_6.7 | all-reduce | flops 256 | bytes 2048 | tf_op jit(solution)/shard_map/psum | solution.py:152
  174.7 1.3 broadcast_in_dim.95
  176.0 9.8 %all-to-all-start = ((bf16[64,1,20,512]{3,2,1,0:T(8,128)(2,1)}), bf16[64,1,20,512]{3,2,1,0:T(8,128)(2,1)S(1)}, u32[]{:S(2)}, u32[]{:S(2)}) async-start(bf16[64,1,20,512]{3,2,1,0:T(8,128)(2,1)} %bitcast.8), calls=%async_computation | async-start | bytes 3145728 | tf_op jit(solution)/shard_map/all_to_all | solution.py:179
  185.8 75.3 %all-to-all-done = bf16[64,1,20,512]{3,2,1,0:T(8,128)(2,1)S(1)} async-done(((bf16[64,1,20,512]{3,2,1,0:T(8,128)(2,1)}), bf16[64,1,20,512]{3,2,1,0:T(8,128)(2,1)S(1)}, u32[]{:S(2)}, u32[]{:S(2)}) %all-to-all-start) | async-done | bytes 1310752 | tf_op jit(solution)/shard_map/all_to_all | solution.py:179
  261.2 1.2 reshape.1064
  262.4 3.5 convolution_convert_fusion
  265.9 1.8 copy-done.2
  267.7 1.4 dynamic-slice_bitcast_fusion
  269.0 1.9 collective-permute-start.18
  271.0 3.8 collective-permute-done.18
  274.9 1.8 convert_add_fusion
  276.7 1.8 copy-done.1
  279.4 1.9 collective-permute-start.19
  281.3 4.3 collective-permute-start.20
  285.6 3.8 collective-permute-start.21
  289.5 15.2 %collective-permute-done.19 = bf16[1,160,1408]{2,1,0:T(8,128)(2,1)S(1)} collective-permute-done((bf16[1,160,1408]{2,1,0:T(8,128)(2,1)}, bf16[1,160,1408]{2,1,0:T(8,128)(2,1)S(1)}, u32[]{:S(2)}, u32[]{:S(2)}) %collective-permute-start.19) | collective-permute-done | bytes 450592 | tf_op jit(solution)/shard_map/ppermute | solution.py:84
  304.7 2.4 collective-permute-done.21
  307.2 1.5 fusion.15
  308.9 3.1 collective-permute-start.22
  312.0 5.0 %collective-permute-start.23 = (bf16[1,160,704]{2,1,0:T(8,128)(2,1)S(1)}, bf16[1,160,704]{2,1,0:T(8,128)(2,1)S(1)}, u32[]{:S(2)}, u32[]{:S(2)}) collective-permute-start(bf16[1,160,704]{2,1,0:T(8,128)(2,1)S(1)} %fusion.26), channel_id=1, source_target_pairs={{0,4},{1,5},{2,6},{3,7},{4,0},{5,1},{6,2},{7,3},{8,12},{9,13},{10,... | collective-permute-start | bytes 675848 | tf_op jit(solution)/shard_map/ppermute | solution.py:91
  317.0 2.1 collective-permute-start.24
  319.6 6.4 %collective-permute-done.23 = bf16[1,160,704]{2,1,0:T(8,128)(2,1)S(1)} collective-permute-done((bf16[1,160,704]{2,1,0:T(8,128)(2,1)S(1)}, bf16[1,160,704]{2,1,0:T(8,128)(2,1)S(1)}, u32[]{:S(2)}, u32[]{:S(2)}) %collective-permute-start.23) | collective-permute-done | bytes 225312 | tf_op jit(solution)/shard_map/ppermute | solution.py:91
  326.0 1.5 collective-permute-done.24
  328.4 1.9 collective-permute-start.25
  330.6 2.3 collective-permute-done.25
  333.1 2.0 gather_fusion.1
  335.1 1.8 bitcast_select_fusion
  338.0 1.2 convolution_convert_fusion.1
  339.2 1.3 reshape.1068
  340.5 8.4 %all-to-all-start.1 = ((bf16[1,64,20,512]{3,2,0,1:T(8,128)(2,1)}), bf16[1,64,20,512]{3,2,0,1:T(8,128)(2,1)S(1)}, u32[]{:S(2)}, u32[]{:S(2)}) async-start(bf16[1,64,20,512]{3,2,0,1:T(8,128)(2,1)} %bitcast.176), calls=%async_computation.1 | async-start | bytes 3145728 | tf_op jit(solution)/shard_map/all_to_all | solution.py:190
  349.3 75.3 %all-to-all-done.1 = bf16[1,64,20,512]{3,2,0,1:T(8,128)(2,1)S(1)} async-done(((bf16[1,64,20,512]{3,2,0,1:T(8,128)(2,1)}), bf16[1,64,20,512]{3,2,0,1:T(8,128)(2,1)S(1)}, u32[]{:S(2)}, u32[]{:S(2)}) %all-to-all-start.1) | async-done | bytes 1310752 | tf_op jit(solution)/shard_map/all_to_all | solution.py:190
  424.5 1.4 convert_reduce_fusion
  426.0 1.5 reshape.1069
  427.4 2.3 gather_fusion.2
  429.8 1.9 reshape.1093
  431.7 1.3 multiply_reduce_fusion
  (210 shorter events, 26.4 us)
Async XLA Ops:
  0.0 262.4 %copy-start = (bf16[1,512,1408]{2,1,0:T(8,128)(2,1)S(1)}, bf16[1,512,1408]{2,1,0:T(8,128)(2,1)}, u32[]{:S(2)}) copy-start(bf16[1,512,1408]{2,1,0:T(8,128)(2,1)} %param.20) | copy-start | bytes 4325380
  5.2 6.7 %collective-permute-start = (bf16[4,130,128]{2,1,0:T(8,128)(2,1)S(1)}, bf16[4,130,128]{2,1,0:T(8,128)(2,1)S(1)}, u32[]{:S(2)}, u32[]{:S(2)}) collective-permute-start(bf16[4,130,128]{2,1,0:T(8,128)(2,1)S(1)} %pad_maximum_fusion), channel_id=1, source_target_pairs={{0,8},{16,24},{32,40},{48,56},{64,72},{80,88},{96,104},{112,120},{... | collective-permute-start | bytes 399368 | tf_op jit(solution)/shard_map/ppermute | solution.py:37
  12.4 0.8 collective-permute-start.1
  13.7 0.7 collective-permute-start.2
  15.0 0.7 collective-permute-start.3
  16.2 0.7 collective-permute-start.4
  17.4 0.7 collective-permute-start.5
  18.6 1.4 collective-permute-start.6
  19.3 0.8 collective-permute-start.7
  20.6 1.4 collective-permute-start.8
  21.2 0.8 collective-permute-start.9
  22.1 0.7 copy-start.9
  22.8 7.3 %copy-start.5 = (bf16[256,512]{1,0:T(8,128)(2,1)S(1)}, bf16[256,512]{1,0:T(8,128)(2,1)}, u32[]{:S(2)}) copy-start(bf16[256,512]{1,0:T(8,128)(2,1)} %param.14) | copy-start | bytes 786436
  22.8 7.3 %copy-start.6 = (bf16[256,512]{1,0:T(8,128)(2,1)S(1)}, bf16[256,512]{1,0:T(8,128)(2,1)}, u32[]{:S(2)}) copy-start(bf16[256,512]{1,0:T(8,128)(2,1)} %param.12) | copy-start | bytes 786436
  24.0 1.4 collective-permute-start.10
  24.7 0.8 collective-permute-start.11
  26.0 1.4 collective-permute-start.12
  26.7 0.8 collective-permute-start.13
  27.5 0.7 copy-start.10
  29.4 1.4 copy-start.11
  29.5 2.8 collective-permute-start.14
  31.1 1.3 collective-permute-start.15
  32.9 122.2 %collective-permute-start.16 = (bf16[4,130,128]{2,1,0:T(8,128)(2,1)S(1)}, bf16[4,130,128]{2,1,0:T(8,128)(2,1)S(1)}, u32[]{:S(2)}, u32[]{:S(2)}) collective-permute-start(bf16[4,130,128]{2,1,0:T(8,128)(2,1)S(1)} %pad_maximum_fusion.11), channel_id=1, source_target_pairs={{0,8},{16,24},{32,40},{48,56},{64,72},{80,88},{96,104},{112,120},{... | collective-permute-start | bytes 399368 | tf_op jit(solution)/shard_map/ppermute | solution.py:53
  152.6 7.1 %collective-permute-start.17 = (bf16[4,130,128]{2,1,0:T(8,128)(2,1)S(1)}, bf16[4,130,128]{2,1,0:T(8,128)(2,1)}, u32[]{:S(2)}, u32[]{:S(2)}) collective-permute-start(bf16[4,130,128]{2,1,0:T(8,128)(2,1)S(1)} %pad_maximum_fusion.11), channel_id=1, source_target_pairs={{8,0},{24,16},{40,32},{56,48},{72,64},{88,80},{104,96},{120,112},{... | collective-permute-start | bytes 399368 | tf_op jit(solution)/shard_map/ppermute | solution.py:52
  155.1 4.5 %copy-start.8 = (bf16[4,130,128]{2,1,0:T(8,128)(2,1)}, bf16[4,130,128]{2,1,0:T(8,128)(2,1)S(1)}, u32[]{:S(2)}) copy-start(bf16[4,130,128]{2,1,0:T(8,128)(2,1)S(1)} %collective-permute-done.16) | copy-start | bytes 399364
  159.6 1.9 copy-start.7
  159.6 1.9 copy-start.12
  161.2 12.9 %copy-start.15 = (f32[512]{0:T(512)S(1)}, f32[512]{0:T(512)}, u32[]{:S(2)}) copy-start(f32[512]{0:T(512)} %param.17) | copy-start | bytes 6148
  161.7 12.4 %copy-start.3 = (bf16[256,512]{1,0:T(8,128)(2,1)}, bf16[256,512]{1,0:T(8,128)(2,1)S(1)}, u32[]{:S(2)}) copy-start(bf16[256,512]{1,0:T(8,128)(2,1)S(1)} %get-tuple-element.14) | copy-start | bytes 786436
  176.0 85.2 %all-to-all-start = ((bf16[64,1,20,512]{3,2,1,0:T(8,128)(2,1)}), bf16[64,1,20,512]{3,2,1,0:T(8,128)(2,1)S(1)}, u32[]{:S(2)}, u32[]{:S(2)}) async-start(bf16[64,1,20,512]{3,2,1,0:T(8,128)(2,1)} %bitcast.8), calls=%async_computation | async-start | bytes 3145728 | tf_op jit(solution)/shard_map/all_to_all | solution.py:179
  265.9 1.8 copy-start.2
  269.0 5.8 %collective-permute-start.18 = (bf16[1,4,160,1408]{3,2,1,0:T(8,128)(2,1)}, bf16[1,4,160,1408]{3,2,1,0:T(8,128)(2,1)S(1)}, u32[]{:S(2)}, u32[]{:S(2)}) collective-permute-start(bf16[1,4,160,1408]{3,2,1,0:T(8,128)(2,1)} %dynamic-slice_bitcast_fusion), channel_id=1, source_target_pairs={{0,1},{1,0},{2,3},{3,2},{4,5},{5,4},{6,7},{7,6},{8,9},{9,8},{10,11... | collective-permute-start | bytes 5406728 | tf_op jit(solution)/shard_map/ppermute | solution.py:78
  276.7 1.8 copy-start.1
  279.4 25.3 %collective-permute-start.19 = (bf16[1,160,1408]{2,1,0:T(8,128)(2,1)}, bf16[1,160,1408]{2,1,0:T(8,128)(2,1)S(1)}, u32[]{:S(2)}, u32[]{:S(2)}) collective-permute-start(bf16[1,160,1408]{2,1,0:T(8,128)(2,1)} %get-tuple-element.56), channel_id=1, source_target_pairs={{0,2},{1,3},{2,4},{3,5},{4,6},{5,7},{6,0},{7,1},{8,10},{9,11},{10,... | collective-permute-start | bytes 1351688 | tf_op jit(solution)/shard_map/ppermute | solution.py:84
  281.3 23.4 %collective-permute-start.20 = (bf16[1,160,1408]{2,1,0:T(8,128)(2,1)S(1)}, bf16[1,160,1408]{2,1,0:T(8,128)(2,1)S(1)}, u32[]{:S(2)}, u32[]{:S(2)}) collective-permute-start(bf16[1,160,1408]{2,1,0:T(8,128)(2,1)S(1)} %get-tuple-element.58), channel_id=1, source_target_pairs={{0,4},{1,5},{2,6},{3,7},{4,0},{5,1},{6,2},{7,3},{8,12},{9,13},{10,... | collective-permute-start | bytes 1351688 | tf_op jit(solution)/shard_map/ppermute | solution.py:84
  285.6 21.6 %collective-permute-start.21 = (bf16[1,160,1408]{2,1,0:T(8,128)(2,1)S(1)}, bf16[1,160,1408]{2,1,0:T(8,128)(2,1)}, u32[]{:S(2)}, u32[]{:S(2)}) collective-permute-start(bf16[1,160,1408]{2,1,0:T(8,128)(2,1)S(1)} %get-tuple-element.57), channel_id=1, source_target_pairs={{0,6},{1,7},{2,0},{3,1},{4,2},{5,3},{6,4},{7,5},{8,14},{9,15},{10,... | collective-permute-start | bytes 1351688 | tf_op jit(solution)/shard_map/ppermute | solution.py:84
  308.9 10.7 %collective-permute-start.22 = (bf16[1,160,704]{2,1,0:T(8,128)(2,1)S(1)}, bf16[1,160,704]{2,1,0:T(8,128)(2,1)S(1)}, u32[]{:S(2)}, u32[]{:S(2)}) collective-permute-start(bf16[1,160,704]{2,1,0:T(8,128)(2,1)S(1)} %fusion.26), channel_id=1, source_target_pairs={{0,2},{1,3},{2,4},{3,5},{4,6},{5,7},{6,0},{7,1},{8,10},{9,11},{10,... | collective-permute-start | bytes 675848 | tf_op jit(solution)/shard_map/ppermute | solution.py:91
  312.0 14.0 %collective-permute-start.23 = (bf16[1,160,704]{2,1,0:T(8,128)(2,1)S(1)}, bf16[1,160,704]{2,1,0:T(8,128)(2,1)S(1)}, u32[]{:S(2)}, u32[]{:S(2)}) collective-permute-start(bf16[1,160,704]{2,1,0:T(8,128)(2,1)S(1)} %fusion.26), channel_id=1, source_target_pairs={{0,4},{1,5},{2,6},{3,7},{4,0},{5,1},{6,2},{7,3},{8,12},{9,13},{10,... | collective-permute-start | bytes 675848 | tf_op jit(solution)/shard_map/ppermute | solution.py:91
  317.0 10.5 %collective-permute-start.24 = (bf16[1,160,704]{2,1,0:T(8,128)(2,1)S(1)}, bf16[1,160,704]{2,1,0:T(8,128)(2,1)S(1)}, u32[]{:S(2)}, u32[]{:S(2)}) collective-permute-start(bf16[1,160,704]{2,1,0:T(8,128)(2,1)S(1)} %fusion.26), channel_id=1, source_target_pairs={{0,6},{1,7},{2,0},{3,1},{4,2},{5,3},{6,4},{7,5},{8,14},{9,15},{10,... | collective-permute-start | bytes 675848 | tf_op jit(solution)/shard_map/ppermute | solution.py:91
  328.4 4.5 %collective-permute-start.25 = (bf16[1,4,160,704]{3,2,1,0:T(8,128)(2,1)S(1)}, bf16[1,4,160,704]{3,2,1,0:T(8,128)(2,1)S(1)}, u32[]{:S(2)}, u32[]{:S(2)}) collective-permute-start(bf16[1,4,160,704]{3,2,1,0:T(8,128)(2,1)S(1)} %bitcast_select_fusion.1), channel_id=1, source_target_pairs={{0,1},{1,0},{2,3},{3,2},{4,5},{5,4},{6,7},{7,6},{8,9},{9,8},{10,11... | collective-permute-start | bytes 2703368 | tf_op jit(solution)/shard_map/ppermute | solution.py:94
  336.8 1.1 copy-start.14
  340.5 8.7 %copy-start.13 = (f32[256,2]{0,1:T(2,128)S(1)}, f32[256,2]{0,1:T(2,128)}, u32[]{:S(2)}) copy-start(f32[256,2]{0,1:T(2,128)} %param.19) | copy-start | bytes 6148
  340.5 84.1 %all-to-all-start.1 = ((bf16[1,64,20,512]{3,2,0,1:T(8,128)(2,1)}), bf16[1,64,20,512]{3,2,0,1:T(8,128)(2,1)S(1)}, u32[]{:S(2)}, u32[]{:S(2)}) async-start(bf16[1,64,20,512]{3,2,0,1:T(8,128)(2,1)} %bitcast.176), calls=%async_computation.1 | async-start | bytes 3145728 | tf_op jit(solution)/shard_map/all_to_all | solution.py:190
  429.8 3.2 copy-start.4

commit v9 on v5

--- a/solution.py
+++ b/solution.py
@@ -77,6 +77,16 @@
     return full.reshape(blocks_here, rows, block_units)
 
 
+def head_sum(value, axis):
+    count = lax.axis_size(axis)
+    pair = value + lax.ppermute(value, axis, [(j, j ^ 1) for j in range(count)])
+    total = pair
+    for step in range(1, count // 2):
+        pairs = [(j, (j + 2 * step) % count) for j in range(count)]
+        total = total + lax.ppermute(pair, axis, pairs)
+    return total
+
+
 def per_device(
     tokens,
     queries,
@@ -129,7 +139,7 @@
     hidden_state = (tokens.astype(jnp.float32) + normed_heads * head_gain).astype(jnp.bfloat16)
     hidden_wide = hidden_state.astype(jnp.float32)
     local_squares = jnp.sum(hidden_wide * hidden_wide, axis=1)
-    total_squares = lax.psum(local_squares, "head")
+    total_squares = head_sum(local_squares, "head")
     inverse_rms = lax.rsqrt(total_squares / D + EPSILON)
     expert_input = (hidden_wide * inverse_rms[:, None] * expert_gain).astype(jnp.bfloat16)
     capacity = CAP

time: 363 us -> 366 us (level)
  starting transfers between devices: 52 us -> 66.2 us
  blocking collectives: 13.1 us -> 0 us
    ppermute x0 -> x4, starting transfers between devices: none -> 13.5 us  [the longest x3 11.5 us: head_sum(): total = total + lax.ppermute(pair, axis, pairs)]
    psum x1 -> x0, blocking collectives: 13.1 us -> none  [per_device(): total_squares = lax.psum(local_squares, 'head')]
  transfers between devices with their start and end apart: 16 -> 20, of which waited for: 15 -> 18; matrix products, arithmetic and copies ran while one was open for 1% -> 1% of each run, Pallas kernels for 0% -> 0%
where the time goes in v9:
time: 366 us; the launch traced here: 365 us
  waiting for transfers between devices  250 us (68%)
  starting transfers between devices  66.2 us (18%)
  local copies, waits for them, and re-layouts  23.7 us (6%)
  other arithmetic  13.3 us (4%)
  matrix products  10.6 us (3%)
    all_to_all x1, waiting for transfers between devices, per_device(): lax.all_to_all(computed, 'seq', split_axis=1, concat_axis=0, tiled=True)  75.2 us
    all_to_all x1, waiting for transfers between devices, per_device(): lax.all_to_all(send_buffer, 'seq', split_axis=0, concat_axis=1, tiled=True)  74.8 us
    ppermute x6, waiting for transfers between devices, exclusive_scan(): got = lax.ppermute(pack_window(window_decay, window_state), axis, pairs)  64.8 us
    ppermute x3, waiting for transfers between devices, head_reduce_activate(): total = total + lax.ppermute(outgoing, axis, pairs).astype(jnp.float32)  18 us
    ppermute x6, starting transfers between devices, exclusive_scan(): got = lax.ppermute(pack_window(window_decay, window_state), axis, pairs)  12.2 us
    ppermute x3, starting transfers between devices, head_sum(): total = total + lax.ppermute(pair, axis, pairs)  11.5 us
    all_to_all x1, starting transfers between devices, per_device(): lax.all_to_all(send_buffer, 'seq', split_axis=0, concat_axis=1, tiled=True)  9.91 us
    ppermute x3, starting transfers between devices, head_reduce_activate(): gathered.append(lax.ppermute(mine, axis, pairs))  9.83 us
  transfers between devices with their start and end apart: 20, of which 18 were waited for; matrix products, arithmetic and copies ran while one was open for 1% of the time, Pallas kernels for 0%

profile of v9, /device:TPU:6, one launch (start us, length us, event | category | flops | bytes accessed | tf_op | source)
XLA Modules:
  0.0 364.9 jit_solution(15655970283735190576)
XLA Ops:
  5.2 3.8 %collective-permute-start = (bf16[4,130,128]{2,1,0:T(8,128)(2,1)S(1)}, bf16[4,130,128]{2,1,0:T(8,128)(2,1)S(1)}, u32[]{:S(2)}, u32[]{:S(2)}) collective-permute-start(bf16[4,130,128]{2,1,0:T(8,128)(2,1)S(1)} %pad_maximum_fusion), channel_id=1, source_target_pairs={{0,8},{8,16},{16,24},{24,32},{32,40},{40,48},{48,56},{56,64},{64,7... | collective-permute-start | bytes 399368 | tf_op jit(solution)/shard_map/ppermute | solution.py:33
  9.0 11.5 %collective-permute-done = bf16[4,130,128]{2,1,0:T(8,128)(2,1)S(1)} collective-permute-done((bf16[4,130,128]{2,1,0:T(8,128)(2,1)S(1)}, bf16[4,130,128]{2,1,0:T(8,128)(2,1)S(1)}, u32[]{:S(2)}, u32[]{:S(2)}) %collective-permute-start) | collective-permute-done | bytes 133152 | tf_op jit(solution)/shard_map/ppermute | solution.py:33
  21.0 1.9 collective-permute-start.1
  23.0 10.1 %collective-permute-done.1 = bf16[4,130,128]{2,1,0:T(8,128)(2,1)S(1)} collective-permute-done((bf16[4,130,128]{2,1,0:T(8,128)(2,1)S(1)}, bf16[4,130,128]{2,1,0:T(8,128)(2,1)S(1)}, u32[]{:S(2)}, u32[]{:S(2)}) %collective-permute-start.1) | collective-permute-done | bytes 133152 | tf_op jit(solution)/shard_map/ppermute | solution.py:33
  33.7 1.9 collective-permute-start.2
  35.7 15.3 %collective-permute-done.2 = bf16[4,130,128]{2,1,0:T(8,128)(2,1)S(1)} collective-permute-done((bf16[4,130,128]{2,1,0:T(8,128)(2,1)S(1)}, bf16[4,130,128]{2,1,0:T(8,128)(2,1)S(1)}, u32[]{:S(2)}, u32[]{:S(2)}) %collective-permute-start.2) | collective-permute-done | bytes 133152 | tf_op jit(solution)/shard_map/ppermute | solution.py:33
  51.5 1.9 collective-permute-start.3
  53.8 17.4 %collective-permute-done.3 = bf16[4,130,128]{2,1,0:T(8,128)(2,1)S(1)} collective-permute-done((bf16[4,130,128]{2,1,0:T(8,128)(2,1)S(1)}, bf16[4,130,128]{2,1,0:T(8,128)(2,1)S(1)}, u32[]{:S(2)}, u32[]{:S(2)}) %collective-permute-start.3) | collective-permute-done | bytes 133152 | tf_op jit(solution)/shard_map/ppermute | solution.py:33
  73.5 5.6 %collective-permute-done.4 = bf16[4,130,128]{2,1,0:T(8,128)(2,1)S(1)} collective-permute-done((bf16[4,130,128]{2,1,0:T(8,128)(2,1)S(1)}, bf16[4,130,128]{2,1,0:T(8,128)(2,1)S(1)}, u32[]{:S(2)}, u32[]{:S(2)}) %collective-permute-start.4) | collective-permute-done | bytes 133152 | tf_op jit(solution)/shard_map/ppermute | solution.py:33
  80.9 2.4 fusion.6
  83.3 4.8 %collective-permute-done.5 = bf16[4,130,128]{2,1,0:T(8,128)(2,1)S(1)} collective-permute-done((bf16[4,130,128]{2,1,0:T(8,128)(2,1)S(1)}, bf16[4,130,128]{2,1,0:T(8,128)(2,1)S(1)}, u32[]{:S(2)}, u32[]{:S(2)}) %collective-permute-start.5) | collective-permute-done | bytes 133152 | tf_op jit(solution)/shard_map/ppermute | solution.py:33
  88.1 1.7 multiply_reduce_fusion.1
  90.3 1.9 collective-permute-start.6
  93.3 3.5 collective-permute-start.7
  96.8 4.8 %collective-permute-start.8 = (f32[256]{0:T(256)S(1)}, f32[256]{0:T(256)S(1)}, u32[]{:S(2)}, u32[]{:S(2)}) collective-permute-start(f32[256]{0:T(256)S(1)} %add.316), channel_id=1, source_target_pairs={{0,4},{1,5},{2,6},{3,7},{4,0},{5,1},{6,2},{7,3},{8,12},{9,13},{10,... | collective-permute-start | bytes 3080 | tf_op jit(solution)/shard_map/ppermute | solution.py:86
  101.6 3.3 collective-permute-start.9
  105.1 2.0 collective-permute-done.9
  109.0 9.9 %all-to-all-start = ((bf16[64,1,20,512]{3,2,1,0:T(8,128)(2,1)}), bf16[64,1,20,512]{3,2,1,0:T(8,128)(2,1)S(1)}, u32[]{:S(2)}, u32[]{:S(2)}) async-start(bf16[64,1,20,512]{3,2,1,0:T(8,128)(2,1)} %bitcast.8), calls=%async_computation | async-start | bytes 3145728 | tf_op jit(solution)/shard_map/all_to_all | solution.py:169
  118.9 74.8 %all-to-all-done = bf16[64,1,20,512]{3,2,1,0:T(8,128)(2,1)S(1)} async-done(((bf16[64,1,20,512]{3,2,1,0:T(8,128)(2,1)}), bf16[64,1,20,512]{3,2,1,0:T(8,128)(2,1)S(1)}, u32[]{:S(2)}, u32[]{:S(2)}) %all-to-all-start) | async-done | bytes 1310752 | tf_op jit(solution)/shard_map/all_to_all | solution.py:169
  194.9 3.5 convolution_convert_fusion
  198.4 1.8 copy-done.2
  200.2 1.4 dynamic-slice_bitcast_fusion
  201.6 1.9 collective-permute-start.10
  203.6 3.8 %collective-permute-done.10 = bf16[1,4,160,1408]{3,2,1,0:T(8,128)(2,1)S(1)} collective-permute-done((bf16[1,4,160,1408]{3,2,1,0:T(8,128)(2,1)}, bf16[1,4,160,1408]{3,2,1,0:T(8,128)(2,1)S(1)}, u32[]{:S(2)}, u32[]{:S(2)}) %collective-permute-start.10) | collective-permute-done | bytes 1802272 | tf_op jit(solution)/shard_map/ppermute | solution.py:58
  207.4 1.8 convert_add_fusion
  209.3 1.8 copy-done.1
  211.9 2.0 collective-permute-start.11
  213.9 5.9 %collective-permute-start.12 = (bf16[1,160,1408]{2,1,0:T(8,128)(2,1)S(1)}, bf16[1,160,1408]{2,1,0:T(8,128)(2,1)S(1)}, u32[]{:S(2)}, u32[]{:S(2)}) collective-permute-start(bf16[1,160,1408]{2,1,0:T(8,128)(2,1)S(1)} %get-tuple-element.37), channel_id=1, source_target_pairs={{0,4},{1,5},{2,6},{3,7},{4,0},{5,1},{6,2},{7,3},{8,12},{9,13},{10,... | collective-permute-start | bytes 1351688 | tf_op jit(solution)/shard_map/ppermute | solution.py:64
  219.8 1.9 collective-permute-start.13
  221.7 5.9 %collective-permute-done.11 = bf16[1,160,1408]{2,1,0:T(8,128)(2,1)S(1)} collective-permute-done((bf16[1,160,1408]{2,1,0:T(8,128)(2,1)}, bf16[1,160,1408]{2,1,0:T(8,128)(2,1)S(1)}, u32[]{:S(2)}, u32[]{:S(2)}) %collective-permute-start.11) | collective-permute-done | bytes 450592 | tf_op jit(solution)/shard_map/ppermute | solution.py:64
  227.6 10.4 %collective-permute-done.12 = bf16[1,160,1408]{2,1,0:T(8,128)(2,1)S(1)} collective-permute-done((bf16[1,160,1408]{2,1,0:T(8,128)(2,1)S(1)}, bf16[1,160,1408]{2,1,0:T(8,128)(2,1)S(1)}, u32[]{:S(2)}, u32[]{:S(2)}) %collective-permute-start.12) | collective-permute-done | bytes 450592 | tf_op jit(solution)/shard_map/ppermute | solution.py:64
  238.0 1.7 collective-permute-done.13
  239.7 1.5 fusion.15
  241.4 2.5 collective-permute-start.14
  244.0 5.4 %collective-permute-start.15 = (bf16[1,160,704]{2,1,0:T(8,128)(2,1)S(1)}, bf16[1,160,704]{2,1,0:T(8,128)(2,1)S(1)}, u32[]{:S(2)}, u32[]{:S(2)}) collective-permute-start(bf16[1,160,704]{2,1,0:T(8,128)(2,1)S(1)} %fusion.26), channel_id=1, source_target_pairs={{0,4},{1,5},{2,6},{3,7},{4,0},{5,1},{6,2},{7,3},{8,12},{9,13},{10,... | collective-permute-start | bytes 675848 | tf_op jit(solution)/shard_map/ppermute | solution.py:71
  249.4 1.9 collective-permute-start.16
  252.1 6.4 %collective-permute-done.15 = bf16[1,160,704]{2,1,0:T(8,128)(2,1)S(1)} collective-permute-done((bf16[1,160,704]{2,1,0:T(8,128)(2,1)S(1)}, bf16[1,160,704]{2,1,0:T(8,128)(2,1)S(1)}, u32[]{:S(2)}, u32[]{:S(2)}) %collective-permute-start.15) | collective-permute-done | bytes 225312 | tf_op jit(solution)/shard_map/ppermute | solution.py:71
  260.8 2.1 collective-permute-start.17
  263.1 2.1 collective-permute-done.17
  265.4 2.0 gather_fusion.1
  267.4 1.8 bitcast_select_fusion
  272.8 7.1 %all-to-all-start.1 = ((bf16[1,64,20,512]{3,2,0,1:T(8,128)(2,1)}), bf16[1,64,20,512]{3,2,0,1:T(8,128)(2,1)S(1)}, u32[]{:S(2)}, u32[]{:S(2)}) async-start(bf16[1,64,20,512]{3,2,0,1:T(8,128)(2,1)} %bitcast.144), calls=%async_computation.1 | async-start | bytes 3145728 | tf_op jit(solution)/shard_map/all_to_all | solution.py:180
  280.3 75.2 %all-to-all-done.1 = bf16[1,64,20,512]{3,2,0,1:T(8,128)(2,1)S(1)} async-done(((bf16[1,64,20,512]{3,2,0,1:T(8,128)(2,1)}), bf16[1,64,20,512]{3,2,0,1:T(8,128)(2,1)S(1)}, u32[]{:S(2)}, u32[]{:S(2)}) %all-to-all-start.1) | async-done | bytes 1310752 | tf_op jit(solution)/shard_map/all_to_all | solution.py:180
  355.6 1.4 convert_reduce_fusion
  357.0 1.5 reshape.564
  358.5 2.3 gather_fusion.2
  360.8 1.9 reshape.588
  362.7 1.3 multiply_reduce_fusion
  (133 shorter events, 25.2 us)
Async XLA Ops:
  0.0 194.9 %copy-start = (bf16[1,512,1408]{2,1,0:T(8,128)(2,1)S(1)}, bf16[1,512,1408]{2,1,0:T(8,128)(2,1)}, u32[]{:S(2)}) copy-start(bf16[1,512,1408]{2,1,0:T(8,128)(2,1)} %param.20) | copy-start | bytes 4325380
  3.9 49.6 %copy-start.7 = (s32[256,2]{0,1:T(2,128)S(1)}, s32[256,2]{0,1:T(2,128)}, u32[]{:S(2)}) copy-start(s32[256,2]{0,1:T(2,128)} %param.18) | copy-start | bytes 6148
  5.2 15.3 %collective-permute-start = (bf16[4,130,128]{2,1,0:T(8,128)(2,1)S(1)}, bf16[4,130,128]{2,1,0:T(8,128)(2,1)S(1)}, u32[]{:S(2)}, u32[]{:S(2)}) collective-permute-start(bf16[4,130,128]{2,1,0:T(8,128)(2,1)S(1)} %pad_maximum_fusion), channel_id=1, source_target_pairs={{0,8},{8,16},{16,24},{24,32},{32,40},{40,48},{48,56},{56,64},{64,7... | collective-permute-start | bytes 399368 | tf_op jit(solution)/shard_map/ppermute | solution.py:33
  21.0 12.2 %collective-permute-start.1 = (bf16[4,130,128]{2,1,0:T(8,128)(2,1)S(1)}, bf16[4,130,128]{2,1,0:T(8,128)(2,1)S(1)}, u32[]{:S(2)}, u32[]{:S(2)}) collective-permute-start(bf16[4,130,128]{2,1,0:T(8,128)(2,1)S(1)} %pad_maximum_fusion.1), channel_id=1, source_target_pairs={{0,16},{8,24},{16,32},{24,40},{32,48},{40,56},{48,64},{56,72},{64,... | collective-permute-start | bytes 399368 | tf_op jit(solution)/shard_map/ppermute | solution.py:33
  33.7 17.3 %collective-permute-start.2 = (bf16[4,130,128]{2,1,0:T(8,128)(2,1)S(1)}, bf16[4,130,128]{2,1,0:T(8,128)(2,1)S(1)}, u32[]{:S(2)}, u32[]{:S(2)}) collective-permute-start(bf16[4,130,128]{2,1,0:T(8,128)(2,1)S(1)} %pad_maximum_fusion.2), channel_id=1, source_target_pairs={{0,32},{8,40},{16,48},{24,56},{32,64},{40,72},{48,80},{56,88},{64,... | collective-permute-start | bytes 399368 | tf_op jit(solution)/shard_map/ppermute | solution.py:33
  51.3 29.7 %copy-start.5 = (bf16[256,512]{1,0:T(8,128)(2,1)S(1)}, bf16[256,512]{1,0:T(8,128)(2,1)}, u32[]{:S(2)}) copy-start(bf16[256,512]{1,0:T(8,128)(2,1)} %param.14) | copy-start | bytes 786436
  51.5 19.6 %collective-permute-start.3 = (bf16[4,130,128]{2,1,0:T(8,128)(2,1)S(1)}, bf16[4,130,128]{2,1,0:T(8,128)(2,1)S(1)}, u32[]{:S(2)}, u32[]{:S(2)}) collective-permute-start(bf16[4,130,128]{2,1,0:T(8,128)(2,1)S(1)} %pad_maximum_fusion.3), channel_id=1, source_target_pairs={{0,64},{8,72},{16,80},{24,88},{32,96},{40,104},{48,112},{56,120},{... | collective-permute-start | bytes 399368 | tf_op jit(solution)/shard_map/ppermute | solution.py:33
  71.6 7.5 %collective-permute-start.4 = (bf16[4,130,128]{2,1,0:T(8,128)(2,1)S(1)}, bf16[4,130,128]{2,1,0:T(8,128)(2,1)S(1)}, u32[]{:S(2)}, u32[]{:S(2)}) collective-permute-start(bf16[4,130,128]{2,1,0:T(8,128)(2,1)S(1)} %pad_maximum_fusion.4), channel_id=1, source_target_pairs={{0,128},{8,136},{16,144},{24,152},{32,160},{40,168},{48,176},{56,1... | collective-permute-start | bytes 399368 | tf_op jit(solution)/shard_map/ppermute | solution.py:33
  79.5 8.6 %copy-start.11 = (bf16[256,512]{1,0:T(8,128)(2,1)S(1)}, bf16[256,512]{1,0:T(8,128)(2,1)}, u32[]{:S(2)}) copy-start(bf16[256,512]{1,0:T(8,128)(2,1)} %param.12) | copy-start | bytes 786436
  79.6 8.5 %collective-permute-start.5 = (bf16[4,130,128]{2,1,0:T(8,128)(2,1)S(1)}, bf16[4,130,128]{2,1,0:T(8,128)(2,1)S(1)}, u32[]{:S(2)}, u32[]{:S(2)}) collective-permute-start(bf16[4,130,128]{2,1,0:T(8,128)(2,1)S(1)} %pad_maximum_fusion.5), channel_id=1, source_target_pairs={{0,256},{8,264},{16,272},{24,280},{32,288},{40,296},{48,304},{56,3... | collective-permute-start | bytes 399368 | tf_op jit(solution)/shard_map/ppermute | solution.py:33
  88.1 2.0 copy-start.6
  88.1 2.0 copy-start.8
  89.8 17.3 %copy-start.12 = (f32[512]{0:T(512)S(1)}, f32[512]{0:T(512)}, u32[]{:S(2)}) copy-start(f32[512]{0:T(512)} %param.17) | copy-start | bytes 6148
  90.3 16.8 %copy-start.3 = (bf16[256,512]{1,0:T(8,128)(2,1)}, bf16[256,512]{1,0:T(8,128)(2,1)S(1)}, u32[]{:S(2)}) copy-start(bf16[256,512]{1,0:T(8,128)(2,1)S(1)} %get-tuple-element.18) | copy-start | bytes 786436
  90.3 3.0 collective-permute-start.6
  93.3 11.8 %collective-permute-start.7 = (f32[256]{0:T(256)S(1)}, f32[256]{0:T(256)S(1)}, u32[]{:S(2)}, u32[]{:S(2)}) collective-permute-start(f32[256]{0:T(256)S(1)} %add.316), channel_id=1, source_target_pairs={{0,2},{1,3},{2,4},{3,5},{4,6},{5,7},{6,0},{7,1},{8,10},{9,11},{10,... | collective-permute-start | bytes 3080 | tf_op jit(solution)/shard_map/ppermute | solution.py:86
  96.8 8.3 %collective-permute-start.8 = (f32[256]{0:T(256)S(1)}, f32[256]{0:T(256)S(1)}, u32[]{:S(2)}, u32[]{:S(2)}) collective-permute-start(f32[256]{0:T(256)S(1)} %add.316), channel_id=1, source_target_pairs={{0,4},{1,5},{2,6},{3,7},{4,0},{5,1},{6,2},{7,3},{8,12},{9,13},{10,... | collective-permute-start | bytes 3080 | tf_op jit(solution)/shard_map/ppermute | solution.py:86
  101.6 5.5 %collective-permute-start.9 = (f32[256]{0:T(256)S(1)}, f32[256]{0:T(256)S(1)}, u32[]{:S(2)}, u32[]{:S(2)}) collective-permute-start(f32[256]{0:T(256)S(1)} %add.316), channel_id=1, source_target_pairs={{0,6},{1,7},{2,0},{3,1},{4,2},{5,3},{6,4},{7,5},{8,14},{9,15},{10,... | collective-permute-start | bytes 3080 | tf_op jit(solution)/shard_map/ppermute | solution.py:86
  109.0 84.7 %all-to-all-start = ((bf16[64,1,20,512]{3,2,1,0:T(8,128)(2,1)}), bf16[64,1,20,512]{3,2,1,0:T(8,128)(2,1)S(1)}, u32[]{:S(2)}, u32[]{:S(2)}) async-start(bf16[64,1,20,512]{3,2,1,0:T(8,128)(2,1)} %bitcast.8), calls=%async_computation | async-start | bytes 3145728 | tf_op jit(solution)/shard_map/all_to_all | solution.py:169
  198.4 1.8 copy-start.2
  201.6 5.8 %collective-permute-start.10 = (bf16[1,4,160,1408]{3,2,1,0:T(8,128)(2,1)}, bf16[1,4,160,1408]{3,2,1,0:T(8,128)(2,1)S(1)}, u32[]{:S(2)}, u32[]{:S(2)}) collective-permute-start(bf16[1,4,160,1408]{3,2,1,0:T(8,128)(2,1)} %dynamic-slice_bitcast_fusion), channel_id=1, source_target_pairs={{0,1},{1,0},{2,3},{3,2},{4,5},{5,4},{6,7},{7,6},{8,9},{9,8},{10,11... | collective-permute-start | bytes 5406728 | tf_op jit(solution)/shard_map/ppermute | solution.py:58
  209.2 1.8 copy-start.1
  211.9 15.7 %collective-permute-start.11 = (bf16[1,160,1408]{2,1,0:T(8,128)(2,1)}, bf16[1,160,1408]{2,1,0:T(8,128)(2,1)S(1)}, u32[]{:S(2)}, u32[]{:S(2)}) collective-permute-start(bf16[1,160,1408]{2,1,0:T(8,128)(2,1)} %get-tuple-element.35), channel_id=1, source_target_pairs={{0,2},{1,3},{2,4},{3,5},{4,6},{5,7},{6,0},{7,1},{8,10},{9,11},{10,... | collective-permute-start | bytes 1351688 | tf_op jit(solution)/shard_map/ppermute | solution.py:64
  213.9 24.1 %collective-permute-start.12 = (bf16[1,160,1408]{2,1,0:T(8,128)(2,1)S(1)}, bf16[1,160,1408]{2,1,0:T(8,128)(2,1)S(1)}, u32[]{:S(2)}, u32[]{:S(2)}) collective-permute-start(bf16[1,160,1408]{2,1,0:T(8,128)(2,1)S(1)} %get-tuple-element.37), channel_id=1, source_target_pairs={{0,4},{1,5},{2,6},{3,7},{4,0},{5,1},{6,2},{7,3},{8,12},{9,13},{10,... | collective-permute-start | bytes 1351688 | tf_op jit(solution)/shard_map/ppermute | solution.py:64
  219.8 19.9 %collective-permute-start.13 = (bf16[1,160,1408]{2,1,0:T(8,128)(2,1)S(1)}, bf16[1,160,1408]{2,1,0:T(8,128)(2,1)}, u32[]{:S(2)}, u32[]{:S(2)}) collective-permute-start(bf16[1,160,1408]{2,1,0:T(8,128)(2,1)S(1)} %get-tuple-element.36), channel_id=1, source_target_pairs={{0,6},{1,7},{2,0},{3,1},{4,2},{5,3},{6,4},{7,5},{8,14},{9,15},{10,... | collective-permute-start | bytes 1351688 | tf_op jit(solution)/shard_map/ppermute | solution.py:64
  241.4 10.7 %collective-permute-start.14 = (bf16[1,160,704]{2,1,0:T(8,128)(2,1)S(1)}, bf16[1,160,704]{2,1,0:T(8,128)(2,1)S(1)}, u32[]{:S(2)}, u32[]{:S(2)}) collective-permute-start(bf16[1,160,704]{2,1,0:T(8,128)(2,1)S(1)} %fusion.26), channel_id=1, source_target_pairs={{0,2},{1,3},{2,4},{3,5},{4,6},{5,7},{6,0},{7,1},{8,10},{9,11},{10,... | collective-permute-start | bytes 675848 | tf_op jit(solution)/shard_map/ppermute | solution.py:71
  244.0 14.6 %collective-permute-start.15 = (bf16[1,160,704]{2,1,0:T(8,128)(2,1)S(1)}, bf16[1,160,704]{2,1,0:T(8,128)(2,1)S(1)}, u32[]{:S(2)}, u32[]{:S(2)}) collective-permute-start(bf16[1,160,704]{2,1,0:T(8,128)(2,1)S(1)} %fusion.26), channel_id=1, source_target_pairs={{0,4},{1,5},{2,6},{3,7},{4,0},{5,1},{6,2},{7,3},{8,12},{9,13},{10,... | collective-permute-start | bytes 675848 | tf_op jit(solution)/shard_map/ppermute | solution.py:71
  249.4 10.5 %collective-permute-start.16 = (bf16[1,160,704]{2,1,0:T(8,128)(2,1)S(1)}, bf16[1,160,704]{2,1,0:T(8,128)(2,1)S(1)}, u32[]{:S(2)}, u32[]{:S(2)}) collective-permute-start(bf16[1,160,704]{2,1,0:T(8,128)(2,1)S(1)} %fusion.26), channel_id=1, source_target_pairs={{0,6},{1,7},{2,0},{3,1},{4,2},{5,3},{6,4},{7,5},{8,14},{9,15},{10,... | collective-permute-start | bytes 675848 | tf_op jit(solution)/shard_map/ppermute | solution.py:71
  260.8 4.5 %collective-permute-start.17 = (bf16[1,4,160,704]{3,2,1,0:T(8,128)(2,1)S(1)}, bf16[1,4,160,704]{3,2,1,0:T(8,128)(2,1)S(1)}, u32[]{:S(2)}, u32[]{:S(2)}) collective-permute-start(bf16[1,4,160,704]{3,2,1,0:T(8,128)(2,1)S(1)} %bitcast_select_fusion.1), channel_id=1, source_target_pairs={{0,1},{1,0},{2,3},{3,2},{4,5},{5,4},{6,7},{7,6},{8,9},{9,8},{10,11... | collective-permute-start | bytes 2703368 | tf_op jit(solution)/shard_map/ppermute | solution.py:74
  269.2 1.1 copy-start.10
  272.8 7.4 %copy-start.9 = (f32[256,2]{0,1:T(2,128)S(1)}, f32[256,2]{0,1:T(2,128)}, u32[]{:S(2)}) copy-start(f32[256,2]{0,1:T(2,128)} %param.19) | copy-start | bytes 6148
  272.8 82.8 %all-to-all-start.1 = ((bf16[1,64,20,512]{3,2,0,1:T(8,128)(2,1)}), bf16[1,64,20,512]{3,2,0,1:T(8,128)(2,1)S(1)}, u32[]{:S(2)}, u32[]{:S(2)}) async-start(bf16[1,64,20,512]{3,2,0,1:T(8,128)(2,1)} %bitcast.144), calls=%async_computation.1 | async-start | bytes 3145728 | tf_op jit(solution)/shard_map/all_to_all | solution.py:180
  360.8 3.2 copy-start.4

commit v10 on v6

--- a/solution.py
+++ b/solution.py
@@ -62,9 +62,9 @@
         outgoing = lax.dynamic_index_in_dim(pair_sum, target, 1, False).astype(jnp.bfloat16)
         pairs = [(j, (j + 2 * step) % count) for j in range(count)]
         total = total + lax.ppermute(outgoing, axis, pairs).astype(jnp.float32)
-    gate = total[:, :, :block_units]
-    up = total[:, :, block_units:]
-    mine = (jax.nn.silu(gate) * up).astype(jnp.bfloat16)
+    split = total.reshape(blocks_here, share, width // (2 * block_units), 2, block_units)
+    mine = (jax.nn.silu(split[:, :, :, 0]) * split[:, :, :, 1]).astype(jnp.bfloat16)
+    mine = mine.reshape(blocks_here, share, width // 2)
     gathered = [mine]
     for step in range(1, chips):
         pairs = [(j, (j + 2 * step) % count) for j in range(count)]
@@ -74,7 +74,7 @@
     other = lax.ppermute(ordered, axis, sibling)
     both = jnp.stack([ordered, other], axis=2)
     full = jnp.take(both, jnp.arange(2) ^ core, axis=2)
-    return full.reshape(blocks_here, rows, block_units)
+    return full.reshape(blocks_here, rows, width // 2)
 
 
 def per_device(
@@ -90,6 +90,9 @@
     expert_in,
     expert_out,
 ):
+    parity = lax.axis_index("seq") % 2
+    partner = [(j, j ^ 1) for j in range(lax.axis_size("seq"))]
+    other_in, other_out = lax.ppermute((expert_in, expert_out), "seq", partner)
     length = tokens.shape[0]
     local_width = tokens.shape[1]
     heads_here = log_decay.shape[0]
@@ -116,6 +119,7 @@
     )
     block_decay = jnp.exp(cumulative[:, -1])
     entering = exclusive_scan(block_decay, block_state, "seq")
+    entering, other_in, other_out = lax.optimization_barrier((entering, other_in, other_out))
     from_before = jnp.einsum(
         "thd,hde->the",
         query_heads.astype(jnp.float32),
@@ -151,29 +155,33 @@
     send_rows = jnp.dot(dispatch_matrix, expert_input, preferred_element_type=jnp.float32).astype(
         jnp.bfloat16
     )
+    even = parity == 0
+    first_in = jnp.where(even, expert_in, other_in)
+    second_in = jnp.where(even, other_in, expert_in)
+    first_out = jnp.where(even, expert_out, other_out)
+    second_out = jnp.where(even, other_out, expert_out)
     half = capacity // 2
-    parity = lax.axis_index("seq") % 2
-    partner = [(j, j ^ 1) for j in range(lax.axis_size("seq"))]
+    block_units = expert_out.shape[1]
     send_buffer = send_rows.reshape(expert_count * 2, 1, half, local_width)
-    block_units = expert_out.shape[1]
     arrived = lax.all_to_all(send_buffer, "seq", split_axis=0, concat_axis=1, tiled=True)
-    swapped = lax.ppermute(arrived, "seq", partner)
-    both = jnp.stack([arrived, swapped], axis=2)
-    arrived = jnp.take(both, jnp.arange(2) ^ parity, axis=2)
     blocks_here, sources = arrived.shape[0], arrived.shape[1]
-    feature_count = arrived.shape[-1]
-    flat_rows = arrived.reshape(blocks_here, sources * capacity, feature_count)
+    flat_rows = arrived.reshape(blocks_here, sources * half, local_width)
+    weight_in = jnp.concatenate([first_in, second_in], axis=2)
     partial_sums = jnp.einsum(
-        "erd,edh->erh", flat_rows, expert_in, preferred_element_type=jnp.float32
+        "erd,edh->erh", flat_rows, weight_in, preferred_element_type=jnp.float32
     )
     activated = head_reduce_activate(partial_sums.astype(jnp.bfloat16), "head", block_units)
-    produced = jnp.einsum(
-        "erh,ehd->erd", activated, expert_out, preferred_element_type=jnp.float32
+    activated = activated.reshape(blocks_here, sources * half, 2, block_units)
+    first_part = jnp.einsum(
+        "erh,ehd->erd", activated[:, :, 0], first_out, preferred_element_type=jnp.float32
     ).astype(jnp.bfloat16)
-    computed = produced.reshape(blocks_here, sources, 2, half, feature_count)
-    kept = lax.dynamic_index_in_dim(computed, parity, 2, False).astype(jnp.float32)
-    given = lax.dynamic_index_in_dim(computed, 1 - parity, 2, False)
-    summed = (kept + lax.ppermute(given, "seq", partner).astype(jnp.float32)).astype(jnp.bfloat16)
+    second_part = jnp.einsum(
+        "erh,ehd->erd", activated[:, :, 1], second_out, preferred_element_type=jnp.float32
+    ).astype(jnp.bfloat16)
+    summed = (first_part.astype(jnp.float32) + second_part.astype(jnp.float32)).astype(
+        jnp.bfloat16
+    )
+    summed = summed.reshape(blocks_here, sources, half, local_width)
     returned = lax.all_to_all(summed, "seq", split_axis=1, concat_axis=0, tiled=True)
     merged = returned.reshape(expert_count, capacity, local_width).astype(jnp.float32)
     merged = merged.reshape(expert_count * capacity, local_width)

time: 365 us -> 365 us (level)
  blocking collectives: 76 us -> 12.9 us
  waiting for transfers between devices: 177 us -> 207 us
  starting transfers between devices: 51.4 us -> 65.1 us
  local copies, waits for them, and re-layouts: 31 us -> 43.6 us
  other arithmetic: 15.2 us -> 22.3 us
    all_to_all x1 -> x0, blocking collectives: 63 us -> none  [per_device(): lax.all_to_all(send_buffer, 'seq', split_axis=0, concat_axis=1, tiled=True)]
    all_to_all x0 -> x1, waiting for transfers between devices: none -> 47.7 us  [per_device(): lax.all_to_all(send_buffer, 'seq', split_axis=0, concat_axis=1, tiled=True)]
    slice x2 -> x6, local copies, waits for them, and re-layouts: 0.18 us -> 15.3 us  [the longest x2 7.2 us: per_device(): activated[:, :, 1]]
    all_to_all x0 -> x1, starting transfers between devices: none -> 13 us  [per_device(): lax.all_to_all(send_buffer, 'seq', split_axis=0, concat_axis=1, tiled=True)]
    ppermute x6, waiting for transfers between devices: 64.6 us -> 56.1 us  [exclusive_scan(): got = lax.ppermute(pack_window(window_decay, window_state), axis, pairs)]
    ppermute x2, waiting for transfers between devices: 28.4 us -> 20.1 us  [per_device(): other_in, other_out = lax.ppermute((expert_in, expert_out), 'seq', partner)]
    gather x1 -> x3, local copies, waits for them, and re-layouts: 2.22 us -> 9.77 us  [head_reduce_activate(): full = jnp.take(both, jnp.arange(2) ^ core, axis=2)]
    dot_general x2 -> x3, matrix products: 5.78 us -> 7.89 us  [the longest x1 3.83 us: per_device(): jnp.einsum('erd,edh->erh', flat_rows, weight_in, preferred_element_type=j...]
  transfers between devices with their start and end apart: 17 -> 18, of which waited for: 15 -> 16; matrix products, arithmetic and copies ran while one was open for 1% -> 3% of each run, Pallas kernels for 0% -> 0%
where the time goes in v10:
time: 365 us; the launch traced here: 364 us
  waiting for transfers between devices  207 us (57%)
  starting transfers between devices  65.1 us (18%)
  local copies, waits for them, and re-layouts  43.6 us (12%)
  other arithmetic  22.3 us (6%)
  blocking collectives  12.9 us (4%)
  matrix products  11.8 us (3%)
    ppermute x6, waiting for transfers between devices, exclusive_scan(): got = lax.ppermute(pack_window(window_decay, window_state), axis, pairs)  56.1 us
    all_to_all x1, waiting for transfers between devices, per_device(): lax.all_to_all(summed, 'seq', split_axis=1, concat_axis=0, tiled=True)  53.7 us
    all_to_all x1, waiting for transfers between devices, per_device(): lax.all_to_all(send_buffer, 'seq', split_axis=0, concat_axis=1, tiled=True)  47.7 us
    ppermute x2, waiting for transfers between devices, per_device(): other_in, other_out = lax.ppermute((expert_in, expert_out), 'seq', partner)  20.1 us
    ppermute x3, waiting for transfers between devices, head_reduce_activate(): total = total + lax.ppermute(outgoing, axis, pairs).astype(jnp.float32)  15.9 us
    all_to_all x1, starting transfers between devices, per_device(): lax.all_to_all(send_buffer, 'seq', split_axis=0, concat_axis=1, tiled=True)  13 us
    psum x1, blocking collectives, per_device(): total_squares = lax.psum(local_squares, 'head')  12.9 us
    ppermute x6, starting transfers between devices, exclusive_scan(): got = lax.ppermute(pack_window(window_decay, window_state), axis, pairs)  12.3 us
  transfers between devices with their start and end apart: 18, of which 16 were waited for; matrix products, arithmetic and copies ran while one was open for 3% of the time, Pallas kernels for 0%

profile of v10, /device:TPU:6, one launch (start us, length us, event | category | flops | bytes accessed | tf_op | source)
XLA Modules:
  0.0 363.9 jit_solution(534709371332798641)
XLA Ops:
  5.1 4.0 %collective-permute-start = (bf16[4,130,128]{2,1,0:T(8,128)(2,1)S(1)}, bf16[4,130,128]{2,1,0:T(8,128)(2,1)S(1)}, u32[]{:S(2)}, u32[]{:S(2)}) collective-permute-start(bf16[4,130,128]{2,1,0:T(8,128)(2,1)S(1)} %pad_maximum_fusion), channel_id=1, source_target_pairs={{0,8},{8,16},{16,24},{24,32},{32,40},{40,48},{48,56},{56,64},{64,7... | collective-permute-start | bytes 399368 | tf_op jit(solution)/shard_map/ppermute | solution.py:33
  9.1 11.5 %collective-permute-done = bf16[4,130,128]{2,1,0:T(8,128)(2,1)S(1)} collective-permute-done((bf16[4,130,128]{2,1,0:T(8,128)(2,1)S(1)}, bf16[4,130,128]{2,1,0:T(8,128)(2,1)S(1)}, u32[]{:S(2)}, u32[]{:S(2)}) %collective-permute-start) | collective-permute-done | bytes 133152 | tf_op jit(solution)/shard_map/ppermute | solution.py:33
  21.0 1.9 collective-permute-start.1
  23.1 10.1 %collective-permute-done.1 = bf16[4,130,128]{2,1,0:T(8,128)(2,1)S(1)} collective-permute-done((bf16[4,130,128]{2,1,0:T(8,128)(2,1)S(1)}, bf16[4,130,128]{2,1,0:T(8,128)(2,1)S(1)}, u32[]{:S(2)}, u32[]{:S(2)}) %collective-permute-start.1) | collective-permute-done | bytes 133152 | tf_op jit(solution)/shard_map/ppermute | solution.py:33
  33.8 1.9 collective-permute-start.2
  35.7 15.3 %collective-permute-done.2 = bf16[4,130,128]{2,1,0:T(8,128)(2,1)S(1)} collective-permute-done((bf16[4,130,128]{2,1,0:T(8,128)(2,1)S(1)}, bf16[4,130,128]{2,1,0:T(8,128)(2,1)S(1)}, u32[]{:S(2)}, u32[]{:S(2)}) %collective-permute-start.2) | collective-permute-done | bytes 133152 | tf_op jit(solution)/shard_map/ppermute | solution.py:33
  51.6 1.9 collective-permute-start.3
  53.5 6.7 %collective-permute-start.6 = (bf16[1,512,1408]{2,1,0:T(8,128)(2,1)S(1)}, bf16[1,512,1408]{2,1,0:T(8,128)(2,1)}, u32[]{:S(2)}, u32[]{:S(2)}) collective-permute-start(bf16[1,512,1408]{2,1,0:T(8,128)(2,1)S(1)} %copy-done.3), channel_id=1, source_target_pairs={{0,8},{8,0},{16,24},{24,16},{32,40},{40,32},{48,56},{56,48},{64,72... | collective-permute-start | bytes 4325384 | tf_op jit(solution)/shard_map/ppermute | solution.py:95
  60.3 1.9 collective-permute-start.7
  62.2 9.3 %collective-permute-done.3 = bf16[4,130,128]{2,1,0:T(8,128)(2,1)S(1)} collective-permute-done((bf16[4,130,128]{2,1,0:T(8,128)(2,1)S(1)}, bf16[4,130,128]{2,1,0:T(8,128)(2,1)S(1)}, u32[]{:S(2)}, u32[]{:S(2)}) %collective-permute-start.3) | collective-permute-done | bytes 133152 | tf_op jit(solution)/shard_map/ppermute | solution.py:33
  76.3 3.7 %collective-permute-done.4 = bf16[4,130,128]{2,1,0:T(8,128)(2,1)} collective-permute-done((bf16[4,130,128]{2,1,0:T(8,128)(2,1)}, bf16[4,130,128]{2,1,0:T(8,128)(2,1)}, u32[]{:S(2)}, u32[]{:S(2)}) %collective-permute-start.4) | collective-permute-done | bytes 133152 | tf_op jit(solution)/shard_map/ppermute | solution.py:33
  84.4 6.2 %collective-permute-done.5 = bf16[4,130,128]{2,1,0:T(8,128)(2,1)S(1)} collective-permute-done((bf16[4,130,128]{2,1,0:T(8,128)(2,1)S(1)}, bf16[4,130,128]{2,1,0:T(8,128)(2,1)S(1)}, u32[]{:S(2)}, u32[]{:S(2)}) %collective-permute-start.5) | collective-permute-done | bytes 133152 | tf_op jit(solution)/shard_map/ppermute | solution.py:33
  91.8 20.1 %collective-permute-done.7 = bf16[1,704,512]{2,1,0:T(8,128)(2,1)} collective-permute-done((bf16[1,704,512]{2,1,0:T(8,128)(2,1)}, bf16[1,704,512]{2,1,0:T(8,128)(2,1)}, u32[]{:S(2)}, u32[]{:S(2)}) %collective-permute-start.7) | collective-permute-done | bytes 720928 | tf_op jit(solution)/shard_map/ppermute | solution.py:95
  113.5 12.9 %psum.7 = f32[256]{0:T(256)S(1)} all-reduce(f32[256]{0:T(256)S(1)} %get-tuple-element.25), channel_id=1, replica_groups=mesh['seq'=64,'head'=8] {'head'}, use_global_device_ids=true, to_apply=%region_6.7 | all-reduce | flops 256 | bytes 2048 | tf_op jit(solution)/shard_map/psum | solution.py:136
  128.1 13.0 %all-to-all-start = ((bf16[64,1,10,512]{3,2,1,0:T(8,128)(2,1)}), bf16[64,1,10,512]{3,2,1,0:T(8,128)(2,1)S(1)}, u32[]{:S(2)}, u32[]{:S(2)}) async-start(bf16[64,1,10,512]{3,2,1,0:T(8,128)(2,1)} %bitcast.8), calls=%async_computation | async-start | bytes 2097152 | tf_op jit(solution)/shard_map/all_to_all | solution.py:166
  141.1 3.2 broadcast_select_fusion.2
  144.3 47.7 %all-to-all-done = bf16[64,1,10,512]{3,2,1,0:T(8,128)(2,1)S(1)} async-done(((bf16[64,1,10,512]{3,2,1,0:T(8,128)(2,1)}), bf16[64,1,10,512]{3,2,1,0:T(8,128)(2,1)S(1)}, u32[]{:S(2)}, u32[]{:S(2)}) %all-to-all-start) | async-done | bytes 655392 | tf_op jit(solution)/shard_map/all_to_all | solution.py:166
  192.3 3.8 %convolution_convert_fusion = bf16[640,2816]{1,0:T(8,128)(2,1)S(1)} fusion(bf16[640,512]{1,0:T(8,128)(2,1)S(1)} %reshape.640, bf16[1,512,1408]{2,1,0:T(8,128)(2,1)} %get-tuple-element.47, bf16[1,512,1408]{2,1,0:T(8,128)(2,1)} %get-tuple-element.46), kind=kOutput, calls=%fused_computation.3 | convolution fusion | flops 1853063168 | bytes 7143424 | tf_op jit(solution)/shard_map/erd,edh->erh/dot_general | solution.py:170
  198.4 1.9 collective-permute-start.8
  200.4 3.8 %collective-permute-done.8 = bf16[1,4,80,2816]{3,2,1,0:T(8,128)(2,1)S(1)} collective-permute-done((bf16[1,4,80,2816]{3,2,1,0:T(8,128)(2,1)}, bf16[1,4,80,2816]{3,2,1,0:T(8,128)(2,1)S(1)}, u32[]{:S(2)}, u32[]{:S(2)}) %collective-permute-start.8) | collective-permute-done | bytes 1802272 | tf_op jit(solution)/shard_map/ppermute | solution.py:58
  204.3 1.9 convert_add_fusion
  206.1 1.8 copy-done.1
  208.0 3.4 collective-permute-start.10
  211.5 2.6 collective-permute-start.11
  214.0 3.5 collective-permute-start.9
  217.6 7.1 %collective-permute-done.10 = bf16[1,80,2816]{2,1,0:T(8,128)(2,1)S(1)} collective-permute-done((bf16[1,80,2816]{2,1,0:T(8,128)(2,1)S(1)}, bf16[1,80,2816]{2,1,0:T(8,128)(2,1)S(1)}, u32[]{:S(2)}, u32[]{:S(2)}) %collective-permute-start.10) | collective-permute-done | bytes 450592 | tf_op jit(solution)/shard_map/ppermute | solution.py:64
  224.7 6.0 %collective-permute-done.11 = bf16[1,80,2816]{2,1,0:T(8,128)(2,1)S(1)} collective-permute-done((bf16[1,80,2816]{2,1,0:T(8,128)(2,1)S(1)}, bf16[1,80,2816]{2,1,0:T(8,128)(2,1)S(1)}, u32[]{:S(2)}, u32[]{:S(2)}) %collective-permute-start.11) | collective-permute-done | bytes 450592 | tf_op jit(solution)/shard_map/ppermute | solution.py:64
  230.6 2.8 collective-permute-done.9
  235.8 3.1 slice_reduce_fusion.1
  240.5 2.0 collective-permute-start.12
  242.5 3.9 %collective-permute-start.13 = (bf16[1,80,1408]{2,1,0:T(8,128)(2,1)S(1)}, bf16[1,80,1408]{2,1,0:T(8,128)(2,1)S(1)}, u32[]{:S(2)}, u32[]{:S(2)}) collective-permute-start(bf16[1,80,1408]{2,1,0:T(8,128)(2,1)S(1)} %multiply_convert_fusion.1), channel_id=1, source_target_pairs={{0,4},{1,5},{2,6},{3,7},{4,0},{5,1},{6,2},{7,3},{8,12},{9,13},{10,... | collective-permute-start | bytes 675848 | tf_op jit(solution)/shard_map/ppermute | solution.py:71
  246.4 4.0 %collective-permute-start.14 = (bf16[1,80,1408]{2,1,0:T(8,128)(2,1)S(1)}, bf16[1,80,1408]{2,1,0:T(8,128)(2,1)S(1)}, u32[]{:S(2)}, u32[]{:S(2)}) collective-permute-start(bf16[1,80,1408]{2,1,0:T(8,128)(2,1)S(1)} %multiply_convert_fusion.1), channel_id=1, source_target_pairs={{0,6},{1,7},{2,0},{3,1},{4,2},{5,3},{6,4},{7,5},{8,14},{9,15},{10,... | collective-permute-start | bytes 675848 | tf_op jit(solution)/shard_map/ppermute | solution.py:71
  250.5 5.3 %collective-permute-done.12 = bf16[1,80,1408]{2,1,0:T(8,128)(2,1)S(1)} collective-permute-done((bf16[1,80,1408]{2,1,0:T(8,128)(2,1)S(1)}, bf16[1,80,1408]{2,1,0:T(8,128)(2,1)S(1)}, u32[]{:S(2)}, u32[]{:S(2)}) %collective-permute-start.12) | collective-permute-done | bytes 225312 | tf_op jit(solution)/shard_map/ppermute | solution.py:71
  255.8 2.5 collective-permute-done.14
  260.3 2.1 collective-permute-start.15
  262.8 2.0 collective-permute-done.15
  267.1 2.0 gather_fusion.1
  269.1 2.8 copy.157
  271.9 4.9 %gather.18 = bf16[1,640,2,704]{3,2,1,0:T(2,128)(2,1)S(1)} reshape(bf16[4,2,80,1408]{3,2,1,0:T(8,128)(2,1)} %copy.157) | data formatting | bytes 3604480 | tf_op jit(solution)/shard_map/jit(_take)/gather | solution.py:76
  276.9 3.2 broadcast_select_fusion
  280.0 3.7 %fusion.91 = (bf16[1,640,1,704]{3,2,1,0:T(2,128)(2,1)S(1)}, bf16[1,640,1,704]{3,2,1,0:T(2,128)(2,1)}) fusion(bf16[1,640,2,704]{3,2,1,0:T(2,128)(2,1)S(1)} %broadcast_select_fusion), kind=kLoop, calls=%fused_computation.209 | loop fusion | bytes 3604480 | tf_op jit(solution)/shard_map/slice | solution.py:179
  283.7 4.8 %copy.158 = bf16[1,640,1,704]{1,3,2,0:T(8,128)(2,1)} copy(bf16[1,640,1,704]{3,2,1,0:T(2,128)(2,1)} %get-tuple-element.49) | data formatting | bytes 1802240 | tf_op jit(solution)/shard_map/slice | solution.py:176
  288.5 3.5 copy.159
  292.1 2.2 fusion.7
  294.3 1.9 fusion.6
  297.4 7.8 %all-to-all-start.1 = ((bf16[1,64,10,512]{3,2,0,1:T(8,128)(2,1)}), bf16[1,64,10,512]{3,2,0,1:T(8,128)(2,1)S(1)}, u32[]{:S(2)}, u32[]{:S(2)}) async-start(bf16[1,64,10,512]{3,2,0,1:T(8,128)(2,1)} %bitcast.33), calls=%async_computation.1 | async-start | bytes 2097152 | tf_op jit(solution)/shard_map/all_to_all | solution.py:185
  305.7 53.7 %all-to-all-done.1 = bf16[1,64,10,512]{3,2,0,1:T(8,128)(2,1)S(1)} async-done(((bf16[1,64,10,512]{3,2,0,1:T(8,128)(2,1)}), bf16[1,64,10,512]{3,2,0,1:T(8,128)(2,1)S(1)}, u32[]{:S(2)}, u32[]{:S(2)}) %all-to-all-start.1) | async-done | bytes 655392 | tf_op jit(solution)/shard_map/all_to_all | solution.py:185
  359.5 1.6 gather_fusion.2
  (146 shorter events, 36.0 us)
Async XLA Ops:
  0.0 73.9 %copy-start = (bf16[256,512]{1,0:T(8,128)(2,1)S(1)}, bf16[256,512]{1,0:T(8,128)(2,1)}, u32[]{:S(2)}) copy-start(bf16[256,512]{1,0:T(8,128)(2,1)} %param.12) | copy-start | bytes 786436
  5.0 48.5 %copy-start.3 = (bf16[1,512,1408]{2,1,0:T(8,128)(2,1)S(1)}, bf16[1,512,1408]{2,1,0:T(8,128)(2,1)}, u32[]{:S(2)}) copy-start(bf16[1,512,1408]{2,1,0:T(8,128)(2,1)} %param.20) | copy-start | bytes 4325380
  5.1 15.5 %collective-permute-start = (bf16[4,130,128]{2,1,0:T(8,128)(2,1)S(1)}, bf16[4,130,128]{2,1,0:T(8,128)(2,1)S(1)}, u32[]{:S(2)}, u32[]{:S(2)}) collective-permute-start(bf16[4,130,128]{2,1,0:T(8,128)(2,1)S(1)} %pad_maximum_fusion), channel_id=1, source_target_pairs={{0,8},{8,16},{16,24},{24,32},{32,40},{40,48},{48,56},{56,64},{64,7... | collective-permute-start | bytes 399368 | tf_op jit(solution)/shard_map/ppermute | solution.py:33
  21.0 12.2 %collective-permute-start.1 = (bf16[4,130,128]{2,1,0:T(8,128)(2,1)S(1)}, bf16[4,130,128]{2,1,0:T(8,128)(2,1)S(1)}, u32[]{:S(2)}, u32[]{:S(2)}) collective-permute-start(bf16[4,130,128]{2,1,0:T(8,128)(2,1)S(1)} %pad_maximum_fusion.1), channel_id=1, source_target_pairs={{0,16},{8,24},{16,32},{24,40},{32,48},{40,56},{48,64},{56,72},{64,... | collective-permute-start | bytes 399368 | tf_op jit(solution)/shard_map/ppermute | solution.py:33
  33.8 17.3 %collective-permute-start.2 = (bf16[4,130,128]{2,1,0:T(8,128)(2,1)S(1)}, bf16[4,130,128]{2,1,0:T(8,128)(2,1)S(1)}, u32[]{:S(2)}, u32[]{:S(2)}) collective-permute-start(bf16[4,130,128]{2,1,0:T(8,128)(2,1)S(1)} %pad_maximum_fusion.2), channel_id=1, source_target_pairs={{0,32},{8,40},{16,48},{24,56},{32,64},{40,72},{48,80},{56,88},{64,... | collective-permute-start | bytes 399368 | tf_op jit(solution)/shard_map/ppermute | solution.py:33
  51.1 21.6 %copy-start.6 = (bf16[4,130,128]{2,1,0:T(8,128)(2,1)}, bf16[4,130,128]{2,1,0:T(8,128)(2,1)S(1)}, u32[]{:S(2)}) copy-start(bf16[4,130,128]{2,1,0:T(8,128)(2,1)S(1)} %collective-permute-done.2) | copy-start | bytes 399364
  51.6 19.9 %collective-permute-start.3 = (bf16[4,130,128]{2,1,0:T(8,128)(2,1)S(1)}, bf16[4,130,128]{2,1,0:T(8,128)(2,1)S(1)}, u32[]{:S(2)}, u32[]{:S(2)}) collective-permute-start(bf16[4,130,128]{2,1,0:T(8,128)(2,1)S(1)} %pad_maximum_fusion.3), channel_id=1, source_target_pairs={{0,64},{8,72},{16,80},{24,88},{32,96},{40,104},{48,112},{56,120},{... | collective-permute-start | bytes 399368 | tf_op jit(solution)/shard_map/ppermute | solution.py:33
  53.5 58.4 %collective-permute-start.6 = (bf16[1,512,1408]{2,1,0:T(8,128)(2,1)S(1)}, bf16[1,512,1408]{2,1,0:T(8,128)(2,1)}, u32[]{:S(2)}, u32[]{:S(2)}) collective-permute-start(bf16[1,512,1408]{2,1,0:T(8,128)(2,1)S(1)} %copy-done.3), channel_id=1, source_target_pairs={{0,8},{8,0},{16,24},{24,16},{32,40},{40,32},{48,56},{56,48},{64,72... | collective-permute-start | bytes 4325384 | tf_op jit(solution)/shard_map/ppermute | solution.py:95
  60.3 51.7 %collective-permute-start.7 = (bf16[1,704,512]{2,1,0:T(8,128)(2,1)}, bf16[1,704,512]{2,1,0:T(8,128)(2,1)}, u32[]{:S(2)}, u32[]{:S(2)}) collective-permute-start(bf16[1,704,512]{2,1,0:T(8,128)(2,1)} %param.21), channel_id=1, source_target_pairs={{0,8},{8,0},{16,24},{24,16},{32,40},{40,32},{48,56},{56,48},{64,72... | collective-permute-start | bytes 2162696 | tf_op jit(solution)/shard_map/ppermute | solution.py:95
  71.9 3.6 copy-start.10
  72.6 7.4 %collective-permute-start.4 = (bf16[4,130,128]{2,1,0:T(8,128)(2,1)}, bf16[4,130,128]{2,1,0:T(8,128)(2,1)}, u32[]{:S(2)}, u32[]{:S(2)}) collective-permute-start(bf16[4,130,128]{2,1,0:T(8,128)(2,1)} %pad_maximum_fusion.4), channel_id=1, source_target_pairs={{0,128},{8,136},{16,144},{24,152},{32,160},{40,168},{48,176},{56,1... | collective-permute-start | bytes 399368 | tf_op jit(solution)/shard_map/ppermute | solution.py:33
  75.5 15.1 %copy-start.7 = (bf16[4,130,128]{2,1,0:T(8,128)(2,1)S(1)}, bf16[4,130,128]{2,1,0:T(8,128)(2,1)}, u32[]{:S(2)}) copy-start(bf16[4,130,128]{2,1,0:T(8,128)(2,1)} %copy-done.6) | copy-start | bytes 399364
  82.2 8.5 %collective-permute-start.5 = (bf16[4,130,128]{2,1,0:T(8,128)(2,1)S(1)}, bf16[4,130,128]{2,1,0:T(8,128)(2,1)S(1)}, u32[]{:S(2)}, u32[]{:S(2)}) collective-permute-start(bf16[4,130,128]{2,1,0:T(8,128)(2,1)S(1)} %pad_maximum_fusion.5), channel_id=1, source_target_pairs={{0,256},{8,264},{16,272},{24,280},{32,288},{40,296},{48,304},{56,3... | collective-permute-start | bytes 399368 | tf_op jit(solution)/shard_map/ppermute | solution.py:33
  111.9 0.8 copy-start.11
  112.4 1.0 copy-start.8
  112.4 14.0 %copy-start.9 = (pred[640,256]{1,0:T(8,128)(4,1)S(1)}, pred[640,256]{1,0:T(8,128)(4,1)}, u32[]{:S(2)}) copy-start(pred[640,256]{1,0:T(8,128)(4,1)} %fusion.8) | copy-start | bytes 491524
  112.4 14.0 %copy-start.14 = (f32[512]{0:T(512)S(1)}, f32[512]{0:T(512)}, u32[]{:S(2)}) copy-start(f32[512]{0:T(512)} %param.17) | copy-start | bytes 6148
  128.1 63.9 %all-to-all-start = ((bf16[64,1,10,512]{3,2,1,0:T(8,128)(2,1)}), bf16[64,1,10,512]{3,2,1,0:T(8,128)(2,1)S(1)}, u32[]{:S(2)}, u32[]{:S(2)}) async-start(bf16[64,1,10,512]{3,2,1,0:T(8,128)(2,1)} %bitcast.8), calls=%async_computation | async-start | bytes 2097152 | tf_op jit(solution)/shard_map/all_to_all | solution.py:166
  196.1 2.3 copy-start.2
  198.4 5.8 %collective-permute-start.8 = (bf16[1,4,80,2816]{3,2,1,0:T(8,128)(2,1)}, bf16[1,4,80,2816]{3,2,1,0:T(8,128)(2,1)S(1)}, u32[]{:S(2)}, u32[]{:S(2)}) collective-permute-start(bf16[1,4,80,2816]{3,2,1,0:T(8,128)(2,1)} %dynamic-slice_bitcast_fusion), channel_id=1, source_target_pairs={{0,1},{1,0},{2,3},{3,2},{4,5},{5,4},{6,7},{7,6},{8,9},{9,8},{10,11... | collective-permute-start | bytes 5406728 | tf_op jit(solution)/shard_map/ppermute | solution.py:58
  206.1 1.8 copy-start.1
  208.0 16.6 %collective-permute-start.10 = (bf16[1,80,2816]{2,1,0:T(8,128)(2,1)S(1)}, bf16[1,80,2816]{2,1,0:T(8,128)(2,1)S(1)}, u32[]{:S(2)}, u32[]{:S(2)}) collective-permute-start(bf16[1,80,2816]{2,1,0:T(8,128)(2,1)S(1)} %get-tuple-element.45), channel_id=1, source_target_pairs={{0,4},{1,5},{2,6},{3,7},{4,0},{5,1},{6,2},{7,3},{8,12},{9,13},{10,... | collective-permute-start | bytes 1351688 | tf_op jit(solution)/shard_map/ppermute | solution.py:64
  211.5 19.2 %collective-permute-start.11 = (bf16[1,80,2816]{2,1,0:T(8,128)(2,1)S(1)}, bf16[1,80,2816]{2,1,0:T(8,128)(2,1)S(1)}, u32[]{:S(2)}, u32[]{:S(2)}) collective-permute-start(bf16[1,80,2816]{2,1,0:T(8,128)(2,1)S(1)} %get-tuple-element.44), channel_id=1, source_target_pairs={{0,6},{1,7},{2,0},{3,1},{4,2},{5,3},{6,4},{7,5},{8,14},{9,15},{10,... | collective-permute-start | bytes 1351688 | tf_op jit(solution)/shard_map/ppermute | solution.py:64
  214.0 19.4 %collective-permute-start.9 = (bf16[1,80,2816]{2,1,0:T(8,128)(2,1)S(1)}, bf16[1,80,2816]{2,1,0:T(8,128)(2,1)S(1)}, u32[]{:S(2)}, u32[]{:S(2)}) collective-permute-start(bf16[1,80,2816]{2,1,0:T(8,128)(2,1)S(1)} %get-tuple-element.43), channel_id=1, source_target_pairs={{0,2},{1,3},{2,4},{3,5},{4,6},{5,7},{6,0},{7,1},{8,10},{9,11},{10,... | collective-permute-start | bytes 1351688 | tf_op jit(solution)/shard_map/ppermute | solution.py:64
  240.5 15.4 %collective-permute-start.12 = (bf16[1,80,1408]{2,1,0:T(8,128)(2,1)S(1)}, bf16[1,80,1408]{2,1,0:T(8,128)(2,1)S(1)}, u32[]{:S(2)}, u32[]{:S(2)}) collective-permute-start(bf16[1,80,1408]{2,1,0:T(8,128)(2,1)S(1)} %multiply_convert_fusion.1), channel_id=1, source_target_pairs={{0,2},{1,3},{2,4},{3,5},{4,6},{5,7},{6,0},{7,1},{8,10},{9,11},{10,... | collective-permute-start | bytes 675848 | tf_op jit(solution)/shard_map/ppermute | solution.py:71
  242.5 13.4 %collective-permute-start.13 = (bf16[1,80,1408]{2,1,0:T(8,128)(2,1)S(1)}, bf16[1,80,1408]{2,1,0:T(8,128)(2,1)S(1)}, u32[]{:S(2)}, u32[]{:S(2)}) collective-permute-start(bf16[1,80,1408]{2,1,0:T(8,128)(2,1)S(1)} %multiply_convert_fusion.1), channel_id=1, source_target_pairs={{0,4},{1,5},{2,6},{3,7},{4,0},{5,1},{6,2},{7,3},{8,12},{9,13},{10,... | collective-permute-start | bytes 675848 | tf_op jit(solution)/shard_map/ppermute | solution.py:71
  246.4 12.0 %collective-permute-start.14 = (bf16[1,80,1408]{2,1,0:T(8,128)(2,1)S(1)}, bf16[1,80,1408]{2,1,0:T(8,128)(2,1)S(1)}, u32[]{:S(2)}, u32[]{:S(2)}) collective-permute-start(bf16[1,80,1408]{2,1,0:T(8,128)(2,1)S(1)} %multiply_convert_fusion.1), channel_id=1, source_target_pairs={{0,6},{1,7},{2,0},{3,1},{4,2},{5,3},{6,4},{7,5},{8,14},{9,15},{10,... | collective-permute-start | bytes 675848 | tf_op jit(solution)/shard_map/ppermute | solution.py:71
  260.3 4.5 %collective-permute-start.15 = (bf16[1,4,80,1408]{3,2,1,0:T(8,128)(2,1)}, bf16[1,4,80,1408]{3,2,1,0:T(8,128)(2,1)S(1)}, u32[]{:S(2)}, u32[]{:S(2)}) collective-permute-start(bf16[1,4,80,1408]{3,2,1,0:T(8,128)(2,1)} %bitcast_select_fusion), channel_id=1, source_target_pairs={{0,1},{1,0},{2,3},{3,2},{4,5},{5,4},{6,7},{7,6},{8,9},{9,8},{10,11... | collective-permute-start | bytes 2703368 | tf_op jit(solution)/shard_map/ppermute | solution.py:74
  264.8 0.9 copy-start.4
  292.1 2.2 copy-start.5
  292.1 2.2 copy-start.13
  296.2 9.3 %copy-start.12 = (f32[256,2]{0,1:T(2,128)S(1)}, f32[256,2]{0,1:T(2,128)}, u32[]{:S(2)}) copy-start(f32[256,2]{0,1:T(2,128)} %param.19) | copy-start | bytes 6148
  297.4 62.0 %all-to-all-start.1 = ((bf16[1,64,10,512]{3,2,0,1:T(8,128)(2,1)}), bf16[1,64,10,512]{3,2,0,1:T(8,128)(2,1)S(1)}, u32[]{:S(2)}, u32[]{:S(2)}) async-start(bf16[1,64,10,512]{3,2,0,1:T(8,128)(2,1)} %bitcast.33), calls=%async_computation.1 | async-start | bytes 2097152 | tf_op jit(solution)/shard_map/all_to_all | solution.py:185

commit v11 on v10

--- a/solution.py
+++ b/solution.py
@@ -155,28 +155,26 @@
     send_rows = jnp.dot(dispatch_matrix, expert_input, preferred_element_type=jnp.float32).astype(
         jnp.bfloat16
     )
-    even = parity == 0
-    first_in = jnp.where(even, expert_in, other_in)
-    second_in = jnp.where(even, other_in, expert_in)
-    first_out = jnp.where(even, expert_out, other_out)
-    second_out = jnp.where(even, other_out, expert_out)
     half = capacity // 2
     block_units = expert_out.shape[1]
     send_buffer = send_rows.reshape(expert_count * 2, 1, half, local_width)
     arrived = lax.all_to_all(send_buffer, "seq", split_axis=0, concat_axis=1, tiled=True)
     blocks_here, sources = arrived.shape[0], arrived.shape[1]
     flat_rows = arrived.reshape(blocks_here, sources * half, local_width)
-    weight_in = jnp.concatenate([first_in, second_in], axis=2)
-    partial_sums = jnp.einsum(
-        "erd,edh->erh", flat_rows, weight_in, preferred_element_type=jnp.float32
-    )
-    activated = head_reduce_activate(partial_sums.astype(jnp.bfloat16), "head", block_units)
+    own_sums = jnp.einsum(
+        "erd,edh->erh", flat_rows, expert_in, preferred_element_type=jnp.float32
+    ).astype(jnp.bfloat16)
+    other_sums = jnp.einsum(
+        "erd,edh->erh", flat_rows, other_in, preferred_element_type=jnp.float32
+    ).astype(jnp.bfloat16)
+    partial_sums = jnp.concatenate([own_sums, other_sums], axis=2)
+    activated = head_reduce_activate(partial_sums, "head", block_units)
     activated = activated.reshape(blocks_here, sources * half, 2, block_units)
     first_part = jnp.einsum(
-        "erh,ehd->erd", activated[:, :, 0], first_out, preferred_element_type=jnp.float32
+        "erh,ehd->erd", activated[:, :, 0], expert_out, preferred_element_type=jnp.float32
     ).astype(jnp.bfloat16)
     second_part = jnp.einsum(
-        "erh,ehd->erd", activated[:, :, 1], second_out, preferred_element_type=jnp.float32
+        "erh,ehd->erd", activated[:, :, 1], other_out, preferred_element_type=jnp.float32
     ).astype(jnp.bfloat16)
     summed = (first_part.astype(jnp.float32) + second_part.astype(jnp.float32)).astype(
         jnp.bfloat16

time: 365 us -> 367 us (level)
  waiting for transfers between devices: 207 us -> 215 us
  other arithmetic: 22.3 us -> 16.9 us
    dot_general x3 -> x4, matrix products: 7.89 us -> 10.8 us  [the longest x1 3.14 us: per_device(): jnp.einsum('erh,ehd->erd', activated[:, :, 0], expert_out, preferred_elem...]
  transfers between devices with their start and end apart: 18 -> 18, of which waited for: 16 -> 16; matrix products, arithmetic and copies ran while one was open for 3% -> 1% of each run, Pallas kernels for 0% -> 0%
where the time goes in v11:
time: 367 us; the launch traced here: 366 us
  waiting for transfers between devices  215 us (59%)
  starting transfers between devices  65.1 us (18%)
  local copies, waits for them, and re-layouts  41.1 us (11%)
  other arithmetic  16.9 us (5%)
  matrix products  13.7 us (4%)
  blocking collectives  13.1 us (4%)
    ppermute x6, waiting for transfers between devices, exclusive_scan(): got = lax.ppermute(pack_window(window_decay, window_state), axis, pairs)  57.5 us
    all_to_all x1, waiting for transfers between devices, per_device(): lax.all_to_all(summed, 'seq', split_axis=1, concat_axis=0, tiled=True)  53.7 us
    all_to_all x1, waiting for transfers between devices, per_device(): lax.all_to_all(send_buffer, 'seq', split_axis=0, concat_axis=1, tiled=True)  50.7 us
    ppermute x2, waiting for transfers between devices, per_device(): other_in, other_out = lax.ppermute((expert_in, expert_out), 'seq', partner)  23.8 us
    ppermute x3, waiting for transfers between devices, head_reduce_activate(): total = total + lax.ppermute(outgoing, axis, pairs).astype(jnp.float32)  15.8 us
    psum x1, blocking collectives, per_device(): total_squares = lax.psum(local_squares, 'head')  13.1 us
    all_to_all x1, starting transfers between devices, per_device(): lax.all_to_all(send_buffer, 'seq', split_axis=0, concat_axis=1, tiled=True)  12.7 us
    ppermute x6, starting transfers between devices, exclusive_scan(): got = lax.ppermute(pack_window(window_decay, window_state), axis, pairs)  12.3 us
  transfers between devices with their start and end apart: 18, of which 16 were waited for; matrix products, arithmetic and copies ran while one was open for 1% of the time, Pallas kernels for 0%

profile of v11, /device:TPU:6, one launch (start us, length us, event | category | flops | bytes accessed | tf_op | source)
XLA Modules:
  0.0 366.2 jit_solution(4749150659385496243)
XLA Ops:
  5.1 4.0 %collective-permute-start = (bf16[4,130,128]{2,1,0:T(8,128)(2,1)S(1)}, bf16[4,130,128]{2,1,0:T(8,128)(2,1)S(1)}, u32[]{:S(2)}, u32[]{:S(2)}) collective-permute-start(bf16[4,130,128]{2,1,0:T(8,128)(2,1)S(1)} %pad_maximum_fusion), channel_id=1, source_target_pairs={{0,8},{8,16},{16,24},{24,32},{32,40},{40,48},{48,56},{56,64},{64,7... | collective-permute-start | bytes 399368 | tf_op jit(solution)/shard_map/ppermute | solution.py:33
  9.1 11.5 %collective-permute-done = bf16[4,130,128]{2,1,0:T(8,128)(2,1)S(1)} collective-permute-done((bf16[4,130,128]{2,1,0:T(8,128)(2,1)S(1)}, bf16[4,130,128]{2,1,0:T(8,128)(2,1)S(1)}, u32[]{:S(2)}, u32[]{:S(2)}) %collective-permute-start) | collective-permute-done | bytes 133152 | tf_op jit(solution)/shard_map/ppermute | solution.py:33
  21.1 1.9 collective-permute-start.1
  23.1 10.1 %collective-permute-done.1 = bf16[4,130,128]{2,1,0:T(8,128)(2,1)S(1)} collective-permute-done((bf16[4,130,128]{2,1,0:T(8,128)(2,1)S(1)}, bf16[4,130,128]{2,1,0:T(8,128)(2,1)S(1)}, u32[]{:S(2)}, u32[]{:S(2)}) %collective-permute-start.1) | collective-permute-done | bytes 133152 | tf_op jit(solution)/shard_map/ppermute | solution.py:33
  33.8 1.9 collective-permute-start.2
  35.7 15.3 %collective-permute-done.2 = bf16[4,130,128]{2,1,0:T(8,128)(2,1)S(1)} collective-permute-done((bf16[4,130,128]{2,1,0:T(8,128)(2,1)S(1)}, bf16[4,130,128]{2,1,0:T(8,128)(2,1)S(1)}, u32[]{:S(2)}, u32[]{:S(2)}) %collective-permute-start.2) | collective-permute-done | bytes 133152 | tf_op jit(solution)/shard_map/ppermute | solution.py:33
  51.6 1.9 collective-permute-start.3
  53.5 6.7 %collective-permute-start.6 = (bf16[1,512,1408]{2,1,0:T(8,128)(2,1)}, bf16[1,512,1408]{2,1,0:T(8,128)(2,1)}, u32[]{:S(2)}, u32[]{:S(2)}) collective-permute-start(bf16[1,512,1408]{2,1,0:T(8,128)(2,1)} %param.20), channel_id=1, source_target_pairs={{0,8},{8,0},{16,24},{24,16},{32,40},{40,32},{48,56},{56,48},{64,72... | collective-permute-start | bytes 4325384 | tf_op jit(solution)/shard_map/ppermute | solution.py:95
  60.3 1.9 collective-permute-start.7
  62.2 9.2 %collective-permute-done.3 = bf16[4,130,128]{2,1,0:T(8,128)(2,1)S(1)} collective-permute-done((bf16[4,130,128]{2,1,0:T(8,128)(2,1)S(1)}, bf16[4,130,128]{2,1,0:T(8,128)(2,1)S(1)}, u32[]{:S(2)}, u32[]{:S(2)}) %collective-permute-start.3) | collective-permute-done | bytes 133152 | tf_op jit(solution)/shard_map/ppermute | solution.py:33
  74.6 4.5 %collective-permute-done.4 = bf16[4,130,128]{2,1,0:T(8,128)(2,1)S(1)} collective-permute-done((bf16[4,130,128]{2,1,0:T(8,128)(2,1)S(1)}, bf16[4,130,128]{2,1,0:T(8,128)(2,1)S(1)}, u32[]{:S(2)}, u32[]{:S(2)}) %collective-permute-start.4) | collective-permute-done | bytes 133152 | tf_op jit(solution)/shard_map/ppermute | solution.py:33
  81.2 6.9 %collective-permute-done.5 = bf16[4,130,128]{2,1,0:T(8,128)(2,1)S(1)} collective-permute-done((bf16[4,130,128]{2,1,0:T(8,128)(2,1)S(1)}, bf16[4,130,128]{2,1,0:T(8,128)(2,1)S(1)}, u32[]{:S(2)}, u32[]{:S(2)}) %collective-permute-start.5) | collective-permute-done | bytes 133152 | tf_op jit(solution)/shard_map/ppermute | solution.py:33
  88.3 23.8 %collective-permute-done.7 = bf16[1,704,512]{2,1,0:T(8,128)(2,1)} collective-permute-done((bf16[1,704,512]{2,1,0:T(8,128)(2,1)S(1)}, bf16[1,704,512]{2,1,0:T(8,128)(2,1)}, u32[]{:S(2)}, u32[]{:S(2)}) %collective-permute-start.7) | collective-permute-done | bytes 720928 | tf_op jit(solution)/shard_map/ppermute | solution.py:95
  113.3 13.1 %psum.7 = f32[256]{0:T(256)S(1)} all-reduce(f32[256]{0:T(256)S(1)} %get-tuple-element.25), channel_id=1, replica_groups=mesh['seq'=64,'head'=8] {'head'}, use_global_device_ids=true, to_apply=%region_6.7 | all-reduce | flops 256 | bytes 2048 | tf_op jit(solution)/shard_map/psum | solution.py:136
  128.0 12.7 %all-to-all-start = ((bf16[64,1,10,512]{3,2,1,0:T(8,128)(2,1)}), bf16[64,1,10,512]{3,2,1,0:T(8,128)(2,1)S(1)}, u32[]{:S(2)}, u32[]{:S(2)}) async-start(bf16[64,1,10,512]{3,2,1,0:T(8,128)(2,1)} %bitcast.8), calls=%async_computation | async-start | bytes 2097152 | tf_op jit(solution)/shard_map/all_to_all | solution.py:161
  140.7 50.7 %all-to-all-done = bf16[64,1,10,512]{3,2,1,0:T(8,128)(2,1)S(1)} async-done(((bf16[64,1,10,512]{3,2,1,0:T(8,128)(2,1)}), bf16[64,1,10,512]{3,2,1,0:T(8,128)(2,1)S(1)}, u32[]{:S(2)}, u32[]{:S(2)}) %all-to-all-start) | async-done | bytes 655392 | tf_op jit(solution)/shard_map/all_to_all | solution.py:161
  191.7 2.6 convolution_convert_fusion.1
  194.2 2.6 convolution_convert_fusion
  198.6 1.9 collective-permute-start.8
  200.6 4.0 %collective-permute-done.8 = bf16[1,4,80,2816]{3,2,1,0:T(8,128)(2,1)} collective-permute-done((bf16[1,4,80,2816]{3,2,1,0:T(8,128)(2,1)}, bf16[1,4,80,2816]{3,2,1,0:T(8,128)(2,1)}, u32[]{:S(2)}, u32[]{:S(2)}) %collective-permute-start.8) | collective-permute-done | bytes 1802272 | tf_op jit(solution)/shard_map/ppermute | solution.py:58
  204.6 2.1 convert_add_fusion
  206.7 1.8 copy-done.1
  208.6 3.5 collective-permute-start.10
  212.1 2.4 collective-permute-start.11
  214.5 3.6 collective-permute-start.9
  218.2 7.0 %collective-permute-done.10 = bf16[1,80,2816]{2,1,0:T(8,128)(2,1)S(1)} collective-permute-done((bf16[1,80,2816]{2,1,0:T(8,128)(2,1)S(1)}, bf16[1,80,2816]{2,1,0:T(8,128)(2,1)S(1)}, u32[]{:S(2)}, u32[]{:S(2)}) %collective-permute-start.10) | collective-permute-done | bytes 450592 | tf_op jit(solution)/shard_map/ppermute | solution.py:64
  225.2 6.1 %collective-permute-done.11 = bf16[1,80,2816]{2,1,0:T(8,128)(2,1)S(1)} collective-permute-done((bf16[1,80,2816]{2,1,0:T(8,128)(2,1)S(1)}, bf16[1,80,2816]{2,1,0:T(8,128)(2,1)S(1)}, u32[]{:S(2)}, u32[]{:S(2)}) %collective-permute-start.11) | collective-permute-done | bytes 450592 | tf_op jit(solution)/shard_map/ppermute | solution.py:64
  231.3 2.7 collective-permute-done.9
  236.4 3.1 slice_reduce_fusion.1
  241.0 2.1 collective-permute-start.12
  243.1 3.8 %collective-permute-start.13 = (bf16[1,80,1408]{2,1,0:T(8,128)(2,1)S(1)}, bf16[1,80,1408]{2,1,0:T(8,128)(2,1)S(1)}, u32[]{:S(2)}, u32[]{:S(2)}) collective-permute-start(bf16[1,80,1408]{2,1,0:T(8,128)(2,1)S(1)} %multiply_convert_fusion.1), channel_id=1, source_target_pairs={{0,4},{1,5},{2,6},{3,7},{4,0},{5,1},{6,2},{7,3},{8,12},{9,13},{10,... | collective-permute-start | bytes 675848 | tf_op jit(solution)/shard_map/ppermute | solution.py:71
  246.9 4.1 %collective-permute-start.14 = (bf16[1,80,1408]{2,1,0:T(8,128)(2,1)S(1)}, bf16[1,80,1408]{2,1,0:T(8,128)(2,1)S(1)}, u32[]{:S(2)}, u32[]{:S(2)}) collective-permute-start(bf16[1,80,1408]{2,1,0:T(8,128)(2,1)S(1)} %multiply_convert_fusion.1), channel_id=1, source_target_pairs={{0,6},{1,7},{2,0},{3,1},{4,2},{5,3},{6,4},{7,5},{8,14},{9,15},{10,... | collective-permute-start | bytes 675848 | tf_op jit(solution)/shard_map/ppermute | solution.py:71
  251.2 5.2 %collective-permute-done.12 = bf16[1,80,1408]{2,1,0:T(8,128)(2,1)S(1)} collective-permute-done((bf16[1,80,1408]{2,1,0:T(8,128)(2,1)S(1)}, bf16[1,80,1408]{2,1,0:T(8,128)(2,1)S(1)}, u32[]{:S(2)}, u32[]{:S(2)}) %collective-permute-start.12) | collective-permute-done | bytes 225312 | tf_op jit(solution)/shard_map/ppermute | solution.py:71
  256.4 2.5 collective-permute-done.14
  260.8 2.1 collective-permute-start.15
  263.3 2.0 collective-permute-done.15
  267.7 2.0 gather_fusion.1
  269.6 2.8 copy.157
  272.5 4.9 %gather.18 = bf16[1,640,2,704]{3,2,1,0:T(2,128)(2,1)S(1)} reshape(bf16[4,2,80,1408]{3,2,1,0:T(8,128)(2,1)} %copy.157) | data formatting | bytes 3604480 | tf_op jit(solution)/shard_map/jit(_take)/gather | solution.py:76
  277.4 3.2 broadcast_select_fusion
  280.6 3.7 fusion.90
  284.3 4.8 %copy.158 = bf16[1,640,1,704]{1,3,2,0:T(8,128)(2,1)} copy(bf16[1,640,1,704]{3,2,1,0:T(2,128)(2,1)} %get-tuple-element.47) | data formatting | bytes 1802240 | tf_op jit(solution)/shard_map/slice | solution.py:174
  289.1 3.1 fusion.11
  292.2 3.6 copy.159
  295.8 2.5 fusion.10
  299.5 7.9 %all-to-all-start.1 = ((bf16[1,64,10,512]{3,2,0,1:T(8,128)(2,1)}), bf16[1,64,10,512]{3,2,0,1:T(8,128)(2,1)S(1)}, u32[]{:S(2)}, u32[]{:S(2)}) async-start(bf16[1,64,10,512]{3,2,0,1:T(8,128)(2,1)} %bitcast.35), calls=%async_computation.1 | async-start | bytes 2097152 | tf_op jit(solution)/shard_map/all_to_all | solution.py:183
  307.9 53.7 %all-to-all-done.1 = bf16[1,64,10,512]{3,2,0,1:T(8,128)(2,1)S(1)} async-done(((bf16[1,64,10,512]{3,2,0,1:T(8,128)(2,1)}), bf16[1,64,10,512]{3,2,0,1:T(8,128)(2,1)S(1)}, u32[]{:S(2)}, u32[]{:S(2)}) %all-to-all-start.1) | async-done | bytes 655392 | tf_op jit(solution)/shard_map/all_to_all | solution.py:183
  361.8 1.6 gather_fusion.2
  (138 shorter events, 30.1 us)
Async XLA Ops:
  0.0 73.2 %copy-start = (bf16[256,512]{1,0:T(8,128)(2,1)S(1)}, bf16[256,512]{1,0:T(8,128)(2,1)}, u32[]{:S(2)}) copy-start(bf16[256,512]{1,0:T(8,128)(2,1)} %param.12) | copy-start | bytes 786436
  5.0 55.2 %copy-start.9 = (bf16[1,704,512]{2,1,0:T(8,128)(2,1)S(1)}, bf16[1,704,512]{2,1,0:T(8,128)(2,1)}, u32[]{:S(2)}) copy-start(bf16[1,704,512]{2,1,0:T(8,128)(2,1)} %param.21) | copy-start | bytes 2162692
  5.1 15.5 %collective-permute-start = (bf16[4,130,128]{2,1,0:T(8,128)(2,1)S(1)}, bf16[4,130,128]{2,1,0:T(8,128)(2,1)S(1)}, u32[]{:S(2)}, u32[]{:S(2)}) collective-permute-start(bf16[4,130,128]{2,1,0:T(8,128)(2,1)S(1)} %pad_maximum_fusion), channel_id=1, source_target_pairs={{0,8},{8,16},{16,24},{24,32},{32,40},{40,48},{48,56},{56,64},{64,7... | collective-permute-start | bytes 399368 | tf_op jit(solution)/shard_map/ppermute | solution.py:33
  20.9 52.2 %copy-start.4 = (bf16[256,512]{1,0:T(8,128)(2,1)S(1)}, bf16[256,512]{1,0:T(8,128)(2,1)}, u32[]{:S(2)}) copy-start(bf16[256,512]{1,0:T(8,128)(2,1)} %param.14) | copy-start | bytes 786436
  21.1 12.2 %collective-permute-start.1 = (bf16[4,130,128]{2,1,0:T(8,128)(2,1)S(1)}, bf16[4,130,128]{2,1,0:T(8,128)(2,1)S(1)}, u32[]{:S(2)}, u32[]{:S(2)}) collective-permute-start(bf16[4,130,128]{2,1,0:T(8,128)(2,1)S(1)} %pad_maximum_fusion.1), channel_id=1, source_target_pairs={{0,16},{8,24},{16,32},{24,40},{32,48},{40,56},{48,64},{56,72},{64,... | collective-permute-start | bytes 399368 | tf_op jit(solution)/shard_map/ppermute | solution.py:33
  33.8 17.3 %collective-permute-start.2 = (bf16[4,130,128]{2,1,0:T(8,128)(2,1)S(1)}, bf16[4,130,128]{2,1,0:T(8,128)(2,1)S(1)}, u32[]{:S(2)}, u32[]{:S(2)}) collective-permute-start(bf16[4,130,128]{2,1,0:T(8,128)(2,1)S(1)} %pad_maximum_fusion.2), channel_id=1, source_target_pairs={{0,32},{8,40},{16,48},{24,56},{32,64},{40,72},{48,80},{56,88},{64,... | collective-permute-start | bytes 399368 | tf_op jit(solution)/shard_map/ppermute | solution.py:33
  51.6 19.8 %collective-permute-start.3 = (bf16[4,130,128]{2,1,0:T(8,128)(2,1)S(1)}, bf16[4,130,128]{2,1,0:T(8,128)(2,1)S(1)}, u32[]{:S(2)}, u32[]{:S(2)}) collective-permute-start(bf16[4,130,128]{2,1,0:T(8,128)(2,1)S(1)} %pad_maximum_fusion.3), channel_id=1, source_target_pairs={{0,64},{8,72},{16,80},{24,88},{32,96},{40,104},{48,112},{56,120},{... | collective-permute-start | bytes 399368 | tf_op jit(solution)/shard_map/ppermute | solution.py:33
  53.5 58.6 %collective-permute-start.6 = (bf16[1,512,1408]{2,1,0:T(8,128)(2,1)}, bf16[1,512,1408]{2,1,0:T(8,128)(2,1)}, u32[]{:S(2)}, u32[]{:S(2)}) collective-permute-start(bf16[1,512,1408]{2,1,0:T(8,128)(2,1)} %param.20), channel_id=1, source_target_pairs={{0,8},{8,0},{16,24},{24,16},{32,40},{40,32},{48,56},{56,48},{64,72... | collective-permute-start | bytes 4325384 | tf_op jit(solution)/shard_map/ppermute | solution.py:95
  60.3 51.9 %collective-permute-start.7 = (bf16[1,704,512]{2,1,0:T(8,128)(2,1)S(1)}, bf16[1,704,512]{2,1,0:T(8,128)(2,1)}, u32[]{:S(2)}, u32[]{:S(2)}) collective-permute-start(bf16[1,704,512]{2,1,0:T(8,128)(2,1)S(1)} %copy-done.9), channel_id=1, source_target_pairs={{0,8},{8,0},{16,24},{24,16},{32,40},{40,32},{48,56},{56,48},{64,72... | collective-permute-start | bytes 2162696 | tf_op jit(solution)/shard_map/ppermute | solution.py:95
  71.8 2.0 copy-start.6
  71.9 7.3 %collective-permute-start.4 = (bf16[4,130,128]{2,1,0:T(8,128)(2,1)S(1)}, bf16[4,130,128]{2,1,0:T(8,128)(2,1)S(1)}, u32[]{:S(2)}, u32[]{:S(2)}) collective-permute-start(bf16[4,130,128]{2,1,0:T(8,128)(2,1)S(1)} %pad_maximum_fusion.4), channel_id=1, source_target_pairs={{0,128},{8,136},{16,144},{24,152},{32,160},{40,168},{48,176},{56,1... | collective-permute-start | bytes 399368 | tf_op jit(solution)/shard_map/ppermute | solution.py:33
  79.6 8.5 %collective-permute-start.5 = (bf16[4,130,128]{2,1,0:T(8,128)(2,1)S(1)}, bf16[4,130,128]{2,1,0:T(8,128)(2,1)S(1)}, u32[]{:S(2)}, u32[]{:S(2)}) collective-permute-start(bf16[4,130,128]{2,1,0:T(8,128)(2,1)S(1)} %pad_maximum_fusion.5), channel_id=1, source_target_pairs={{0,256},{8,264},{16,272},{24,280},{32,288},{40,296},{48,304},{56,3... | collective-permute-start | bytes 399368 | tf_op jit(solution)/shard_map/ppermute | solution.py:33
  112.1 1.0 copy-start.5
  112.1 1.0 copy-start.7
  112.6 13.8 %copy-start.10 = (f32[512]{0:T(512)S(1)}, f32[512]{0:T(512)}, u32[]{:S(2)}) copy-start(f32[512]{0:T(512)} %param.17) | copy-start | bytes 6148
  128.0 63.4 %all-to-all-start = ((bf16[64,1,10,512]{3,2,1,0:T(8,128)(2,1)}), bf16[64,1,10,512]{3,2,1,0:T(8,128)(2,1)S(1)}, u32[]{:S(2)}, u32[]{:S(2)}) async-start(bf16[64,1,10,512]{3,2,1,0:T(8,128)(2,1)} %bitcast.8), calls=%async_computation | async-start | bytes 2097152 | tf_op jit(solution)/shard_map/all_to_all | solution.py:161
  196.8 1.8 copy-start.2
  198.6 6.0 %collective-permute-start.8 = (bf16[1,4,80,2816]{3,2,1,0:T(8,128)(2,1)}, bf16[1,4,80,2816]{3,2,1,0:T(8,128)(2,1)}, u32[]{:S(2)}, u32[]{:S(2)}) collective-permute-start(bf16[1,4,80,2816]{3,2,1,0:T(8,128)(2,1)} %fusion.1), channel_id=1, source_target_pairs={{0,1},{1,0},{2,3},{3,2},{4,5},{5,4},{6,7},{7,6},{8,9},{9,8},{10,11... | collective-permute-start | bytes 5406728 | tf_op jit(solution)/shard_map/ppermute | solution.py:58
  206.7 1.8 copy-start.1
  208.6 16.6 %collective-permute-start.10 = (bf16[1,80,2816]{2,1,0:T(8,128)(2,1)S(1)}, bf16[1,80,2816]{2,1,0:T(8,128)(2,1)S(1)}, u32[]{:S(2)}, u32[]{:S(2)}) collective-permute-start(bf16[1,80,2816]{2,1,0:T(8,128)(2,1)S(1)} %get-tuple-element.45), channel_id=1, source_target_pairs={{0,4},{1,5},{2,6},{3,7},{4,0},{5,1},{6,2},{7,3},{8,12},{9,13},{10,... | collective-permute-start | bytes 1351688 | tf_op jit(solution)/shard_map/ppermute | solution.py:64
  212.1 19.2 %collective-permute-start.11 = (bf16[1,80,2816]{2,1,0:T(8,128)(2,1)S(1)}, bf16[1,80,2816]{2,1,0:T(8,128)(2,1)S(1)}, u32[]{:S(2)}, u32[]{:S(2)}) collective-permute-start(bf16[1,80,2816]{2,1,0:T(8,128)(2,1)S(1)} %get-tuple-element.44), channel_id=1, source_target_pairs={{0,6},{1,7},{2,0},{3,1},{4,2},{5,3},{6,4},{7,5},{8,14},{9,15},{10,... | collective-permute-start | bytes 1351688 | tf_op jit(solution)/shard_map/ppermute | solution.py:64
  214.5 19.5 %collective-permute-start.9 = (bf16[1,80,2816]{2,1,0:T(8,128)(2,1)S(1)}, bf16[1,80,2816]{2,1,0:T(8,128)(2,1)S(1)}, u32[]{:S(2)}, u32[]{:S(2)}) collective-permute-start(bf16[1,80,2816]{2,1,0:T(8,128)(2,1)S(1)} %get-tuple-element.43), channel_id=1, source_target_pairs={{0,2},{1,3},{2,4},{3,5},{4,6},{5,7},{6,0},{7,1},{8,10},{9,11},{10,... | collective-permute-start | bytes 1351688 | tf_op jit(solution)/shard_map/ppermute | solution.py:64
  241.0 15.4 %collective-permute-start.12 = (bf16[1,80,1408]{2,1,0:T(8,128)(2,1)S(1)}, bf16[1,80,1408]{2,1,0:T(8,128)(2,1)S(1)}, u32[]{:S(2)}, u32[]{:S(2)}) collective-permute-start(bf16[1,80,1408]{2,1,0:T(8,128)(2,1)S(1)} %multiply_convert_fusion.1), channel_id=1, source_target_pairs={{0,2},{1,3},{2,4},{3,5},{4,6},{5,7},{6,0},{7,1},{8,10},{9,11},{10,... | collective-permute-start | bytes 675848 | tf_op jit(solution)/shard_map/ppermute | solution.py:71
  243.1 13.3 %collective-permute-start.13 = (bf16[1,80,1408]{2,1,0:T(8,128)(2,1)S(1)}, bf16[1,80,1408]{2,1,0:T(8,128)(2,1)S(1)}, u32[]{:S(2)}, u32[]{:S(2)}) collective-permute-start(bf16[1,80,1408]{2,1,0:T(8,128)(2,1)S(1)} %multiply_convert_fusion.1), channel_id=1, source_target_pairs={{0,4},{1,5},{2,6},{3,7},{4,0},{5,1},{6,2},{7,3},{8,12},{9,13},{10,... | collective-permute-start | bytes 675848 | tf_op jit(solution)/shard_map/ppermute | solution.py:71
  246.9 12.0 %collective-permute-start.14 = (bf16[1,80,1408]{2,1,0:T(8,128)(2,1)S(1)}, bf16[1,80,1408]{2,1,0:T(8,128)(2,1)S(1)}, u32[]{:S(2)}, u32[]{:S(2)}) collective-permute-start(bf16[1,80,1408]{2,1,0:T(8,128)(2,1)S(1)} %multiply_convert_fusion.1), channel_id=1, source_target_pairs={{0,6},{1,7},{2,0},{3,1},{4,2},{5,3},{6,4},{7,5},{8,14},{9,15},{10,... | collective-permute-start | bytes 675848 | tf_op jit(solution)/shard_map/ppermute | solution.py:71
  260.8 4.5 %collective-permute-start.15 = (bf16[1,4,80,1408]{3,2,1,0:T(8,128)(2,1)}, bf16[1,4,80,1408]{3,2,1,0:T(8,128)(2,1)S(1)}, u32[]{:S(2)}, u32[]{:S(2)}) collective-permute-start(bf16[1,4,80,1408]{3,2,1,0:T(8,128)(2,1)} %bitcast_select_fusion), channel_id=1, source_target_pairs={{0,1},{1,0},{2,3},{3,2},{4,5},{5,4},{6,7},{7,6},{8,9},{9,8},{10,11... | collective-permute-start | bytes 2703368 | tf_op jit(solution)/shard_map/ppermute | solution.py:74
  265.4 0.9 copy-start.3
  298.3 9.4 %copy-start.8 = (f32[256,2]{0,1:T(2,128)S(1)}, f32[256,2]{0,1:T(2,128)}, u32[]{:S(2)}) copy-start(f32[256,2]{0,1:T(2,128)} %param.19) | copy-start | bytes 6148
  299.5 62.1 %all-to-all-start.1 = ((bf16[1,64,10,512]{3,2,0,1:T(8,128)(2,1)}), bf16[1,64,10,512]{3,2,0,1:T(8,128)(2,1)S(1)}, u32[]{:S(2)}, u32[]{:S(2)}) async-start(bf16[1,64,10,512]{3,2,0,1:T(8,128)(2,1)} %bitcast.35), calls=%async_computation.1 | async-start | bytes 2097152 | tf_op jit(solution)/shard_map/all_to_all | solution.py:183

commit v12 on v11

--- a/solution.py
+++ b/solution.py
@@ -70,10 +70,12 @@
         pairs = [(j, (j + 2 * step) % count) for j in range(count)]
         gathered.append(lax.ppermute(mine, axis, pairs))
     stacked = jnp.stack(gathered, axis=1)
-    ordered = jnp.take(stacked, (chip - jnp.arange(chips)) % chips, axis=1)
+    reverse = stacked[:, ::-1]
+    doubled = jnp.concatenate([reverse, reverse], axis=1)
+    ordered = lax.dynamic_slice_in_dim(doubled, (chips - 1 - chip) % chips, chips, 1)
     other = lax.ppermute(ordered, axis, sibling)
-    both = jnp.stack([ordered, other], axis=2)
-    full = jnp.take(both, jnp.arange(2) ^ core, axis=2)
+    three = jnp.stack([ordered, other, ordered], axis=2)
+    full = lax.dynamic_slice_in_dim(three, core, 2, 2)
     return full.reshape(blocks_here, rows, width // 2)
 
 
@@ -170,15 +172,10 @@
     partial_sums = jnp.concatenate([own_sums, other_sums], axis=2)
     activated = head_reduce_activate(partial_sums, "head", block_units)
     activated = activated.reshape(blocks_here, sources * half, 2, block_units)
-    first_part = jnp.einsum(
-        "erh,ehd->erd", activated[:, :, 0], expert_out, preferred_element_type=jnp.float32
+    weight_out = jnp.stack([expert_out, other_out], axis=1)
+    summed = jnp.einsum(
+        "erkh,ekhd->erd", activated, weight_out, preferred_element_type=jnp.float32
     ).astype(jnp.bfloat16)
-    second_part = jnp.einsum(
-        "erh,ehd->erd", activated[:, :, 1], other_out, preferred_element_type=jnp.float32
-    ).astype(jnp.bfloat16)
-    summed = (first_part.astype(jnp.float32) + second_part.astype(jnp.float32)).astype(
-        jnp.bfloat16
-    )
     summed = summed.reshape(blocks_here, sources, half, local_width)
     returned = lax.all_to_all(summed, "seq", split_axis=1, concat_axis=0, tiled=True)
     merged = returned.reshape(expert_count, capacity, local_width).astype(jnp.float32)

time: 367 us -> 349 us (0.951)
  local copies, waits for them, and re-layouts: 41.1 us -> 25.7 us
    slice x5 -> x2, local copies, waits for them, and re-layouts: 12.2 us -> 0.18 us  [the longest x2 7.22 us: per_device(): activated[:, :, 1]]
    gather x4 -> x0, local copies, waits for them, and re-layouts: 10.4 us -> none  [the longest x3 9.77 us: head_reduce_activate(): full = jnp.take(both, jnp.arange(2) ^ core, axis=2)]
    another operation x3 -> x5, local copies, waits for them, and re-layouts: 0.33 us -> 10.2 us
    select_n x5 -> x0, other arithmetic: 4.43 us -> none  [the longest x2 3.16 us: head_reduce_activate(): full = jnp.take(both, jnp.arange(2) ^ core, axis=2)]
  transfers between devices with their start and end apart: 18 -> 18, of which waited for: 16 -> 17; matrix products, arithmetic and copies ran while one was open for 1% -> 1% of each run, Pallas kernels for 0% -> 0%
where the time goes in v12:
time: 349 us; the launch traced here: 348 us
  waiting for transfers between devices  218 us (62%)
  starting transfers between devices  65.5 us (19%)
  local copies, waits for them, and re-layouts  25.7 us (7%)
  other arithmetic  14.2 us (4%)
  blocking collectives  12.4 us (4%)
  matrix products  11.1 us (3%)
    ppermute x6, waiting for transfers between devices, exclusive_scan(): got = lax.ppermute(pack_window(window_decay, window_state), axis, pairs)  57.5 us
    all_to_all x1, waiting for transfers between devices, per_device(): lax.all_to_all(summed, 'seq', split_axis=1, concat_axis=0, tiled=True)  53.7 us
    all_to_all x1, waiting for transfers between devices, per_device(): lax.all_to_all(send_buffer, 'seq', split_axis=0, concat_axis=1, tiled=True)  50.7 us
    ppermute x2, waiting for transfers between devices, per_device(): other_in, other_out = lax.ppermute((expert_in, expert_out), 'seq', partner)  23.8 us
    ppermute x3, waiting for transfers between devices, head_reduce_activate(): total = total + lax.ppermute(outgoing, axis, pairs).astype(jnp.float32)  18.3 us
    all_to_all x1, starting transfers between devices, per_device(): lax.all_to_all(send_buffer, 'seq', split_axis=0, concat_axis=1, tiled=True)  13.4 us
    psum x1, blocking collectives, per_device(): total_squares = lax.psum(local_squares, 'head')  12.4 us
    ppermute x6, starting transfers between devices, exclusive_scan(): got = lax.ppermute(pack_window(window_decay, window_state), axis, pairs)  12.3 us
  transfers between devices with their start and end apart: 18, of which 17 were waited for; matrix products, arithmetic and copies ran while one was open for 1% of the time, Pallas kernels for 0%

profile of v12, /device:TPU:6, one launch (start us, length us, event | category | flops | bytes accessed | tf_op | source)
XLA Modules:
  0.0 347.7 jit_solution(7025317830855655592)
XLA Ops:
  1.8 1.2 reduce-window.6
  5.1 4.0 %collective-permute-start = (bf16[4,130,128]{2,1,0:T(8,128)(2,1)S(1)}, bf16[4,130,128]{2,1,0:T(8,128)(2,1)S(1)}, u32[]{:S(2)}, u32[]{:S(2)}) collective-permute-start(bf16[4,130,128]{2,1,0:T(8,128)(2,1)S(1)} %pad_maximum_fusion.1), channel_id=1, source_target_pairs={{0,8},{8,16},{16,24},{24,32},{32,40},{40,48},{48,56},{56,64},{64,7... | collective-permute-start | bytes 399368 | tf_op jit(solution)/shard_map/ppermute | solution.py:33
  9.1 11.5 %collective-permute-done = bf16[4,130,128]{2,1,0:T(8,128)(2,1)S(1)} collective-permute-done((bf16[4,130,128]{2,1,0:T(8,128)(2,1)S(1)}, bf16[4,130,128]{2,1,0:T(8,128)(2,1)S(1)}, u32[]{:S(2)}, u32[]{:S(2)}) %collective-permute-start) | collective-permute-done | bytes 133152 | tf_op jit(solution)/shard_map/ppermute | solution.py:33
  21.0 1.9 collective-permute-start.1
  23.1 10.1 %collective-permute-done.1 = bf16[4,130,128]{2,1,0:T(8,128)(2,1)S(1)} collective-permute-done((bf16[4,130,128]{2,1,0:T(8,128)(2,1)S(1)}, bf16[4,130,128]{2,1,0:T(8,128)(2,1)S(1)}, u32[]{:S(2)}, u32[]{:S(2)}) %collective-permute-start.1) | collective-permute-done | bytes 133152 | tf_op jit(solution)/shard_map/ppermute | solution.py:33
  33.8 1.9 collective-permute-start.2
  35.8 15.3 %collective-permute-done.2 = bf16[4,130,128]{2,1,0:T(8,128)(2,1)S(1)} collective-permute-done((bf16[4,130,128]{2,1,0:T(8,128)(2,1)S(1)}, bf16[4,130,128]{2,1,0:T(8,128)(2,1)S(1)}, u32[]{:S(2)}, u32[]{:S(2)}) %collective-permute-start.2) | collective-permute-done | bytes 133152 | tf_op jit(solution)/shard_map/ppermute | solution.py:33
  51.6 1.9 collective-permute-start.3
  53.5 6.7 %collective-permute-start.6 = (bf16[1,512,1408]{2,1,0:T(8,128)(2,1)}, bf16[1,512,1408]{2,1,0:T(8,128)(2,1)}, u32[]{:S(2)}, u32[]{:S(2)}) collective-permute-start(bf16[1,512,1408]{2,1,0:T(8,128)(2,1)} %param.20), channel_id=1, source_target_pairs={{0,8},{8,0},{16,24},{24,16},{32,40},{40,32},{48,56},{56,48},{64,72... | collective-permute-start | bytes 4325384 | tf_op jit(solution)/shard_map/ppermute | solution.py:97
  60.3 1.9 collective-permute-start.7
  62.2 9.2 %collective-permute-done.3 = bf16[4,130,128]{2,1,0:T(8,128)(2,1)S(1)} collective-permute-done((bf16[4,130,128]{2,1,0:T(8,128)(2,1)S(1)}, bf16[4,130,128]{2,1,0:T(8,128)(2,1)S(1)}, u32[]{:S(2)}, u32[]{:S(2)}) %collective-permute-start.3) | collective-permute-done | bytes 133152 | tf_op jit(solution)/shard_map/ppermute | solution.py:33
  71.9 1.3 collective-permute-start.4
  74.7 4.5 %collective-permute-done.4 = bf16[4,130,128]{2,1,0:T(8,128)(2,1)S(1)} collective-permute-done((bf16[4,130,128]{2,1,0:T(8,128)(2,1)S(1)}, bf16[4,130,128]{2,1,0:T(8,128)(2,1)S(1)}, u32[]{:S(2)}, u32[]{:S(2)}) %collective-permute-start.4) | collective-permute-done | bytes 133152 | tf_op jit(solution)/shard_map/ppermute | solution.py:33
  79.6 1.3 collective-permute-start.5
  81.1 6.9 %collective-permute-done.5 = bf16[4,130,128]{2,1,0:T(8,128)(2,1)S(1)} collective-permute-done((bf16[4,130,128]{2,1,0:T(8,128)(2,1)S(1)}, bf16[4,130,128]{2,1,0:T(8,128)(2,1)S(1)}, u32[]{:S(2)}, u32[]{:S(2)}) %collective-permute-start.5) | collective-permute-done | bytes 133152 | tf_op jit(solution)/shard_map/ppermute | solution.py:33
  88.3 23.8 %collective-permute-done.7 = bf16[1,704,512]{2,1,0:T(8,128)(2,1)} collective-permute-done((bf16[1,704,512]{2,1,0:T(8,128)(2,1)S(1)}, bf16[1,704,512]{2,1,0:T(8,128)(2,1)}, u32[]{:S(2)}, u32[]{:S(2)}) %collective-permute-start.7) | collective-permute-done | bytes 720928 | tf_op jit(solution)/shard_map/ppermute | solution.py:97
  113.3 12.4 %psum.7 = f32[256]{0:T(256)S(1)} all-reduce(f32[256]{0:T(256)S(1)} %get-tuple-element.23), channel_id=1, replica_groups=mesh['seq'=64,'head'=8] {'head'}, use_global_device_ids=true, to_apply=%region_6.7 | all-reduce | flops 256 | bytes 2048 | tf_op jit(solution)/shard_map/psum | solution.py:138
  127.3 13.4 %all-to-all-start = ((bf16[64,1,10,512]{3,2,1,0:T(8,128)(2,1)}), bf16[64,1,10,512]{3,2,1,0:T(8,128)(2,1)S(1)}, u32[]{:S(2)}, u32[]{:S(2)}) async-start(bf16[64,1,10,512]{3,2,1,0:T(8,128)(2,1)} %bitcast.8), calls=%async_computation | async-start | bytes 2097152 | tf_op jit(solution)/shard_map/all_to_all | solution.py:163
  140.7 50.7 %all-to-all-done = bf16[64,1,10,512]{3,2,1,0:T(8,128)(2,1)S(1)} async-done(((bf16[64,1,10,512]{3,2,1,0:T(8,128)(2,1)}), bf16[64,1,10,512]{3,2,1,0:T(8,128)(2,1)S(1)}, u32[]{:S(2)}, u32[]{:S(2)}) %all-to-all-start) | async-done | bytes 655392 | tf_op jit(solution)/shard_map/all_to_all | solution.py:163
  191.6 2.5 convolution_convert_fusion.1
  194.2 2.5 convolution_convert_fusion
  196.8 1.5 fusion.3
  198.6 1.9 collective-permute-start.8
  200.6 4.0 %collective-permute-done.8 = bf16[1,4,80,2816]{3,2,1,0:T(8,128)(2,1)} collective-permute-done((bf16[1,4,80,2816]{3,2,1,0:T(8,128)(2,1)}, bf16[1,4,80,2816]{3,2,1,0:T(8,128)(2,1)}, u32[]{:S(2)}, u32[]{:S(2)}) %collective-permute-start.8) | collective-permute-done | bytes 1802272 | tf_op jit(solution)/shard_map/ppermute | solution.py:58
  204.5 2.1 convert_add_fusion
  206.6 1.8 copy-done.1
  208.5 1.9 collective-permute-start.11
  210.4 3.7 %collective-permute-start.10 = (bf16[1,80,2816]{2,1,0:T(8,128)(2,1)S(1)}, bf16[1,80,2816]{2,1,0:T(8,128)(2,1)S(1)}, u32[]{:S(2)}, u32[]{:S(2)}) collective-permute-start(bf16[1,80,2816]{2,1,0:T(8,128)(2,1)S(1)} %get-tuple-element.43), channel_id=1, source_target_pairs={{0,4},{1,5},{2,6},{3,7},{4,0},{5,1},{6,2},{7,3},{8,12},{9,13},{10,... | collective-permute-start | bytes 1351688 | tf_op jit(solution)/shard_map/ppermute | solution.py:64
  214.1 3.4 collective-permute-start.9
  217.6 6.0 %collective-permute-done.11 = bf16[1,80,2816]{2,1,0:T(8,128)(2,1)S(1)} collective-permute-done((bf16[1,80,2816]{2,1,0:T(8,128)(2,1)S(1)}, bf16[1,80,2816]{2,1,0:T(8,128)(2,1)S(1)}, u32[]{:S(2)}, u32[]{:S(2)}) %collective-permute-start.11) | collective-permute-done | bytes 450592 | tf_op jit(solution)/shard_map/ppermute | solution.py:64
  223.6 3.5 collective-permute-done.10
  227.1 8.8 %collective-permute-done.9 = bf16[1,80,2816]{2,1,0:T(8,128)(2,1)S(1)} collective-permute-done((bf16[1,80,2816]{2,1,0:T(8,128)(2,1)S(1)}, bf16[1,80,2816]{2,1,0:T(8,128)(2,1)S(1)}, u32[]{:S(2)}, u32[]{:S(2)}) %collective-permute-start.9) | collective-permute-done | bytes 450592 | tf_op jit(solution)/shard_map/ppermute | solution.py:64
  235.9 1.4 fusion.27
  240.4 2.5 collective-permute-start.14
  242.9 3.6 %collective-permute-start.13 = (bf16[1,80,1408]{2,1,0:T(8,128)(2,1)S(1)}, bf16[1,80,1408]{2,1,0:T(8,128)(2,1)S(1)}, u32[]{:S(2)}, u32[]{:S(2)}) collective-permute-start(bf16[1,80,1408]{2,1,0:T(8,128)(2,1)S(1)} %multiply_convert_fusion.1), channel_id=1, source_target_pairs={{0,4},{1,5},{2,6},{3,7},{4,0},{5,1},{6,2},{7,3},{8,12},{9,13},{10,... | collective-permute-start | bytes 675848 | tf_op jit(solution)/shard_map/ppermute | solution.py:71
  246.5 2.7 collective-permute-start.12
  250.7 3.3 collective-permute-done.13
  253.9 4.0 %collective-permute-done.12 = bf16[1,80,1408]{2,1,0:T(8,128)(2,1)S(1)} collective-permute-done((bf16[1,80,1408]{2,1,0:T(8,128)(2,1)S(1)}, bf16[1,80,1408]{2,1,0:T(8,128)(2,1)S(1)}, u32[]{:S(2)}, u32[]{:S(2)}) %collective-permute-start.12) | collective-permute-done | bytes 225312 | tf_op jit(solution)/shard_map/ppermute | solution.py:71
  258.6 1.9 collective-permute-start.15
  260.9 2.0 collective-permute-done.15
  262.9 2.2 fusion.1
  265.2 6.6 %copy.146 = bf16[1,4,2,80,1408]{3,2,1,4,0:T(2,128)(2,1)S(1)} copy(bf16[1,4,2,80,1408]{4,3,1,2,0:T(8,128)(2,1)} %fusion.1) | data formatting | bytes 3604480 | tf_op jit(solution)/shard_map/reshape.29
  271.8 3.3 reshape.549
  275.1 3.1 fusion.14
  279.4 9.6 %all-to-all-start.1 = ((bf16[1,64,10,512]{3,2,0,1:T(8,128)(2,1)}), bf16[1,64,10,512]{3,2,0,1:T(8,128)(2,1)S(1)}, u32[]{:S(2)}, u32[]{:S(2)}) async-start(bf16[1,64,10,512]{3,2,0,1:T(8,128)(2,1)} %bitcast.28), calls=%async_computation.1 | async-start | bytes 2097152 | tf_op jit(solution)/shard_map/all_to_all | solution.py:180
  289.4 53.7 %all-to-all-done.1 = bf16[1,64,10,512]{3,2,0,1:T(8,128)(2,1)S(1)} async-done(((bf16[1,64,10,512]{3,2,0,1:T(8,128)(2,1)}), bf16[1,64,10,512]{3,2,0,1:T(8,128)(2,1)S(1)}, u32[]{:S(2)}, u32[]{:S(2)}) %all-to-all-start.1) | async-done | bytes 655392 | tf_op jit(solution)/shard_map/all_to_all | solution.py:180
  343.3 1.6 gather_fusion
  345.5 1.3 multiply_reduce_fusion
  (124 shorter events, 20.4 us)
Async XLA Ops:
  0.0 73.2 %copy-start = (bf16[256,512]{1,0:T(8,128)(2,1)S(1)}, bf16[256,512]{1,0:T(8,128)(2,1)}, u32[]{:S(2)}) copy-start(bf16[256,512]{1,0:T(8,128)(2,1)} %param.12) | copy-start | bytes 786436
  5.0 55.3 %copy-start.8 = (bf16[1,704,512]{2,1,0:T(8,128)(2,1)S(1)}, bf16[1,704,512]{2,1,0:T(8,128)(2,1)}, u32[]{:S(2)}) copy-start(bf16[1,704,512]{2,1,0:T(8,128)(2,1)} %param.21) | copy-start | bytes 2162692
  5.1 15.5 %collective-permute-start = (bf16[4,130,128]{2,1,0:T(8,128)(2,1)S(1)}, bf16[4,130,128]{2,1,0:T(8,128)(2,1)S(1)}, u32[]{:S(2)}, u32[]{:S(2)}) collective-permute-start(bf16[4,130,128]{2,1,0:T(8,128)(2,1)S(1)} %pad_maximum_fusion.1), channel_id=1, source_target_pairs={{0,8},{8,16},{16,24},{24,32},{32,40},{40,48},{48,56},{56,64},{64,7... | collective-permute-start | bytes 399368 | tf_op jit(solution)/shard_map/ppermute | solution.py:33
  20.9 52.3 %copy-start.3 = (bf16[256,512]{1,0:T(8,128)(2,1)S(1)}, bf16[256,512]{1,0:T(8,128)(2,1)}, u32[]{:S(2)}) copy-start(bf16[256,512]{1,0:T(8,128)(2,1)} %param.14) | copy-start | bytes 786436
  21.0 12.2 %collective-permute-start.1 = (bf16[4,130,128]{2,1,0:T(8,128)(2,1)S(1)}, bf16[4,130,128]{2,1,0:T(8,128)(2,1)S(1)}, u32[]{:S(2)}, u32[]{:S(2)}) collective-permute-start(bf16[4,130,128]{2,1,0:T(8,128)(2,1)S(1)} %pad_maximum_fusion.2), channel_id=1, source_target_pairs={{0,16},{8,24},{16,32},{24,40},{32,48},{40,56},{48,64},{56,72},{64,... | collective-permute-start | bytes 399368 | tf_op jit(solution)/shard_map/ppermute | solution.py:33
  33.8 17.3 %collective-permute-start.2 = (bf16[4,130,128]{2,1,0:T(8,128)(2,1)S(1)}, bf16[4,130,128]{2,1,0:T(8,128)(2,1)S(1)}, u32[]{:S(2)}, u32[]{:S(2)}) collective-permute-start(bf16[4,130,128]{2,1,0:T(8,128)(2,1)S(1)} %pad_maximum_fusion.3), channel_id=1, source_target_pairs={{0,32},{8,40},{16,48},{24,56},{32,64},{40,72},{48,80},{56,88},{64,... | collective-permute-start | bytes 399368 | tf_op jit(solution)/shard_map/ppermute | solution.py:33
  51.6 19.8 %collective-permute-start.3 = (bf16[4,130,128]{2,1,0:T(8,128)(2,1)S(1)}, bf16[4,130,128]{2,1,0:T(8,128)(2,1)S(1)}, u32[]{:S(2)}, u32[]{:S(2)}) collective-permute-start(bf16[4,130,128]{2,1,0:T(8,128)(2,1)S(1)} %pad_maximum_fusion.4), channel_id=1, source_target_pairs={{0,64},{8,72},{16,80},{24,88},{32,96},{40,104},{48,112},{56,120},{... | collective-permute-start | bytes 399368 | tf_op jit(solution)/shard_map/ppermute | solution.py:33
  53.5 58.6 %collective-permute-start.6 = (bf16[1,512,1408]{2,1,0:T(8,128)(2,1)}, bf16[1,512,1408]{2,1,0:T(8,128)(2,1)}, u32[]{:S(2)}, u32[]{:S(2)}) collective-permute-start(bf16[1,512,1408]{2,1,0:T(8,128)(2,1)} %param.20), channel_id=1, source_target_pairs={{0,8},{8,0},{16,24},{24,16},{32,40},{40,32},{48,56},{56,48},{64,72... | collective-permute-start | bytes 4325384 | tf_op jit(solution)/shard_map/ppermute | solution.py:97
  60.3 51.9 %collective-permute-start.7 = (bf16[1,704,512]{2,1,0:T(8,128)(2,1)S(1)}, bf16[1,704,512]{2,1,0:T(8,128)(2,1)}, u32[]{:S(2)}, u32[]{:S(2)}) collective-permute-start(bf16[1,704,512]{2,1,0:T(8,128)(2,1)S(1)} %copy-done.8), channel_id=1, source_target_pairs={{0,8},{8,0},{16,24},{24,16},{32,40},{40,32},{48,56},{56,48},{64,72... | collective-permute-start | bytes 2162696 | tf_op jit(solution)/shard_map/ppermute | solution.py:97
  71.8 2.0 copy-start.5
  71.9 7.2 %collective-permute-start.4 = (bf16[4,130,128]{2,1,0:T(8,128)(2,1)S(1)}, bf16[4,130,128]{2,1,0:T(8,128)(2,1)S(1)}, u32[]{:S(2)}, u32[]{:S(2)}) collective-permute-start(bf16[4,130,128]{2,1,0:T(8,128)(2,1)S(1)} %pad_maximum_fusion.5), channel_id=1, source_target_pairs={{0,128},{8,136},{16,144},{24,152},{32,160},{40,168},{48,176},{56,1... | collective-permute-start | bytes 399368 | tf_op jit(solution)/shard_map/ppermute | solution.py:33
  79.6 8.5 %collective-permute-start.5 = (bf16[4,130,128]{2,1,0:T(8,128)(2,1)S(1)}, bf16[4,130,128]{2,1,0:T(8,128)(2,1)S(1)}, u32[]{:S(2)}, u32[]{:S(2)}) collective-permute-start(bf16[4,130,128]{2,1,0:T(8,128)(2,1)S(1)} %pad_maximum_fusion.6), channel_id=1, source_target_pairs={{0,256},{8,264},{16,272},{24,280},{32,288},{40,296},{48,304},{56,3... | collective-permute-start | bytes 399368 | tf_op jit(solution)/shard_map/ppermute | solution.py:33
  112.1 1.0 copy-start.4
  112.1 1.0 copy-start.6
  112.6 13.1 %copy-start.9 = (f32[512]{0:T(512)S(1)}, f32[512]{0:T(512)}, u32[]{:S(2)}) copy-start(f32[512]{0:T(512)} %param.17) | copy-start | bytes 6148
  127.3 64.1 %all-to-all-start = ((bf16[64,1,10,512]{3,2,1,0:T(8,128)(2,1)}), bf16[64,1,10,512]{3,2,1,0:T(8,128)(2,1)S(1)}, u32[]{:S(2)}, u32[]{:S(2)}) async-start(bf16[64,1,10,512]{3,2,1,0:T(8,128)(2,1)} %bitcast.8), calls=%async_computation | async-start | bytes 2097152 | tf_op jit(solution)/shard_map/all_to_all | solution.py:163
  196.8 1.8 copy-start.2
  198.6 6.0 %collective-permute-start.8 = (bf16[1,4,80,2816]{3,2,1,0:T(8,128)(2,1)}, bf16[1,4,80,2816]{3,2,1,0:T(8,128)(2,1)}, u32[]{:S(2)}, u32[]{:S(2)}) collective-permute-start(bf16[1,4,80,2816]{3,2,1,0:T(8,128)(2,1)} %fusion.3), channel_id=1, source_target_pairs={{0,1},{1,0},{2,3},{3,2},{4,5},{5,4},{6,7},{7,6},{8,9},{9,8},{10,11... | collective-permute-start | bytes 5406728 | tf_op jit(solution)/shard_map/ppermute | solution.py:58
  206.6 1.8 copy-start.1
  208.5 15.1 %collective-permute-start.11 = (bf16[1,80,2816]{2,1,0:T(8,128)(2,1)S(1)}, bf16[1,80,2816]{2,1,0:T(8,128)(2,1)S(1)}, u32[]{:S(2)}, u32[]{:S(2)}) collective-permute-start(bf16[1,80,2816]{2,1,0:T(8,128)(2,1)S(1)} %get-tuple-element.42), channel_id=1, source_target_pairs={{0,6},{1,7},{2,0},{3,1},{4,2},{5,3},{6,4},{7,5},{8,14},{9,15},{10,... | collective-permute-start | bytes 1351688 | tf_op jit(solution)/shard_map/ppermute | solution.py:64
  210.4 16.6 %collective-permute-start.10 = (bf16[1,80,2816]{2,1,0:T(8,128)(2,1)S(1)}, bf16[1,80,2816]{2,1,0:T(8,128)(2,1)S(1)}, u32[]{:S(2)}, u32[]{:S(2)}) collective-permute-start(bf16[1,80,2816]{2,1,0:T(8,128)(2,1)S(1)} %get-tuple-element.43), channel_id=1, source_target_pairs={{0,4},{1,5},{2,6},{3,7},{4,0},{5,1},{6,2},{7,3},{8,12},{9,13},{10,... | collective-permute-start | bytes 1351688 | tf_op jit(solution)/shard_map/ppermute | solution.py:64
  214.1 21.8 %collective-permute-start.9 = (bf16[1,80,2816]{2,1,0:T(8,128)(2,1)S(1)}, bf16[1,80,2816]{2,1,0:T(8,128)(2,1)S(1)}, u32[]{:S(2)}, u32[]{:S(2)}) collective-permute-start(bf16[1,80,2816]{2,1,0:T(8,128)(2,1)S(1)} %get-tuple-element.41), channel_id=1, source_target_pairs={{0,2},{1,3},{2,4},{3,5},{4,6},{5,7},{6,0},{7,1},{8,10},{9,11},{10,... | collective-permute-start | bytes 1351688 | tf_op jit(solution)/shard_map/ppermute | solution.py:64
  240.4 10.3 %collective-permute-start.14 = (bf16[1,80,1408]{2,1,0:T(8,128)(2,1)S(1)}, bf16[1,80,1408]{2,1,0:T(8,128)(2,1)S(1)}, u32[]{:S(2)}, u32[]{:S(2)}) collective-permute-start(bf16[1,80,1408]{2,1,0:T(8,128)(2,1)S(1)} %multiply_convert_fusion.1), channel_id=1, source_target_pairs={{0,6},{1,7},{2,0},{3,1},{4,2},{5,3},{6,4},{7,5},{8,14},{9,15},{10,... | collective-permute-start | bytes 675848 | tf_op jit(solution)/shard_map/ppermute | solution.py:71
  242.9 11.0 %collective-permute-start.13 = (bf16[1,80,1408]{2,1,0:T(8,128)(2,1)S(1)}, bf16[1,80,1408]{2,1,0:T(8,128)(2,1)S(1)}, u32[]{:S(2)}, u32[]{:S(2)}) collective-permute-start(bf16[1,80,1408]{2,1,0:T(8,128)(2,1)S(1)} %multiply_convert_fusion.1), channel_id=1, source_target_pairs={{0,4},{1,5},{2,6},{3,7},{4,0},{5,1},{6,2},{7,3},{8,12},{9,13},{10,... | collective-permute-start | bytes 675848 | tf_op jit(solution)/shard_map/ppermute | solution.py:71
  246.5 11.5 %collective-permute-start.12 = (bf16[1,80,1408]{2,1,0:T(8,128)(2,1)S(1)}, bf16[1,80,1408]{2,1,0:T(8,128)(2,1)S(1)}, u32[]{:S(2)}, u32[]{:S(2)}) collective-permute-start(bf16[1,80,1408]{2,1,0:T(8,128)(2,1)S(1)} %multiply_convert_fusion.1), channel_id=1, source_target_pairs={{0,2},{1,3},{2,4},{3,5},{4,6},{5,7},{6,0},{7,1},{8,10},{9,11},{10,... | collective-permute-start | bytes 675848 | tf_op jit(solution)/shard_map/ppermute | solution.py:71
  258.6 4.3 %collective-permute-start.15 = (bf16[1,4,80,1408]{3,2,1,0:T(8,128)(2,1)S(1)}, bf16[1,4,80,1408]{3,2,1,0:T(8,128)(2,1)S(1)}, u32[]{:S(2)}, u32[]{:S(2)}) collective-permute-start(bf16[1,4,80,1408]{3,2,1,0:T(8,128)(2,1)S(1)} %fusion.25), channel_id=1, source_target_pairs={{0,1},{1,0},{2,3},{3,2},{4,5},{5,4},{6,7},{7,6},{8,9},{9,8},{10,11... | collective-permute-start | bytes 2703368 | tf_op jit(solution)/shard_map/ppermute | solution.py:76
  278.2 11.1 %copy-start.7 = (f32[256,2]{0,1:T(2,128)S(1)}, f32[256,2]{0,1:T(2,128)}, u32[]{:S(2)}) copy-start(f32[256,2]{0,1:T(2,128)} %param.19) | copy-start | bytes 6148
  279.4 63.7 %all-to-all-start.1 = ((bf16[1,64,10,512]{3,2,0,1:T(8,128)(2,1)}), bf16[1,64,10,512]{3,2,0,1:T(8,128)(2,1)S(1)}, u32[]{:S(2)}, u32[]{:S(2)}) async-start(bf16[1,64,10,512]{3,2,0,1:T(8,128)(2,1)} %bitcast.28), calls=%async_computation.1 | async-start | bytes 2097152 | tf_op jit(solution)/shard_map/all_to_all | solution.py:180

commit v13 on v12

--- a/solution.py
+++ b/solution.py
@@ -94,7 +94,8 @@
 ):
     parity = lax.axis_index("seq") % 2
     partner = [(j, j ^ 1) for j in range(lax.axis_size("seq"))]
-    other_in, other_out = lax.ppermute((expert_in, expert_out), "seq", partner)
+    other_in = lax.ppermute(expert_in, "seq", partner)
+    other_out = lax.ppermute(expert_out, "seq", partner)
     length = tokens.shape[0]
     local_width = tokens.shape[1]
     heads_here = log_decay.shape[0]
@@ -121,7 +122,7 @@
     )
     block_decay = jnp.exp(cumulative[:, -1])
     entering = exclusive_scan(block_decay, block_state, "seq")
-    entering, other_in, other_out = lax.optimization_barrier((entering, other_in, other_out))
+    entering, other_in = lax.optimization_barrier((entering, other_in))
     from_before = jnp.einsum(
         "thd,hde->the",
         query_heads.astype(jnp.float32),
@@ -162,6 +163,7 @@
     send_buffer = send_rows.reshape(expert_count * 2, 1, half, local_width)
     arrived = lax.all_to_all(send_buffer, "seq", split_axis=0, concat_axis=1, tiled=True)
     blocks_here, sources = arrived.shape[0], arrived.shape[1]
+    arrived, other_out = lax.optimization_barrier((arrived, other_out))
     flat_rows = arrived.reshape(blocks_here, sources * half, local_width)
     own_sums = jnp.einsum(
         "erd,edh->erh", flat_rows, expert_in, preferred_element_type=jnp.float32

time: 349 us -> 350 us (level)
  waiting for transfers between devices: 218 us -> 213 us
  starting transfers between devices: 65.5 us -> 70.2 us
    all_to_all x1, waiting for transfers between devices: 50.7 us -> 0.01 us  [per_device(): lax.all_to_all(send_buffer, 'seq', split_axis=0, concat_axis=1, tiled=True)]
    ppermute x2, waiting for transfers between devices: 23.8 us -> 64.8 us  [the longest x1 56.5 us: per_device(): other_out = lax.ppermute(expert_out, 'seq', partner)]
    all_to_all x1, starting transfers between devices: 9.57 us -> 14.2 us  [per_device(): lax.all_to_all(summed, 'seq', split_axis=1, concat_axis=0, tiled=True)]
  transfers between devices with their start and end apart: 18 -> 18, of which waited for: 17 -> 16; matrix products, arithmetic and copies ran while one was open for 1% -> 1% of each run, Pallas kernels for 0% -> 0%
where the time goes in v13:
time: 350 us; the launch traced here: 348 us
  waiting for transfers between devices  213 us (61%)
  starting transfers between devices  70.2 us (20%)
  local copies, waits for them, and re-layouts  26.6 us (8%)
  other arithmetic  14.2 us (4%)
  blocking collectives  12.4 us (4%)
  matrix products  11.1 us (3%)
    ppermute x6, waiting for transfers between devices, exclusive_scan(): got = lax.ppermute(pack_window(window_decay, window_state), axis, pairs)  59.5 us
    ppermute x1, waiting for transfers between devices, per_device(): other_out = lax.ppermute(expert_out, 'seq', partner)  56.5 us
    all_to_all x1, waiting for transfers between devices, per_device(): lax.all_to_all(summed, 'seq', split_axis=1, concat_axis=0, tiled=True)  53.7 us
    ppermute x3, waiting for transfers between devices, head_reduce_activate(): total = total + lax.ppermute(outgoing, axis, pairs).astype(jnp.float32)  20.3 us
    all_to_all x1, starting transfers between devices, per_device(): lax.all_to_all(summed, 'seq', split_axis=1, concat_axis=0, tiled=True)  14.2 us
    all_to_all x1, starting transfers between devices, per_device(): lax.all_to_all(send_buffer, 'seq', split_axis=0, concat_axis=1, tiled=True)  13.4 us
    psum x1, blocking collectives, per_device(): total_squares = lax.psum(local_squares, 'head')  12.4 us
    ppermute x6, starting transfers between devices, exclusive_scan(): got = lax.ppermute(pack_window(window_decay, window_state), axis, pairs)  12.2 us
  transfers between devices with their start and end apart: 18, of which 16 were waited for; matrix products, arithmetic and copies ran while one was open for 1% of the time, Pallas kernels for 0%

profile of v13, /device:TPU:6, one launch (start us, length us, event | category | flops | bytes accessed | tf_op | source)
XLA Modules:
  0.0 348.4 jit_solution(1284481808524036494)
XLA Ops:
  1.8 1.2 reduce-window.6
  5.1 3.8 %collective-permute-start = (bf16[4,130,128]{2,1,0:T(8,128)(2,1)S(1)}, bf16[4,130,128]{2,1,0:T(8,128)(2,1)S(1)}, u32[]{:S(2)}, u32[]{:S(2)}) collective-permute-start(bf16[4,130,128]{2,1,0:T(8,128)(2,1)S(1)} %pad_maximum_fusion.1), channel_id=1, source_target_pairs={{0,8},{8,16},{16,24},{24,32},{32,40},{40,48},{48,56},{56,64},{64,7... | collective-permute-start | bytes 399368 | tf_op jit(solution)/shard_map/ppermute | solution.py:33
  9.0 11.5 %collective-permute-done = bf16[4,130,128]{2,1,0:T(8,128)(2,1)S(1)} collective-permute-done((bf16[4,130,128]{2,1,0:T(8,128)(2,1)S(1)}, bf16[4,130,128]{2,1,0:T(8,128)(2,1)S(1)}, u32[]{:S(2)}, u32[]{:S(2)}) %collective-permute-start) | collective-permute-done | bytes 133152 | tf_op jit(solution)/shard_map/ppermute | solution.py:33
  20.9 1.9 collective-permute-start.1
  22.9 10.1 %collective-permute-done.1 = bf16[4,130,128]{2,1,0:T(8,128)(2,1)S(1)} collective-permute-done((bf16[4,130,128]{2,1,0:T(8,128)(2,1)S(1)}, bf16[4,130,128]{2,1,0:T(8,128)(2,1)S(1)}, u32[]{:S(2)}, u32[]{:S(2)}) %collective-permute-start.1) | collective-permute-done | bytes 133152 | tf_op jit(solution)/shard_map/ppermute | solution.py:33
  33.7 1.9 collective-permute-start.2
  35.6 15.3 %collective-permute-done.2 = bf16[4,130,128]{2,1,0:T(8,128)(2,1)S(1)} collective-permute-done((bf16[4,130,128]{2,1,0:T(8,128)(2,1)S(1)}, bf16[4,130,128]{2,1,0:T(8,128)(2,1)S(1)}, u32[]{:S(2)}, u32[]{:S(2)}) %collective-permute-start.2) | collective-permute-done | bytes 133152 | tf_op jit(solution)/shard_map/ppermute | solution.py:33
  51.5 1.9 collective-permute-start.3
  53.4 6.7 %collective-permute-start.6 = (bf16[1,512,1408]{2,1,0:T(8,128)(2,1)}, bf16[1,512,1408]{2,1,0:T(8,128)(2,1)}, u32[]{:S(2)}, u32[]{:S(2)}) collective-permute-start(bf16[1,512,1408]{2,1,0:T(8,128)(2,1)} %param.20), channel_id=1, source_target_pairs={{0,8},{8,0},{16,24},{24,16},{32,40},{40,32},{48,56},{56,48},{64,72... | collective-permute-start | bytes 4325384 | tf_op jit(solution)/shard_map/ppermute | solution.py:97
  60.2 11.1 %collective-permute-done.3 = bf16[4,130,128]{2,1,0:T(8,128)(2,1)S(1)} collective-permute-done((bf16[4,130,128]{2,1,0:T(8,128)(2,1)S(1)}, bf16[4,130,128]{2,1,0:T(8,128)(2,1)S(1)}, u32[]{:S(2)}, u32[]{:S(2)}) %collective-permute-start.3) | collective-permute-done | bytes 133152 | tf_op jit(solution)/shard_map/ppermute | solution.py:33
  71.8 1.3 collective-permute-start.4
  74.5 4.5 %collective-permute-done.4 = bf16[4,130,128]{2,1,0:T(8,128)(2,1)S(1)} collective-permute-done((bf16[4,130,128]{2,1,0:T(8,128)(2,1)S(1)}, bf16[4,130,128]{2,1,0:T(8,128)(2,1)S(1)}, u32[]{:S(2)}, u32[]{:S(2)}) %collective-permute-start.4) | collective-permute-done | bytes 133152 | tf_op jit(solution)/shard_map/ppermute | solution.py:33
  79.5 1.3 collective-permute-start.5
  81.0 6.9 %collective-permute-done.5 = bf16[4,130,128]{2,1,0:T(8,128)(2,1)S(1)} collective-permute-done((bf16[4,130,128]{2,1,0:T(8,128)(2,1)S(1)}, bf16[4,130,128]{2,1,0:T(8,128)(2,1)S(1)}, u32[]{:S(2)}, u32[]{:S(2)}) %collective-permute-start.5) | collective-permute-done | bytes 133152 | tf_op jit(solution)/shard_map/ppermute | solution.py:33
  88.2 8.4 %collective-permute-done.6 = bf16[1,512,1408]{2,1,0:T(8,128)(2,1)} collective-permute-done((bf16[1,512,1408]{2,1,0:T(8,128)(2,1)}, bf16[1,512,1408]{2,1,0:T(8,128)(2,1)}, u32[]{:S(2)}, u32[]{:S(2)}) %collective-permute-start.6) | collective-permute-done | bytes 1441824 | tf_op jit(solution)/shard_map/ppermute | solution.py:97
  97.7 12.4 %psum.7 = f32[256]{0:T(256)S(1)} all-reduce(f32[256]{0:T(256)S(1)} %get-tuple-element.25), channel_id=1, replica_groups=mesh['seq'=64,'head'=8] {'head'}, use_global_device_ids=true, to_apply=%region_6.7 | all-reduce | flops 256 | bytes 2048 | tf_op jit(solution)/shard_map/psum | solution.py:139
  111.7 13.4 %all-to-all-start = ((bf16[64,1,10,512]{3,2,1,0:T(8,128)(2,1)}), bf16[64,1,10,512]{3,2,1,0:T(8,128)(2,1)S(1)}, u32[]{:S(2)}, u32[]{:S(2)}) async-start(bf16[64,1,10,512]{3,2,1,0:T(8,128)(2,1)} %bitcast.8), calls=%async_computation | async-start | bytes 2097152 | tf_op jit(solution)/shard_map/all_to_all | solution.py:164
  125.1 3.4 collective-permute-start.7
  128.5 56.5 %collective-permute-done.7 = bf16[1,704,512]{2,1,0:T(8,128)(2,1)S(1)} collective-permute-done((bf16[1,704,512]{2,1,0:T(8,128)(2,1)S(1)}, bf16[1,704,512]{2,1,0:T(8,128)(2,1)S(1)}, u32[]{:S(2)}, u32[]{:S(2)}) %collective-permute-start.7) | collective-permute-done | bytes 720928 | tf_op jit(solution)/shard_map/ppermute | solution.py:98
  186.1 2.5 convolution_convert_fusion.1
  188.7 2.5 convolution_convert_fusion
  191.2 1.5 fusion.3
  193.0 1.9 collective-permute-start.8
  195.0 4.0 %collective-permute-done.8 = bf16[1,4,80,2816]{3,2,1,0:T(8,128)(2,1)} collective-permute-done((bf16[1,4,80,2816]{3,2,1,0:T(8,128)(2,1)}, bf16[1,4,80,2816]{3,2,1,0:T(8,128)(2,1)}, u32[]{:S(2)}, u32[]{:S(2)}) %collective-permute-start.8) | collective-permute-done | bytes 1802272 | tf_op jit(solution)/shard_map/ppermute | solution.py:58
  199.0 2.1 convert_add_fusion
  201.1 1.8 copy-done.1
  203.0 3.8 %collective-permute-start.11 = (bf16[1,80,2816]{2,1,0:T(8,128)(2,1)S(1)}, bf16[1,80,2816]{2,1,0:T(8,128)(2,1)S(1)}, u32[]{:S(2)}, u32[]{:S(2)}) collective-permute-start(bf16[1,80,2816]{2,1,0:T(8,128)(2,1)S(1)} %get-tuple-element.44), channel_id=1, source_target_pairs={{0,6},{1,7},{2,0},{3,1},{4,2},{5,3},{6,4},{7,5},{8,14},{9,15},{10,... | collective-permute-start | bytes 1351688 | tf_op jit(solution)/shard_map/ppermute | solution.py:64
  206.8 1.9 collective-permute-start.10
  208.8 2.9 collective-permute-start.9
  211.7 14.7 %collective-permute-done.11 = bf16[1,80,2816]{2,1,0:T(8,128)(2,1)S(1)} collective-permute-done((bf16[1,80,2816]{2,1,0:T(8,128)(2,1)S(1)}, bf16[1,80,2816]{2,1,0:T(8,128)(2,1)S(1)}, u32[]{:S(2)}, u32[]{:S(2)}) %collective-permute-start.11) | collective-permute-done | bytes 450592 | tf_op jit(solution)/shard_map/ppermute | solution.py:64
  226.4 5.6 %collective-permute-done.9 = bf16[1,80,2816]{2,1,0:T(8,128)(2,1)S(1)} collective-permute-done((bf16[1,80,2816]{2,1,0:T(8,128)(2,1)S(1)}, bf16[1,80,2816]{2,1,0:T(8,128)(2,1)S(1)}, u32[]{:S(2)}, u32[]{:S(2)}) %collective-permute-start.9) | collective-permute-done | bytes 450592 | tf_op jit(solution)/shard_map/ppermute | solution.py:64
  232.0 1.4 fusion.27
  236.5 2.5 collective-permute-start.14
  239.0 2.2 collective-permute-start.13
  241.2 3.0 collective-permute-start.12
  245.2 1.6 collective-permute-done.14
  246.8 3.3 collective-permute-done.13
  250.1 4.0 %collective-permute-done.12 = bf16[1,80,1408]{2,1,0:T(8,128)(2,1)S(1)} collective-permute-done((bf16[1,80,1408]{2,1,0:T(8,128)(2,1)S(1)}, bf16[1,80,1408]{2,1,0:T(8,128)(2,1)S(1)}, u32[]{:S(2)}, u32[]{:S(2)}) %collective-permute-start.12) | collective-permute-done | bytes 225312 | tf_op jit(solution)/shard_map/ppermute | solution.py:71
  254.7 1.9 collective-permute-start.15
  257.0 2.0 collective-permute-done.15
  259.0 2.2 fusion.1
  261.3 6.6 %copy.146 = bf16[1,4,2,80,1408]{3,2,1,4,0:T(2,128)(2,1)S(1)} copy(bf16[1,4,2,80,1408]{4,3,1,2,0:T(8,128)(2,1)} %fusion.1) | data formatting | bytes 3604480 | tf_op jit(solution)/shard_map/reshape.13
  267.9 3.3 reshape.548
  271.2 3.1 fusion.14
  275.5 14.2 %all-to-all-start.1 = ((bf16[1,64,10,512]{3,2,0,1:T(8,128)(2,1)}), bf16[1,64,10,512]{3,2,0,1:T(8,128)(2,1)S(1)}, u32[]{:S(2)}, u32[]{:S(2)}) async-start(bf16[1,64,10,512]{3,2,0,1:T(8,128)(2,1)} %bitcast.29), calls=%async_computation.1 | async-start | bytes 2097152 | tf_op jit(solution)/shard_map/all_to_all | solution.py:182
  290.2 53.7 %all-to-all-done.1 = bf16[1,64,10,512]{3,2,0,1:T(8,128)(2,1)S(1)} async-done(((bf16[1,64,10,512]{3,2,0,1:T(8,128)(2,1)}), bf16[1,64,10,512]{3,2,0,1:T(8,128)(2,1)S(1)}, u32[]{:S(2)}, u32[]{:S(2)}) %all-to-all-start.1) | async-done | bytes 655392 | tf_op jit(solution)/shard_map/all_to_all | solution.py:182
  344.0 1.6 gather_fusion
  346.3 1.3 multiply_reduce_fusion
  (126 shorter events, 20.7 us)
Async XLA Ops:
  0.0 73.1 %copy-start = (bf16[256,512]{1,0:T(8,128)(2,1)S(1)}, bf16[256,512]{1,0:T(8,128)(2,1)}, u32[]{:S(2)}) copy-start(bf16[256,512]{1,0:T(8,128)(2,1)} %param.12) | copy-start | bytes 786436
  5.1 15.3 %collective-permute-start = (bf16[4,130,128]{2,1,0:T(8,128)(2,1)S(1)}, bf16[4,130,128]{2,1,0:T(8,128)(2,1)S(1)}, u32[]{:S(2)}, u32[]{:S(2)}) collective-permute-start(bf16[4,130,128]{2,1,0:T(8,128)(2,1)S(1)} %pad_maximum_fusion.1), channel_id=1, source_target_pairs={{0,8},{8,16},{16,24},{24,32},{32,40},{40,48},{48,56},{56,64},{64,7... | collective-permute-start | bytes 399368 | tf_op jit(solution)/shard_map/ppermute | solution.py:33
  20.8 52.3 %copy-start.3 = (bf16[256,512]{1,0:T(8,128)(2,1)S(1)}, bf16[256,512]{1,0:T(8,128)(2,1)}, u32[]{:S(2)}) copy-start(bf16[256,512]{1,0:T(8,128)(2,1)} %param.14) | copy-start | bytes 786436
  20.9 12.2 %collective-permute-start.1 = (bf16[4,130,128]{2,1,0:T(8,128)(2,1)S(1)}, bf16[4,130,128]{2,1,0:T(8,128)(2,1)S(1)}, u32[]{:S(2)}, u32[]{:S(2)}) collective-permute-start(bf16[4,130,128]{2,1,0:T(8,128)(2,1)S(1)} %pad_maximum_fusion.2), channel_id=1, source_target_pairs={{0,16},{8,24},{16,32},{24,40},{32,48},{40,56},{48,64},{56,72},{64,... | collective-permute-start | bytes 399368 | tf_op jit(solution)/shard_map/ppermute | solution.py:33
  33.7 17.3 %collective-permute-start.2 = (bf16[4,130,128]{2,1,0:T(8,128)(2,1)S(1)}, bf16[4,130,128]{2,1,0:T(8,128)(2,1)S(1)}, u32[]{:S(2)}, u32[]{:S(2)}) collective-permute-start(bf16[4,130,128]{2,1,0:T(8,128)(2,1)S(1)} %pad_maximum_fusion.3), channel_id=1, source_target_pairs={{0,32},{8,40},{16,48},{24,56},{32,64},{40,72},{48,80},{56,88},{64,... | collective-permute-start | bytes 399368 | tf_op jit(solution)/shard_map/ppermute | solution.py:33
  51.5 19.8 %collective-permute-start.3 = (bf16[4,130,128]{2,1,0:T(8,128)(2,1)S(1)}, bf16[4,130,128]{2,1,0:T(8,128)(2,1)S(1)}, u32[]{:S(2)}, u32[]{:S(2)}) collective-permute-start(bf16[4,130,128]{2,1,0:T(8,128)(2,1)S(1)} %pad_maximum_fusion.4), channel_id=1, source_target_pairs={{0,64},{8,72},{16,80},{24,88},{32,96},{40,104},{48,112},{56,120},{... | collective-permute-start | bytes 399368 | tf_op jit(solution)/shard_map/ppermute | solution.py:33
  53.4 43.2 %collective-permute-start.6 = (bf16[1,512,1408]{2,1,0:T(8,128)(2,1)}, bf16[1,512,1408]{2,1,0:T(8,128)(2,1)}, u32[]{:S(2)}, u32[]{:S(2)}) collective-permute-start(bf16[1,512,1408]{2,1,0:T(8,128)(2,1)} %param.20), channel_id=1, source_target_pairs={{0,8},{8,0},{16,24},{24,16},{32,40},{40,32},{48,56},{56,48},{64,72... | collective-permute-start | bytes 4325384 | tf_op jit(solution)/shard_map/ppermute | solution.py:97
  71.7 2.0 copy-start.5
  71.8 7.2 %collective-permute-start.4 = (bf16[4,130,128]{2,1,0:T(8,128)(2,1)S(1)}, bf16[4,130,128]{2,1,0:T(8,128)(2,1)S(1)}, u32[]{:S(2)}, u32[]{:S(2)}) collective-permute-start(bf16[4,130,128]{2,1,0:T(8,128)(2,1)S(1)} %pad_maximum_fusion.5), channel_id=1, source_target_pairs={{0,128},{8,136},{16,144},{24,152},{32,160},{40,168},{48,176},{56,1... | collective-permute-start | bytes 399368 | tf_op jit(solution)/shard_map/ppermute | solution.py:33
  79.5 8.5 %collective-permute-start.5 = (bf16[4,130,128]{2,1,0:T(8,128)(2,1)S(1)}, bf16[4,130,128]{2,1,0:T(8,128)(2,1)S(1)}, u32[]{:S(2)}, u32[]{:S(2)}) collective-permute-start(bf16[4,130,128]{2,1,0:T(8,128)(2,1)S(1)} %pad_maximum_fusion.6), channel_id=1, source_target_pairs={{0,256},{8,264},{16,272},{24,280},{32,288},{40,296},{48,304},{56,3... | collective-permute-start | bytes 399368 | tf_op jit(solution)/shard_map/ppermute | solution.py:33
  96.5 1.0 copy-start.4
  96.6 1.0 copy-start.6
  97.0 13.1 %copy-start.10 = (f32[512]{0:T(512)S(1)}, f32[512]{0:T(512)}, u32[]{:S(2)}) copy-start(f32[512]{0:T(512)} %param.17) | copy-start | bytes 6148
  110.6 14.6 %copy-start.8 = (bf16[1,704,512]{2,1,0:T(8,128)(2,1)S(1)}, bf16[1,704,512]{2,1,0:T(8,128)(2,1)}, u32[]{:S(2)}) copy-start(bf16[1,704,512]{2,1,0:T(8,128)(2,1)} %param.21) | copy-start | bytes 2162692
  111.7 73.3 %all-to-all-start = ((bf16[64,1,10,512]{3,2,1,0:T(8,128)(2,1)}), bf16[64,1,10,512]{3,2,1,0:T(8,128)(2,1)S(1)}, u32[]{:S(2)}, u32[]{:S(2)}) async-start(bf16[64,1,10,512]{3,2,1,0:T(8,128)(2,1)} %bitcast.8), calls=%async_computation | async-start | bytes 2097152 | tf_op jit(solution)/shard_map/all_to_all | solution.py:164
  125.1 59.9 %collective-permute-start.7 = (bf16[1,704,512]{2,1,0:T(8,128)(2,1)S(1)}, bf16[1,704,512]{2,1,0:T(8,128)(2,1)S(1)}, u32[]{:S(2)}, u32[]{:S(2)}) collective-permute-start(bf16[1,704,512]{2,1,0:T(8,128)(2,1)S(1)} %copy-done.8), channel_id=1, source_target_pairs={{0,8},{8,0},{16,24},{24,16},{32,40},{40,32},{48,56},{56,48},{64,72... | collective-permute-start | bytes 2162696 | tf_op jit(solution)/shard_map/ppermute | solution.py:98
  185.0 0.9 copy-start.9
  191.2 1.8 copy-start.2
  193.0 6.0 %collective-permute-start.8 = (bf16[1,4,80,2816]{3,2,1,0:T(8,128)(2,1)}, bf16[1,4,80,2816]{3,2,1,0:T(8,128)(2,1)}, u32[]{:S(2)}, u32[]{:S(2)}) collective-permute-start(bf16[1,4,80,2816]{3,2,1,0:T(8,128)(2,1)} %fusion.3), channel_id=1, source_target_pairs={{0,1},{1,0},{2,3},{3,2},{4,5},{5,4},{6,7},{7,6},{8,9},{9,8},{10,11... | collective-permute-start | bytes 5406728 | tf_op jit(solution)/shard_map/ppermute | solution.py:58
  201.1 1.8 copy-start.1
  203.0 23.4 %collective-permute-start.11 = (bf16[1,80,2816]{2,1,0:T(8,128)(2,1)S(1)}, bf16[1,80,2816]{2,1,0:T(8,128)(2,1)S(1)}, u32[]{:S(2)}, u32[]{:S(2)}) collective-permute-start(bf16[1,80,2816]{2,1,0:T(8,128)(2,1)S(1)} %get-tuple-element.44), channel_id=1, source_target_pairs={{0,6},{1,7},{2,0},{3,1},{4,2},{5,3},{6,4},{7,5},{8,14},{9,15},{10,... | collective-permute-start | bytes 1351688 | tf_op jit(solution)/shard_map/ppermute | solution.py:64
  206.8 19.6 %collective-permute-start.10 = (bf16[1,80,2816]{2,1,0:T(8,128)(2,1)S(1)}, bf16[1,80,2816]{2,1,0:T(8,128)(2,1)S(1)}, u32[]{:S(2)}, u32[]{:S(2)}) collective-permute-start(bf16[1,80,2816]{2,1,0:T(8,128)(2,1)S(1)} %get-tuple-element.45), channel_id=1, source_target_pairs={{0,4},{1,5},{2,6},{3,7},{4,0},{5,1},{6,2},{7,3},{8,12},{9,13},{10,... | collective-permute-start | bytes 1351688 | tf_op jit(solution)/shard_map/ppermute | solution.py:64
  208.8 23.3 %collective-permute-start.9 = (bf16[1,80,2816]{2,1,0:T(8,128)(2,1)S(1)}, bf16[1,80,2816]{2,1,0:T(8,128)(2,1)S(1)}, u32[]{:S(2)}, u32[]{:S(2)}) collective-permute-start(bf16[1,80,2816]{2,1,0:T(8,128)(2,1)S(1)} %get-tuple-element.43), channel_id=1, source_target_pairs={{0,2},{1,3},{2,4},{3,5},{4,6},{5,7},{6,0},{7,1},{8,10},{9,11},{10,... | collective-permute-start | bytes 1351688 | tf_op jit(solution)/shard_map/ppermute | solution.py:64
  236.5 10.3 %collective-permute-start.14 = (bf16[1,80,1408]{2,1,0:T(8,128)(2,1)S(1)}, bf16[1,80,1408]{2,1,0:T(8,128)(2,1)S(1)}, u32[]{:S(2)}, u32[]{:S(2)}) collective-permute-start(bf16[1,80,1408]{2,1,0:T(8,128)(2,1)S(1)} %multiply_convert_fusion.1), channel_id=1, source_target_pairs={{0,6},{1,7},{2,0},{3,1},{4,2},{5,3},{6,4},{7,5},{8,14},{9,15},{10,... | collective-permute-start | bytes 675848 | tf_op jit(solution)/shard_map/ppermute | solution.py:71
  239.0 11.0 %collective-permute-start.13 = (bf16[1,80,1408]{2,1,0:T(8,128)(2,1)S(1)}, bf16[1,80,1408]{2,1,0:T(8,128)(2,1)S(1)}, u32[]{:S(2)}, u32[]{:S(2)}) collective-permute-start(bf16[1,80,1408]{2,1,0:T(8,128)(2,1)S(1)} %multiply_convert_fusion.1), channel_id=1, source_target_pairs={{0,4},{1,5},{2,6},{3,7},{4,0},{5,1},{6,2},{7,3},{8,12},{9,13},{10,... | collective-permute-start | bytes 675848 | tf_op jit(solution)/shard_map/ppermute | solution.py:71
  241.2 12.9 %collective-permute-start.12 = (bf16[1,80,1408]{2,1,0:T(8,128)(2,1)S(1)}, bf16[1,80,1408]{2,1,0:T(8,128)(2,1)S(1)}, u32[]{:S(2)}, u32[]{:S(2)}) collective-permute-start(bf16[1,80,1408]{2,1,0:T(8,128)(2,1)S(1)} %multiply_convert_fusion.1), channel_id=1, source_target_pairs={{0,2},{1,3},{2,4},{3,5},{4,6},{5,7},{6,0},{7,1},{8,10},{9,11},{10,... | collective-permute-start | bytes 675848 | tf_op jit(solution)/shard_map/ppermute | solution.py:71
  254.7 4.3 %collective-permute-start.15 = (bf16[1,4,80,1408]{3,2,1,0:T(8,128)(2,1)S(1)}, bf16[1,4,80,1408]{3,2,1,0:T(8,128)(2,1)S(1)}, u32[]{:S(2)}, u32[]{:S(2)}) collective-permute-start(bf16[1,4,80,1408]{3,2,1,0:T(8,128)(2,1)S(1)} %fusion.25), channel_id=1, source_target_pairs={{0,1},{1,0},{2,3},{3,2},{4,5},{5,4},{6,7},{7,6},{8,9},{9,8},{10,11... | collective-permute-start | bytes 2703368 | tf_op jit(solution)/shard_map/ppermute | solution.py:76
  274.3 15.7 %copy-start.7 = (f32[256,2]{0,1:T(2,128)S(1)}, f32[256,2]{0,1:T(2,128)}, u32[]{:S(2)}) copy-start(f32[256,2]{0,1:T(2,128)} %param.19) | copy-start | bytes 6148
  275.5 68.3 %all-to-all-start.1 = ((bf16[1,64,10,512]{3,2,0,1:T(8,128)(2,1)}), bf16[1,64,10,512]{3,2,0,1:T(8,128)(2,1)S(1)}, u32[]{:S(2)}, u32[]{:S(2)}) async-start(bf16[1,64,10,512]{3,2,0,1:T(8,128)(2,1)} %bitcast.29), calls=%async_computation.1 | async-start | bytes 2097152 | tf_op jit(solution)/shard_map/all_to_all | solution.py:182

commit v14 on v13

--- a/solution.py
+++ b/solution.py
@@ -163,7 +163,6 @@
     send_buffer = send_rows.reshape(expert_count * 2, 1, half, local_width)
     arrived = lax.all_to_all(send_buffer, "seq", split_axis=0, concat_axis=1, tiled=True)
     blocks_here, sources = arrived.shape[0], arrived.shape[1]
-    arrived, other_out = lax.optimization_barrier((arrived, other_out))
     flat_rows = arrived.reshape(blocks_here, sources * half, local_width)
     own_sums = jnp.einsum(
         "erd,edh->erh", flat_rows, expert_in, preferred_element_type=jnp.float32
@@ -173,6 +172,7 @@
     ).astype(jnp.bfloat16)
     partial_sums = jnp.concatenate([own_sums, other_sums], axis=2)
     activated = head_reduce_activate(partial_sums, "head", block_units)
+    activated, other_out = lax.optimization_barrier((activated, other_out))
     activated = activated.reshape(blocks_here, sources * half, 2, block_units)
     weight_out = jnp.stack([expert_out, other_out], axis=1)
     summed = jnp.einsum(

time: 350 us -> 342 us (0.977)
  local copies, waits for them, and re-layouts: 26.6 us -> 18.2 us
  waiting for transfers between devices: 213 us -> 217 us
    all_to_all x1, waiting for transfers between devices: 0.01 us -> 50.7 us  [per_device(): lax.all_to_all(send_buffer, 'seq', split_axis=0, concat_axis=1, tiled=True)]
    ppermute x1, waiting for transfers between devices: 56.5 us -> 15.5 us  [per_device(): other_out = lax.ppermute(expert_out, 'seq', partner)]
    another operation x5 -> x3, local copies, waits for them, and re-layouts: 10.2 us -> 0.33 us
    all_to_all x1, starting transfers between devices: 14.2 us -> 7.92 us  [per_device(): lax.all_to_all(summed, 'seq', split_axis=1, concat_axis=0, tiled=True)]
  transfers between devices with their start and end apart: 18 -> 18, of which waited for: 16 -> 17; matrix products, arithmetic and copies ran while one was open for 1% -> 2% of each run, Pallas kernels for 0% -> 0%
where the time goes in v14:
time: 342 us; the launch traced here: 341 us
  waiting for transfers between devices  217 us (63%)
  starting transfers between devices  67.1 us (20%)
  local copies, waits for them, and re-layouts  18.2 us (5%)
  other arithmetic  13.8 us (4%)
  blocking collectives  12.4 us (4%)
  matrix products  11.1 us (3%)
    ppermute x6, waiting for transfers between devices, exclusive_scan(): got = lax.ppermute(pack_window(window_decay, window_state), axis, pairs)  59.5 us
    all_to_all x1, waiting for transfers between devices, per_device(): lax.all_to_all(summed, 'seq', split_axis=1, concat_axis=0, tiled=True)  53.2 us
    all_to_all x1, waiting for transfers between devices, per_device(): lax.all_to_all(send_buffer, 'seq', split_axis=0, concat_axis=1, tiled=True)  50.7 us
    ppermute x3, waiting for transfers between devices, head_reduce_activate(): total = total + lax.ppermute(outgoing, axis, pairs).astype(jnp.float32)  18.4 us
    ppermute x1, waiting for transfers between devices, per_device(): other_out = lax.ppermute(expert_out, 'seq', partner)  15.5 us
    all_to_all x1, starting transfers between devices, per_device(): lax.all_to_all(send_buffer, 'seq', split_axis=0, concat_axis=1, tiled=True)  13.4 us
    psum x1, blocking collectives, per_device(): total_squares = lax.psum(local_squares, 'head')  12.4 us
    ppermute x6, starting transfers between devices, exclusive_scan(): got = lax.ppermute(pack_window(window_decay, window_state), axis, pairs)  12.2 us
  transfers between devices with their start and end apart: 18, of which 17 were waited for; matrix products, arithmetic and copies ran while one was open for 2% of the time, Pallas kernels for 0%

profile of v14, /device:TPU:6, one launch (start us, length us, event | category | flops | bytes accessed | tf_op | source)
XLA Modules:
  0.0 340.9 jit_solution(1136357605575012222)
XLA Ops:
  1.8 1.2 reduce-window.6
  5.1 3.8 %collective-permute-start = (bf16[4,130,128]{2,1,0:T(8,128)(2,1)S(1)}, bf16[4,130,128]{2,1,0:T(8,128)(2,1)S(1)}, u32[]{:S(2)}, u32[]{:S(2)}) collective-permute-start(bf16[4,130,128]{2,1,0:T(8,128)(2,1)S(1)} %pad_maximum_fusion.1), channel_id=1, source_target_pairs={{0,8},{8,16},{16,24},{24,32},{32,40},{40,48},{48,56},{56,64},{64,7... | collective-permute-start | bytes 399368 | tf_op jit(solution)/shard_map/ppermute | solution.py:33
  9.0 11.5 %collective-permute-done = bf16[4,130,128]{2,1,0:T(8,128)(2,1)S(1)} collective-permute-done((bf16[4,130,128]{2,1,0:T(8,128)(2,1)S(1)}, bf16[4,130,128]{2,1,0:T(8,128)(2,1)S(1)}, u32[]{:S(2)}, u32[]{:S(2)}) %collective-permute-start) | collective-permute-done | bytes 133152 | tf_op jit(solution)/shard_map/ppermute | solution.py:33
  20.9 1.9 collective-permute-start.1
  22.9 10.1 %collective-permute-done.1 = bf16[4,130,128]{2,1,0:T(8,128)(2,1)S(1)} collective-permute-done((bf16[4,130,128]{2,1,0:T(8,128)(2,1)S(1)}, bf16[4,130,128]{2,1,0:T(8,128)(2,1)S(1)}, u32[]{:S(2)}, u32[]{:S(2)}) %collective-permute-start.1) | collective-permute-done | bytes 133152 | tf_op jit(solution)/shard_map/ppermute | solution.py:33
  33.7 1.9 collective-permute-start.2
  35.6 15.3 %collective-permute-done.2 = bf16[4,130,128]{2,1,0:T(8,128)(2,1)S(1)} collective-permute-done((bf16[4,130,128]{2,1,0:T(8,128)(2,1)S(1)}, bf16[4,130,128]{2,1,0:T(8,128)(2,1)S(1)}, u32[]{:S(2)}, u32[]{:S(2)}) %collective-permute-start.2) | collective-permute-done | bytes 133152 | tf_op jit(solution)/shard_map/ppermute | solution.py:33
  51.5 1.9 collective-permute-start.3
  53.4 6.7 %collective-permute-start.6 = (bf16[1,512,1408]{2,1,0:T(8,128)(2,1)}, bf16[1,512,1408]{2,1,0:T(8,128)(2,1)}, u32[]{:S(2)}, u32[]{:S(2)}) collective-permute-start(bf16[1,512,1408]{2,1,0:T(8,128)(2,1)} %param.20), channel_id=1, source_target_pairs={{0,8},{8,0},{16,24},{24,16},{32,40},{40,32},{48,56},{56,48},{64,72... | collective-permute-start | bytes 4325384 | tf_op jit(solution)/shard_map/ppermute | solution.py:97
  60.2 11.1 %collective-permute-done.3 = bf16[4,130,128]{2,1,0:T(8,128)(2,1)S(1)} collective-permute-done((bf16[4,130,128]{2,1,0:T(8,128)(2,1)S(1)}, bf16[4,130,128]{2,1,0:T(8,128)(2,1)S(1)}, u32[]{:S(2)}, u32[]{:S(2)}) %collective-permute-start.3) | collective-permute-done | bytes 133152 | tf_op jit(solution)/shard_map/ppermute | solution.py:33
  71.8 1.3 collective-permute-start.4
  74.5 4.5 %collective-permute-done.4 = bf16[4,130,128]{2,1,0:T(8,128)(2,1)S(1)} collective-permute-done((bf16[4,130,128]{2,1,0:T(8,128)(2,1)S(1)}, bf16[4,130,128]{2,1,0:T(8,128)(2,1)S(1)}, u32[]{:S(2)}, u32[]{:S(2)}) %collective-permute-start.4) | collective-permute-done | bytes 133152 | tf_op jit(solution)/shard_map/ppermute | solution.py:33
  79.5 1.3 collective-permute-start.5
  81.0 6.9 %collective-permute-done.5 = bf16[4,130,128]{2,1,0:T(8,128)(2,1)S(1)} collective-permute-done((bf16[4,130,128]{2,1,0:T(8,128)(2,1)S(1)}, bf16[4,130,128]{2,1,0:T(8,128)(2,1)S(1)}, u32[]{:S(2)}, u32[]{:S(2)}) %collective-permute-start.5) | collective-permute-done | bytes 133152 | tf_op jit(solution)/shard_map/ppermute | solution.py:33
  88.2 8.4 %collective-permute-done.6 = bf16[1,512,1408]{2,1,0:T(8,128)(2,1)} collective-permute-done((bf16[1,512,1408]{2,1,0:T(8,128)(2,1)}, bf16[1,512,1408]{2,1,0:T(8,128)(2,1)}, u32[]{:S(2)}, u32[]{:S(2)}) %collective-permute-start.6) | collective-permute-done | bytes 1441824 | tf_op jit(solution)/shard_map/ppermute | solution.py:97
  97.7 12.4 %psum.7 = f32[256]{0:T(256)S(1)} all-reduce(f32[256]{0:T(256)S(1)} %get-tuple-element.25), channel_id=1, replica_groups=mesh['seq'=64,'head'=8] {'head'}, use_global_device_ids=true, to_apply=%region_6.7 | all-reduce | flops 256 | bytes 2048 | tf_op jit(solution)/shard_map/psum | solution.py:139
  111.7 13.4 %all-to-all-start = ((bf16[64,1,10,512]{3,2,1,0:T(8,128)(2,1)}), bf16[64,1,10,512]{3,2,1,0:T(8,128)(2,1)S(1)}, u32[]{:S(2)}, u32[]{:S(2)}) async-start(bf16[64,1,10,512]{3,2,1,0:T(8,128)(2,1)} %bitcast.8), calls=%async_computation | async-start | bytes 2097152 | tf_op jit(solution)/shard_map/all_to_all | solution.py:164
  125.1 50.7 %all-to-all-done = bf16[64,1,10,512]{3,2,1,0:T(8,128)(2,1)S(1)} async-done(((bf16[64,1,10,512]{3,2,1,0:T(8,128)(2,1)}), bf16[64,1,10,512]{3,2,1,0:T(8,128)(2,1)S(1)}, u32[]{:S(2)}, u32[]{:S(2)}) %all-to-all-start) | async-done | bytes 655392 | tf_op jit(solution)/shard_map/all_to_all | solution.py:164
  176.1 2.5 convolution_convert_fusion.1
  178.6 2.5 convolution_convert_fusion
  181.2 1.5 fusion.3
  183.0 1.9 collective-permute-start.7
  185.0 4.0 %collective-permute-done.7 = bf16[1,4,80,2816]{3,2,1,0:T(8,128)(2,1)} collective-permute-done((bf16[1,4,80,2816]{3,2,1,0:T(8,128)(2,1)}, bf16[1,4,80,2816]{3,2,1,0:T(8,128)(2,1)}, u32[]{:S(2)}, u32[]{:S(2)}) %collective-permute-start.7) | collective-permute-done | bytes 1802272 | tf_op jit(solution)/shard_map/ppermute | solution.py:58
  188.9 2.1 convert_add_fusion
  191.0 1.8 copy-done.1
  192.9 1.9 collective-permute-start.10
  194.8 3.7 %collective-permute-start.9 = (bf16[1,80,2816]{2,1,0:T(8,128)(2,1)S(1)}, bf16[1,80,2816]{2,1,0:T(8,128)(2,1)S(1)}, u32[]{:S(2)}, u32[]{:S(2)}) collective-permute-start(bf16[1,80,2816]{2,1,0:T(8,128)(2,1)S(1)} %get-tuple-element.45), channel_id=1, source_target_pairs={{0,4},{1,5},{2,6},{3,7},{4,0},{5,1},{6,2},{7,3},{8,12},{9,13},{10,... | collective-permute-start | bytes 1351688 | tf_op jit(solution)/shard_map/ppermute | solution.py:64
  198.5 3.4 collective-permute-start.8
  202.0 6.0 %collective-permute-done.10 = bf16[1,80,2816]{2,1,0:T(8,128)(2,1)S(1)} collective-permute-done((bf16[1,80,2816]{2,1,0:T(8,128)(2,1)S(1)}, bf16[1,80,2816]{2,1,0:T(8,128)(2,1)S(1)}, u32[]{:S(2)}, u32[]{:S(2)}) %collective-permute-start.10) | collective-permute-done | bytes 450592 | tf_op jit(solution)/shard_map/ppermute | solution.py:64
  208.0 3.5 %collective-permute-done.9 = bf16[1,80,2816]{2,1,0:T(8,128)(2,1)S(1)} collective-permute-done((bf16[1,80,2816]{2,1,0:T(8,128)(2,1)S(1)}, bf16[1,80,2816]{2,1,0:T(8,128)(2,1)S(1)}, u32[]{:S(2)}, u32[]{:S(2)}) %collective-permute-start.9) | collective-permute-done | bytes 450592 | tf_op jit(solution)/shard_map/ppermute | solution.py:64
  211.5 8.8 %collective-permute-done.8 = bf16[1,80,2816]{2,1,0:T(8,128)(2,1)S(1)} collective-permute-done((bf16[1,80,2816]{2,1,0:T(8,128)(2,1)S(1)}, bf16[1,80,2816]{2,1,0:T(8,128)(2,1)S(1)}, u32[]{:S(2)}, u32[]{:S(2)}) %collective-permute-start.8) | collective-permute-done | bytes 450592 | tf_op jit(solution)/shard_map/ppermute | solution.py:64
  220.3 1.4 fusion.27
  224.8 2.5 collective-permute-start.13
  227.3 3.6 %collective-permute-start.12 = (bf16[1,80,1408]{2,1,0:T(8,128)(2,1)S(1)}, bf16[1,80,1408]{2,1,0:T(8,128)(2,1)S(1)}, u32[]{:S(2)}, u32[]{:S(2)}) collective-permute-start(bf16[1,80,1408]{2,1,0:T(8,128)(2,1)S(1)} %multiply_convert_fusion.1), channel_id=1, source_target_pairs={{0,4},{1,5},{2,6},{3,7},{4,0},{5,1},{6,2},{7,3},{8,12},{9,13},{10,... | collective-permute-start | bytes 675848 | tf_op jit(solution)/shard_map/ppermute | solution.py:71
  230.9 2.7 collective-permute-start.11
  235.1 3.3 collective-permute-done.12
  238.3 4.0 %collective-permute-done.11 = bf16[1,80,1408]{2,1,0:T(8,128)(2,1)S(1)} collective-permute-done((bf16[1,80,1408]{2,1,0:T(8,128)(2,1)S(1)}, bf16[1,80,1408]{2,1,0:T(8,128)(2,1)S(1)}, u32[]{:S(2)}, u32[]{:S(2)}) %collective-permute-start.11) | collective-permute-done | bytes 225312 | tf_op jit(solution)/shard_map/ppermute | solution.py:71
  242.6 1.3 fusion.25
  243.9 1.9 collective-permute-start.14
  245.8 5.3 %collective-permute-start.15 = (bf16[1,704,512]{2,1,0:T(8,128)(2,1)}, bf16[1,704,512]{2,1,0:T(8,128)(2,1)}, u32[]{:S(2)}, u32[]{:S(2)}) collective-permute-start(bf16[1,704,512]{2,1,0:T(8,128)(2,1)} %param.21), channel_id=1, source_target_pairs={{0,8},{8,0},{16,24},{24,16},{32,40},{40,32},{48,56},{56,48},{64,72... | collective-permute-start | bytes 2162696 | tf_op jit(solution)/shard_map/ppermute | solution.py:98
  252.7 15.5 %collective-permute-done.15 = bf16[1,704,512]{2,1,0:T(8,128)(2,1)} collective-permute-done((bf16[1,704,512]{2,1,0:T(8,128)(2,1)}, bf16[1,704,512]{2,1,0:T(8,128)(2,1)}, u32[]{:S(2)}, u32[]{:S(2)}) %collective-permute-start.15) | collective-permute-done | bytes 720928 | tf_op jit(solution)/shard_map/ppermute | solution.py:98
  268.2 2.3 copy.169
  270.5 3.1 fusion.14
  273.6 1.2 reshape.540
  274.8 7.9 %all-to-all-start.1 = ((bf16[1,64,10,512]{3,2,0,1:T(8,128)(2,1)}), bf16[1,64,10,512]{3,2,0,1:T(8,128)(2,1)S(1)}, u32[]{:S(2)}, u32[]{:S(2)}) async-start(bf16[1,64,10,512]{3,2,0,1:T(8,128)(2,1)} %bitcast.30), calls=%async_computation.1 | async-start | bytes 2097152 | tf_op jit(solution)/shard_map/all_to_all | solution.py:182
  283.2 53.2 %all-to-all-done.1 = bf16[1,64,10,512]{3,2,0,1:T(8,128)(2,1)S(1)} async-done(((bf16[1,64,10,512]{3,2,0,1:T(8,128)(2,1)}), bf16[1,64,10,512]{3,2,0,1:T(8,128)(2,1)S(1)}, u32[]{:S(2)}, u32[]{:S(2)}) %all-to-all-start.1) | async-done | bytes 655392 | tf_op jit(solution)/shard_map/all_to_all | solution.py:182
  336.5 1.6 gather_fusion
  338.8 1.3 multiply_reduce_fusion
  (122 shorter events, 19.9 us)
Async XLA Ops:
  0.0 73.1 %copy-start = (bf16[256,512]{1,0:T(8,128)(2,1)S(1)}, bf16[256,512]{1,0:T(8,128)(2,1)}, u32[]{:S(2)}) copy-start(bf16[256,512]{1,0:T(8,128)(2,1)} %param.12) | copy-start | bytes 786436
  5.1 15.3 %collective-permute-start = (bf16[4,130,128]{2,1,0:T(8,128)(2,1)S(1)}, bf16[4,130,128]{2,1,0:T(8,128)(2,1)S(1)}, u32[]{:S(2)}, u32[]{:S(2)}) collective-permute-start(bf16[4,130,128]{2,1,0:T(8,128)(2,1)S(1)} %pad_maximum_fusion.1), channel_id=1, source_target_pairs={{0,8},{8,16},{16,24},{24,32},{32,40},{40,48},{48,56},{56,64},{64,7... | collective-permute-start | bytes 399368 | tf_op jit(solution)/shard_map/ppermute | solution.py:33
  20.8 52.3 %copy-start.3 = (bf16[256,512]{1,0:T(8,128)(2,1)S(1)}, bf16[256,512]{1,0:T(8,128)(2,1)}, u32[]{:S(2)}) copy-start(bf16[256,512]{1,0:T(8,128)(2,1)} %param.14) | copy-start | bytes 786436
  20.9 12.2 %collective-permute-start.1 = (bf16[4,130,128]{2,1,0:T(8,128)(2,1)S(1)}, bf16[4,130,128]{2,1,0:T(8,128)(2,1)S(1)}, u32[]{:S(2)}, u32[]{:S(2)}) collective-permute-start(bf16[4,130,128]{2,1,0:T(8,128)(2,1)S(1)} %pad_maximum_fusion.2), channel_id=1, source_target_pairs={{0,16},{8,24},{16,32},{24,40},{32,48},{40,56},{48,64},{56,72},{64,... | collective-permute-start | bytes 399368 | tf_op jit(solution)/shard_map/ppermute | solution.py:33
  33.7 17.3 %collective-permute-start.2 = (bf16[4,130,128]{2,1,0:T(8,128)(2,1)S(1)}, bf16[4,130,128]{2,1,0:T(8,128)(2,1)S(1)}, u32[]{:S(2)}, u32[]{:S(2)}) collective-permute-start(bf16[4,130,128]{2,1,0:T(8,128)(2,1)S(1)} %pad_maximum_fusion.3), channel_id=1, source_target_pairs={{0,32},{8,40},{16,48},{24,56},{32,64},{40,72},{48,80},{56,88},{64,... | collective-permute-start | bytes 399368 | tf_op jit(solution)/shard_map/ppermute | solution.py:33
  51.5 19.8 %collective-permute-start.3 = (bf16[4,130,128]{2,1,0:T(8,128)(2,1)S(1)}, bf16[4,130,128]{2,1,0:T(8,128)(2,1)S(1)}, u32[]{:S(2)}, u32[]{:S(2)}) collective-permute-start(bf16[4,130,128]{2,1,0:T(8,128)(2,1)S(1)} %pad_maximum_fusion.4), channel_id=1, source_target_pairs={{0,64},{8,72},{16,80},{24,88},{32,96},{40,104},{48,112},{56,120},{... | collective-permute-start | bytes 399368 | tf_op jit(solution)/shard_map/ppermute | solution.py:33
  53.4 43.2 %collective-permute-start.6 = (bf16[1,512,1408]{2,1,0:T(8,128)(2,1)}, bf16[1,512,1408]{2,1,0:T(8,128)(2,1)}, u32[]{:S(2)}, u32[]{:S(2)}) collective-permute-start(bf16[1,512,1408]{2,1,0:T(8,128)(2,1)} %param.20), channel_id=1, source_target_pairs={{0,8},{8,0},{16,24},{24,16},{32,40},{40,32},{48,56},{56,48},{64,72... | collective-permute-start | bytes 4325384 | tf_op jit(solution)/shard_map/ppermute | solution.py:97
  71.7 2.0 copy-start.5
  71.8 7.2 %collective-permute-start.4 = (bf16[4,130,128]{2,1,0:T(8,128)(2,1)S(1)}, bf16[4,130,128]{2,1,0:T(8,128)(2,1)S(1)}, u32[]{:S(2)}, u32[]{:S(2)}) collective-permute-start(bf16[4,130,128]{2,1,0:T(8,128)(2,1)S(1)} %pad_maximum_fusion.5), channel_id=1, source_target_pairs={{0,128},{8,136},{16,144},{24,152},{32,160},{40,168},{48,176},{56,1... | collective-permute-start | bytes 399368 | tf_op jit(solution)/shard_map/ppermute | solution.py:33
  79.5 8.5 %collective-permute-start.5 = (bf16[4,130,128]{2,1,0:T(8,128)(2,1)S(1)}, bf16[4,130,128]{2,1,0:T(8,128)(2,1)S(1)}, u32[]{:S(2)}, u32[]{:S(2)}) collective-permute-start(bf16[4,130,128]{2,1,0:T(8,128)(2,1)S(1)} %pad_maximum_fusion.6), channel_id=1, source_target_pairs={{0,256},{8,264},{16,272},{24,280},{32,288},{40,296},{48,304},{56,3... | collective-permute-start | bytes 399368 | tf_op jit(solution)/shard_map/ppermute | solution.py:33
  96.5 1.0 copy-start.4
  96.6 1.0 copy-start.6
  97.0 13.1 %copy-start.8 = (f32[512]{0:T(512)S(1)}, f32[512]{0:T(512)}, u32[]{:S(2)}) copy-start(f32[512]{0:T(512)} %param.17) | copy-start | bytes 6148
  111.7 64.1 %all-to-all-start = ((bf16[64,1,10,512]{3,2,1,0:T(8,128)(2,1)}), bf16[64,1,10,512]{3,2,1,0:T(8,128)(2,1)S(1)}, u32[]{:S(2)}, u32[]{:S(2)}) async-start(bf16[64,1,10,512]{3,2,1,0:T(8,128)(2,1)} %bitcast.8), calls=%async_computation | async-start | bytes 2097152 | tf_op jit(solution)/shard_map/all_to_all | solution.py:164
  181.2 1.8 copy-start.2
  183.0 6.0 %collective-permute-start.7 = (bf16[1,4,80,2816]{3,2,1,0:T(8,128)(2,1)}, bf16[1,4,80,2816]{3,2,1,0:T(8,128)(2,1)}, u32[]{:S(2)}, u32[]{:S(2)}) collective-permute-start(bf16[1,4,80,2816]{3,2,1,0:T(8,128)(2,1)} %fusion.3), channel_id=1, source_target_pairs={{0,1},{1,0},{2,3},{3,2},{4,5},{5,4},{6,7},{7,6},{8,9},{9,8},{10,11... | collective-permute-start | bytes 5406728 | tf_op jit(solution)/shard_map/ppermute | solution.py:58
  191.0 1.8 copy-start.1
  192.9 15.1 %collective-permute-start.10 = (bf16[1,80,2816]{2,1,0:T(8,128)(2,1)S(1)}, bf16[1,80,2816]{2,1,0:T(8,128)(2,1)S(1)}, u32[]{:S(2)}, u32[]{:S(2)}) collective-permute-start(bf16[1,80,2816]{2,1,0:T(8,128)(2,1)S(1)} %get-tuple-element.44), channel_id=1, source_target_pairs={{0,6},{1,7},{2,0},{3,1},{4,2},{5,3},{6,4},{7,5},{8,14},{9,15},{10,... | collective-permute-start | bytes 1351688 | tf_op jit(solution)/shard_map/ppermute | solution.py:64
  194.8 16.6 %collective-permute-start.9 = (bf16[1,80,2816]{2,1,0:T(8,128)(2,1)S(1)}, bf16[1,80,2816]{2,1,0:T(8,128)(2,1)S(1)}, u32[]{:S(2)}, u32[]{:S(2)}) collective-permute-start(bf16[1,80,2816]{2,1,0:T(8,128)(2,1)S(1)} %get-tuple-element.45), channel_id=1, source_target_pairs={{0,4},{1,5},{2,6},{3,7},{4,0},{5,1},{6,2},{7,3},{8,12},{9,13},{10,... | collective-permute-start | bytes 1351688 | tf_op jit(solution)/shard_map/ppermute | solution.py:64
  198.5 21.8 %collective-permute-start.8 = (bf16[1,80,2816]{2,1,0:T(8,128)(2,1)S(1)}, bf16[1,80,2816]{2,1,0:T(8,128)(2,1)S(1)}, u32[]{:S(2)}, u32[]{:S(2)}) collective-permute-start(bf16[1,80,2816]{2,1,0:T(8,128)(2,1)S(1)} %get-tuple-element.43), channel_id=1, source_target_pairs={{0,2},{1,3},{2,4},{3,5},{4,6},{5,7},{6,0},{7,1},{8,10},{9,11},{10,... | collective-permute-start | bytes 1351688 | tf_op jit(solution)/shard_map/ppermute | solution.py:64
  224.8 10.3 %collective-permute-start.13 = (bf16[1,80,1408]{2,1,0:T(8,128)(2,1)S(1)}, bf16[1,80,1408]{2,1,0:T(8,128)(2,1)S(1)}, u32[]{:S(2)}, u32[]{:S(2)}) collective-permute-start(bf16[1,80,1408]{2,1,0:T(8,128)(2,1)S(1)} %multiply_convert_fusion.1), channel_id=1, source_target_pairs={{0,6},{1,7},{2,0},{3,1},{4,2},{5,3},{6,4},{7,5},{8,14},{9,15},{10,... | collective-permute-start | bytes 675848 | tf_op jit(solution)/shard_map/ppermute | solution.py:71
  227.3 11.0 %collective-permute-start.12 = (bf16[1,80,1408]{2,1,0:T(8,128)(2,1)S(1)}, bf16[1,80,1408]{2,1,0:T(8,128)(2,1)S(1)}, u32[]{:S(2)}, u32[]{:S(2)}) collective-permute-start(bf16[1,80,1408]{2,1,0:T(8,128)(2,1)S(1)} %multiply_convert_fusion.1), channel_id=1, source_target_pairs={{0,4},{1,5},{2,6},{3,7},{4,0},{5,1},{6,2},{7,3},{8,12},{9,13},{10,... | collective-permute-start | bytes 675848 | tf_op jit(solution)/shard_map/ppermute | solution.py:71
  230.9 11.5 %collective-permute-start.11 = (bf16[1,80,1408]{2,1,0:T(8,128)(2,1)S(1)}, bf16[1,80,1408]{2,1,0:T(8,128)(2,1)S(1)}, u32[]{:S(2)}, u32[]{:S(2)}) collective-permute-start(bf16[1,80,1408]{2,1,0:T(8,128)(2,1)S(1)} %multiply_convert_fusion.1), channel_id=1, source_target_pairs={{0,2},{1,3},{2,4},{3,5},{4,6},{5,7},{6,0},{7,1},{8,10},{9,11},{10,... | collective-permute-start | bytes 675848 | tf_op jit(solution)/shard_map/ppermute | solution.py:71
  243.9 7.6 %collective-permute-start.14 = (bf16[1,4,80,1408]{3,2,1,0:T(8,128)(2,1)}, bf16[1,4,80,1408]{3,2,1,0:T(8,128)(2,1)S(1)}, u32[]{:S(2)}, u32[]{:S(2)}) collective-permute-start(bf16[1,4,80,1408]{3,2,1,0:T(8,128)(2,1)} %fusion.25), channel_id=1, source_target_pairs={{0,1},{1,0},{2,3},{3,2},{4,5},{5,4},{6,7},{7,6},{8,9},{9,8},{10,11... | collective-permute-start | bytes 2703368 | tf_op jit(solution)/shard_map/ppermute | solution.py:76
  245.8 22.4 %collective-permute-start.15 = (bf16[1,704,512]{2,1,0:T(8,128)(2,1)}, bf16[1,704,512]{2,1,0:T(8,128)(2,1)}, u32[]{:S(2)}, u32[]{:S(2)}) collective-permute-start(bf16[1,704,512]{2,1,0:T(8,128)(2,1)} %param.21), channel_id=1, source_target_pairs={{0,8},{8,0},{16,24},{24,16},{32,40},{40,32},{48,56},{56,48},{64,72... | collective-permute-start | bytes 2162696 | tf_op jit(solution)/shard_map/ppermute | solution.py:98
  273.6 9.4 %copy-start.7 = (f32[256,2]{0,1:T(2,128)S(1)}, f32[256,2]{0,1:T(2,128)}, u32[]{:S(2)}) copy-start(f32[256,2]{0,1:T(2,128)} %param.19) | copy-start | bytes 6148
  274.8 61.5 %all-to-all-start.1 = ((bf16[1,64,10,512]{3,2,0,1:T(8,128)(2,1)}), bf16[1,64,10,512]{3,2,0,1:T(8,128)(2,1)S(1)}, u32[]{:S(2)}, u32[]{:S(2)}) async-start(bf16[1,64,10,512]{3,2,0,1:T(8,128)(2,1)} %bitcast.30), calls=%async_computation.1 | async-start | bytes 2097152 | tf_op jit(solution)/shard_map/all_to_all | solution.py:182

commit v15 on v14

--- a/solution.py
+++ b/solution.py
@@ -122,7 +122,6 @@
     )
     block_decay = jnp.exp(cumulative[:, -1])
     entering = exclusive_scan(block_decay, block_state, "seq")
-    entering, other_in = lax.optimization_barrier((entering, other_in))
     from_before = jnp.einsum(
         "thd,hde->the",
         query_heads.astype(jnp.float32),
@@ -137,6 +136,7 @@
     hidden_wide = hidden_state.astype(jnp.float32)
     local_squares = jnp.sum(hidden_wide * hidden_wide, axis=1)
     total_squares = lax.psum(local_squares, "head")
+    total_squares, other_in = lax.optimization_barrier((total_squares, other_in))
     inverse_rms = lax.rsqrt(total_squares / D + EPSILON)
     expert_input = (hidden_wide * inverse_rms[:, None] * expert_gain).astype(jnp.bfloat16)
     capacity = CAP

time: 342 us -> 353 us (1.032)
  waiting for transfers between devices: 217 us -> 237 us
  starting transfers between devices: 67.1 us -> 59.1 us
    ppermute x6, waiting for transfers between devices: 59.5 us -> 82.3 us  [exclusive_scan(): got = lax.ppermute(pack_window(window_decay, window_state), axis, pairs)]
    ppermute x1, waiting for transfers between devices: 8.38 us -> 0.01 us  [per_device(): other_in = lax.ppermute(expert_in, 'seq', partner)]
    ppermute x1, starting transfers between devices: 6.72 us -> 2.76 us  [per_device(): other_in = lax.ppermute(expert_in, 'seq', partner)]
  transfers between devices with their start and end apart: 18 -> 18, of which waited for: 17 -> 16; matrix products, arithmetic and copies ran while one was open for 2% -> 2% of each run, Pallas kernels for 0% -> 0%
where the time goes in v15:
time: 353 us; the launch traced here: 352 us
  waiting for transfers between devices  237 us (67%)
  starting transfers between devices  59.1 us (17%)
  local copies, waits for them, and re-layouts  18 us (5%)
  other arithmetic  13.6 us (4%)
  blocking collectives  12.4 us (4%)
  matrix products  11.3 us (3%)
    ppermute x6, waiting for transfers between devices, exclusive_scan(): got = lax.ppermute(pack_window(window_decay, window_state), axis, pairs)  82.3 us
    all_to_all x1, waiting for transfers between devices, per_device(): lax.all_to_all(send_buffer, 'seq', split_axis=0, concat_axis=1, tiled=True)  53.2 us
    all_to_all x1, waiting for transfers between devices, per_device(): lax.all_to_all(summed, 'seq', split_axis=1, concat_axis=0, tiled=True)  53.2 us
    ppermute x3, waiting for transfers between devices, head_reduce_activate(): total = total + lax.ppermute(outgoing, axis, pairs).astype(jnp.float32)  19.7 us
    ppermute x1, waiting for transfers between devices, per_device(): other_out = lax.ppermute(expert_out, 'seq', partner)  15.9 us
    ppermute x6, starting transfers between devices, exclusive_scan(): got = lax.ppermute(pack_window(window_decay, window_state), axis, pairs)  15.5 us
    psum x1, blocking collectives, per_device(): total_squares = lax.psum(local_squares, 'head')  12.4 us
    all_to_all x1, starting transfers between devices, per_device(): lax.all_to_all(send_buffer, 'seq', split_axis=0, concat_axis=1, tiled=True)  11 us
  transfers between devices with their start and end apart: 18, of which 16 were waited for; matrix products, arithmetic and copies ran while one was open for 2% of the time, Pallas kernels for 0%

profile of v15, /device:TPU:6, one launch (start us, length us, event | category | flops | bytes accessed | tf_op | source)
XLA Modules:
  0.0 352.3 jit_solution(2986680854681582753)
XLA Ops:
  1.9 1.2 reduce-window.6
  5.1 3.8 %collective-permute-start = (bf16[4,130,128]{2,1,0:T(8,128)(2,1)S(1)}, bf16[4,130,128]{2,1,0:T(8,128)(2,1)S(1)}, u32[]{:S(2)}, u32[]{:S(2)}) collective-permute-start(bf16[4,130,128]{2,1,0:T(8,128)(2,1)S(1)} %pad_maximum_fusion.1), channel_id=1, source_target_pairs={{0,8},{8,16},{16,24},{24,32},{32,40},{40,48},{48,56},{56,64},{64,7... | collective-permute-start | bytes 399368 | tf_op jit(solution)/shard_map/ppermute | solution.py:33
  9.0 11.5 %collective-permute-done = bf16[4,130,128]{2,1,0:T(8,128)(2,1)S(1)} collective-permute-done((bf16[4,130,128]{2,1,0:T(8,128)(2,1)S(1)}, bf16[4,130,128]{2,1,0:T(8,128)(2,1)S(1)}, u32[]{:S(2)}, u32[]{:S(2)}) %collective-permute-start) | collective-permute-done | bytes 133152 | tf_op jit(solution)/shard_map/ppermute | solution.py:33
  20.9 1.9 collective-permute-start.1
  22.9 10.1 %collective-permute-done.1 = bf16[4,130,128]{2,1,0:T(8,128)(2,1)S(1)} collective-permute-done((bf16[4,130,128]{2,1,0:T(8,128)(2,1)S(1)}, bf16[4,130,128]{2,1,0:T(8,128)(2,1)S(1)}, u32[]{:S(2)}, u32[]{:S(2)}) %collective-permute-start.1) | collective-permute-done | bytes 133152 | tf_op jit(solution)/shard_map/ppermute | solution.py:33
  33.7 1.9 collective-permute-start.2
  35.6 2.8 collective-permute-start.6
  38.7 13.1 %collective-permute-done.2 = bf16[4,130,128]{2,1,0:T(8,128)(2,1)S(1)} collective-permute-done((bf16[4,130,128]{2,1,0:T(8,128)(2,1)S(1)}, bf16[4,130,128]{2,1,0:T(8,128)(2,1)S(1)}, u32[]{:S(2)}, u32[]{:S(2)}) %collective-permute-start.2) | collective-permute-done | bytes 133152 | tf_op jit(solution)/shard_map/ppermute | solution.py:33
  52.3 5.2 %collective-permute-start.3 = (bf16[4,130,128]{2,1,0:T(8,128)(2,1)S(1)}, bf16[4,130,128]{2,1,0:T(8,128)(2,1)S(1)}, u32[]{:S(2)}, u32[]{:S(2)}) collective-permute-start(bf16[4,130,128]{2,1,0:T(8,128)(2,1)S(1)} %pad_maximum_fusion.4), channel_id=1, source_target_pairs={{0,64},{8,72},{16,80},{24,88},{32,96},{40,104},{48,112},{56,120},{... | collective-permute-start | bytes 399368 | tf_op jit(solution)/shard_map/ppermute | solution.py:33
  58.1 35.6 %collective-permute-done.3 = bf16[4,130,128]{2,1,0:T(8,128)(2,1)S(1)} collective-permute-done((bf16[4,130,128]{2,1,0:T(8,128)(2,1)S(1)}, bf16[4,130,128]{2,1,0:T(8,128)(2,1)S(1)}, u32[]{:S(2)}, u32[]{:S(2)}) %collective-permute-start.3) | collective-permute-done | bytes 133152 | tf_op jit(solution)/shard_map/ppermute | solution.py:33
  94.2 1.3 collective-permute-start.4
  96.1 5.0 %collective-permute-done.4 = bf16[4,130,128]{2,1,0:T(8,128)(2,1)S(1)} collective-permute-done((bf16[4,130,128]{2,1,0:T(8,128)(2,1)S(1)}, bf16[4,130,128]{2,1,0:T(8,128)(2,1)S(1)}, u32[]{:S(2)}, u32[]{:S(2)}) %collective-permute-start.4) | collective-permute-done | bytes 133152 | tf_op jit(solution)/shard_map/ppermute | solution.py:33
  101.7 1.3 collective-permute-start.5
  103.2 6.9 %collective-permute-done.5 = bf16[4,130,128]{2,1,0:T(8,128)(2,1)S(1)} collective-permute-done((bf16[4,130,128]{2,1,0:T(8,128)(2,1)S(1)}, bf16[4,130,128]{2,1,0:T(8,128)(2,1)S(1)}, u32[]{:S(2)}, u32[]{:S(2)}) %collective-permute-start.5) | collective-permute-done | bytes 133152 | tf_op jit(solution)/shard_map/ppermute | solution.py:33
  111.2 12.4 %psum.7 = f32[256]{0:T(256)S(1)} all-reduce(f32[256]{0:T(256)S(1)} %get-tuple-element.25), channel_id=1, replica_groups=mesh['seq'=64,'head'=8] {'head'}, use_global_device_ids=true, to_apply=%region_6.7 | all-reduce | flops 256 | bytes 2048 | tf_op jit(solution)/shard_map/psum | solution.py:138
  125.3 11.0 %all-to-all-start = ((bf16[64,1,10,512]{3,2,1,0:T(8,128)(2,1)}), bf16[64,1,10,512]{3,2,1,0:T(8,128)(2,1)S(1)}, u32[]{:S(2)}, u32[]{:S(2)}) async-start(bf16[64,1,10,512]{3,2,1,0:T(8,128)(2,1)} %bitcast.8), calls=%async_computation | async-start | bytes 2097152 | tf_op jit(solution)/shard_map/all_to_all | solution.py:164
  136.4 53.2 %all-to-all-done = bf16[64,1,10,512]{3,2,1,0:T(8,128)(2,1)S(1)} async-done(((bf16[64,1,10,512]{3,2,1,0:T(8,128)(2,1)}), bf16[64,1,10,512]{3,2,1,0:T(8,128)(2,1)S(1)}, u32[]{:S(2)}, u32[]{:S(2)}) %all-to-all-start) | async-done | bytes 655392 | tf_op jit(solution)/shard_map/all_to_all | solution.py:164
  189.8 2.5 convolution_convert_fusion.1
  192.4 2.5 convolution_convert_fusion
  195.0 1.5 fusion.3
  196.8 1.9 collective-permute-start.7
  198.8 4.0 %collective-permute-done.7 = bf16[1,4,80,2816]{3,2,1,0:T(8,128)(2,1)} collective-permute-done((bf16[1,4,80,2816]{3,2,1,0:T(8,128)(2,1)}, bf16[1,4,80,2816]{3,2,1,0:T(8,128)(2,1)}, u32[]{:S(2)}, u32[]{:S(2)}) %collective-permute-start.7) | collective-permute-done | bytes 1802272 | tf_op jit(solution)/shard_map/ppermute | solution.py:58
  202.7 2.1 convert_add_fusion
  204.8 1.8 copy-done.1
  206.7 2.5 collective-permute-start.10
  209.2 2.8 collective-permute-start.9
  212.0 2.7 collective-permute-start.8
  214.7 7.1 %collective-permute-done.10 = bf16[1,80,2816]{2,1,0:T(8,128)(2,1)S(1)} collective-permute-done((bf16[1,80,2816]{2,1,0:T(8,128)(2,1)S(1)}, bf16[1,80,2816]{2,1,0:T(8,128)(2,1)S(1)}, u32[]{:S(2)}, u32[]{:S(2)}) %collective-permute-start.10) | collective-permute-done | bytes 450592 | tf_op jit(solution)/shard_map/ppermute | solution.py:64
  221.8 4.1 %collective-permute-done.9 = bf16[1,80,2816]{2,1,0:T(8,128)(2,1)S(1)} collective-permute-done((bf16[1,80,2816]{2,1,0:T(8,128)(2,1)S(1)}, bf16[1,80,2816]{2,1,0:T(8,128)(2,1)S(1)}, u32[]{:S(2)}, u32[]{:S(2)}) %collective-permute-start.9) | collective-permute-done | bytes 450592 | tf_op jit(solution)/shard_map/ppermute | solution.py:64
  225.9 8.5 %collective-permute-done.8 = bf16[1,80,2816]{2,1,0:T(8,128)(2,1)S(1)} collective-permute-done((bf16[1,80,2816]{2,1,0:T(8,128)(2,1)S(1)}, bf16[1,80,2816]{2,1,0:T(8,128)(2,1)S(1)}, u32[]{:S(2)}, u32[]{:S(2)}) %collective-permute-start.8) | collective-permute-done | bytes 450592 | tf_op jit(solution)/shard_map/ppermute | solution.py:64
  234.4 1.4 fusion.27
  238.9 2.5 collective-permute-start.13
  241.4 2.8 collective-permute-start.12
  244.2 2.7 collective-permute-start.11
  247.8 1.3 collective-permute-done.13
  249.1 3.3 collective-permute-done.12
  252.4 4.0 %collective-permute-done.11 = bf16[1,80,1408]{2,1,0:T(8,128)(2,1)S(1)} collective-permute-done((bf16[1,80,1408]{2,1,0:T(8,128)(2,1)S(1)}, bf16[1,80,1408]{2,1,0:T(8,128)(2,1)S(1)}, u32[]{:S(2)}, u32[]{:S(2)}) %collective-permute-start.11) | collective-permute-done | bytes 225312 | tf_op jit(solution)/shard_map/ppermute | solution.py:71
  256.7 1.3 fusion.25
  258.0 1.9 collective-permute-start.14
  259.9 3.2 collective-permute-start.15
  264.7 15.9 %collective-permute-done.15 = bf16[1,704,512]{2,1,0:T(8,128)(2,1)} collective-permute-done((bf16[1,704,512]{2,1,0:T(8,128)(2,1)}, bf16[1,704,512]{2,1,0:T(8,128)(2,1)}, u32[]{:S(2)}, u32[]{:S(2)}) %collective-permute-start.15) | collective-permute-done | bytes 720928 | tf_op jit(solution)/shard_map/ppermute | solution.py:98
  280.6 2.3 copy.169
  282.9 3.1 fusion.14
  286.0 1.2 reshape.540
  287.2 6.8 %all-to-all-start.1 = ((bf16[1,64,10,512]{3,2,0,1:T(8,128)(2,1)}), bf16[1,64,10,512]{3,2,0,1:T(8,128)(2,1)S(1)}, u32[]{:S(2)}, u32[]{:S(2)}) async-start(bf16[1,64,10,512]{3,2,0,1:T(8,128)(2,1)} %bitcast.30), calls=%async_computation.1 | async-start | bytes 2097152 | tf_op jit(solution)/shard_map/all_to_all | solution.py:182
  294.5 53.2 %all-to-all-done.1 = bf16[1,64,10,512]{3,2,0,1:T(8,128)(2,1)S(1)} async-done(((bf16[1,64,10,512]{3,2,0,1:T(8,128)(2,1)}), bf16[1,64,10,512]{3,2,0,1:T(8,128)(2,1)S(1)}, u32[]{:S(2)}, u32[]{:S(2)}) %all-to-all-start.1) | async-done | bytes 655392 | tf_op jit(solution)/shard_map/all_to_all | solution.py:182
  347.9 1.6 gather_fusion
  350.1 1.3 multiply_reduce_fusion
  (121 shorter events, 19.1 us)
Async XLA Ops:
  0.0 95.5 %copy-start = (bf16[256,512]{1,0:T(8,128)(2,1)S(1)}, bf16[256,512]{1,0:T(8,128)(2,1)}, u32[]{:S(2)}) copy-start(bf16[256,512]{1,0:T(8,128)(2,1)} %param.12) | copy-start | bytes 786436
  0.0 38.4 %copy-start.5 = (s32[256,2]{0,1:T(2,128)S(1)}, s32[256,2]{0,1:T(2,128)}, u32[]{:S(2)}) copy-start(s32[256,2]{0,1:T(2,128)} %param.18) | copy-start | bytes 6148
  5.1 15.3 %collective-permute-start = (bf16[4,130,128]{2,1,0:T(8,128)(2,1)S(1)}, bf16[4,130,128]{2,1,0:T(8,128)(2,1)S(1)}, u32[]{:S(2)}, u32[]{:S(2)}) collective-permute-start(bf16[4,130,128]{2,1,0:T(8,128)(2,1)S(1)} %pad_maximum_fusion.1), channel_id=1, source_target_pairs={{0,8},{8,16},{16,24},{24,32},{32,40},{40,48},{48,56},{56,64},{64,7... | collective-permute-start | bytes 399368 | tf_op jit(solution)/shard_map/ppermute | solution.py:33
  20.9 12.2 %collective-permute-start.1 = (bf16[4,130,128]{2,1,0:T(8,128)(2,1)S(1)}, bf16[4,130,128]{2,1,0:T(8,128)(2,1)S(1)}, u32[]{:S(2)}, u32[]{:S(2)}) collective-permute-start(bf16[4,130,128]{2,1,0:T(8,128)(2,1)S(1)} %pad_maximum_fusion.2), channel_id=1, source_target_pairs={{0,16},{8,24},{16,32},{24,40},{32,48},{40,56},{48,64},{56,72},{64,... | collective-permute-start | bytes 399368 | tf_op jit(solution)/shard_map/ppermute | solution.py:33
  33.6 62.0 %copy-start.3 = (bf16[256,512]{1,0:T(8,128)(2,1)S(1)}, bf16[256,512]{1,0:T(8,128)(2,1)}, u32[]{:S(2)}) copy-start(bf16[256,512]{1,0:T(8,128)(2,1)} %param.14) | copy-start | bytes 786436
  33.7 18.1 %collective-permute-start.2 = (bf16[4,130,128]{2,1,0:T(8,128)(2,1)S(1)}, bf16[4,130,128]{2,1,0:T(8,128)(2,1)S(1)}, u32[]{:S(2)}, u32[]{:S(2)}) collective-permute-start(bf16[4,130,128]{2,1,0:T(8,128)(2,1)S(1)} %pad_maximum_fusion.3), channel_id=1, source_target_pairs={{0,32},{8,40},{16,48},{24,56},{32,64},{40,72},{48,80},{56,88},{64,... | collective-permute-start | bytes 399368 | tf_op jit(solution)/shard_map/ppermute | solution.py:33
  35.6 88.1 %collective-permute-start.6 = (bf16[1,512,1408]{2,1,0:T(8,128)(2,1)}, bf16[1,512,1408]{2,1,0:T(8,128)(2,1)}, u32[]{:S(2)}, u32[]{:S(2)}) collective-permute-start(bf16[1,512,1408]{2,1,0:T(8,128)(2,1)} %param.20), channel_id=1, source_target_pairs={{0,8},{8,0},{16,24},{24,16},{32,40},{40,32},{48,56},{56,48},{64,72... | collective-permute-start | bytes 4325384 | tf_op jit(solution)/shard_map/ppermute | solution.py:97
  52.3 41.4 %collective-permute-start.3 = (bf16[4,130,128]{2,1,0:T(8,128)(2,1)S(1)}, bf16[4,130,128]{2,1,0:T(8,128)(2,1)S(1)}, u32[]{:S(2)}, u32[]{:S(2)}) collective-permute-start(bf16[4,130,128]{2,1,0:T(8,128)(2,1)S(1)} %pad_maximum_fusion.4), channel_id=1, source_target_pairs={{0,64},{8,72},{16,80},{24,88},{32,96},{40,104},{48,112},{56,120},{... | collective-permute-start | bytes 399368 | tf_op jit(solution)/shard_map/ppermute | solution.py:33
  94.2 6.9 %collective-permute-start.4 = (bf16[4,130,128]{2,1,0:T(8,128)(2,1)S(1)}, bf16[4,130,128]{2,1,0:T(8,128)(2,1)S(1)}, u32[]{:S(2)}, u32[]{:S(2)}) collective-permute-start(bf16[4,130,128]{2,1,0:T(8,128)(2,1)S(1)} %pad_maximum_fusion.5), channel_id=1, source_target_pairs={{0,128},{8,136},{16,144},{24,152},{32,160},{40,168},{48,176},{56,1... | collective-permute-start | bytes 399368 | tf_op jit(solution)/shard_map/ppermute | solution.py:33
  101.7 8.5 %collective-permute-start.5 = (bf16[4,130,128]{2,1,0:T(8,128)(2,1)S(1)}, bf16[4,130,128]{2,1,0:T(8,128)(2,1)S(1)}, u32[]{:S(2)}, u32[]{:S(2)}) collective-permute-start(bf16[4,130,128]{2,1,0:T(8,128)(2,1)S(1)} %pad_maximum_fusion.6), channel_id=1, source_target_pairs={{0,256},{8,264},{16,272},{24,280},{32,288},{40,296},{48,304},{56,3... | collective-permute-start | bytes 399368 | tf_op jit(solution)/shard_map/ppermute | solution.py:33
  110.1 1.0 copy-start.4
  110.1 1.0 copy-start.6
  110.7 12.9 %copy-start.8 = (f32[512]{0:T(512)S(1)}, f32[512]{0:T(512)}, u32[]{:S(2)}) copy-start(f32[512]{0:T(512)} %param.17) | copy-start | bytes 6148
  125.3 64.3 %all-to-all-start = ((bf16[64,1,10,512]{3,2,1,0:T(8,128)(2,1)}), bf16[64,1,10,512]{3,2,1,0:T(8,128)(2,1)S(1)}, u32[]{:S(2)}, u32[]{:S(2)}) async-start(bf16[64,1,10,512]{3,2,1,0:T(8,128)(2,1)} %bitcast.8), calls=%async_computation | async-start | bytes 2097152 | tf_op jit(solution)/shard_map/all_to_all | solution.py:164
  195.0 1.8 copy-start.2
  196.8 6.0 %collective-permute-start.7 = (bf16[1,4,80,2816]{3,2,1,0:T(8,128)(2,1)}, bf16[1,4,80,2816]{3,2,1,0:T(8,128)(2,1)}, u32[]{:S(2)}, u32[]{:S(2)}) collective-permute-start(bf16[1,4,80,2816]{3,2,1,0:T(8,128)(2,1)} %fusion.3), channel_id=1, source_target_pairs={{0,1},{1,0},{2,3},{3,2},{4,5},{5,4},{6,7},{7,6},{8,9},{9,8},{10,11... | collective-permute-start | bytes 5406728 | tf_op jit(solution)/shard_map/ppermute | solution.py:58
  204.8 1.8 copy-start.1
  206.7 15.1 %collective-permute-start.10 = (bf16[1,80,2816]{2,1,0:T(8,128)(2,1)S(1)}, bf16[1,80,2816]{2,1,0:T(8,128)(2,1)S(1)}, u32[]{:S(2)}, u32[]{:S(2)}) collective-permute-start(bf16[1,80,2816]{2,1,0:T(8,128)(2,1)S(1)} %get-tuple-element.44), channel_id=1, source_target_pairs={{0,6},{1,7},{2,0},{3,1},{4,2},{5,3},{6,4},{7,5},{8,14},{9,15},{10,... | collective-permute-start | bytes 1351688 | tf_op jit(solution)/shard_map/ppermute | solution.py:64
  209.2 16.7 %collective-permute-start.9 = (bf16[1,80,2816]{2,1,0:T(8,128)(2,1)S(1)}, bf16[1,80,2816]{2,1,0:T(8,128)(2,1)S(1)}, u32[]{:S(2)}, u32[]{:S(2)}) collective-permute-start(bf16[1,80,2816]{2,1,0:T(8,128)(2,1)S(1)} %get-tuple-element.45), channel_id=1, source_target_pairs={{0,4},{1,5},{2,6},{3,7},{4,0},{5,1},{6,2},{7,3},{8,12},{9,13},{10,... | collective-permute-start | bytes 1351688 | tf_op jit(solution)/shard_map/ppermute | solution.py:64
  212.0 22.4 %collective-permute-start.8 = (bf16[1,80,2816]{2,1,0:T(8,128)(2,1)S(1)}, bf16[1,80,2816]{2,1,0:T(8,128)(2,1)S(1)}, u32[]{:S(2)}, u32[]{:S(2)}) collective-permute-start(bf16[1,80,2816]{2,1,0:T(8,128)(2,1)S(1)} %get-tuple-element.43), channel_id=1, source_target_pairs={{0,2},{1,3},{2,4},{3,5},{4,6},{5,7},{6,0},{7,1},{8,10},{9,11},{10,... | collective-permute-start | bytes 1351688 | tf_op jit(solution)/shard_map/ppermute | solution.py:64
  238.9 10.3 %collective-permute-start.13 = (bf16[1,80,1408]{2,1,0:T(8,128)(2,1)S(1)}, bf16[1,80,1408]{2,1,0:T(8,128)(2,1)S(1)}, u32[]{:S(2)}, u32[]{:S(2)}) collective-permute-start(bf16[1,80,1408]{2,1,0:T(8,128)(2,1)S(1)} %multiply_convert_fusion.1), channel_id=1, source_target_pairs={{0,6},{1,7},{2,0},{3,1},{4,2},{5,3},{6,4},{7,5},{8,14},{9,15},{10,... | collective-permute-start | bytes 675848 | tf_op jit(solution)/shard_map/ppermute | solution.py:71
  241.4 11.0 %collective-permute-start.12 = (bf16[1,80,1408]{2,1,0:T(8,128)(2,1)S(1)}, bf16[1,80,1408]{2,1,0:T(8,128)(2,1)S(1)}, u32[]{:S(2)}, u32[]{:S(2)}) collective-permute-start(bf16[1,80,1408]{2,1,0:T(8,128)(2,1)S(1)} %multiply_convert_fusion.1), channel_id=1, source_target_pairs={{0,4},{1,5},{2,6},{3,7},{4,0},{5,1},{6,2},{7,3},{8,12},{9,13},{10,... | collective-permute-start | bytes 675848 | tf_op jit(solution)/shard_map/ppermute | solution.py:71
  244.2 12.3 %collective-permute-start.11 = (bf16[1,80,1408]{2,1,0:T(8,128)(2,1)S(1)}, bf16[1,80,1408]{2,1,0:T(8,128)(2,1)S(1)}, u32[]{:S(2)}, u32[]{:S(2)}) collective-permute-start(bf16[1,80,1408]{2,1,0:T(8,128)(2,1)S(1)} %multiply_convert_fusion.1), channel_id=1, source_target_pairs={{0,2},{1,3},{2,4},{3,5},{4,6},{5,7},{6,0},{7,1},{8,10},{9,11},{10,... | collective-permute-start | bytes 675848 | tf_op jit(solution)/shard_map/ppermute | solution.py:71
  258.0 5.6 %collective-permute-start.14 = (bf16[1,4,80,1408]{3,2,1,0:T(8,128)(2,1)}, bf16[1,4,80,1408]{3,2,1,0:T(8,128)(2,1)S(1)}, u32[]{:S(2)}, u32[]{:S(2)}) collective-permute-start(bf16[1,4,80,1408]{3,2,1,0:T(8,128)(2,1)} %fusion.25), channel_id=1, source_target_pairs={{0,1},{1,0},{2,3},{3,2},{4,5},{5,4},{6,7},{7,6},{8,9},{9,8},{10,11... | collective-permute-start | bytes 2703368 | tf_op jit(solution)/shard_map/ppermute | solution.py:76
  259.9 20.7 %collective-permute-start.15 = (bf16[1,704,512]{2,1,0:T(8,128)(2,1)}, bf16[1,704,512]{2,1,0:T(8,128)(2,1)}, u32[]{:S(2)}, u32[]{:S(2)}) collective-permute-start(bf16[1,704,512]{2,1,0:T(8,128)(2,1)} %param.21), channel_id=1, source_target_pairs={{0,8},{8,0},{16,24},{24,16},{32,40},{40,32},{48,56},{56,48},{64,72... | collective-permute-start | bytes 2162696 | tf_op jit(solution)/shard_map/ppermute | solution.py:98
  286.0 8.3 %copy-start.7 = (f32[256,2]{0,1:T(2,128)S(1)}, f32[256,2]{0,1:T(2,128)}, u32[]{:S(2)}) copy-start(f32[256,2]{0,1:T(2,128)} %param.19) | copy-start | bytes 6148
  287.2 60.5 %all-to-all-start.1 = ((bf16[1,64,10,512]{3,2,0,1:T(8,128)(2,1)}), bf16[1,64,10,512]{3,2,0,1:T(8,128)(2,1)S(1)}, u32[]{:S(2)}, u32[]{:S(2)}) async-start(bf16[1,64,10,512]{3,2,0,1:T(8,128)(2,1)} %bitcast.30), calls=%async_computation.1 | async-start | bytes 2097152 | tf_op jit(solution)/shard_map/all_to_all | solution.py:182
